TPU v7x, 128 devices: a whole 4x4x4 slice. The times are simulated.
128 devices in a mesh: ctx: 16 (over y_lo, z, core), head: 8 (over x, y_hi).
Axes of the slice: x: 4, y: 4 (y_hi: 2, y_lo: 2; y = y_hi * 2 + y_lo), z: 4, core: 2. Of those that a mesh axis runs over, the one named last changes fastest.
Arguments:
- hidden_in: bfloat16 [4096, 8192], P('ctx', 'head'), may hold values from -90 to 90
- query_rows: bfloat16 [4096, 8192], P('ctx', 'head'), may hold values from -5 to 5
- key_rows: bfloat16 [4096, 1024], P('ctx', 'head'), may hold values from -5 to 5
- value_rows: bfloat16 [4096, 1024], P('ctx', 'head'), may hold values from -6 to 6
- out_weight: bfloat16 [8192, 8192], P('head'), may hold values from -0.0625 to 0.0625
- grad_out: bfloat16 [4096, 8192], P('ctx', 'head'), may hold values from -6 to 6
- answer_mask: int32 [4096], P('ctx'), may hold values 0 or 1
Outputs:
- grad_query: bfloat16 [4096, 8192], P('ctx', 'head')
- grad_key: bfloat16 [4096, 1024], P('ctx', 'head')
- grad_value: bfloat16 [4096, 1024], P('ctx', 'head')
- fisher_q: float32 [16, 64], P('ctx', 'head')
- fisher_o: float32 [16, 64], P('ctx', 'head')
All inputs are finite; a program needn't handle non-finite values. No bound on the sum of `answer_mask` on one device may be relied on, other than what follows from the above.
Results may differ from a plain program's by a relative error of at most 0.019.
Values may be sent and summed in bfloat16 or wider, within the bound.
No kernel may reach another device: no remote copies, remote signals or barrier semaphores. Data moves between devices by JAX's collectives and lax.ppermute only.
A program may use at most 128 MiB of HBM per device.

v0:
```python
import math

import jax
import jax.numpy as jnp
from jax import lax
from jax.sharding import PartitionSpec as P

D = 8192
HEADS = 64
KVH = 8
HD = 128


NEGATIVE = -1e30
EPSILON = 1e-06


def block_scores(query_group, key_block, scaling, row_pos, col_pos):
    scores = (
        jnp.einsum("tgd,kd->tgk", query_group, key_block, preferred_element_type=jnp.float32)
        * scaling
    )
    return jnp.where(row_pos[:, None, None] >= col_pos[None, None, :], scores, NEGATIVE)


def head_squares(left_side, right_side, head_dim):
    product = lax.dot_general(
        left_side, right_side, (((0,), (0,)), ((), ())), preferred_element_type=jnp.float32
    )
    shaped = (product * product).reshape(
        product.shape[0], right_side.shape[1] // head_dim, head_dim
    )
    return jnp.sum(shaped, axis=(0, 2))


def body(hidden_in, query_rows, key_rows, value_rows, out_weight, grad_out, answer_mask):
    tok_dev = query_rows.shape[0]
    head_dim = HD
    group_size = HEADS // KVH
    local_groups = key_rows.shape[1] // head_dim
    scaling = head_dim ** (-0.5)
    own_index = lax.axis_index("ctx")
    first_row = own_index * tok_dev
    loss_weight = 0.25 + answer_mask.astype(jnp.float32)
    weighted = (grad_out.astype(jnp.float32) * loss_weight[:, None]).astype(jnp.bfloat16)
    keys_all, values_all = (
        lax.all_gather(key_rows, "ctx", axis=0, tiled=True),
        lax.all_gather(value_rows, "ctx", axis=0, tiled=True),
    )
    tokens = keys_all.shape[0]
    block_rows = math.gcd(512, tokens)

    def fetch(table, block_number):
        return lax.dynamic_slice_in_dim(table, block_number * block_rows, block_rows, 0)

    def column_pos(block_number):
        return block_number * block_rows + jnp.arange(block_rows, dtype=jnp.int32)

    buffer = jnp.zeros((tokens, 2 * local_groups * head_dim), jnp.float32)
    rows = query_rows.shape[0]
    row_pos = first_row + jnp.arange(rows, dtype=jnp.int32)
    needed = (first_row + rows - 1) // block_rows + 1
    query_heads = query_rows.reshape(rows, local_groups, group_size, head_dim)
    log_totals = []
    shared_head = 0
    query_group = query_heads[:, shared_head]

    def stats_step(block_number, carried):
        running_max, running_sum = carried
        key_block = fetch(keys_all, block_number)
        scores = block_scores(query_group, key_block, scaling, row_pos, column_pos(block_number))
        new_max = jnp.maximum(running_max, jnp.max(scores, axis=-1))
        running_sum = running_sum * jnp.exp(running_max - new_max) + jnp.sum(
            jnp.exp(scores - new_max[..., None]), axis=-1
        )
        return (new_max, running_sum)

    start_max = jnp.full((rows, group_size), NEGATIVE, jnp.float32)
    start_sum = jnp.zeros((rows, group_size), jnp.float32)
    running_max, running_sum = lax.fori_loop(0, needed, stats_step, (start_max, start_sum))
    log_total = running_max + jnp.log(running_sum)

    def value_step(block_number, accumulated):
        key_block = fetch(keys_all, block_number)
        value_block = fetch(values_all, block_number)
        scores = block_scores(query_group, key_block, scaling, row_pos, column_pos(block_number))
        rounded = jnp.exp(scores - log_total[..., None]).astype(jnp.bfloat16)
        return accumulated + jnp.einsum(
            "tgk,kd->tgd", rounded, value_block, preferred_element_type=jnp.float32
        )

    accumulated = lax.fori_loop(
        0, needed, value_step, jnp.zeros((rows, group_size, head_dim), jnp.float32)
    )
    log_totals.append(log_total)
    attended_list = [accumulated.astype(jnp.bfloat16)]
    attended_part = jnp.stack(attended_list, axis=1).reshape(
        rows, local_groups * group_size * head_dim
    )
    log_totals, attended = (log_totals, attended_part)
    piece_part = lax.all_gather(weighted, "head", axis=1, tiled=True)
    grad_sum = lax.dot_general(
        piece_part, out_weight, (((1,), (1,)), ((), ())), preferred_element_type=jnp.float32
    )
    grad_sum, squares_out = (grad_sum, head_squares(piece_part, attended, head_dim))
    grad_attended, squares_out = (grad_sum.astype(jnp.bfloat16), squares_out)
    backward_buffer = buffer
    rows = query_rows.shape[0]
    backward_row_pos = first_row + jnp.arange(rows, dtype=jnp.int32)
    needed = (first_row + rows - 1) // block_rows + 1
    query_heads = query_rows.reshape(rows, local_groups, group_size, head_dim)
    grad_heads = grad_attended.reshape(rows, local_groups, group_size, head_dim)
    attended_heads = attended.reshape(rows, local_groups, group_size, head_dim)
    shared_head = 0
    backward_query_group = query_heads[:, shared_head]
    grad_group = grad_heads[:, shared_head]
    backward_log_total = log_totals[shared_head]
    row_dot = jnp.sum(
        grad_group.astype(jnp.float32) * attended_heads[:, shared_head].astype(jnp.float32), axis=-1
    )
    key_column = jnp.int32(shared_head * head_dim)
    value_column = jnp.int32((local_groups + shared_head) * head_dim)

    def back_step(block_number, carried):
        query_sum, buffer_now = carried
        key_block = fetch(keys_all, block_number)
        value_block = fetch(values_all, block_number)
        scores = block_scores(
            backward_query_group, key_block, scaling, backward_row_pos, column_pos(block_number)
        )
        softmax = jnp.exp(scores - backward_log_total[..., None])
        rounded = softmax.astype(jnp.bfloat16)
        grad_prob = jnp.einsum(
            "tgd,kd->tgk", grad_group, value_block, preferred_element_type=jnp.float32
        )
        grad_score = (softmax * (grad_prob - row_dot[..., None]) * scaling).astype(jnp.bfloat16)
        query_sum = query_sum + jnp.einsum(
            "tgk,kd->tgd", grad_score, key_block, preferred_element_type=jnp.float32
        )
        key_part = jnp.einsum(
            "tgk,tgd->kd", grad_score, backward_query_group, preferred_element_type=jnp.float32
        )
        value_part = jnp.einsum(
            "tgk,tgd->kd", rounded, grad_group, preferred_element_type=jnp.float32
        )
        row_start = (block_number * block_rows).astype(jnp.int32)
        old_key = lax.dynamic_slice(buffer_now, (row_start, key_column), (block_rows, head_dim))
        buffer_now = lax.dynamic_update_slice(
            buffer_now, old_key + key_part, (row_start, key_column)
        )
        old_value = lax.dynamic_slice(buffer_now, (row_start, value_column), (block_rows, head_dim))
        buffer_now = lax.dynamic_update_slice(
            buffer_now, old_value + value_part, (row_start, value_column)
        )
        return (query_sum, buffer_now)

    start_query = jnp.zeros((rows, group_size, head_dim), jnp.float32)
    query_sum, backward_buffer = lax.fori_loop(0, needed, back_step, (start_query, backward_buffer))
    query_grads = [query_sum.astype(jnp.bfloat16)]
    grad_query_part = jnp.stack(query_grads, axis=1).reshape(
        rows, local_groups * group_size * head_dim
    )
    key_sums = lax.psum_scatter(
        backward_buffer.astype(jnp.bfloat16), "ctx", scatter_dimension=0, tiled=True
    ).astype(jnp.float32)
    grad_key = key_sums[:, : local_groups * head_dim].astype(jnp.bfloat16)
    grad_value = key_sums[:, local_groups * head_dim :].astype(jnp.bfloat16)
    squares_query = head_squares(
        lax.all_gather(hidden_in, "head", axis=1, tiled=True), grad_query_part, head_dim
    )
    normal_size = D * head_dim * tok_dev
    fisher_q = jnp.log(squares_query / normal_size + EPSILON).reshape(1, -1)
    fisher_o = jnp.log(squares_out / normal_size + EPSILON).reshape(1, -1)
    return (grad_query_part, grad_key, grad_value, fisher_q, fisher_o)


def solution(mesh):
    return jax.shard_map(
        body,
        mesh=mesh,
        in_specs=(
            P("ctx", "head"),
            P("ctx", "head"),
            P("ctx", "head"),
            P("ctx", "head"),
            P("head", None),
            P("ctx", "head"),
            P("ctx"),
        ),
        out_specs=(
            P("ctx", "head"),
            P("ctx", "head"),
            P("ctx", "head"),
            P("ctx", "head"),
            P("ctx", "head"),
        ),
        check_vma=False,
    )
```

profile of v0, /device:TPU:1, one launch (start us, length us, event | category | flops | bytes accessed | tf_op | source)
XLA Modules:
  0.0 328.2 jit_solution(14228058823165366588)
XLA Ops:
  9.4 2.0 multiply_convert_fusion
  12.0 1.2 copy.28
  13.6 32.4 %all-gather.5.cloned.1.call-done = bf16[4096,128]{1,0:T(8,128)(2,1)} async-done(((bf16[256,128]{1,0:T(8,128)(2,1)}), bf16[4096,128]{1,0:T(8,128)(2,1)}) %all-gather.5.cloned.1.call-update) | async-done | bytes 1048592 | tf_op jit(solution)/shard_map/all_gather | solution.py:47
  45.9 2.8 while.37
  46.1 1.7 fusion.94
  47.8 0.9 exponential_reduce_fusion.2
  48.7 31.5 %all-gather.7.cloned.1.call-done = bf16[4096,128]{1,0:T(8,128)(2,1)} async-done(((bf16[256,128]{1,0:T(8,128)(2,1)}), bf16[4096,128]{1,0:T(8,128)(2,1)}) %all-gather.7.cloned.1.call-update) | async-done | bytes 1048592 | tf_op jit(solution)/shard_map/all_gather | solution.py:48
  80.3 2.9 while.38
  80.5 2.7 fusion.98
  83.4 70.3 %all-gather.9.cloned.1.call-done = bf16[256,8192]{1,0:T(8,128)(2,1)} async-done(((bf16[256,1024]{1,0:T(8,128)(2,1)}), bf16[256,8192]{1,0:T(8,128)(2,1)}) %all-gather.9.cloned.1.call-update) | async-done | bytes 4194320 | tf_op jit(solution)/shard_map/all_gather | solution.py:101
  153.8 11.6 %convolution_convert_fusion = bf16[256,1024]{1,0:T(8,128)(2,1)S(1)} fusion(bf16[256,8192]{1,0:T(8,128)(2,1)} %all-gather.9.cloned.1.call-done, bf16[1024,8192]{1,0:T(8,128)(2,1)} %param.17), kind=kOutput, calls=%fused_computation.63 | convolution fusion | flops 4295229440 | bytes 21495808 | tf_op jit(solution)/shard_map/dot_general | solution.py:102
  166.1 2.2 broadcast_in_dim.48
  168.3 11.3 %while.39 = (s32[]{:T(128)}, f32[256,8,128]{2,0,1:T(8,128)S(1)}, f32[4096,256]{1,0:T(8,128)}, s32[]{:T(128)}, bf16[4096,128]{1,0:T(8,128)(2,1)}, /*index=5*/bf16...) while((s32[]{:T(128)}, f32[256,8,128]{2,0,1:T(8,128)S(1)}, ...), condition=%wide.region_8.9_spmd.clone, body=%wide.region_7.8_spmd.clone.sunk | while | flops 1354236672 | bytes 24934616 | solution.py:158
  168.5 1.6 fusion.109
  170.1 2.4 fusion.110
  172.6 1.8 convolution_add_fusion.2
  174.4 2.4 fusion.111
  176.8 2.8 fusion.112
  179.6 3.8 %convert_element_type.47 = bf16[4096,256]{1,0:T(8,128)(2,1)} convert(f32[4096,256]{1,0:T(8,128)} %get-tuple-element.150) | non-fusion elementwise | flops 1048576 | bytes 6291456 | tf_op jit(solution)/shard_map/convert_element_type | solution.py:164
  183.4 7.0 %multiply_reduce_fusion = f32[1024]{0:T(1024)S(1)} fusion(bf16[256,8192]{1,0:T(8,128)(2,1)} %all-gather.9.cloned.1.call-done, bf16[256,1024]{0,1:T(8,128)(2,1)S(1)} %bitcast.153), kind=kOutput, calls=%fused_computation.61 | convolution fusion | flops 4311743488 | bytes 4722688 | tf_op jit(solution)/shard_map/dot_general | solution.py:27
  190.7 34.7 %all-gather.11.cloned.1.call-done = bf16[256,8192]{1,0:T(8,128)(2,1)} async-done(((bf16[256,1024]{1,0:T(8,128)(2,1)}), bf16[256,8192]{1,0:T(8,128)(2,1)}) %all-gather.11.cloned.1.call-update) | async-done | bytes 4194320 | tf_op jit(solution)/shard_map/all_gather | solution.py:169
  225.4 7.1 %multiply_reduce_fusion.1 = f32[1024]{0:T(1024)S(1)} fusion(bf16[256,1024]{1,0:T(8,128)(2,1)S(1)} %copy_bitcast_fusion, bf16[256,8192]{1,0:T(8,128)(2,1)} %all-gather.11.cloned.1.call-done), kind=kOutput, calls=%fused_computation.62 | convolution fusion | flops 4311743488 | bytes 4722688 | tf_op jit(solution)/shard_map/dot_general | solution.py:27
  233.7 86.5 %reduce-scatter.2.cloned.1.call-done = bf16[256,256]{1,0:T(8,128)(2,1)} async-done(((bf16[4096,256]{1,0:T(8,128)(2,1)}), bf16[256,256]{1,0:T(8,128)(2,1)}) %reduce-scatter.2.cloned.1.call-update) | async-done | bytes 131088 | tf_op jit(solution)/shard_map/reduce_scatter | solution.py:163
  320.2 1.5 fusion.57
  (41 shorter events, 5.9 us)
Async XLA Ops:
  7.2 38.8 %all-gather.5.cloned.1.call-start = ((), (), s32[]{:S(2)}) async-start(), calls=%async_computation.1 | async-start | bytes 1114112 | tf_op jit(solution)/shard_map/all_gather | solution.py:47
  7.9 72.3 %all-gather.7.cloned.1.call-start = ((), (), s32[]{:S(2)}) async-start(), calls=%async_computation.2 | async-start | bytes 1114112 | tf_op jit(solution)/shard_map/all_gather | solution.py:48
  8.7 145.1 %all-gather.9.cloned.1.call-start = ((), (), s32[]{:S(2)}) async-start(), calls=%async_computation.3 | async-start | bytes 4718592 | tf_op jit(solution)/shard_map/all_gather | solution.py:101
  11.4 214.0 %all-gather.11.cloned.1.call-start = ((), (), s32[]{:S(2)}) async-start(), calls=%async_computation.5 | async-start | bytes 4718592 | tf_op jit(solution)/shard_map/all_gather | solution.py:169
  12.0 308.2 %reduce-scatter.2.cloned.1.call-start = ((), (), s32[]{:S(2)}) async-start(), calls=%async_computation.4 | async-start | bytes 2228224 | tf_op jit(solution)/shard_map/reduce_scatter | solution.py:163
  190.6 41.9 %copy-start = (bf16[256,1024]{1,0:T(8,128)(2,1)}, bf16[256,1024]{1,0:T(8,128)(2,1)S(1)}, u32[]{:S(2)}) copy-start(bf16[256,1024]{1,0:T(8,128)(2,1)S(1)} %copy_bitcast_fusion) | copy-start | bytes 1572868
Sparse Core Ops, SparseCore 0:
  9.7 36.1 all-gather.4
  47.6 32.5 all-gather.6
  83.1 70.5 all-gather.8
  156.0 69.3 all-gather.10
  227.6 92.4 reduce-scatter.1
where the time goes:
time: 333 us; the launch traced here: 328 us
  waiting for transfers between devices  257 us (77%)
  matrix products  41.2 us (12%)
  between operations  13.9 us (4%)
  other arithmetic  9.25 us (3%)
  local copies, waits for them, and re-layouts  6.17 us (2%)
    reduce_scatter x1, waiting for transfers between devices, body(): lax.psum_scatter(backward_buffer.astype(jnp.bfloat16), 'ctx', scatter_dim...  86.5 us
    all_gather x1, waiting for transfers between devices, body(): piece_part = lax.all_gather(weighted, 'head', axis=1, tiled=True)  70.3 us
    all_gather x1, waiting for transfers between devices, body(): lax.all_gather(hidden_in, 'head', axis=1, tiled=True)  34.7 us
    all_gather x1, waiting for transfers between devices, body(): lax.all_gather(key_rows, 'ctx', axis=0, tiled=True)  32.4 us
    all_gather x1, waiting for transfers between devices, body(): lax.all_gather(value_rows, 'ctx', axis=0, tiled=True)  31.5 us
    dot_general x2, matrix products, head_squares(): lax.dot_general(left_side, right_side, (((0,), (0,)), ((), ())), preferre...  14.2 us
    dot_general x1, matrix products, body(): lax.dot_general(piece_part, out_weight, (((1,), (1,)), ((), ())), preferr...  11.6 us
  transfers between devices with their start and end apart: 5, of which 5 were waited for; matrix products, arithmetic and copies ran while one was open for 17% of the time, Pallas kernels for 0%

commit v1 on v0

--- a/solution.py
+++ b/solution.py
@@ -31,6 +31,22 @@
         product.shape[0], right_side.shape[1] // head_dim, head_dim
     )
     return jnp.sum(shaped, axis=(0, 2))
+
+
+def gram_pair_squares(left_gram, right_side, head_dim):
+    rows = right_side.shape[0]
+    right_heads = right_side.reshape(rows, right_side.shape[1] // head_dim, head_dim)
+    right_gram = jnp.einsum(
+        "ihd,jhd->hij", right_heads, right_heads, preferred_element_type=jnp.float32
+    )
+    return jnp.sum(right_gram * left_gram[None], axis=(1, 2))
+
+
+def gram_squares(left_side, right_side, head_dim):
+    left_gram = lax.dot_general(
+        left_side, left_side, (((1,), (1,)), ((), ())), preferred_element_type=jnp.float32
+    )
+    return gram_pair_squares(left_gram, right_side, head_dim)
 
 
 def body(hidden_in, query_rows, key_rows, value_rows, out_weight, grad_out, answer_mask):
@@ -43,10 +59,17 @@
     first_row = own_index * tok_dev
     loss_weight = 0.25 + answer_mask.astype(jnp.float32)
     weighted = (grad_out.astype(jnp.float32) * loss_weight[:, None]).astype(jnp.bfloat16)
-    keys_all, values_all = (
-        lax.all_gather(key_rows, "ctx", axis=0, tiled=True),
-        lax.all_gather(value_rows, "ctx", axis=0, tiled=True),
-    )
+    hidden_gram = lax.psum(
+        lax.dot_general(
+            hidden_in, hidden_in, (((1,), (1,)), ((), ())), preferred_element_type=jnp.float32
+        ),
+        "head",
+    )
+    pair_all = lax.all_gather(
+        jnp.concatenate([key_rows, value_rows], axis=1), "ctx", axis=0, tiled=True
+    )
+    kv_width = key_rows.shape[1]
+    keys_all, values_all = (pair_all[:, :kv_width], pair_all[:, kv_width:])
     tokens = keys_all.shape[0]
     block_rows = math.gcd(512, tokens)
 
@@ -102,7 +125,7 @@
     grad_sum = lax.dot_general(
         piece_part, out_weight, (((1,), (1,)), ((), ())), preferred_element_type=jnp.float32
     )
-    grad_sum, squares_out = (grad_sum, head_squares(piece_part, attended, head_dim))
+    grad_sum, squares_out = (grad_sum, gram_squares(piece_part, attended, head_dim))
     grad_attended, squares_out = (grad_sum.astype(jnp.bfloat16), squares_out)
     backward_buffer = buffer
     rows = query_rows.shape[0]
@@ -165,9 +188,7 @@
     ).astype(jnp.float32)
     grad_key = key_sums[:, : local_groups * head_dim].astype(jnp.bfloat16)
     grad_value = key_sums[:, local_groups * head_dim :].astype(jnp.bfloat16)
-    squares_query = head_squares(
-        lax.all_gather(hidden_in, "head", axis=1, tiled=True), grad_query_part, head_dim
-    )
+    squares_query = gram_pair_squares(hidden_gram, grad_query_part, head_dim)
     normal_size = D * head_dim * tok_dev
     fisher_q = jnp.log(squares_query / normal_size + EPSILON).reshape(1, -1)
     fisher_o = jnp.log(squares_out / normal_size + EPSILON).reshape(1, -1)

time: 333 us -> 289 us (0.87)
  waiting for transfers between devices: 257 us -> 213 us
  matrix products: 41.2 us -> 33 us
  local copies, waits for them, and re-layouts: 6.17 us -> 11.4 us
  other arithmetic: 9.25 us -> 12.7 us
    all_gather x3 -> x1, waiting for transfers between devices: 98.6 us -> 32.2 us  [body(): lax.all_gather(jnp.concatenate([key_rows, value_rows], axis=1), 'ctx', ax...]
    psum x0 -> x1, waiting for transfers between devices: none -> 43 us  [body(): lax.psum(lax.dot_general(hidden_in, hidden_in, (((1,), (1,)), ((), ())),...]
    reduce_scatter x1, waiting for transfers between devices: 86.5 us -> 73 us  [body(): lax.psum_scatter(backward_buffer.astype(jnp.bfloat16), 'ctx', scatter_dim...]
    dot_general x2 -> x4, matrix products: 14.2 us -> 7.89 us  [the longest x1 4.84 us: gram_squares(): lax.dot_general(left_side, left_side, (((1,), (1,)), ((), ())), preferred...]
    all_gather x1, waiting for transfers between devices: 70.3 us -> 65.1 us  [body(): piece_part = lax.all_gather(weighted, 'head', axis=1, tiled=True)]
  transfers between devices with their start and end apart: 5 -> 4, of which waited for: 5 -> 4; matrix products, arithmetic and copies ran while one was open for 17% -> 19% of each run, Pallas kernels for 0% -> 0%
where the time goes in v1:
time: 289 us; the launch traced here: 285 us
  waiting for transfers between devices  213 us (74%)
  matrix products  33 us (11%)
  between operations  13.9 us (5%)
  other arithmetic  12.7 us (4%)
  local copies, waits for them, and re-layouts  11.4 us (4%)
    reduce_scatter x1, waiting for transfers between devices, body(): lax.psum_scatter(backward_buffer.astype(jnp.bfloat16), 'ctx', scatter_dim...  73 us
    all_gather x1, waiting for transfers between devices, body(): piece_part = lax.all_gather(weighted, 'head', axis=1, tiled=True)  65.1 us
    psum x1, waiting for transfers between devices, body(): lax.psum(lax.dot_general(hidden_in, hidden_in, (((1,), (1,)), ((), ())),...  43 us
    all_gather x1, waiting for transfers between devices, body(): lax.all_gather(jnp.concatenate([key_rows, value_rows], axis=1), 'ctx', ax...  32.2 us
    dot_general x1, matrix products, body(): lax.dot_general(piece_part, out_weight, (((1,), (1,)), ((), ())), preferr...  12.4 us
  transfers between devices with their start and end apart: 4, of which 4 were waited for; matrix products, arithmetic and copies ran while one was open for 19% of the time, Pallas kernels for 0%

profile of v1, /device:TPU:1, one launch (start us, length us, event | category | flops | bytes accessed | tf_op | source)
XLA Modules:
  0.0 284.6 jit_solution(4906694200121494240)
XLA Ops:
  7.2 1.6 pad_maximum_fusion
  9.6 2.0 multiply_convert_fusion
  12.8 1.2 copy.18
  14.3 1.1 copy.21
  15.4 32.2 %all-gather.3.cloned.1.call-done = bf16[4096,256]{1,0:T(8,128)(2,1)} async-done(((bf16[256,256]{1,0:T(8,128)(2,1)}), bf16[4096,256]{1,0:T(8,128)(2,1)}) %all-gather.3.cloned.1.call-update) | async-done | bytes 2097168 | tf_op jit(solution)/shard_map/all_gather | solution.py:68
  47.6 2.7 fusion.62
  50.3 1.9 while.37
  52.3 3.0 %while.38 = (s32[]{:T(128)}, f32[256,8,128]{2,0,1:T(8,128)S(1)}, s32[]{:T(128)}, bf16[4096,128]{1,0:T(8,128)(2,1)S(1)}, bf16[256,8,128]{2,1,0:T(8,128)(2,1)}, /*...) while((s32[]{:T(128)}, f32[256,8,128]{2,0,1:T(8,128)S(1)}, ...), condition=%wide.region_5.6_spmd.clone, body=%wide.region_4.5_spmd.clone.sunk | while | flops 541459200 | bytes 3161259 | solution.py:115
  52.5 2.8 fusion.104
  55.3 65.1 %all-gather.5.cloned.1.call-done = bf16[256,8192]{1,0:T(8,128)(2,1)} async-done(((bf16[256,1024]{1,0:T(8,128)(2,1)}), bf16[256,8192]{1,0:T(8,128)(2,1)}) %all-gather.5.cloned.1.call-update) | async-done | bytes 4194320 | tf_op jit(solution)/shard_map/all_gather | solution.py:124
  120.4 12.4 %fusion.59 = bf16[32,8,8,128]{3,2,1,0:T(8,128)(2,1)} fusion(bf16[256,8192]{1,0:T(8,128)(2,1)} %all-gather.5.cloned.1.call-done, bf16[1024,8192]{1,0:T(8,128)(2,1)} %param.17), kind=kOutput, calls=%fused_computation.65 | convolution fusion | flops 4295229440 | bytes 21495808 | tf_op jit(solution)/shard_map/dot_general | solution.py:125
  132.8 1.9 copy.36
  134.7 1.4 multiply_reduce_fusion.2
  136.2 2.2 broadcast_in_dim.50
  138.4 9.5 %while.39 = (s32[]{:T(128)}, f32[256,8,128]{2,0,1:T(8,128)S(1)}, f32[4096,256]{1,0:T(8,128)}, s32[]{:T(128)}, bf16[4096,128]{1,0:T(8,128)(2,1)S(1)}, /*index=5*/...) while((s32[]{:T(128)}, f32[256,8,128]{2,0,1:T(8,128)S(1)}, ...), condition=%wide.region_8.9_spmd.clone, body=%wide.region_7.8_spmd.clone.sunk | while | flops 1354236672 | bytes 27031796 | solution.py:181
  139.5 2.4 fusion.116
  142.8 2.4 fusion.117
  145.2 2.7 fusion.118
  148.0 3.8 %convert_element_type.47 = bf16[4096,256]{1,0:T(8,128)(2,1)} convert(f32[4096,256]{1,0:T(8,128)} %get-tuple-element.150) | non-fusion elementwise | flops 1048576 | bytes 6291456 | tf_op jit(solution)/shard_map/convert_element_type | solution.py:187
  151.8 4.8 %fusion.65 = f32[256,256]{1,0:T(8,128)S(1)} fusion(bf16[256,8192]{1,0:T(8,128)(2,1)} %all-gather.5.cloned.1.call-done), kind=kOutput, calls=%fused_computation.81 | convolution fusion | flops 1073741824 | bytes 4456448 | tf_op jit(solution)/shard_map/dot_general | solution.py:46
  157.2 43.0 %all-reduce.2.cloned.1.call-done = f32[256,256]{1,0:T(8,128)} async-done(((f32[256,256]{1,0:T(8,128)}), f32[256,256]{1,0:T(8,128)}) %all-reduce.2.cloned.1.call-update) | async-done | bytes 262160 | tf_op jit(solution)/shard_map/psum | solution.py:62
  200.2 1.5 multiply_reduce_fusion.1
  203.6 73.0 %reduce-scatter.2.cloned.1.call-done = bf16[256,256]{1,0:T(8,128)(2,1)} async-done(((bf16[4096,256]{1,0:T(8,128)(2,1)}), bf16[256,256]{1,0:T(8,128)(2,1)}) %reduce-scatter.2.cloned.1.call-update) | async-done | bytes 131088 | tf_op jit(solution)/shard_map/reduce_scatter | solution.py:186
  276.6 1.5 fusion.63
  (44 shorter events, 8.8 us)
Async XLA Ops:
  7.2 4.5 %copy-start = (bf16[256,1024]{1,0:T(8,128)(2,1)S(1)}, bf16[256,1024]{1,0:T(8,128)(2,1)}, u32[]{:S(2)}) copy-start(bf16[256,1024]{1,0:T(8,128)(2,1)} %param.13) | copy-start | bytes 1572868
  7.2 40.4 %all-gather.3.cloned.1.call-start = ((), (), s32[]{:S(2)}) async-start(), calls=%async_computation.1 | async-start | bytes 2228224 | tf_op jit(solution)/shard_map/all_gather | solution.py:68
  8.8 111.6 %all-gather.5.cloned.1.call-start = ((), (), s32[]{:S(2)}) async-start(), calls=%async_computation.2 | async-start | bytes 4718592 | tf_op jit(solution)/shard_map/all_gather | solution.py:124
  11.6 188.6 %all-reduce.2.cloned.1.call-start = ((), (), s32[]{:S(2)}) async-start(), calls=%async_computation.4 | async-start | bytes 524288 | tf_op jit(solution)/shard_map/psum | solution.py:62
  12.7 263.9 %reduce-scatter.2.cloned.1.call-start = ((), (), s32[]{:S(2)}) async-start(), calls=%async_computation.3 | async-start | bytes 2228224 | tf_op jit(solution)/shard_map/reduce_scatter | solution.py:186
  55.3 79.4 %copy-start.1 = (f32[256,8,128]{2,0,1:T(8,128)}, f32[256,8,128]{2,0,1:T(8,128)S(1)}, u32[]{:S(2)}) copy-start(f32[256,8,128]{2,0,1:T(8,128)S(1)} %get-tuple-element.148) | copy-start | bytes 3145732
  138.4 1.0 copy-start.3
  151.8 4.9 %copy-start.2 = (f32[256,8,128]{2,0,1:T(8,128)S(1)}, f32[256,8,128]{2,0,1:T(8,128)}, u32[]{:S(2)}) copy-start(f32[256,8,128]{2,0,1:T(8,128)} %copy-done.1) | copy-start | bytes 3145732
Sparse Core Ops, SparseCore 0:
  9.7 37.8 all-gather.2
  49.9 70.4 all-gather.4
  122.9 77.2 all-reduce.1
  202.6 73.9 reduce-scatter.1

commit v2 on v1

--- a/solution.py
+++ b/solution.py
@@ -31,6 +31,16 @@
         product.shape[0], right_side.shape[1] // head_dim, head_dim
     )
     return jnp.sum(shaped, axis=(0, 2))
+
+
+def butterfly_sum(value, axis_name):
+    size = lax.axis_size(axis_name)
+    stride = 1
+    while stride < size:
+        pairs = [(i, i ^ stride) for i in range(size)]
+        value = value + lax.ppermute(value, axis_name, pairs)
+        stride *= 2
+    return value
 
 
 def gram_pair_squares(left_gram, right_side, head_dim):
@@ -59,7 +69,7 @@
     first_row = own_index * tok_dev
     loss_weight = 0.25 + answer_mask.astype(jnp.float32)
     weighted = (grad_out.astype(jnp.float32) * loss_weight[:, None]).astype(jnp.bfloat16)
-    hidden_gram = lax.psum(
+    hidden_gram = butterfly_sum(
         lax.dot_general(
             hidden_in, hidden_in, (((1,), (1,)), ((), ())), preferred_element_type=jnp.float32
         ),

time: 289 us -> 289 us (level)
    psum x1 -> x0, waiting for transfers between devices: 43 us -> none  [body(): lax.psum(lax.dot_general(hidden_in, hidden_in, (((1,), (1,)), ((), ())),...]
    reduce_scatter x1, waiting for transfers between devices: 73 us -> 95.7 us  [body(): lax.psum_scatter(backward_buffer.astype(jnp.bfloat16), 'ctx', scatter_dim...]
    ppermute x0 -> x3, waiting for transfers between devices: none -> 19.2 us  [butterfly_sum(): value = value + lax.ppermute(value, axis_name, pairs)]
  transfers between devices with their start and end apart: 4 -> 6, of which waited for: 4 -> 6; matrix products, arithmetic and copies ran while one was open for 19% -> 7% of each run, Pallas kernels for 0% -> 0%
where the time goes in v2:
time: 289 us; the launch traced here: 285 us
  waiting for transfers between devices  213 us (74%)
  matrix products  31.3 us (11%)
  between operations  13.9 us (5%)
  other arithmetic  12.7 us (4%)
  local copies, waits for them, and re-layouts  11.3 us (4%)
    reduce_scatter x1, waiting for transfers between devices, body(): lax.psum_scatter(backward_buffer.astype(jnp.bfloat16), 'ctx', scatter_dim...  95.7 us
    all_gather x1, waiting for transfers between devices, body(): piece_part = lax.all_gather(weighted, 'head', axis=1, tiled=True)  65.2 us
    all_gather x1, waiting for transfers between devices, body(): lax.all_gather(jnp.concatenate([key_rows, value_rows], axis=1), 'ctx', ax...  33.3 us
    ppermute x3, waiting for transfers between devices, butterfly_sum(): value = value + lax.ppermute(value, axis_name, pairs)  19.2 us
    dot_general x1, matrix products, body(): lax.dot_general(piece_part, out_weight, (((1,), (1,)), ((), ())), preferr...  12.4 us
  transfers between devices with their start and end apart: 6, of which 6 were waited for; matrix products, arithmetic and copies ran while one was open for 7% of the time, Pallas kernels for 0%

profile of v2, /device:TPU:1, one launch (start us, length us, event | category | flops | bytes accessed | tf_op | source)
XLA Modules:
  0.0 284.7 jit_solution(7135431936659293070)
XLA Ops:
  7.2 1.6 pad_maximum_fusion
  9.6 2.0 multiply_convert_fusion
  14.2 33.3 %all-gather.3.cloned.1.call-done = bf16[4096,256]{1,0:T(8,128)(2,1)} async-done(((bf16[256,256]{1,0:T(8,128)(2,1)}), bf16[4096,256]{1,0:T(8,128)(2,1)}) %all-gather.3.cloned.1.call-update) | async-done | bytes 2097168 | tf_op jit(solution)/shard_map/all_gather | solution.py:78
  47.6 2.7 fusion.65
  50.3 1.9 while.37
  52.3 3.0 %while.38 = (s32[]{:T(128)}, f32[256,8,128]{2,0,1:T(8,128)S(1)}, s32[]{:T(128)}, bf16[4096,128]{1,0:T(8,128)(2,1)S(1)}, bf16[256,8,128]{2,1,0:T(8,128)(2,1)}, /*...) while((s32[]{:T(128)}, f32[256,8,128]{2,0,1:T(8,128)S(1)}, ...), condition=%wide.region_5.6_spmd.clone, body=%wide.region_4.5_spmd.clone.sunk | while | flops 541459200 | bytes 3161259 | solution.py:125
  52.5 2.8 fusion.107
  55.3 65.2 %all-gather.5.cloned.1.call-done = bf16[256,8192]{1,0:T(8,128)(2,1)} async-done(((bf16[256,1024]{1,0:T(8,128)(2,1)}), bf16[256,8192]{1,0:T(8,128)(2,1)}) %all-gather.5.cloned.1.call-update) | async-done | bytes 4194320 | tf_op jit(solution)/shard_map/all_gather | solution.py:134
  120.4 12.4 %fusion.59 = bf16[32,8,8,128]{3,2,1,0:T(8,128)(2,1)} fusion(bf16[256,8192]{1,0:T(8,128)(2,1)} %all-gather.5.cloned.1.call-done, bf16[1024,8192]{1,0:T(8,128)(2,1)} %param.17), kind=kOutput, calls=%fused_computation.65 | convolution fusion | flops 4295229440 | bytes 21495808 | tf_op jit(solution)/shard_map/dot_general | solution.py:135
  132.8 1.9 copy.36
  134.7 1.4 multiply_reduce_fusion.2
  136.2 2.2 broadcast_in_dim.50
  138.4 9.5 %while.39 = (s32[]{:T(128)}, f32[256,8,128]{2,0,1:T(8,128)S(1)}, f32[4096,256]{1,0:T(8,128)}, s32[]{:T(128)}, bf16[4096,128]{1,0:T(8,128)(2,1)S(1)}, /*index=5*/...) while((s32[]{:T(128)}, f32[256,8,128]{2,0,1:T(8,128)S(1)}, ...), condition=%wide.region_8.9_spmd.clone, body=%wide.region_7.8_spmd.clone.sunk | while | flops 1354236672 | bytes 27031796 | solution.py:191
  139.5 2.4 fusion.119
  142.8 2.4 fusion.120
  145.2 2.7 fusion.121
  147.9 3.7 %convert_element_type.47 = bf16[4096,256]{1,0:T(8,128)(2,1)} convert(f32[4096,256]{1,0:T(8,128)} %get-tuple-element.150) | non-fusion elementwise | flops 1048576 | bytes 6291456 | tf_op jit(solution)/shard_map/convert_element_type | solution.py:197
  152.4 8.0 %collective-permute-done = f32[256,256]{1,0:T(8,128)S(1)} collective-permute-done((f32[256,256]{1,0:T(8,128)S(1)}, f32[256,256]{1,0:T(8,128)S(1)}, u32[]{:S(2)}, u32[]{:S(2)}) %collective-permute-start) | collective-permute-done | bytes 262176 | tf_op jit(solution)/shard_map/ppermute | solution.py:41
  160.5 5.7 %collective-permute-done.1 = f32[256,256]{1,0:T(8,128)S(1)} collective-permute-done((f32[256,256]{1,0:T(8,128)S(1)}, f32[256,256]{1,0:T(8,128)S(1)}, u32[]{:S(2)}, u32[]{:S(2)}) %collective-permute-start.1) | collective-permute-done | bytes 262176 | tf_op jit(solution)/shard_map/ppermute | solution.py:41
  166.3 1.3 collective-permute-start.2
  167.6 5.5 %collective-permute-done.2 = f32[256,256]{1,0:T(8,128)S(1)} collective-permute-done((f32[256,256]{1,0:T(8,128)S(1)}, f32[256,256]{1,0:T(8,128)S(1)}, u32[]{:S(2)}, u32[]{:S(2)}) %collective-permute-start.2) | collective-permute-done | bytes 262176 | tf_op jit(solution)/shard_map/ppermute | solution.py:41
  173.1 4.8 %fusion.68 = f32[256,256]{1,0:T(8,128)S(1)} fusion(bf16[256,8192]{1,0:T(8,128)(2,1)} %all-gather.5.cloned.1.call-done), kind=kOutput, calls=%fused_computation.82 | convolution fusion | flops 1073741824 | bytes 4456448 | tf_op jit(solution)/shard_map/dot_general | solution.py:56
  181.0 95.7 %reduce-scatter.2.cloned.1.call-done = bf16[256,256]{1,0:T(8,128)(2,1)} async-done(((bf16[4096,256]{1,0:T(8,128)(2,1)}), bf16[256,256]{1,0:T(8,128)(2,1)}) %reduce-scatter.2.cloned.1.call-update) | async-done | bytes 131088 | tf_op jit(solution)/shard_map/reduce_scatter | solution.py:196
  276.7 1.5 fusion.66
  (50 shorter events, 11.4 us)
Async XLA Ops:
  7.2 144.5 %copy-start = (bf16[256,1024]{1,0:T(8,128)(2,1)S(1)}, bf16[256,1024]{1,0:T(8,128)(2,1)}, u32[]{:S(2)}) copy-start(bf16[256,1024]{1,0:T(8,128)(2,1)} %param.13) | copy-start | bytes 1572868
  7.2 40.4 %all-gather.3.cloned.1.call-start = ((), (), s32[]{:S(2)}) async-start(), calls=%async_computation.1 | async-start | bytes 2228224 | tf_op jit(solution)/shard_map/all_gather | solution.py:78
  8.8 111.6 %all-gather.5.cloned.1.call-start = ((), (), s32[]{:S(2)}) async-start(), calls=%async_computation.2 | async-start | bytes 4718592 | tf_op jit(solution)/shard_map/all_gather | solution.py:134
  11.6 265.1 %reduce-scatter.2.cloned.1.call-start = ((), (), s32[]{:S(2)}) async-start(), calls=%async_computation.3 | async-start | bytes 2228224 | tf_op jit(solution)/shard_map/reduce_scatter | solution.py:196
  55.3 79.4 %copy-start.1 = (f32[256,8,128]{2,0,1:T(8,128)}, f32[256,8,128]{2,0,1:T(8,128)S(1)}, u32[]{:S(2)}) copy-start(f32[256,8,128]{2,0,1:T(8,128)S(1)} %get-tuple-element.148) | copy-start | bytes 3145732
  138.4 1.0 copy-start.3
  152.0 8.3 %collective-permute-start = (f32[256,256]{1,0:T(8,128)S(1)}, f32[256,256]{1,0:T(8,128)S(1)}, u32[]{:S(2)}, u32[]{:S(2)}) collective-permute-start(f32[256,256]{1,0:T(8,128)S(1)} %fusion.67), channel_id=1, source_target_pairs={{0,1},{1,0},{2,3},{3,2},{4,5},{5,4},{6,7},{7,6},{8,9},{9,8},{10,11... | collective-permute-start | bytes 786440 | tf_op jit(solution)/shard_map/ppermute | solution.py:41
  160.4 5.9 %collective-permute-start.1 = (f32[256,256]{1,0:T(8,128)S(1)}, f32[256,256]{1,0:T(8,128)S(1)}, u32[]{:S(2)}, u32[]{:S(2)}) collective-permute-start(f32[256,256]{1,0:T(8,128)S(1)} %add.135), channel_id=1, source_target_pairs={{0,2},{1,3},{2,0},{3,1},{4,6},{5,7},{6,4},{7,5},{8,10},{9,11},{10,... | collective-permute-start | bytes 786440 | tf_op jit(solution)/shard_map/ppermute | solution.py:41
  166.3 6.8 %collective-permute-start.2 = (f32[256,256]{1,0:T(8,128)S(1)}, f32[256,256]{1,0:T(8,128)S(1)}, u32[]{:S(2)}, u32[]{:S(2)}) collective-permute-start(f32[256,256]{1,0:T(8,128)S(1)} %add.136), channel_id=1, source_target_pairs={{0,4},{1,5},{2,6},{3,7},{4,0},{5,1},{6,2},{7,3},{8,12},{9,13},{10,... | collective-permute-start | bytes 786440 | tf_op jit(solution)/shard_map/ppermute | solution.py:41
  173.1 4.8 %copy-start.2 = (f32[256,8,128]{2,0,1:T(8,128)S(1)}, f32[256,8,128]{2,0,1:T(8,128)}, u32[]{:S(2)}) copy-start(f32[256,8,128]{2,0,1:T(8,128)} %copy-done.1) | copy-start | bytes 3145732
Sparse Core Ops, SparseCore 0:
  9.7 37.8 all-gather.2
  49.9 70.4 all-gather.4
  151.8 124.7 reduce-scatter.1

commit v3 on v2

--- a/solution.py
+++ b/solution.py
@@ -3,6 +3,8 @@
 import jax
 import jax.numpy as jnp
 from jax import lax
+from jax.experimental import pallas as pl
+from jax.experimental.pallas import tpu as pltpu
 from jax.sharding import PartitionSpec as P
 
 D = 8192
@@ -31,6 +33,86 @@
         product.shape[0], right_side.shape[1] // head_dim, head_dim
     )
     return jnp.sum(shaped, axis=(0, 2))
+
+
+def flash_backward(query_rows, grad_attended, keys_all, values_all, log_total, row_dot, first_row, head_dim, block_rows):
+    rows, width = query_rows.shape
+    heads = width // head_dim
+    tokens = keys_all.shape[0]
+    blocks = tokens // block_rows
+    scaling = head_dim ** (-0.5)
+    needed = (first_row + rows - 1) // block_rows + 1
+    scalars = jnp.stack([needed, first_row]).astype(jnp.int32)
+
+    def kernel(scalar_ref, q_ref, do_ref, k_ref, v_ref, lt_ref, rd_ref, dq_ref, dkv_ref, dq_acc):
+        j = pl.program_id(0)
+
+        @pl.when(j == 0)
+        def _():
+            dq_acc[...] = jnp.zeros_like(dq_acc)
+
+        @pl.when(j < scalar_ref[0])
+        def _():
+            k = k_ref[...]
+            v = v_ref[...]
+            row_pos = scalar_ref[1] + lax.broadcasted_iota(jnp.int32, (rows, block_rows), 0)
+            col_pos = j * block_rows + lax.broadcasted_iota(jnp.int32, (rows, block_rows), 1)
+            keep = row_pos >= col_pos
+            dk = jnp.zeros((block_rows, head_dim), jnp.float32)
+            dv = jnp.zeros((block_rows, head_dim), jnp.float32)
+            for h in range(heads):
+                cols = slice(h * head_dim, (h + 1) * head_dim)
+                q = q_ref[:, cols]
+                do = do_ref[:, cols]
+                s = lax.dot_general(q, k, (((1,), (1,)), ((), ())), preferred_element_type=jnp.float32) * scaling
+                s = jnp.where(keep, s, NEGATIVE)
+                p = jnp.exp(s - lt_ref[:, h : h + 1])
+                dp = lax.dot_general(do, v, (((1,), (1,)), ((), ())), preferred_element_type=jnp.float32)
+                ds = (p * (dp - rd_ref[:, h : h + 1]) * scaling).astype(jnp.bfloat16)
+                dq_acc[:, cols] += jnp.dot(ds, k, preferred_element_type=jnp.float32)
+                dk += lax.dot_general(ds, q, (((0,), (0,)), ((), ())), preferred_element_type=jnp.float32)
+                dv += lax.dot_general(p.astype(jnp.bfloat16), do, (((0,), (0,)), ((), ())), preferred_element_type=jnp.float32)
+            dkv_ref[:, :head_dim] = dk.astype(dkv_ref.dtype)
+            dkv_ref[:, head_dim:] = dv.astype(dkv_ref.dtype)
+
+        @pl.when(j >= scalar_ref[0])
+        def _():
+            dkv_ref[...] = jnp.zeros_like(dkv_ref)
+
+        @pl.when(j == blocks - 1)
+        def _():
+            dq_ref[...] = dq_acc[...].astype(dq_ref.dtype)
+
+    def kv_map(j, s):
+        return (jnp.minimum(j, s[0] - 1), 0)
+
+    full = lambda j, s: (0, 0)
+    grid_spec = pltpu.PrefetchScalarGridSpec(
+        num_scalar_prefetch=1,
+        grid=(blocks,),
+        in_specs=[
+            pl.BlockSpec((rows, width), full),
+            pl.BlockSpec((rows, width), full),
+            pl.BlockSpec((block_rows, head_dim), kv_map),
+            pl.BlockSpec((block_rows, head_dim), kv_map),
+            pl.BlockSpec((rows, heads), full),
+            pl.BlockSpec((rows, heads), full),
+        ],
+        out_specs=[
+            pl.BlockSpec((rows, width), full),
+            pl.BlockSpec((block_rows, 2 * head_dim), lambda j, s: (j, 0)),
+        ],
+        scratch_shapes=[pltpu.VMEM((rows, width), jnp.float32)],
+    )
+    return pl.pallas_call(
+        kernel,
+        grid_spec=grid_spec,
+        out_shape=[
+            jax.ShapeDtypeStruct((rows, width), jnp.bfloat16),
+            jax.ShapeDtypeStruct((tokens, 2 * head_dim), jnp.bfloat16),
+        ],
+        compiler_params=pltpu.CompilerParams(dimension_semantics=("arbitrary",)),
+    )(scalars, query_rows, grad_attended, keys_all, values_all, log_total, row_dot)
 
 
 def butterfly_sum(value, axis_name):
@@ -151,50 +233,19 @@
     row_dot = jnp.sum(
         grad_group.astype(jnp.float32) * attended_heads[:, shared_head].astype(jnp.float32), axis=-1
     )
-    key_column = jnp.int32(shared_head * head_dim)
-    value_column = jnp.int32((local_groups + shared_head) * head_dim)
-
-    def back_step(block_number, carried):
-        query_sum, buffer_now = carried
-        key_block = fetch(keys_all, block_number)
-        value_block = fetch(values_all, block_number)
-        scores = block_scores(
-            backward_query_group, key_block, scaling, backward_row_pos, column_pos(block_number)
-        )
-        softmax = jnp.exp(scores - backward_log_total[..., None])
-        rounded = softmax.astype(jnp.bfloat16)
-        grad_prob = jnp.einsum(
-            "tgd,kd->tgk", grad_group, value_block, preferred_element_type=jnp.float32
-        )
-        grad_score = (softmax * (grad_prob - row_dot[..., None]) * scaling).astype(jnp.bfloat16)
-        query_sum = query_sum + jnp.einsum(
-            "tgk,kd->tgd", grad_score, key_block, preferred_element_type=jnp.float32
-        )
-        key_part = jnp.einsum(
-            "tgk,tgd->kd", grad_score, backward_query_group, preferred_element_type=jnp.float32
-        )
-        value_part = jnp.einsum(
-            "tgk,tgd->kd", rounded, grad_group, preferred_element_type=jnp.float32
-        )
-        row_start = (block_number * block_rows).astype(jnp.int32)
-        old_key = lax.dynamic_slice(buffer_now, (row_start, key_column), (block_rows, head_dim))
-        buffer_now = lax.dynamic_update_slice(
-            buffer_now, old_key + key_part, (row_start, key_column)
-        )
-        old_value = lax.dynamic_slice(buffer_now, (row_start, value_column), (block_rows, head_dim))
-        buffer_now = lax.dynamic_update_slice(
-            buffer_now, old_value + value_part, (row_start, value_column)
-        )
-        return (query_sum, buffer_now)
-
-    start_query = jnp.zeros((rows, group_size, head_dim), jnp.float32)
-    query_sum, backward_buffer = lax.fori_loop(0, needed, back_step, (start_query, backward_buffer))
-    query_grads = [query_sum.astype(jnp.bfloat16)]
-    grad_query_part = jnp.stack(query_grads, axis=1).reshape(
-        rows, local_groups * group_size * head_dim
+    grad_query_part, backward_buffer = flash_backward(
+        backward_query_group.reshape(rows, group_size * head_dim),
+        grad_group.reshape(rows, group_size * head_dim),
+        keys_all,
+        values_all,
+        backward_log_total,
+        row_dot,
+        first_row,
+        head_dim,
+        block_rows,
     )
     key_sums = lax.psum_scatter(
-        backward_buffer.astype(jnp.bfloat16), "ctx", scatter_dimension=0, tiled=True
+        backward_buffer, "ctx", scatter_dimension=0, tiled=True
     ).astype(jnp.float32)
     grad_key = key_sums[:, : local_groups * head_dim].astype(jnp.bfloat16)
     grad_value = key_sums[:, local_groups * head_dim :].astype(jnp.bfloat16)

time: 289 us -> 239 us (0.83)
  waiting for transfers between devices: 213 us -> 176 us
  matrix products: 31.3 us -> 17.7 us
  Pallas kernels: 0 us -> 9.25 us
  other arithmetic: 12.7 us -> 7.56 us
  local copies, waits for them, and re-layouts: 11.3 us -> 8.17 us
    reduce_scatter x1, waiting for transfers between devices: 95.7 us -> 59.2 us  [body(): lax.psum_scatter(backward_buffer, 'ctx', scatter_dimension=0, tiled=True)]
    pallas_call x0 -> x1, Pallas kernels: none -> 9.25 us  [flash_backward(): pl.pallas_call(kernel, grid_spec=grid_spec, out_shape=[jax.ShapeDtypeStru...]
    dot_general x4 -> x0, matrix products: 8.45 us -> none  [the longest x1 2.75 us: back_step(): jnp.einsum('tgk,tgd->kd', rounded, grad_group, preferred_element_type=jnp...]
    convert_element_type x1 -> x0, other arithmetic: 3.74 us -> none  [body(): backward_buffer.astype(jnp.bfloat16)]
    dot_general x1, matrix products: 4.81 us -> 1.28 us  [gram_squares(): lax.dot_general(left_side, left_side, (((1,), (1,)), ((), ())), preferred...]
where the time goes in v3:
time: 239 us; the launch traced here: 235 us
  waiting for transfers between devices  176 us (74%)
  matrix products  17.7 us (7%)
  between operations  13.9 us (6%)
  Pallas kernels  9.25 us (4%)
  local copies, waits for them, and re-layouts  8.17 us (3%)
  other arithmetic  7.56 us (3%)
    all_gather x1, waiting for transfers between devices, body(): piece_part = lax.all_gather(weighted, 'head', axis=1, tiled=True)  64.9 us
    reduce_scatter x1, waiting for transfers between devices, body(): lax.psum_scatter(backward_buffer, 'ctx', scatter_dimension=0, tiled=True)  59.2 us
    all_gather x1, waiting for transfers between devices, body(): lax.all_gather(jnp.concatenate([key_rows, value_rows], axis=1), 'ctx', ax...  33.1 us
    ppermute x3, waiting for transfers between devices, butterfly_sum(): value = value + lax.ppermute(value, axis_name, pairs)  19.2 us
    dot_general x1, matrix products, body(): lax.dot_general(piece_part, out_weight, (((1,), (1,)), ((), ())), preferr...  11.6 us
    pallas_call x1, Pallas kernels, flash_backward(): pl.pallas_call(kernel, grid_spec=grid_spec, out_shape=[jax.ShapeDtypeStru...  9.25 us
  transfers between devices with their start and end apart: 6, of which 6 were waited for; matrix products, arithmetic and copies ran while one was open for 7% of the time, Pallas kernels for 0%

profile of v3, /device:TPU:1, one launch (start us, length us, event | category | flops | bytes accessed | tf_op | source)
XLA Modules:
  0.0 235.1 jit_solution(7208096270361334122)
XLA Ops:
  7.2 1.6 pad_maximum_fusion
  8.9 0.7 convert_add_fusion
  9.6 2.0 multiply_convert_fusion
  11.6 1.1 copy_bitcast_fusion
  12.8 1.1 copy.31
  13.9 0.6 pad_add_fusion.scalar_ref
  14.5 33.1 %all-gather.5.cloned.1.call-done = bf16[4096,256]{1,0:T(8,128)(2,1)} async-done(((bf16[256,256]{1,0:T(8,128)(2,1)}), bf16[4096,256]{1,0:T(8,128)(2,1)}) %all-gather.5.cloned.1.call-update) | async-done | bytes 2097168 | tf_op jit(solution)/shard_map/all_gather | solution.py:160
  47.6 2.7 %fusion.33 = (bf16[4096,128]{1,0:T(8,128)(2,1)}, bf16[4096,128]{1,0:T(8,128)(2,1)S(1)}) fusion(bf16[4096,256]{1,0:T(8,128)(2,1)} %all-gather.5.cloned.1.call-done), kind=kLoop, calls=%fused_computation.47 | loop fusion | bytes 4194304 | tf_op jit(solution)/shard_map/slice | solution.py:164
  50.3 1.9 while.24
  50.4 0.8 fusion.53
  51.2 0.9 exponential_reduce_fusion.2
  53.1 3.0 %while.25 = (s32[]{:T(128)}, f32[256,8,128]{2,0,1:T(8,128)S(1)}, s32[]{:T(128)}, bf16[4096,128]{1,0:T(8,128)(2,1)S(1)}, bf16[256,8,128]{2,1,0:T(8,128)(2,1)S(1)}...) while((s32[]{:T(128)}, f32[256,8,128]{2,0,1:T(8,128)S(1)}, ...), condition=%wide.region_5.6_spmd.clone, body=%wide.region_4.5_spmd.clone.sunk | while | flops 541459200 | bytes 3161259 | solution.py:207
  53.3 2.6 %fusion.57 = f32[256,8,128]{2,0,1:T(8,128)S(1)} fusion(f32[256,8,128]{2,0,1:T(8,128)S(1)} %get-tuple-element.342, f32[256,8]{0,1:T(8,128)S(1)} %get-tuple-element.358, pred[256,512]{1,0:T(8,128)(4,1)S(1)} %broadcast_compare_fusion.5, bf16[256,8,128]{2,1,0:T(8,128)(2,1)S(1)} %get-tuple-element.357, bf16[4096,128]{1,0:T(8,128)(2,1)} %get-tuple-element.359, ...), kind=kOutput, calls=%fused_computation.18.clone.1 | convolution fusion | flops 541327360 | bytes 3023872 | tf_op jit(solution)/shard_map/while/body/tgk,kd->tgd/dot_general | solution.py:203
  56.1 64.9 %all-gather.3.cloned.1.call-done = bf16[256,8192]{1,0:T(8,128)(2,1)} async-done(((bf16[256,1024]{1,0:T(8,128)(2,1)}), bf16[256,8192]{1,0:T(8,128)(2,1)}) %all-gather.3.cloned.1.call-update) | async-done | bytes 4194320 | tf_op jit(solution)/shard_map/all_gather | solution.py:216
  121.0 11.6 %convolution_convert_fusion.do_ref = bf16[256,1024]{1,0:T(8,128)(2,1)S(1)} fusion(bf16[256,8192]{1,0:T(8,128)(2,1)} %all-gather.3.cloned.1.call-done, bf16[1024,8192]{1,0:T(8,128)(2,1)} %param.15), kind=kOutput, calls=%fused_computation.32 | convolution fusion | flops 4295229440 | bytes 21495808 | tf_op jit(solution)/shard_map/dot_general | solution.py:217
  133.0 0.8 copy.24.rd_ref
  133.8 9.2 %shard_map.110 = (bf16[256,1024]{1,0:T(8,128)(2,1)}, bf16[4096,256]{1,0:T(8,128)(2,1)}) custom-call(s32[2]{0:T(128)} %pad_add_fusion.scalar_ref, bf16[256,1024]{1,0:T(8,128)(2,1)} %q_ref.1, bf16[256,1024]{1,0:T(8,128)(2,1)} %copy-done.1, bf16[4096,128]{1,0:T(8,128)(2,1)S(1)} %get-tuple-element.369, bf16[4096,128]{1,0:T(8,128)(2,1)} %get-tuple-element.370, ...), custom_call_target="tpu_custom_call" | custom-call | tf_op jit(solution)/shard_map/pallas_call | solution.py:107
  143.7 8.0 %collective-permute-done = f32[256,256]{1,0:T(8,128)S(1)} collective-permute-done((f32[256,256]{1,0:T(8,128)S(1)}, f32[256,256]{1,0:T(8,128)S(1)}, u32[]{:S(2)}, u32[]{:S(2)}) %collective-permute-start) | collective-permute-done | bytes 262176 | tf_op jit(solution)/shard_map/ppermute | solution.py:123
  151.8 5.8 %collective-permute-done.1 = f32[256,256]{1,0:T(8,128)S(1)} collective-permute-done((f32[256,256]{1,0:T(8,128)S(1)}, f32[256,256]{1,0:T(8,128)S(1)}, u32[]{:S(2)}, u32[]{:S(2)}) %collective-permute-start.1) | collective-permute-done | bytes 262176 | tf_op jit(solution)/shard_map/ppermute | solution.py:123
  157.6 1.4 collective-permute-start.2
  159.0 5.4 %collective-permute-done.2 = f32[256,256]{1,0:T(8,128)S(1)} collective-permute-done((f32[256,256]{1,0:T(8,128)S(1)}, f32[256,256]{1,0:T(8,128)S(1)}, u32[]{:S(2)}, u32[]{:S(2)}) %collective-permute-start.2) | collective-permute-done | bytes 262176 | tf_op jit(solution)/shard_map/ppermute | solution.py:123
  165.0 1.3 fusion.36
  167.9 59.2 %reduce-scatter.2.cloned.1.call-done = bf16[256,256]{1,0:T(8,128)(2,1)} async-done(((bf16[4096,256]{1,0:T(8,128)(2,1)}), bf16[256,256]{1,0:T(8,128)(2,1)}) %reduce-scatter.2.cloned.1.call-update) | async-done | bytes 131088 | tf_op jit(solution)/shard_map/reduce_scatter | solution.py:247
  227.1 1.5 fusion.34
  (44 shorter events, 4.8 us)
Async XLA Ops:
  7.2 135.9 %copy-start = (bf16[256,1024]{1,0:T(8,128)(2,1)S(1)}, bf16[256,1024]{1,0:T(8,128)(2,1)}, u32[]{:S(2)}) copy-start(bf16[256,1024]{1,0:T(8,128)(2,1)} %param.11) | copy-start | bytes 1572868
  7.2 40.4 %all-gather.5.cloned.1.call-start = ((), (), s32[]{:S(2)}) async-start(), calls=%async_computation.2 | async-start | bytes 2228224 | tf_op jit(solution)/shard_map/all_gather | solution.py:160
  8.8 112.2 %all-gather.3.cloned.1.call-start = ((), (), s32[]{:S(2)}) async-start(), calls=%async_computation.1 | async-start | bytes 4718592 | tf_op jit(solution)/shard_map/all_gather | solution.py:216
  11.6 215.5 %reduce-scatter.2.cloned.1.call-start = ((), (), s32[]{:S(2)}) async-start(), calls=%async_computation.3 | async-start | bytes 2228224 | tf_op jit(solution)/shard_map/reduce_scatter | solution.py:247
  52.4 0.7 copy-start.2
  132.6 1.2 copy-start.1
  143.0 21.5 %copy-start.4 = (bf16[256,1024]{1,0:T(8,128)(2,1)S(1)}, bf16[256,1024]{1,0:T(8,128)(2,1)}, u32[]{:S(2)}) copy-start(bf16[256,1024]{1,0:T(8,128)(2,1)} %get-tuple-element.84) | copy-start | bytes 1572868
  143.0 22.0 %copy-start.3 = (bf16[256,8192]{1,0:T(8,128)(2,1)S(1)}, bf16[256,8192]{1,0:T(8,128)(2,1)}, u32[]{:S(2)}) copy-start(bf16[256,8192]{1,0:T(8,128)(2,1)} %all-gather.3.cloned.1.call-done) | copy-start | bytes 12582916
  143.4 8.3 %collective-permute-start = (f32[256,256]{1,0:T(8,128)S(1)}, f32[256,256]{1,0:T(8,128)S(1)}, u32[]{:S(2)}, u32[]{:S(2)}) collective-permute-start(f32[256,256]{1,0:T(8,128)S(1)} %fusion.35), channel_id=1, source_target_pairs={{0,1},{1,0},{2,3},{3,2},{4,5},{5,4},{6,7},{7,6},{8,9},{9,8},{10,11... | collective-permute-start | bytes 786440 | tf_op jit(solution)/shard_map/ppermute | solution.py:123
  151.7 5.9 %collective-permute-start.1 = (f32[256,256]{1,0:T(8,128)S(1)}, f32[256,256]{1,0:T(8,128)S(1)}, u32[]{:S(2)}, u32[]{:S(2)}) collective-permute-start(f32[256,256]{1,0:T(8,128)S(1)} %add.103), channel_id=1, source_target_pairs={{0,2},{1,3},{2,0},{3,1},{4,6},{5,7},{6,4},{7,5},{8,10},{9,11},{10,... | collective-permute-start | bytes 786440 | tf_op jit(solution)/shard_map/ppermute | solution.py:123
  157.6 6.8 %collective-permute-start.2 = (f32[256,256]{1,0:T(8,128)S(1)}, f32[256,256]{1,0:T(8,128)S(1)}, u32[]{:S(2)}, u32[]{:S(2)}) collective-permute-start(f32[256,256]{1,0:T(8,128)S(1)} %add.104), channel_id=1, source_target_pairs={{0,4},{1,5},{2,6},{3,7},{4,0},{5,1},{6,2},{7,3},{8,12},{9,13},{10,... | collective-permute-start | bytes 786440 | tf_op jit(solution)/shard_map/ppermute | solution.py:123
Sparse Core Ops, SparseCore 0:
  9.7 37.8 all-gather.4
  50.5 70.4 all-gather.2
  143.1 83.8 reduce-scatter.1

commit v4 on v3

--- a/solution.py
+++ b/solution.py
@@ -115,6 +115,26 @@
     )(scalars, query_rows, grad_attended, keys_all, values_all, log_total, row_dot)
 
 
+def butterfly_gather(value, axis_name):
+    size = lax.axis_size(axis_name)
+    own = lax.axis_index(axis_name)
+    held = value[None]
+    stride = size // 2
+    bits = 0
+    while stride >= 1:
+        pairs = [(i, i ^ stride) for i in range(size)]
+        other = lax.ppermute(held, axis_name, pairs)
+        low = (own & stride) == 0
+        held = jnp.where(
+            low, jnp.concatenate([held, other], 0), jnp.concatenate([other, held], 0)
+        )
+        stride //= 2
+        bits += 1
+    held = held.reshape((2,) * bits + value.shape)
+    held = held.transpose(tuple(range(bits))[::-1] + tuple(range(bits, bits + value.ndim)))
+    return held.reshape((size * value.shape[0],) + value.shape[1:])
+
+
 def butterfly_sum(value, axis_name):
     size = lax.axis_size(axis_name)
     stride = 1
@@ -157,9 +177,11 @@
         ),
         "head",
     )
-    pair_all = lax.all_gather(
-        jnp.concatenate([key_rows, value_rows], axis=1), "ctx", axis=0, tiled=True
-    )
+    piece_part = lax.all_gather(weighted, "head", axis=1, tiled=True)
+    pair, _ = lax.optimization_barrier(
+        (jnp.concatenate([key_rows, value_rows], axis=1), weighted)
+    )
+    pair_all = butterfly_gather(pair, "ctx")
     kv_width = key_rows.shape[1]
     keys_all, values_all = (pair_all[:, :kv_width], pair_all[:, kv_width:])
     tokens = keys_all.shape[0]
@@ -213,7 +235,6 @@
         rows, local_groups * group_size * head_dim
     )
     log_totals, attended = (log_totals, attended_part)
-    piece_part = lax.all_gather(weighted, "head", axis=1, tiled=True)
     grad_sum = lax.dot_general(
         piece_part, out_weight, (((1,), (1,)), ((), ())), preferred_element_type=jnp.float32
     )

time: 239 us -> 230 us (0.962)
  waiting for transfers between devices: 176 us -> 158 us
  starting transfers between devices: 1.9 us -> 11.9 us
  local copies, waits for them, and re-layouts: 8.17 us -> 5.53 us
    all_gather x1 -> x0, waiting for transfers between devices: 33.1 us -> none  [body(): lax.all_gather(jnp.concatenate([key_rows, value_rows], axis=1), 'ctx', ax...]
    ppermute x0 -> x4, waiting for transfers between devices: none -> 19.1 us  [butterfly_gather(): other = lax.ppermute(held, axis_name, pairs)]
    ppermute x0 -> x4, starting transfers between devices: none -> 10.1 us  [butterfly_gather(): other = lax.ppermute(held, axis_name, pairs)]
    all_gather x1, waiting for transfers between devices: 64.9 us -> 60.8 us  [body(): piece_part = lax.all_gather(weighted, 'head', axis=1, tiled=True)]
  transfers between devices with their start and end apart: 6 -> 9, of which waited for: 6 -> 9; matrix products, arithmetic and copies ran while one was open for 7% -> 6% of each run, Pallas kernels for 0% -> 0%
where the time goes in v4:
time: 230 us; the launch traced here: 226 us
  waiting for transfers between devices  158 us (69%)
  matrix products  17.7 us (8%)
  between operations  14.3 us (6%)
  starting transfers between devices  11.9 us (5%)
  Pallas kernels  9.27 us (4%)
  other arithmetic  9.09 us (4%)
  local copies, waits for them, and re-layouts  5.53 us (2%)
    all_gather x1, waiting for transfers between devices, body(): piece_part = lax.all_gather(weighted, 'head', axis=1, tiled=True)  60.8 us
    reduce_scatter x1, waiting for transfers between devices, body(): lax.psum_scatter(backward_buffer, 'ctx', scatter_dimension=0, tiled=True)  59.1 us
    ppermute x3, waiting for transfers between devices, butterfly_sum(): value = value + lax.ppermute(value, axis_name, pairs)  19.1 us
    ppermute x4, waiting for transfers between devices, butterfly_gather(): other = lax.ppermute(held, axis_name, pairs)  19.1 us
    dot_general x1, matrix products, body(): lax.dot_general(piece_part, out_weight, (((1,), (1,)), ((), ())), preferr...  11.6 us
    ppermute x4, starting transfers between devices, butterfly_gather(): other = lax.ppermute(held, axis_name, pairs)  10.1 us
    pallas_call x1, Pallas kernels, flash_backward(): pl.pallas_call(kernel, grid_spec=grid_spec, out_shape=[jax.ShapeDtypeStru...  9.27 us
  transfers between devices with their start and end apart: 9, of which 9 were waited for; matrix products, arithmetic and copies ran while one was open for 6% of the time, Pallas kernels for 0%

profile of v4, /device:TPU:1, one launch (start us, length us, event | category | flops | bytes accessed | tf_op | source)
XLA Modules:
  0.0 226.2 jit_solution(2955951061647998487)
XLA Ops:
  8.0 0.9 pad_maximum_fusion
  8.9 2.0 multiply_convert_fusion
  10.9 2.1 collective-permute-start
  13.0 2.8 %collective-permute-done = bf16[1,256,256]{2,1,0:T(8,128)(2,1)S(1)} collective-permute-done((bf16[1,256,256]{2,1,0:T(8,128)(2,1)S(1)}, bf16[1,256,256]{2,1,0:T(8,128)(2,1)S(1)}, u32[]{:S(2)}, u32[]{:S(2)}) %collective-permute-start) | collective-permute-done | bytes 131104 | tf_op jit(solution)/shard_map/ppermute | solution.py:126
  15.9 3.9 %collective-permute-start.1 = (bf16[2,256,256]{2,1,0:T(8,128)(2,1)S(1)}, bf16[2,256,256]{2,1,0:T(8,128)(2,1)S(1)}, u32[]{:S(2)}, u32[]{:S(2)}) collective-permute-start(bf16[2,256,256]{2,1,0:T(8,128)(2,1)S(1)} %maximum_select_fusion.3), channel_id=1, source_target_pairs={{0,32},{8,40},{16,48},{24,56},{32,0},{40,8},{48,16},{56,24},{64,96... | collective-permute-start | bytes 786440 | tf_op jit(solution)/shard_map/ppermute | solution.py:126
  19.8 5.1 %collective-permute-done.1 = bf16[2,256,256]{2,1,0:T(8,128)(2,1)S(1)} collective-permute-done((bf16[2,256,256]{2,1,0:T(8,128)(2,1)S(1)}, bf16[2,256,256]{2,1,0:T(8,128)(2,1)S(1)}, u32[]{:S(2)}, u32[]{:S(2)}) %collective-permute-start.1) | collective-permute-done | bytes 262176 | tf_op jit(solution)/shard_map/ppermute | solution.py:126
  25.8 10.5 %collective-permute-done.2 = bf16[4,256,256]{2,1,0:T(8,128)(2,1)S(1)} collective-permute-done((bf16[4,256,256]{2,1,0:T(8,128)(2,1)S(1)}, bf16[4,256,256]{2,1,0:T(8,128)(2,1)S(1)}, u32[]{:S(2)}, u32[]{:S(2)}) %collective-permute-start.2) | collective-permute-done | bytes 524320 | tf_op jit(solution)/shard_map/ppermute | solution.py:126
  36.4 3.2 %collective-permute-start.3 = (bf16[8,256,256]{2,1,0:T(8,128)(2,1)S(1)}, bf16[8,256,256]{2,1,0:T(8,128)(2,1)}, u32[]{:S(2)}, u32[]{:S(2)}) collective-permute-start(bf16[8,256,256]{2,1,0:T(8,128)(2,1)S(1)} %maximum_select_fusion.1), channel_id=1, source_target_pairs={{0,8},{8,0},{16,24},{24,16},{32,40},{40,32},{48,56},{56,48},{64,72... | collective-permute-start | bytes 3145736 | tf_op jit(solution)/shard_map/ppermute | solution.py:126
  39.7 0.9 copy.33
  42.0 1.9 maximum_select_fusion
  44.1 1.1 fusion.33
  45.2 1.9 while.24
  48.0 3.0 %while.25 = (s32[]{:T(128)}, f32[256,8,128]{2,0,1:T(8,128)S(1)}, s32[]{:T(128)}, bf16[4096,128]{1,0:T(8,128)(2,1)S(1)}, bf16[256,8,128]{2,1,0:T(8,128)(2,1)S(1)}...) while((s32[]{:T(128)}, f32[256,8,128]{2,0,1:T(8,128)S(1)}, ...), condition=%wide.region_5.6_spmd.clone, body=%wide.region_4.5_spmd.clone.sunk | while | flops 541459200 | bytes 3161259 | solution.py:229
  48.2 2.6 %fusion.57 = f32[256,8,128]{2,0,1:T(8,128)S(1)} fusion(f32[256,8,128]{2,0,1:T(8,128)S(1)} %get-tuple-element.344, f32[256,8]{0,1:T(8,128)S(1)} %get-tuple-element.360, pred[256,512]{1,0:T(8,128)(4,1)S(1)} %broadcast_compare_fusion.5, bf16[256,8,128]{2,1,0:T(8,128)(2,1)S(1)} %get-tuple-element.359, bf16[4096,128]{1,0:T(8,128)(2,1)} %get-tuple-element.361, ...), kind=kOutput, calls=%fused_computation.18.clone.1 | convolution fusion | flops 541327360 | bytes 3023872 | tf_op jit(solution)/shard_map/while/body/tgk,kd->tgd/dot_general | solution.py:225
  51.0 60.8 %all-gather.2.cloned.1.call-done = bf16[256,8192]{1,0:T(8,128)(2,1)} async-done(((bf16[256,1024]{1,0:T(8,128)(2,1)}), bf16[256,8192]{1,0:T(8,128)(2,1)}) %all-gather.2.cloned.1.call-update) | async-done | bytes 4194320 | tf_op jit(solution)/shard_map/all_gather | solution.py:180
  111.8 11.6 %convolution_convert_fusion.do_ref = bf16[256,1024]{1,0:T(8,128)(2,1)S(1)} fusion(bf16[256,8192]{1,0:T(8,128)(2,1)} %all-gather.2.cloned.1.call-done, bf16[1024,8192]{1,0:T(8,128)(2,1)} %param.15), kind=kOutput, calls=%fused_computation.33 | convolution fusion | flops 4295229440 | bytes 21495808 | tf_op jit(solution)/shard_map/dot_general | solution.py:238
  124.6 9.3 %shard_map.110 = (bf16[256,1024]{1,0:T(8,128)(2,1)}, bf16[4096,256]{1,0:T(8,128)(2,1)}) custom-call(s32[2]{0:T(128)} %pad_add_fusion.scalar_ref, bf16[256,1024]{1,0:T(8,128)(2,1)} %q_ref.1, bf16[256,1024]{1,0:T(8,128)(2,1)} %copy-done.2, bf16[4096,128]{1,0:T(8,128)(2,1)S(1)} %get-tuple-element.370, bf16[4096,128]{1,0:T(8,128)(2,1)} %get-tuple-element.372, ...), custom_call_target="tpu_custom_call" | custom-call | tf_op jit(solution)/shard_map/pallas_call | solution.py:107
  134.5 8.0 %collective-permute-done.4 = f32[256,256]{1,0:T(8,128)S(1)} collective-permute-done((f32[256,256]{1,0:T(8,128)S(1)}, f32[256,256]{1,0:T(8,128)S(1)}, u32[]{:S(2)}, u32[]{:S(2)}) %collective-permute-start.4) | collective-permute-done | bytes 262176 | tf_op jit(solution)/shard_map/ppermute | solution.py:143
  142.7 5.7 %collective-permute-done.5 = f32[256,256]{1,0:T(8,128)S(1)} collective-permute-done((f32[256,256]{1,0:T(8,128)S(1)}, f32[256,256]{1,0:T(8,128)S(1)}, u32[]{:S(2)}, u32[]{:S(2)}) %collective-permute-start.5) | collective-permute-done | bytes 262176 | tf_op jit(solution)/shard_map/ppermute | solution.py:143
  148.4 1.3 collective-permute-start.6
  149.8 5.5 %collective-permute-done.6 = f32[256,256]{1,0:T(8,128)S(1)} collective-permute-done((f32[256,256]{1,0:T(8,128)S(1)}, f32[256,256]{1,0:T(8,128)S(1)}, u32[]{:S(2)}, u32[]{:S(2)}) %collective-permute-start.6) | collective-permute-done | bytes 262176 | tf_op jit(solution)/shard_map/ppermute | solution.py:143
  155.8 1.3 fusion.36
  158.7 59.1 %reduce-scatter.2.cloned.1.call-done = bf16[256,256]{1,0:T(8,128)(2,1)} async-done(((bf16[4096,256]{1,0:T(8,128)(2,1)}), bf16[256,256]{1,0:T(8,128)(2,1)}) %reduce-scatter.2.cloned.1.call-update) | async-done | bytes 131088 | tf_op jit(solution)/shard_map/reduce_scatter | solution.py:268
  217.8 1.5 fusion.34
  (58 shorter events, 10.6 us)
Async XLA Ops:
  7.2 126.7 %copy-start = (bf16[256,1024]{1,0:T(8,128)(2,1)S(1)}, bf16[256,1024]{1,0:T(8,128)(2,1)}, u32[]{:S(2)}) copy-start(bf16[256,1024]{1,0:T(8,128)(2,1)} %param.11) | copy-start | bytes 1572868
  7.2 32.5 %copy-start.1 = (bf16[256,1024]{1,0:T(8,128)(2,1)S(1)}, bf16[256,1024]{1,0:T(8,128)(2,1)}, u32[]{:S(2)}) copy-start(bf16[256,1024]{1,0:T(8,128)(2,1)} %q_ref.1) | copy-start | bytes 1572868
  7.2 104.6 %all-gather.2.cloned.1.call-start = ((), (), s32[]{:S(2)}) async-start(), calls=%async_computation.1 | async-start | bytes 4718592 | tf_op jit(solution)/shard_map/all_gather | solution.py:180
  10.9 4.9 %collective-permute-start = (bf16[1,256,256]{2,1,0:T(8,128)(2,1)S(1)}, bf16[1,256,256]{2,1,0:T(8,128)(2,1)S(1)}, u32[]{:S(2)}, u32[]{:S(2)}) collective-permute-start(bf16[1,256,256]{2,1,0:T(8,128)(2,1)S(1)} %bitcast.88), channel_id=1, source_target_pairs={{0,64},{8,72},{16,80},{24,88},{32,96},{40,104},{48,112},{56,120},{... | collective-permute-start | bytes 393224 | tf_op jit(solution)/shard_map/ppermute | solution.py:126
  15.9 9.0 %collective-permute-start.1 = (bf16[2,256,256]{2,1,0:T(8,128)(2,1)S(1)}, bf16[2,256,256]{2,1,0:T(8,128)(2,1)S(1)}, u32[]{:S(2)}, u32[]{:S(2)}) collective-permute-start(bf16[2,256,256]{2,1,0:T(8,128)(2,1)S(1)} %maximum_select_fusion.3), channel_id=1, source_target_pairs={{0,32},{8,40},{16,48},{24,56},{32,0},{40,8},{48,16},{56,24},{64,96... | collective-permute-start | bytes 786440 | tf_op jit(solution)/shard_map/ppermute | solution.py:126
  25.0 11.3 %collective-permute-start.2 = (bf16[4,256,256]{2,1,0:T(8,128)(2,1)S(1)}, bf16[4,256,256]{2,1,0:T(8,128)(2,1)S(1)}, u32[]{:S(2)}, u32[]{:S(2)}) collective-permute-start(bf16[4,256,256]{2,1,0:T(8,128)(2,1)S(1)} %maximum_select_fusion.2), channel_id=1, source_target_pairs={{0,16},{8,24},{16,0},{24,8},{32,48},{40,56},{48,32},{56,40},{64,80... | collective-permute-start | bytes 1572872 | tf_op jit(solution)/shard_map/ppermute | solution.py:126
  36.4 5.6 %collective-permute-start.3 = (bf16[8,256,256]{2,1,0:T(8,128)(2,1)S(1)}, bf16[8,256,256]{2,1,0:T(8,128)(2,1)}, u32[]{:S(2)}, u32[]{:S(2)}) collective-permute-start(bf16[8,256,256]{2,1,0:T(8,128)(2,1)S(1)} %maximum_select_fusion.1), channel_id=1, source_target_pairs={{0,8},{8,0},{16,24},{24,16},{32,40},{40,32},{48,56},{56,48},{64,72... | collective-permute-start | bytes 3145736 | tf_op jit(solution)/shard_map/ppermute | solution.py:126
  39.6 178.2 %reduce-scatter.2.cloned.1.call-start = ((), (), s32[]{:S(2)}) async-start(), calls=%async_computation.2 | async-start | bytes 2228224 | tf_op jit(solution)/shard_map/reduce_scatter | solution.py:268
  45.2 2.3 %copy-start.4 = (bf16[32,8,8,128]{3,2,1,0:T(8,128)(2,1)S(1)}, bf16[32,8,8,128]{3,2,1,0:T(8,128)(2,1)}, u32[]{:S(2)}) copy-start(bf16[32,8,8,128]{3,2,1,0:T(8,128)(2,1)} %copy.33) | copy-start | bytes 1572868
  47.4 0.7 copy-start.3
  123.4 1.2 copy-start.2
  133.8 21.4 %copy-start.6 = (bf16[256,1024]{1,0:T(8,128)(2,1)S(1)}, bf16[256,1024]{1,0:T(8,128)(2,1)}, u32[]{:S(2)}) copy-start(bf16[256,1024]{1,0:T(8,128)(2,1)} %get-tuple-element.85) | copy-start | bytes 1572868
  133.9 22.0 %copy-start.5 = (bf16[256,8192]{1,0:T(8,128)(2,1)S(1)}, bf16[256,8192]{1,0:T(8,128)(2,1)}, u32[]{:S(2)}) copy-start(bf16[256,8192]{1,0:T(8,128)(2,1)} %all-gather.2.cloned.1.call-done) | copy-start | bytes 12582916
  134.2 8.3 %collective-permute-start.4 = (f32[256,256]{1,0:T(8,128)S(1)}, f32[256,256]{1,0:T(8,128)S(1)}, u32[]{:S(2)}, u32[]{:S(2)}) collective-permute-start(f32[256,256]{1,0:T(8,128)S(1)} %fusion.35), channel_id=1, source_target_pairs={{0,1},{1,0},{2,3},{3,2},{4,5},{5,4},{6,7},{7,6},{8,9},{9,8},{10,11... | collective-permute-start | bytes 786440 | tf_op jit(solution)/shard_map/ppermute | solution.py:143
  142.5 5.9 %collective-permute-start.5 = (f32[256,256]{1,0:T(8,128)S(1)}, f32[256,256]{1,0:T(8,128)S(1)}, u32[]{:S(2)}, u32[]{:S(2)}) collective-permute-start(f32[256,256]{1,0:T(8,128)S(1)} %add.103), channel_id=1, source_target_pairs={{0,2},{1,3},{2,0},{3,1},{4,6},{5,7},{6,4},{7,5},{8,10},{9,11},{10,... | collective-permute-start | bytes 786440 | tf_op jit(solution)/shard_map/ppermute | solution.py:143
  148.4 6.8 %collective-permute-start.6 = (f32[256,256]{1,0:T(8,128)S(1)}, f32[256,256]{1,0:T(8,128)S(1)}, u32[]{:S(2)}, u32[]{:S(2)}) collective-permute-start(f32[256,256]{1,0:T(8,128)S(1)} %add.104), channel_id=1, source_target_pairs={{0,4},{1,5},{2,6},{3,7},{4,0},{5,1},{6,2},{7,3},{8,12},{9,13},{10,... | collective-permute-start | bytes 786440 | tf_op jit(solution)/shard_map/ppermute | solution.py:143
Sparse Core Ops, SparseCore 0:
  39.8 71.9 all-gather.1
  134.0 83.8 reduce-scatter.1

commit v5 on v4

--- a/solution.py
+++ b/solution.py
@@ -135,6 +135,30 @@
     return held.reshape((size * value.shape[0],) + value.shape[1:])
 
 
+def causal_gather(value, axis_name):
+    size = lax.axis_size(axis_name)
+    own = lax.axis_index(axis_name)
+    received = [value]
+    for shift in range(1, size):
+        pairs = [(i, i + shift) for i in range(size - shift)]
+        received.append(lax.ppermute(value, axis_name, pairs))
+    by_shift = jnp.stack(received[::-1], 0)
+    doubled = jnp.concatenate([by_shift, by_shift], 0)
+    blocks = lax.dynamic_slice_in_dim(doubled, size - 1 - own, size, 0)
+    return blocks.reshape((size * value.shape[0],) + value.shape[1:])
+
+
+def causal_reduce(parts, axis_name):
+    size = lax.axis_size(axis_name)
+    own = lax.axis_index(axis_name)
+    total = lax.dynamic_index_in_dim(parts, own, 0, keepdims=False).astype(jnp.float32)
+    for shift in range(1, size):
+        pairs = [(i, i - shift) for i in range(shift, size)]
+        sent = lax.dynamic_index_in_dim(parts, jnp.maximum(own - shift, 0), 0, keepdims=False)
+        total = total + lax.ppermute(sent, axis_name, pairs).astype(jnp.float32)
+    return total
+
+
 def butterfly_sum(value, axis_name):
     size = lax.axis_size(axis_name)
     stride = 1
@@ -177,11 +201,11 @@
         ),
         "head",
     )
-    piece_part = lax.all_gather(weighted, "head", axis=1, tiled=True)
-    pair, _ = lax.optimization_barrier(
-        (jnp.concatenate([key_rows, value_rows], axis=1), weighted)
-    )
-    pair_all = butterfly_gather(pair, "ctx")
+    piece_part = (
+        lax.all_gather(grad_out, "head", axis=1, tiled=True).astype(jnp.float32)
+        * loss_weight[:, None]
+    ).astype(jnp.bfloat16)
+    pair_all = causal_gather(jnp.concatenate([key_rows, value_rows], axis=1), "ctx")
     kv_width = key_rows.shape[1]
     keys_all, values_all = (pair_all[:, :kv_width], pair_all[:, kv_width:])
     tokens = keys_all.shape[0]
@@ -265,9 +289,10 @@
         head_dim,
         block_rows,
     )
-    key_sums = lax.psum_scatter(
-        backward_buffer, "ctx", scatter_dimension=0, tiled=True
-    ).astype(jnp.float32)
+    ctx_size = lax.axis_size("ctx")
+    key_sums = causal_reduce(
+        backward_buffer.reshape((ctx_size, tokens // ctx_size) + backward_buffer.shape[1:]), "ctx"
+    )
     grad_key = key_sums[:, : local_groups * head_dim].astype(jnp.bfloat16)
     grad_value = key_sums[:, local_groups * head_dim :].astype(jnp.bfloat16)
     squares_query = gram_pair_squares(hidden_gram, grad_query_part, head_dim)

time: 230 us -> 204 us (0.89)
  waiting for transfers between devices: 158 us -> 72 us
  starting transfers between devices: 11.9 us -> 69.2 us
  local copies, waits for them, and re-layouts: 5.53 us -> 11.3 us
  other arithmetic: 9.09 us -> 5.93 us
    reduce_scatter x1 -> x0, waiting for transfers between devices: 59.1 us -> none  [body(): lax.psum_scatter(backward_buffer, 'ctx', scatter_dimension=0, tiled=True)]
    ppermute x4 -> x30, starting transfers between devices: 10.1 us -> 62.8 us  [the longest x15 42.7 us: causal_gather(): received.append(lax.ppermute(value, axis_name, pairs))]
    all_gather x1, waiting for transfers between devices: 60.8 us -> 10.6 us  [body(): lax.all_gather(grad_out, 'head', axis=1, tiled=True).astype(jnp.float32)]
    ppermute x4 -> x30, waiting for transfers between devices: 19.1 us -> 42.9 us  [the longest x15 42.6 us: causal_reduce(): total = total + lax.ppermute(sent, axis_name, pairs).astype(jnp.float32)]
    ppermute x3, starting transfers between devices: 1.8 us -> 6.38 us  [butterfly_sum(): value = value + lax.ppermute(value, axis_name, pairs)]
    squeeze x0 -> x1, local copies, waits for them, and re-layouts: none -> 2.98 us  [causal_reduce(): lax.dynamic_index_in_dim(parts, jnp.maximum(own - shift, 0), 0, keepdims=...]
    unnamed x17 -> x45, local copies, waits for them, and re-layouts: 1.61 us -> 4.39 us
  transfers between devices with their start and end apart: 9 -> 34, of which waited for: 9 -> 17; matrix products, arithmetic and copies ran while one was open for 6% -> 9% of each run, Pallas kernels for 0% -> 0%
where the time goes in v5:
time: 204 us; the launch traced here: 202 us
  waiting for transfers between devices  72 us (35%)
  starting transfers between devices  69.2 us (34%)
  matrix products  19.4 us (10%)
  between operations  14.8 us (7%)
  local copies, waits for them, and re-layouts  11.3 us (6%)
  Pallas kernels  9.29 us (5%)
  other arithmetic  5.93 us (3%)
    ppermute x15, starting transfers between devices, causal_gather(): received.append(lax.ppermute(value, axis_name, pairs))  42.7 us
    ppermute x15, waiting for transfers between devices, causal_reduce(): total = total + lax.ppermute(sent, axis_name, pairs).astype(jnp.float32)  42.6 us
    ppermute x15, starting transfers between devices, causal_reduce(): total = total + lax.ppermute(sent, axis_name, pairs).astype(jnp.float32)  20.1 us
    ppermute x3, waiting for transfers between devices, butterfly_sum(): value = value + lax.ppermute(value, axis_name, pairs)  18.5 us
    dot_general x1, matrix products, body(): lax.dot_general(piece_part, out_weight, (((1,), (1,)), ((), ())), preferr...  11.6 us
    all_gather x1, waiting for transfers between devices, body(): lax.all_gather(grad_out, 'head', axis=1, tiled=True).astype(jnp.float32)  10.6 us
    pallas_call x1, Pallas kernels, flash_backward(): pl.pallas_call(kernel, grid_spec=grid_spec, out_shape=[jax.ShapeDtypeStru...  9.29 us
    ppermute x3, starting transfers between devices, butterfly_sum(): value = value + lax.ppermute(value, axis_name, pairs)  6.38 us
  transfers between devices with their start and end apart: 34, of which 17 were waited for; matrix products, arithmetic and copies ran while one was open for 9% of the time, Pallas kernels for 0%

profile of v5, /device:TPU:1, one launch (start us, length us, event | category | flops | bytes accessed | tf_op | source)
XLA Modules:
  0.0 202.2 jit_solution(11128833743207846927)
XLA Ops:
  9.7 8.1 %collective-permute-start.1 = (bf16[256,256]{1,0:T(8,128)(2,1)S(1)}, bf16[256,256]{1,0:T(8,128)(2,1)S(1)}, u32[]{:S(2)}, u32[]{:S(2)}) collective-permute-start(bf16[256,256]{1,0:T(8,128)(2,1)S(1)} %constant_dynamic-update-slice_fusion), channel_id=1, source_target_pairs={{0,112},{8,120},{1,113},{9,121},{2,114},{10,122},{3,115},{11,123},... | collective-permute-start | bytes 393224 | tf_op jit(solution)/shard_map/ppermute | solution.py:144
  31.8 5.0 %collective-permute-start.9 = (bf16[256,256]{1,0:T(8,128)(2,1)S(1)}, bf16[256,256]{1,0:T(8,128)(2,1)S(1)}, u32[]{:S(2)}, u32[]{:S(2)}) collective-permute-start(bf16[256,256]{1,0:T(8,128)(2,1)S(1)} %constant_dynamic-update-slice_fusion), channel_id=1, source_target_pairs={{0,48},{8,56},{16,64},{24,72},{32,80},{40,88},{48,96},{56,104},{64... | collective-permute-start | bytes 393224 | tf_op jit(solution)/shard_map/ppermute | solution.py:144
  36.9 5.0 %collective-permute-start.10 = (bf16[256,256]{1,0:T(8,128)(2,1)S(1)}, bf16[256,256]{1,0:T(8,128)(2,1)S(1)}, u32[]{:S(2)}, u32[]{:S(2)}) collective-permute-start(bf16[256,256]{1,0:T(8,128)(2,1)S(1)} %constant_dynamic-update-slice_fusion), channel_id=1, source_target_pairs={{0,40},{8,48},{16,56},{24,64},{32,72},{40,80},{48,88},{56,96},{64,... | collective-permute-start | bytes 393224 | tf_op jit(solution)/shard_map/ppermute | solution.py:144
  42.1 6.3 %collective-permute-start.11 = (bf16[256,256]{1,0:T(8,128)(2,1)S(1)}, bf16[256,256]{1,0:T(8,128)(2,1)S(1)}, u32[]{:S(2)}, u32[]{:S(2)}) collective-permute-start(bf16[256,256]{1,0:T(8,128)(2,1)S(1)} %constant_dynamic-update-slice_fusion), channel_id=1, source_target_pairs={{0,32},{8,40},{16,48},{24,56},{32,64},{40,72},{48,80},{56,88},{64,... | collective-permute-start | bytes 393224 | tf_op jit(solution)/shard_map/ppermute | solution.py:144
  49.8 4.8 %collective-permute-start.13 = (bf16[256,256]{1,0:T(8,128)(2,1)S(1)}, bf16[256,256]{1,0:T(8,128)(2,1)S(1)}, u32[]{:S(2)}, u32[]{:S(2)}) collective-permute-start(bf16[256,256]{1,0:T(8,128)(2,1)S(1)} %constant_dynamic-update-slice_fusion), channel_id=1, source_target_pairs={{0,16},{8,24},{16,32},{24,40},{32,48},{40,56},{48,64},{56,72},{64,... | collective-permute-start | bytes 393224 | tf_op jit(solution)/shard_map/ppermute | solution.py:144
  57.0 2.7 %collective-permute-start.30 = (f32[256,256]{1,0:T(8,128)S(1)}, f32[256,256]{1,0:T(8,128)S(1)}, u32[]{:S(2)}, u32[]{:S(2)}) collective-permute-start(f32[256,256]{1,0:T(8,128)S(1)} %fusion.53), channel_id=1, source_target_pairs={{0,1},{1,0},{2,3},{3,2},{4,5},{5,4},{6,7},{7,6},{8,9},{9,8},{10,11... | collective-permute-start | bytes 786440 | tf_op jit(solution)/shard_map/ppermute | solution.py:167
  61.5 9.8 %collective-permute-done.30 = f32[256,256]{1,0:T(8,128)S(1)} collective-permute-done((f32[256,256]{1,0:T(8,128)S(1)}, f32[256,256]{1,0:T(8,128)S(1)}, u32[]{:S(2)}, u32[]{:S(2)}) %collective-permute-start.30) | collective-permute-done | bytes 262176 | tf_op jit(solution)/shard_map/ppermute | solution.py:167
  74.6 5.7 %collective-permute-done.31 = f32[256,256]{1,0:T(8,128)S(1)} collective-permute-done((f32[256,256]{1,0:T(8,128)S(1)}, f32[256,256]{1,0:T(8,128)S(1)}, u32[]{:S(2)}, u32[]{:S(2)}) %collective-permute-start.31) | collective-permute-done | bytes 262176 | tf_op jit(solution)/shard_map/ppermute | solution.py:167
  80.4 2.6 %collective-permute-start.32 = (f32[256,256]{1,0:T(8,128)S(1)}, f32[256,256]{1,0:T(8,128)S(1)}, u32[]{:S(2)}, u32[]{:S(2)}) collective-permute-start(f32[256,256]{1,0:T(8,128)S(1)} %add.202), channel_id=1, source_target_pairs={{0,4},{1,5},{2,6},{3,7},{4,0},{5,1},{6,2},{7,3},{8,12},{9,13},{10,... | collective-permute-start | bytes 786440 | tf_op jit(solution)/shard_map/ppermute | solution.py:167
  83.1 3.2 %while.25 = (s32[]{:T(128)}, f32[256,8,128]{2,0,1:T(8,128)S(1)}, s32[]{:T(128)}, bf16[4096,128]{1,0:T(8,128)(2,1)S(1)}, bf16[256,8,128]{2,1,0:T(8,128)(2,1)}, /*...) while((s32[]{:T(128)}, f32[256,8,128]{2,0,1:T(8,128)S(1)}, ...), condition=%wide.region_5.6_spmd.clone, body=%wide.region_4.5_spmd.clone.sunk | while | flops 541459200 | bytes 3161259 | solution.py:253
  83.3 2.8 %fusion.71 = f32[256,8,128]{2,0,1:T(8,128)S(1)} fusion(f32[256,8,128]{2,0,1:T(8,128)S(1)} %get-tuple-element.357, f32[256,8]{0,1:T(8,128)S(1)} %get-tuple-element.373, pred[256,512]{1,0:T(8,128)(4,1)S(1)} %broadcast_compare_fusion.5, bf16[256,8,128]{2,1,0:T(8,128)(2,1)} %get-tuple-element.372, bf16[4096,128]{1,0:T(8,128)(2,1)} %get-tuple-element.374, ...), kind=kOutput, calls=%fused_computation.18.clone.1 | convolution fusion | flops 541327360 | bytes 3023872 | tf_op jit(solution)/shard_map/while/body/tgk,kd->tgd/dot_general | solution.py:249
  86.2 3.0 %collective-permute-done.32 = f32[256,256]{1,0:T(8,128)S(1)} collective-permute-done((f32[256,256]{1,0:T(8,128)S(1)}, f32[256,256]{1,0:T(8,128)S(1)}, u32[]{:S(2)}, u32[]{:S(2)}) %collective-permute-start.32) | collective-permute-done | bytes 262176 | tf_op jit(solution)/shard_map/ppermute | solution.py:167
  90.0 10.6 %all-gather.2.cloned.1.call-done = bf16[256,8192]{1,0:T(8,128)(2,1)} async-done(((bf16[256,1024]{1,0:T(8,128)(2,1)}), bf16[256,8192]{1,0:T(8,128)(2,1)}) %all-gather.2.cloned.1.call-update) | async-done | bytes 4194320 | tf_op jit(solution)/shard_map/all_gather | solution.py:205
  100.6 11.6 %fusion.28.do_ref = bf16[256,1024]{1,0:T(8,128)(2,1)S(1)} fusion(bf16[1024,8192]{1,0:T(8,128)(2,1)} %param.15, bf16[256,8192]{1,0:T(8,128)(2,1)} %all-gather.2.cloned.1.call-done, f32[256]{0:T(256)S(1)} %convert_add_fusion.1), kind=kOutput, calls=%fused_computation.35 | convolution fusion | flops 4301520896 | bytes 21496832 | tf_op jit(solution)/shard_map/dot_general | solution.py:262
  113.3 9.3 %shard_map.110 = (bf16[256,1024]{1,0:T(8,128)(2,1)}, bf16[4096,256]{1,0:T(8,128)(2,1)}) custom-call(s32[2]{0:T(128)} %pad_add_fusion.scalar_ref, bf16[256,1024]{1,0:T(8,128)(2,1)} %q_ref.1, bf16[256,1024]{1,0:T(8,128)(2,1)} %copy-done.1, bf16[4096,128]{1,0:T(8,128)(2,1)S(1)} %get-tuple-element.382, bf16[4096,128]{1,0:T(8,128)(2,1)} %get-tuple-element.383, ...), custom_call_target="tpu_custom_call" | custom-call | tf_op jit(solution)/shard_map/pallas_call | solution.py:107
  122.6 3.0 %dynamic-slice_bitcast_fusion.14 = (bf16[256,256]{1,0:T(8,128)(2,1)S(1)}, bf16[256,256]{1,0:T(8,128)(2,1)S(1)}, bf16[256,256]{1,0:T(8,128)(2,1)S(1)}, bf16[256,2...) fusion(bf16[16,256,256]{2,1,0:T(8,128)(2,1)} %bitcast.162, ...), kind=kLoop, calls=%fused_computation.106 | loop fusion | bytes 3932220 | tf_op jit(solution)/shard_map/jit(dynamic_index_in_dim)/squeeze | solution.py:157
  125.6 2.7 %collective-permute-start.15 = (bf16[256,256]{1,0:T(8,128)(2,1)S(1)}, bf16[256,256]{1,0:T(8,128)(2,1)S(1)}, u32[]{:S(2)}, u32[]{:S(2)}) collective-permute-start(bf16[256,256]{1,0:T(8,128)(2,1)S(1)} %get-tuple-element.194), channel_id=1, source_target_pairs={{8,0},{16,8},{24,16},{32,24},{40,32},{48,40},{56,48},{64,56},{72,6... | collective-permute-start | bytes 393224 | tf_op jit(solution)/shard_map/ppermute | solution.py:158
  140.4 3.5 %collective-permute-done.17 = bf16[256,256]{1,0:T(8,128)(2,1)S(1)} collective-permute-done((bf16[256,256]{1,0:T(8,128)(2,1)S(1)}, bf16[256,256]{1,0:T(8,128)(2,1)S(1)}, u32[]{:S(2)}, u32[]{:S(2)}) %collective-permute-start.17) | collective-permute-done | bytes 131104 | tf_op jit(solution)/shard_map/ppermute | solution.py:158
  148.4 4.5 %collective-permute-done.19 = bf16[256,256]{1,0:T(8,128)(2,1)S(1)} collective-permute-done((bf16[256,256]{1,0:T(8,128)(2,1)S(1)}, bf16[256,256]{1,0:T(8,128)(2,1)S(1)}, u32[]{:S(2)}, u32[]{:S(2)}) %collective-permute-start.19) | collective-permute-done | bytes 131104 | tf_op jit(solution)/shard_map/ppermute | solution.py:158
  154.8 5.4 %collective-permute-done.20 = bf16[256,256]{1,0:T(8,128)(2,1)S(1)} collective-permute-done((bf16[256,256]{1,0:T(8,128)(2,1)S(1)}, bf16[256,256]{1,0:T(8,128)(2,1)S(1)}, u32[]{:S(2)}, u32[]{:S(2)}) %collective-permute-start.20) | collective-permute-done | bytes 131104 | tf_op jit(solution)/shard_map/ppermute | solution.py:158
  161.5 3.0 %collective-permute-done.21 = bf16[256,256]{1,0:T(8,128)(2,1)S(1)} collective-permute-done((bf16[256,256]{1,0:T(8,128)(2,1)S(1)}, bf16[256,256]{1,0:T(8,128)(2,1)S(1)}, u32[]{:S(2)}, u32[]{:S(2)}) %collective-permute-start.21) | collective-permute-done | bytes 131104 | tf_op jit(solution)/shard_map/ppermute | solution.py:158
  168.0 9.1 %collective-permute-done.23 = bf16[256,256]{1,0:T(8,128)(2,1)S(1)} collective-permute-done((bf16[256,256]{1,0:T(8,128)(2,1)S(1)}, bf16[256,256]{1,0:T(8,128)(2,1)S(1)}, u32[]{:S(2)}, u32[]{:S(2)}) %collective-permute-start.23) | collective-permute-done | bytes 131104 | tf_op jit(solution)/shard_map/ppermute | solution.py:158
  179.7 3.7 %collective-permute-done.25 = bf16[256,256]{1,0:T(8,128)(2,1)S(1)} collective-permute-done((bf16[256,256]{1,0:T(8,128)(2,1)S(1)}, bf16[256,256]{1,0:T(8,128)(2,1)S(1)}, u32[]{:S(2)}, u32[]{:S(2)}) %collective-permute-start.25) | collective-permute-done | bytes 131104 | tf_op jit(solution)/shard_map/ppermute | solution.py:158
  184.2 6.7 %collective-permute-done.27 = bf16[256,256]{1,0:T(8,128)(2,1)S(1)} collective-permute-done((bf16[256,256]{1,0:T(8,128)(2,1)S(1)}, bf16[256,256]{1,0:T(8,128)(2,1)S(1)}, u32[]{:S(2)}, u32[]{:S(2)}) %collective-permute-start.27) | collective-permute-done | bytes 131104 | tf_op jit(solution)/shard_map/ppermute | solution.py:158
  (133 shorter events, 60.1 us)
Async XLA Ops:
  7.2 93.4 %all-gather.2.cloned.1.call-start = ((), (), s32[]{:S(2)}) async-start(), calls=%async_computation | async-start | bytes 4718592 | tf_op jit(solution)/shard_map/all_gather | solution.py:205
  9.0 17.5 %collective-permute-start = (bf16[256,256]{1,0:T(8,128)(2,1)S(1)}, bf16[256,256]{1,0:T(8,128)(2,1)S(1)}, u32[]{:S(2)}, u32[]{:S(2)}) collective-permute-start(bf16[256,256]{1,0:T(8,128)(2,1)S(1)} %constant_dynamic-update-slice_fusion), channel_id=1, source_target_pairs={{0,120},{1,121},{2,122},{3,123},{4,124},{5,125},{6,126},{7,127}} | collective-permute-start | bytes 393224 | tf_op jit(solution)/shard_map/ppermute | solution.py:144
  9.7 18.1 %collective-permute-start.1 = (bf16[256,256]{1,0:T(8,128)(2,1)S(1)}, bf16[256,256]{1,0:T(8,128)(2,1)S(1)}, u32[]{:S(2)}, u32[]{:S(2)}) collective-permute-start(bf16[256,256]{1,0:T(8,128)(2,1)S(1)} %constant_dynamic-update-slice_fusion), channel_id=1, source_target_pairs={{0,112},{8,120},{1,113},{9,121},{2,114},{10,122},{3,115},{11,123},... | collective-permute-start | bytes 393224 | tf_op jit(solution)/shard_map/ppermute | solution.py:144
  27.8 14.3 %collective-permute-start.6 = (bf16[256,256]{1,0:T(8,128)(2,1)S(1)}, bf16[256,256]{1,0:T(8,128)(2,1)S(1)}, u32[]{:S(2)}, u32[]{:S(2)}) collective-permute-start(bf16[256,256]{1,0:T(8,128)(2,1)S(1)} %constant_dynamic-update-slice_fusion), channel_id=1, source_target_pairs={{0,72},{8,80},{16,88},{24,96},{32,104},{40,112},{48,120},{1,73},{9... | collective-permute-start | bytes 393224 | tf_op jit(solution)/shard_map/ppermute | solution.py:144
  29.1 19.3 %collective-permute-start.7 = (bf16[256,256]{1,0:T(8,128)(2,1)S(1)}, bf16[256,256]{1,0:T(8,128)(2,1)S(1)}, u32[]{:S(2)}, u32[]{:S(2)}) collective-permute-start(bf16[256,256]{1,0:T(8,128)(2,1)S(1)} %constant_dynamic-update-slice_fusion), channel_id=1, source_target_pairs={{0,64},{8,72},{16,80},{24,88},{32,96},{40,104},{48,112},{56,120},{... | collective-permute-start | bytes 393224 | tf_op jit(solution)/shard_map/ppermute | solution.py:144
  30.5 19.3 %collective-permute-start.8 = (bf16[256,256]{1,0:T(8,128)(2,1)S(1)}, bf16[256,256]{1,0:T(8,128)(2,1)S(1)}, u32[]{:S(2)}, u32[]{:S(2)}) collective-permute-start(bf16[256,256]{1,0:T(8,128)(2,1)S(1)} %constant_dynamic-update-slice_fusion), channel_id=1, source_target_pairs={{0,56},{8,64},{16,72},{24,80},{32,88},{40,96},{48,104},{56,112},{6... | collective-permute-start | bytes 393224 | tf_op jit(solution)/shard_map/ppermute | solution.py:144
  31.8 22.8 %collective-permute-start.9 = (bf16[256,256]{1,0:T(8,128)(2,1)S(1)}, bf16[256,256]{1,0:T(8,128)(2,1)S(1)}, u32[]{:S(2)}, u32[]{:S(2)}) collective-permute-start(bf16[256,256]{1,0:T(8,128)(2,1)S(1)} %constant_dynamic-update-slice_fusion), channel_id=1, source_target_pairs={{0,48},{8,56},{16,64},{24,72},{32,80},{40,88},{48,96},{56,104},{64... | collective-permute-start | bytes 393224 | tf_op jit(solution)/shard_map/ppermute | solution.py:144
  36.9 20.2 %collective-permute-start.10 = (bf16[256,256]{1,0:T(8,128)(2,1)S(1)}, bf16[256,256]{1,0:T(8,128)(2,1)S(1)}, u32[]{:S(2)}, u32[]{:S(2)}) collective-permute-start(bf16[256,256]{1,0:T(8,128)(2,1)S(1)} %constant_dynamic-update-slice_fusion), channel_id=1, source_target_pairs={{0,40},{8,48},{16,56},{24,64},{32,72},{40,80},{48,88},{56,96},{64,... | collective-permute-start | bytes 393224 | tf_op jit(solution)/shard_map/ppermute | solution.py:144
  42.1 17.6 %collective-permute-start.11 = (bf16[256,256]{1,0:T(8,128)(2,1)S(1)}, bf16[256,256]{1,0:T(8,128)(2,1)S(1)}, u32[]{:S(2)}, u32[]{:S(2)}) collective-permute-start(bf16[256,256]{1,0:T(8,128)(2,1)S(1)} %constant_dynamic-update-slice_fusion), channel_id=1, source_target_pairs={{0,32},{8,40},{16,48},{24,56},{32,64},{40,72},{48,80},{56,88},{64,... | collective-permute-start | bytes 393224 | tf_op jit(solution)/shard_map/ppermute | solution.py:144
  57.0 14.2 %collective-permute-start.30 = (f32[256,256]{1,0:T(8,128)S(1)}, f32[256,256]{1,0:T(8,128)S(1)}, u32[]{:S(2)}, u32[]{:S(2)}) collective-permute-start(f32[256,256]{1,0:T(8,128)S(1)} %fusion.53), channel_id=1, source_target_pairs={{0,1},{1,0},{2,3},{3,2},{4,5},{5,4},{6,7},{7,6},{8,9},{9,8},{10,11... | collective-permute-start | bytes 786440 | tf_op jit(solution)/shard_map/ppermute | solution.py:167
  125.6 11.9 %collective-permute-start.15 = (bf16[256,256]{1,0:T(8,128)(2,1)S(1)}, bf16[256,256]{1,0:T(8,128)(2,1)S(1)}, u32[]{:S(2)}, u32[]{:S(2)}) collective-permute-start(bf16[256,256]{1,0:T(8,128)(2,1)S(1)} %get-tuple-element.194), channel_id=1, source_target_pairs={{8,0},{16,8},{24,16},{32,24},{40,32},{48,40},{56,48},{64,56},{72,6... | collective-permute-start | bytes 393224 | tf_op jit(solution)/shard_map/ppermute | solution.py:158
  129.7 14.3 %collective-permute-start.17 = (bf16[256,256]{1,0:T(8,128)(2,1)S(1)}, bf16[256,256]{1,0:T(8,128)(2,1)S(1)}, u32[]{:S(2)}, u32[]{:S(2)}) collective-permute-start(bf16[256,256]{1,0:T(8,128)(2,1)S(1)} %get-tuple-element.207), channel_id=1, source_target_pairs={{24,0},{32,8},{40,16},{48,24},{56,32},{64,40},{72,48},{80,56},{88,... | collective-permute-start | bytes 393224 | tf_op jit(solution)/shard_map/ppermute | solution.py:158
  131.0 16.2 %collective-permute-start.18 = (bf16[256,256]{1,0:T(8,128)(2,1)S(1)}, bf16[256,256]{1,0:T(8,128)(2,1)S(1)}, u32[]{:S(2)}, u32[]{:S(2)}) collective-permute-start(bf16[256,256]{1,0:T(8,128)(2,1)S(1)} %get-tuple-element.206), channel_id=1, source_target_pairs={{32,0},{40,8},{48,16},{56,24},{64,32},{72,40},{80,48},{88,56},{96,... | collective-permute-start | bytes 393224 | tf_op jit(solution)/shard_map/ppermute | solution.py:158
  132.3 20.7 %collective-permute-start.19 = (bf16[256,256]{1,0:T(8,128)(2,1)S(1)}, bf16[256,256]{1,0:T(8,128)(2,1)S(1)}, u32[]{:S(2)}, u32[]{:S(2)}) collective-permute-start(bf16[256,256]{1,0:T(8,128)(2,1)S(1)} %get-tuple-element.205), channel_id=1, source_target_pairs={{40,0},{48,8},{56,16},{64,24},{72,32},{80,40},{88,48},{96,56},{104... | collective-permute-start | bytes 393224 | tf_op jit(solution)/shard_map/ppermute | solution.py:158
  137.5 22.6 %collective-permute-start.20 = (bf16[256,256]{1,0:T(8,128)(2,1)S(1)}, bf16[256,256]{1,0:T(8,128)(2,1)S(1)}, u32[]{:S(2)}, u32[]{:S(2)}) collective-permute-start(bf16[256,256]{1,0:T(8,128)(2,1)S(1)} %get-tuple-element.204), channel_id=1, source_target_pairs={{48,0},{56,8},{64,16},{72,24},{80,32},{88,40},{96,48},{104,56},{11... | collective-permute-start | bytes 393224 | tf_op jit(solution)/shard_map/ppermute | solution.py:158
  139.1 25.3 %collective-permute-start.21 = (bf16[256,256]{1,0:T(8,128)(2,1)S(1)}, bf16[256,256]{1,0:T(8,128)(2,1)S(1)}, u32[]{:S(2)}, u32[]{:S(2)}) collective-permute-start(bf16[256,256]{1,0:T(8,128)(2,1)S(1)} %get-tuple-element.203), channel_id=1, source_target_pairs={{56,0},{64,8},{72,16},{80,24},{88,32},{96,40},{104,48},{112,56},{1... | collective-permute-start | bytes 393224 | tf_op jit(solution)/shard_map/ppermute | solution.py:158
  143.9 22.8 %collective-permute-start.22 = (bf16[256,256]{1,0:T(8,128)(2,1)S(1)}, bf16[256,256]{1,0:T(8,128)(2,1)S(1)}, u32[]{:S(2)}, u32[]{:S(2)}) collective-permute-start(bf16[256,256]{1,0:T(8,128)(2,1)S(1)} %get-tuple-element.202), channel_id=1, source_target_pairs={{64,0},{72,8},{80,16},{88,24},{96,32},{104,40},{112,48},{120,56},{... | collective-permute-start | bytes 393224 | tf_op jit(solution)/shard_map/ppermute | solution.py:158
  147.2 30.0 %collective-permute-start.23 = (bf16[256,256]{1,0:T(8,128)(2,1)S(1)}, bf16[256,256]{1,0:T(8,128)(2,1)S(1)}, u32[]{:S(2)}, u32[]{:S(2)}) collective-permute-start(bf16[256,256]{1,0:T(8,128)(2,1)S(1)} %get-tuple-element.201), channel_id=1, source_target_pairs={{72,0},{80,8},{88,16},{96,24},{104,32},{112,40},{120,48},{73,1},{8... | collective-permute-start | bytes 393224 | tf_op jit(solution)/shard_map/ppermute | solution.py:158
  153.0 25.5 %collective-permute-start.24 = (bf16[256,256]{1,0:T(8,128)(2,1)S(1)}, bf16[256,256]{1,0:T(8,128)(2,1)S(1)}, u32[]{:S(2)}, u32[]{:S(2)}) collective-permute-start(bf16[256,256]{1,0:T(8,128)(2,1)S(1)} %get-tuple-element.200), channel_id=1, source_target_pairs={{80,0},{88,8},{96,16},{104,24},{112,32},{120,40},{81,1},{89,9},{97... | collective-permute-start | bytes 393224 | tf_op jit(solution)/shard_map/ppermute | solution.py:158
  160.2 23.2 %collective-permute-start.25 = (bf16[256,256]{1,0:T(8,128)(2,1)S(1)}, bf16[256,256]{1,0:T(8,128)(2,1)S(1)}, u32[]{:S(2)}, u32[]{:S(2)}) collective-permute-start(bf16[256,256]{1,0:T(8,128)(2,1)S(1)} %get-tuple-element.199), channel_id=1, source_target_pairs={{88,0},{96,8},{104,16},{112,24},{120,32},{89,1},{97,9},{105,17},{1... | collective-permute-start | bytes 393224 | tf_op jit(solution)/shard_map/ppermute | solution.py:158
  164.4 19.7 %collective-permute-start.26 = (bf16[256,256]{1,0:T(8,128)(2,1)S(1)}, bf16[256,256]{1,0:T(8,128)(2,1)S(1)}, u32[]{:S(2)}, u32[]{:S(2)}) collective-permute-start(bf16[256,256]{1,0:T(8,128)(2,1)S(1)} %get-tuple-element.198), channel_id=1, source_target_pairs={{96,0},{104,8},{112,16},{120,24},{97,1},{105,9},{113,17},{121,25},... | collective-permute-start | bytes 393224 | tf_op jit(solution)/shard_map/ppermute | solution.py:158
  166.8 24.1 %collective-permute-start.27 = (bf16[256,256]{1,0:T(8,128)(2,1)S(1)}, bf16[256,256]{1,0:T(8,128)(2,1)S(1)}, u32[]{:S(2)}, u32[]{:S(2)}) collective-permute-start(bf16[256,256]{1,0:T(8,128)(2,1)S(1)} %get-tuple-element.197), channel_id=1, source_target_pairs={{104,0},{112,8},{120,16},{105,1},{113,9},{121,17},{106,2},{114,10}... | collective-permute-start | bytes 393224 | tf_op jit(solution)/shard_map/ppermute | solution.py:158
  177.2 16.3 %collective-permute-start.28 = (bf16[256,256]{1,0:T(8,128)(2,1)S(1)}, bf16[256,256]{1,0:T(8,128)(2,1)S(1)}, u32[]{:S(2)}, u32[]{:S(2)}) collective-permute-start(bf16[256,256]{1,0:T(8,128)(2,1)S(1)} %get-tuple-element.196), channel_id=1, source_target_pairs={{112,0},{120,8},{113,1},{121,9},{114,2},{122,10},{115,3},{123,11},... | collective-permute-start | bytes 393224 | tf_op jit(solution)/shard_map/ppermute | solution.py:158
  178.5 15.0 %collective-permute-start.29 = (bf16[256,256]{1,0:T(8,128)(2,1)S(1)}, bf16[256,256]{1,0:T(8,128)(2,1)S(1)}, u32[]{:S(2)}, u32[]{:S(2)}) collective-permute-start(bf16[256,256]{1,0:T(8,128)(2,1)S(1)} %get-tuple-element.195), channel_id=1, source_target_pairs={{120,0},{121,1},{122,2},{123,3},{124,4},{125,5},{126,6},{127,7}} | collective-permute-start | bytes 393224 | tf_op jit(solution)/shard_map/ppermute | solution.py:158
  (15 other events, 159.2 us)
Sparse Core Ops, SparseCore 0:
  21.9 78.6 all-gather.1

commit v6 on v5

--- a/solution.py
+++ b/solution.py
@@ -51,8 +51,7 @@
         def _():
             dq_acc[...] = jnp.zeros_like(dq_acc)
 
-        @pl.when(j < scalar_ref[0])
-        def _():
+        def block(masked):
             k = k_ref[...]
             v = v_ref[...]
             row_pos = scalar_ref[1] + lax.broadcasted_iota(jnp.int32, (rows, block_rows), 0)
@@ -65,7 +64,8 @@
                 q = q_ref[:, cols]
                 do = do_ref[:, cols]
                 s = lax.dot_general(q, k, (((1,), (1,)), ((), ())), preferred_element_type=jnp.float32) * scaling
-                s = jnp.where(keep, s, NEGATIVE)
+                if masked:
+                    s = jnp.where(keep, s, NEGATIVE)
                 p = jnp.exp(s - lt_ref[:, h : h + 1])
                 dp = lax.dot_general(do, v, (((1,), (1,)), ((), ())), preferred_element_type=jnp.float32)
                 ds = (p * (dp - rd_ref[:, h : h + 1]) * scaling).astype(jnp.bfloat16)
@@ -74,6 +74,16 @@
                 dv += lax.dot_general(p.astype(jnp.bfloat16), do, (((0,), (0,)), ((), ())), preferred_element_type=jnp.float32)
             dkv_ref[:, :head_dim] = dk.astype(dkv_ref.dtype)
             dkv_ref[:, head_dim:] = dv.astype(dkv_ref.dtype)
+
+        below = j * block_rows + block_rows - 1 <= scalar_ref[1]
+
+        @pl.when(jnp.logical_and(j < scalar_ref[0], below))
+        def _():
+            block(False)
+
+        @pl.when(jnp.logical_and(j < scalar_ref[0], jnp.logical_not(below)))
+        def _():
+            block(True)
 
         @pl.when(j >= scalar_ref[0])
         def _():
@@ -159,6 +169,22 @@
     return total
 
 
+def halving_reduce(parts, axis_name):
+    size = lax.axis_size(axis_name)
+    own = lax.axis_index(axis_name)
+    held = parts.astype(jnp.float32)
+    stride = 1
+    while stride < size:
+        halves = held.reshape((held.shape[0] // 2, 2) + held.shape[1:])
+        high = (own & stride) != 0
+        keep = jnp.where(high, halves[:, 1], halves[:, 0])
+        send = jnp.where(high, halves[:, 0], halves[:, 1]).astype(parts.dtype)
+        pairs = [(i, i ^ stride) for i in range(size)]
+        held = keep + lax.ppermute(send, axis_name, pairs).astype(jnp.float32)
+        stride *= 2
+    return held[0]
+
+
 def butterfly_sum(value, axis_name):
     size = lax.axis_size(axis_name)
     stride = 1
@@ -290,7 +316,7 @@
         block_rows,
     )
     ctx_size = lax.axis_size("ctx")
-    key_sums = causal_reduce(
+    key_sums = halving_reduce(
         backward_buffer.reshape((ctx_size, tokens // ctx_size) + backward_buffer.shape[1:]), "ctx"
     )
     grad_key = key_sums[:, : local_groups * head_dim].astype(jnp.bfloat16)

time: 204 us -> 213 us (1.044)
  starting transfers between devices: 69.2 us -> 76.6 us
  other arithmetic: 5.93 us -> 10.7 us
    ppermute x15 -> x4, waiting for transfers between devices: 42.6 us -> 13.7 us  [halving_reduce(): held = keep + lax.ppermute(send, axis_name, pairs).astype(jnp.float32)]
    all_gather x1, waiting for transfers between devices: 10.6 us -> 29.7 us  [body(): lax.all_gather(grad_out, 'head', axis=1, tiled=True).astype(jnp.float32)]
    ppermute x15 -> x4, starting transfers between devices: 20.1 us -> 32 us  [halving_reduce(): held = keep + lax.ppermute(send, axis_name, pairs).astype(jnp.float32)]
    ppermute x3, starting transfers between devices: 6.38 us -> 1.73 us  [butterfly_sum(): value = value + lax.ppermute(value, axis_name, pairs)]
    ppermute x3, waiting for transfers between devices: 18.5 us -> 22.6 us  [butterfly_sum(): value = value + lax.ppermute(value, axis_name, pairs)]
    ppermute x15, waiting for transfers between devices: 0.28 us -> 4.12 us  [causal_gather(): received.append(lax.ppermute(value, axis_name, pairs))]
    convert_element_type x0 -> x5, other arithmetic: none -> 3.38 us  [the longest x1 2.03 us: halving_reduce(): held = parts.astype(jnp.float32)]
    add x0 -> x2, other arithmetic: none -> 3.22 us  [halving_reduce(): held = keep + lax.ppermute(send, axis_name, pairs).astype(jnp.float32)]
  transfers between devices with their start and end apart: 34 -> 23, of which waited for: 17 -> 10; matrix products, arithmetic and copies ran while one was open for 9% -> 7% of each run, Pallas kernels for 0% -> 0%
where the time goes in v6:
time: 213 us; the launch traced here: 209 us
  starting transfers between devices  76.6 us (36%)
  waiting for transfers between devices  70.1 us (33%)
  matrix products  18 us (8%)
  between operations  14.7 us (7%)
  other arithmetic  10.7 us (5%)
  local copies, waits for them, and re-layouts  9.34 us (4%)
  Pallas kernels  9.29 us (4%)
    ppermute x15, starting transfers between devices, causal_gather(): received.append(lax.ppermute(value, axis_name, pairs))  42.8 us
    ppermute x4, starting transfers between devices, halving_reduce(): held = keep + lax.ppermute(send, axis_name, pairs).astype(jnp.float32)  32 us
    all_gather x1, waiting for transfers between devices, body(): lax.all_gather(grad_out, 'head', axis=1, tiled=True).astype(jnp.float32)  29.7 us
    ppermute x3, waiting for transfers between devices, butterfly_sum(): value = value + lax.ppermute(value, axis_name, pairs)  22.6 us
    ppermute x4, waiting for transfers between devices, halving_reduce(): held = keep + lax.ppermute(send, axis_name, pairs).astype(jnp.float32)  13.7 us
    dot_general x1, matrix products, body(): lax.dot_general(piece_part, out_weight, (((1,), (1,)), ((), ())), preferr...  11.6 us
    pallas_call x1, Pallas kernels, flash_backward(): pl.pallas_call(kernel, grid_spec=grid_spec, out_shape=[jax.ShapeDtypeStru...  9.29 us
    unnamed x47, local copies, waits for them, and re-layouts  5.36 us
  transfers between devices with their start and end apart: 23, of which 10 were waited for; matrix products, arithmetic and copies ran while one was open for 7% of the time, Pallas kernels for 0%

profile of v6, /device:TPU:1, one launch (start us, length us, event | category | flops | bytes accessed | tf_op | source)
XLA Modules:
  0.0 209.1 jit_solution(2047518741937393252)
XLA Ops:
  9.7 8.1 %collective-permute-start.1 = (bf16[256,256]{1,0:T(8,128)(2,1)S(1)}, bf16[256,256]{1,0:T(8,128)(2,1)S(1)}, u32[]{:S(2)}, u32[]{:S(2)}) collective-permute-start(bf16[256,256]{1,0:T(8,128)(2,1)S(1)} %constant_dynamic-update-slice_fusion), channel_id=1, source_target_pairs={{0,112},{8,120},{1,113},{9,121},{2,114},{10,122},{3,115},{11,123},... | collective-permute-start | bytes 393224 | tf_op jit(solution)/shard_map/ppermute | solution.py:154
  31.6 5.2 %collective-permute-start.9 = (bf16[256,256]{1,0:T(8,128)(2,1)S(1)}, bf16[256,256]{1,0:T(8,128)(2,1)S(1)}, u32[]{:S(2)}, u32[]{:S(2)}) collective-permute-start(bf16[256,256]{1,0:T(8,128)(2,1)S(1)} %constant_dynamic-update-slice_fusion), channel_id=1, source_target_pairs={{0,48},{8,56},{16,64},{24,72},{32,80},{40,88},{48,96},{56,104},{64... | collective-permute-start | bytes 393224 | tf_op jit(solution)/shard_map/ppermute | solution.py:154
  36.9 5.0 %collective-permute-start.10 = (bf16[256,256]{1,0:T(8,128)(2,1)S(1)}, bf16[256,256]{1,0:T(8,128)(2,1)S(1)}, u32[]{:S(2)}, u32[]{:S(2)}) collective-permute-start(bf16[256,256]{1,0:T(8,128)(2,1)S(1)} %constant_dynamic-update-slice_fusion), channel_id=1, source_target_pairs={{0,40},{8,48},{16,56},{24,64},{32,72},{40,80},{48,88},{56,96},{64,... | collective-permute-start | bytes 393224 | tf_op jit(solution)/shard_map/ppermute | solution.py:154
  42.1 6.3 %collective-permute-start.11 = (bf16[256,256]{1,0:T(8,128)(2,1)S(1)}, bf16[256,256]{1,0:T(8,128)(2,1)S(1)}, u32[]{:S(2)}, u32[]{:S(2)}) collective-permute-start(bf16[256,256]{1,0:T(8,128)(2,1)S(1)} %constant_dynamic-update-slice_fusion), channel_id=1, source_target_pairs={{0,32},{8,40},{16,48},{24,56},{32,64},{40,72},{48,80},{56,88},{64,... | collective-permute-start | bytes 393224 | tf_op jit(solution)/shard_map/ppermute | solution.py:154
  49.8 4.8 %collective-permute-start.13 = (bf16[256,256]{1,0:T(8,128)(2,1)S(1)}, bf16[256,256]{1,0:T(8,128)(2,1)S(1)}, u32[]{:S(2)}, u32[]{:S(2)}) collective-permute-start(bf16[256,256]{1,0:T(8,128)(2,1)S(1)} %constant_dynamic-update-slice_fusion), channel_id=1, source_target_pairs={{0,16},{8,24},{16,32},{24,40},{32,48},{40,56},{48,64},{56,72},{64,... | collective-permute-start | bytes 393224 | tf_op jit(solution)/shard_map/ppermute | solution.py:154
  54.6 2.4 %collective-permute-start.14 = (bf16[256,256]{1,0:T(8,128)(2,1)S(1)}, bf16[256,256]{1,0:T(8,128)(2,1)S(1)}, u32[]{:S(2)}, u32[]{:S(2)}) collective-permute-start(bf16[256,256]{1,0:T(8,128)(2,1)S(1)} %constant_dynamic-update-slice_fusion), channel_id=1, source_target_pairs={{0,8},{8,16},{16,24},{24,32},{32,40},{40,48},{48,56},{56,64},{64,7... | collective-permute-start | bytes 393224 | tf_op jit(solution)/shard_map/ppermute | solution.py:154
  57.1 2.1 %collective-permute-done.14 = bf16[256,256]{1,0:T(8,128)(2,1)S(1)} collective-permute-done((bf16[256,256]{1,0:T(8,128)(2,1)S(1)}, bf16[256,256]{1,0:T(8,128)(2,1)S(1)}, u32[]{:S(2)}, u32[]{:S(2)}) %collective-permute-start.14) | collective-permute-done | bytes 131104 | tf_op jit(solution)/shard_map/ppermute | solution.py:154
  60.9 1.9 while.24
  63.8 3.0 %while.25 = (s32[]{:T(128)}, f32[256,8,128]{2,0,1:T(8,128)S(1)}, s32[]{:T(128)}, bf16[4096,128]{1,0:T(8,128)(2,1)S(1)}, bf16[256,8,128]{2,0,1:T(8,128)(2,1)S(1)}...) while((s32[]{:T(128)}, f32[256,8,128]{2,0,1:T(8,128)S(1)}, ...), condition=%wide.region_5.6_spmd.clone, body=%wide.region_4.5_spmd.clone.sunk | while | flops 541459200 | bytes 3161259 | solution.py:279
  63.9 2.7 %fusion.65 = f32[256,8,128]{2,0,1:T(8,128)S(1)} fusion(f32[256,8,128]{2,0,1:T(8,128)S(1)} %get-tuple-element.380, bf16[256,8,128]{2,0,1:T(8,128)(2,1)S(1)} %get-tuple-element.395, f32[256,8]{0,1:T(8,128)S(1)} %get-tuple-element.396, pred[256,512]{0,1:T(8,128)(4,1)S(1)} %broadcast_compare_fusion.5, bf16[4096,128]{1,0:T(8,128)(2,1)} %get-tuple-element.397, ...), kind=kOutput, calls=%fused_computation.18.clone.1 | convolution fusion | flops 541327360 | bytes 3023872 | tf_op jit(solution)/shard_map/while/body/tgk,kd->tgd/dot_general | solution.py:275
  66.8 29.7 %all-gather.2.cloned.1.call-done = bf16[256,8192]{1,0:T(8,128)(2,1)} async-done(((bf16[256,1024]{1,0:T(8,128)(2,1)}), bf16[256,8192]{1,0:T(8,128)(2,1)}) %all-gather.2.cloned.1.call-update) | async-done | bytes 4194320 | tf_op jit(solution)/shard_map/all_gather | solution.py:231
  96.4 11.6 %fusion.26.do_ref = bf16[256,1024]{1,0:T(8,128)(2,1)S(1)} fusion(bf16[1024,8192]{1,0:T(8,128)(2,1)} %param.15, bf16[256,8192]{1,0:T(8,128)(2,1)} %all-gather.2.cloned.1.call-done, f32[256]{0:T(256)S(1)} %convert_add_fusion), kind=kOutput, calls=%fused_computation.38 | convolution fusion | flops 4301520896 | bytes 21496832 | tf_op jit(solution)/shard_map/dot_general | solution.py:288
  109.2 9.3 %shard_map.110 = (bf16[256,1024]{1,0:T(8,128)(2,1)}, bf16[4096,256]{1,0:T(8,128)(2,1)}) custom-call(s32[2]{0:T(128)} %pad_add_fusion.scalar_ref, bf16[256,1024]{1,0:T(8,128)(2,1)} %q_ref.1, bf16[256,1024]{1,0:T(8,128)(2,1)} %copy-done.2, bf16[4096,128]{1,0:T(8,128)(2,1)S(1)} %get-tuple-element.406, bf16[4096,128]{1,0:T(8,128)(2,1)} %get-tuple-element.407, ...), custom_call_target="tpu_custom_call" | custom-call | tf_op jit(solution)/shard_map/pallas_call | solution.py:117
  118.5 2.0 convert.8
  120.6 2.0 copy-done.1
  125.5 9.2 %collective-permute-done.19 = f32[256,256]{1,0:T(8,128)S(1)} collective-permute-done((f32[256,256]{1,0:T(8,128)S(1)}, f32[256,256]{1,0:T(8,128)S(1)}, u32[]{:S(2)}, u32[]{:S(2)}) %collective-permute-start.19) | collective-permute-done | bytes 262176 | tf_op jit(solution)/shard_map/ppermute | solution.py:193
  134.8 7.0 %collective-permute-done.20 = f32[256,256]{1,0:T(8,128)S(1)} collective-permute-done((f32[256,256]{1,0:T(8,128)S(1)}, f32[256,256]{1,0:T(8,128)S(1)}, u32[]{:S(2)}, u32[]{:S(2)}) %collective-permute-start.20) | collective-permute-done | bytes 262176 | tf_op jit(solution)/shard_map/ppermute | solution.py:193
  143.2 6.4 %collective-permute-done.21 = f32[256,256]{1,0:T(8,128)S(1)} collective-permute-done((f32[256,256]{1,0:T(8,128)S(1)}, f32[256,256]{1,0:T(8,128)S(1)}, u32[]{:S(2)}, u32[]{:S(2)}) %collective-permute-start.21) | collective-permute-done | bytes 262176 | tf_op jit(solution)/shard_map/ppermute | solution.py:193
  149.7 3.0 %bitcast_add_fusion = f32[8,256,256]{2,1,0:T(8,128)S(1)} fusion(bf16[8,256,256]{2,1,0:T(8,128)(2,1)} %collective-permute-done.15, f32[8,2,256,256]{3,2,1,0:T(8,128)} %copy-done.1, pred[]{:T(512)S(6)} %ne.27), kind=kLoop, calls=%fused_computation.32 | loop fusion | flops 1572864 | bytes 7340033 | tf_op jit(solution)/shard_map/add | solution.py:183
  152.8 5.1 %collective-permute-start.16 = (bf16[4,256,256]{2,1,0:T(8,128)(2,1)S(1)}, bf16[4,256,256]{2,1,0:T(8,128)(2,1)S(1)}, u32[]{:S(2)}, u32[]{:S(2)}) collective-permute-start(bf16[4,256,256]{2,1,0:T(8,128)(2,1)S(1)} %fusion.31), channel_id=1, source_target_pairs={{0,16},{8,24},{16,0},{24,8},{32,48},{40,56},{48,32},{56,40},{64,80... | collective-permute-start | bytes 1572872 | tf_op jit(solution)/shard_map/ppermute | solution.py:183
  160.1 7.5 %collective-permute-done.16 = bf16[4,256,256]{2,1,0:T(8,128)(2,1)S(1)} collective-permute-done((bf16[4,256,256]{2,1,0:T(8,128)(2,1)S(1)}, bf16[4,256,256]{2,1,0:T(8,128)(2,1)S(1)}, u32[]{:S(2)}, u32[]{:S(2)}) %collective-permute-start.16) | collective-permute-done | bytes 524320 | tf_op jit(solution)/shard_map/ppermute | solution.py:183
  167.8 9.6 %collective-permute-start.17 = (bf16[2,256,256]{2,1,0:T(8,128)(2,1)S(1)}, bf16[2,256,256]{2,1,0:T(8,128)(2,1)S(1)}, u32[]{:S(2)}, u32[]{:S(2)}) collective-permute-start(bf16[2,256,256]{2,1,0:T(8,128)(2,1)S(1)} %fusion.40), channel_id=1, source_target_pairs={{0,32},{8,40},{16,48},{24,56},{32,0},{40,8},{48,16},{56,24},{64,96... | collective-permute-start | bytes 786440 | tf_op jit(solution)/shard_map/ppermute | solution.py:183
  178.5 4.4 %collective-permute-done.17 = bf16[2,256,256]{2,1,0:T(8,128)(2,1)S(1)} collective-permute-done((bf16[2,256,256]{2,1,0:T(8,128)(2,1)S(1)}, bf16[2,256,256]{2,1,0:T(8,128)(2,1)S(1)}, u32[]{:S(2)}, u32[]{:S(2)}) %collective-permute-start.17) | collective-permute-done | bytes 262176 | tf_op jit(solution)/shard_map/ppermute | solution.py:183
  183.0 16.2 %collective-permute-start.18 = (bf16[1,256,256]{2,1,0:T(8,128)(2,1)S(1)}, bf16[1,256,256]{2,1,0:T(8,128)(2,1)S(1)}, u32[]{:S(2)}, u32[]{:S(2)}) collective-permute-start(bf16[1,256,256]{2,1,0:T(8,128)(2,1)S(1)} %fusion.43), channel_id=1, source_target_pairs={{0,64},{8,72},{16,80},{24,88},{32,96},{40,104},{48,112},{56,120},{... | collective-permute-start | bytes 393224 | tf_op jit(solution)/shard_map/ppermute | solution.py:183
  (120 shorter events, 34.6 us)
Async XLA Ops:
  7.2 117.7 %copy-start = (bf16[256,1024]{1,0:T(8,128)(2,1)S(1)}, bf16[256,1024]{1,0:T(8,128)(2,1)}, u32[]{:S(2)}) copy-start(bf16[256,1024]{1,0:T(8,128)(2,1)} %param.11) | copy-start | bytes 1572868
  7.2 89.3 %all-gather.2.cloned.1.call-start = ((), (), s32[]{:S(2)}) async-start(), calls=%async_computation | async-start | bytes 4718592 | tf_op jit(solution)/shard_map/all_gather | solution.py:231
  9.0 15.6 %collective-permute-start = (bf16[256,256]{1,0:T(8,128)(2,1)S(1)}, bf16[256,256]{1,0:T(8,128)(2,1)S(1)}, u32[]{:S(2)}, u32[]{:S(2)}) collective-permute-start(bf16[256,256]{1,0:T(8,128)(2,1)S(1)} %constant_dynamic-update-slice_fusion), channel_id=1, source_target_pairs={{0,120},{1,121},{2,122},{3,123},{4,124},{5,125},{6,126},{7,127}} | collective-permute-start | bytes 393224 | tf_op jit(solution)/shard_map/ppermute | solution.py:154
  9.7 16.2 %collective-permute-start.1 = (bf16[256,256]{1,0:T(8,128)(2,1)S(1)}, bf16[256,256]{1,0:T(8,128)(2,1)S(1)}, u32[]{:S(2)}, u32[]{:S(2)}) collective-permute-start(bf16[256,256]{1,0:T(8,128)(2,1)S(1)} %constant_dynamic-update-slice_fusion), channel_id=1, source_target_pairs={{0,112},{8,120},{1,113},{9,121},{2,114},{10,122},{3,115},{11,123},... | collective-permute-start | bytes 393224 | tf_op jit(solution)/shard_map/ppermute | solution.py:154
  17.8 9.4 %collective-permute-start.2 = (bf16[256,256]{1,0:T(8,128)(2,1)S(1)}, bf16[256,256]{1,0:T(8,128)(2,1)S(1)}, u32[]{:S(2)}, u32[]{:S(2)}) collective-permute-start(bf16[256,256]{1,0:T(8,128)(2,1)S(1)} %constant_dynamic-update-slice_fusion), channel_id=1, source_target_pairs={{0,104},{8,112},{16,120},{1,105},{9,113},{17,121},{2,106},{10,114}... | collective-permute-start | bytes 393224 | tf_op jit(solution)/shard_map/ppermute | solution.py:154
  19.1 9.4 %collective-permute-start.3 = (bf16[256,256]{1,0:T(8,128)(2,1)S(1)}, bf16[256,256]{1,0:T(8,128)(2,1)S(1)}, u32[]{:S(2)}, u32[]{:S(2)}) collective-permute-start(bf16[256,256]{1,0:T(8,128)(2,1)S(1)} %constant_dynamic-update-slice_fusion), channel_id=1, source_target_pairs={{0,96},{8,104},{16,112},{24,120},{1,97},{9,105},{17,113},{25,121},... | collective-permute-start | bytes 393224 | tf_op jit(solution)/shard_map/ppermute | solution.py:154
  20.4 11.2 %collective-permute-start.4 = (bf16[256,256]{1,0:T(8,128)(2,1)S(1)}, bf16[256,256]{1,0:T(8,128)(2,1)S(1)}, u32[]{:S(2)}, u32[]{:S(2)}) collective-permute-start(bf16[256,256]{1,0:T(8,128)(2,1)S(1)} %constant_dynamic-update-slice_fusion), channel_id=1, source_target_pairs={{0,88},{8,96},{16,104},{24,112},{32,120},{1,89},{9,97},{17,105},{2... | collective-permute-start | bytes 393224 | tf_op jit(solution)/shard_map/ppermute | solution.py:154
  24.6 12.3 %collective-permute-start.5 = (bf16[256,256]{1,0:T(8,128)(2,1)S(1)}, bf16[256,256]{1,0:T(8,128)(2,1)S(1)}, u32[]{:S(2)}, u32[]{:S(2)}) collective-permute-start(bf16[256,256]{1,0:T(8,128)(2,1)S(1)} %constant_dynamic-update-slice_fusion), channel_id=1, source_target_pairs={{0,80},{8,88},{16,96},{24,104},{32,112},{40,120},{1,81},{9,89},{17... | collective-permute-start | bytes 393224 | tf_op jit(solution)/shard_map/ppermute | solution.py:154
  25.9 16.3 %collective-permute-start.6 = (bf16[256,256]{1,0:T(8,128)(2,1)S(1)}, bf16[256,256]{1,0:T(8,128)(2,1)S(1)}, u32[]{:S(2)}, u32[]{:S(2)}) collective-permute-start(bf16[256,256]{1,0:T(8,128)(2,1)S(1)} %constant_dynamic-update-slice_fusion), channel_id=1, source_target_pairs={{0,72},{8,80},{16,88},{24,96},{32,104},{40,112},{48,120},{1,73},{9... | collective-permute-start | bytes 393224 | tf_op jit(solution)/shard_map/ppermute | solution.py:154
  27.2 21.2 %collective-permute-start.7 = (bf16[256,256]{1,0:T(8,128)(2,1)S(1)}, bf16[256,256]{1,0:T(8,128)(2,1)S(1)}, u32[]{:S(2)}, u32[]{:S(2)}) collective-permute-start(bf16[256,256]{1,0:T(8,128)(2,1)S(1)} %constant_dynamic-update-slice_fusion), channel_id=1, source_target_pairs={{0,64},{8,72},{16,80},{24,88},{32,96},{40,104},{48,112},{56,120},{... | collective-permute-start | bytes 393224 | tf_op jit(solution)/shard_map/ppermute | solution.py:154
  28.5 21.2 %collective-permute-start.8 = (bf16[256,256]{1,0:T(8,128)(2,1)S(1)}, bf16[256,256]{1,0:T(8,128)(2,1)S(1)}, u32[]{:S(2)}, u32[]{:S(2)}) collective-permute-start(bf16[256,256]{1,0:T(8,128)(2,1)S(1)} %constant_dynamic-update-slice_fusion), channel_id=1, source_target_pairs={{0,56},{8,64},{16,72},{24,80},{32,88},{40,96},{48,104},{56,112},{6... | collective-permute-start | bytes 393224 | tf_op jit(solution)/shard_map/ppermute | solution.py:154
  31.6 23.0 %collective-permute-start.9 = (bf16[256,256]{1,0:T(8,128)(2,1)S(1)}, bf16[256,256]{1,0:T(8,128)(2,1)S(1)}, u32[]{:S(2)}, u32[]{:S(2)}) collective-permute-start(bf16[256,256]{1,0:T(8,128)(2,1)S(1)} %constant_dynamic-update-slice_fusion), channel_id=1, source_target_pairs={{0,48},{8,56},{16,64},{24,72},{32,80},{40,88},{48,96},{56,104},{64... | collective-permute-start | bytes 393224 | tf_op jit(solution)/shard_map/ppermute | solution.py:154
  36.9 20.2 %collective-permute-start.10 = (bf16[256,256]{1,0:T(8,128)(2,1)S(1)}, bf16[256,256]{1,0:T(8,128)(2,1)S(1)}, u32[]{:S(2)}, u32[]{:S(2)}) collective-permute-start(bf16[256,256]{1,0:T(8,128)(2,1)S(1)} %constant_dynamic-update-slice_fusion), channel_id=1, source_target_pairs={{0,40},{8,48},{16,56},{24,64},{32,72},{40,80},{48,88},{56,96},{64,... | collective-permute-start | bytes 393224 | tf_op jit(solution)/shard_map/ppermute | solution.py:154
  42.1 14.9 %collective-permute-start.11 = (bf16[256,256]{1,0:T(8,128)(2,1)S(1)}, bf16[256,256]{1,0:T(8,128)(2,1)S(1)}, u32[]{:S(2)}, u32[]{:S(2)}) collective-permute-start(bf16[256,256]{1,0:T(8,128)(2,1)S(1)} %constant_dynamic-update-slice_fusion), channel_id=1, source_target_pairs={{0,32},{8,40},{16,48},{24,56},{32,64},{40,72},{48,80},{56,88},{64,... | collective-permute-start | bytes 393224 | tf_op jit(solution)/shard_map/ppermute | solution.py:154
  48.4 8.7 %collective-permute-start.12 = (bf16[256,256]{1,0:T(8,128)(2,1)S(1)}, bf16[256,256]{1,0:T(8,128)(2,1)S(1)}, u32[]{:S(2)}, u32[]{:S(2)}) collective-permute-start(bf16[256,256]{1,0:T(8,128)(2,1)S(1)} %constant_dynamic-update-slice_fusion), channel_id=1, source_target_pairs={{0,24},{8,32},{16,40},{24,48},{32,56},{40,64},{48,72},{56,80},{64,... | collective-permute-start | bytes 393224 | tf_op jit(solution)/shard_map/ppermute | solution.py:154
  49.8 7.3 %collective-permute-start.13 = (bf16[256,256]{1,0:T(8,128)(2,1)S(1)}, bf16[256,256]{1,0:T(8,128)(2,1)S(1)}, u32[]{:S(2)}, u32[]{:S(2)}) collective-permute-start(bf16[256,256]{1,0:T(8,128)(2,1)S(1)} %constant_dynamic-update-slice_fusion), channel_id=1, source_target_pairs={{0,16},{8,24},{16,32},{24,40},{32,48},{40,56},{48,64},{56,72},{64,... | collective-permute-start | bytes 393224 | tf_op jit(solution)/shard_map/ppermute | solution.py:154
  54.6 4.7 %collective-permute-start.14 = (bf16[256,256]{1,0:T(8,128)(2,1)S(1)}, bf16[256,256]{1,0:T(8,128)(2,1)S(1)}, u32[]{:S(2)}, u32[]{:S(2)}) collective-permute-start(bf16[256,256]{1,0:T(8,128)(2,1)S(1)} %constant_dynamic-update-slice_fusion), channel_id=1, source_target_pairs={{0,8},{8,16},{16,24},{24,32},{32,40},{40,48},{48,56},{56,64},{64,7... | collective-permute-start | bytes 393224 | tf_op jit(solution)/shard_map/ppermute | solution.py:154
  123.7 25.9 %collective-permute-start.15 = (bf16[8,256,256]{2,1,0:T(8,128)(2,1)}, bf16[8,256,256]{2,1,0:T(8,128)(2,1)}, u32[]{:S(2)}, u32[]{:S(2)}) collective-permute-start(bf16[8,256,256]{2,1,0:T(8,128)(2,1)} %fusion.27), channel_id=1, source_target_pairs={{0,8},{8,0},{16,24},{24,16},{32,40},{40,32},{48,56},{56,48},{64,72... | collective-permute-start | bytes 3145736 | tf_op jit(solution)/shard_map/ppermute | solution.py:183
  125.2 9.5 %collective-permute-start.19 = (f32[256,256]{1,0:T(8,128)S(1)}, f32[256,256]{1,0:T(8,128)S(1)}, u32[]{:S(2)}, u32[]{:S(2)}) collective-permute-start(f32[256,256]{1,0:T(8,128)S(1)} %fusion.47), channel_id=1, source_target_pairs={{0,1},{1,0},{2,3},{3,2},{4,5},{5,4},{6,7},{7,6},{8,9},{9,8},{10,11... | collective-permute-start | bytes 786440 | tf_op jit(solution)/shard_map/ppermute | solution.py:193
  134.7 7.1 %collective-permute-start.20 = (f32[256,256]{1,0:T(8,128)S(1)}, f32[256,256]{1,0:T(8,128)S(1)}, u32[]{:S(2)}, u32[]{:S(2)}) collective-permute-start(f32[256,256]{1,0:T(8,128)S(1)} %add.122), channel_id=1, source_target_pairs={{0,2},{1,3},{2,0},{3,1},{4,6},{5,7},{6,4},{7,5},{8,10},{9,11},{10,... | collective-permute-start | bytes 786440 | tf_op jit(solution)/shard_map/ppermute | solution.py:193
  141.9 7.7 %collective-permute-start.21 = (f32[256,256]{1,0:T(8,128)S(1)}, f32[256,256]{1,0:T(8,128)S(1)}, u32[]{:S(2)}, u32[]{:S(2)}) collective-permute-start(f32[256,256]{1,0:T(8,128)S(1)} %add.123), channel_id=1, source_target_pairs={{0,4},{1,5},{2,6},{3,7},{4,0},{5,1},{6,2},{7,3},{8,12},{9,13},{10,... | collective-permute-start | bytes 786440 | tf_op jit(solution)/shard_map/ppermute | solution.py:193
  152.8 14.7 %collective-permute-start.16 = (bf16[4,256,256]{2,1,0:T(8,128)(2,1)S(1)}, bf16[4,256,256]{2,1,0:T(8,128)(2,1)S(1)}, u32[]{:S(2)}, u32[]{:S(2)}) collective-permute-start(bf16[4,256,256]{2,1,0:T(8,128)(2,1)S(1)} %fusion.31), channel_id=1, source_target_pairs={{0,16},{8,24},{16,0},{24,8},{32,48},{40,56},{48,32},{56,40},{64,80... | collective-permute-start | bytes 1572872 | tf_op jit(solution)/shard_map/ppermute | solution.py:183
  167.8 15.1 %collective-permute-start.17 = (bf16[2,256,256]{2,1,0:T(8,128)(2,1)S(1)}, bf16[2,256,256]{2,1,0:T(8,128)(2,1)S(1)}, u32[]{:S(2)}, u32[]{:S(2)}) collective-permute-start(bf16[2,256,256]{2,1,0:T(8,128)(2,1)S(1)} %fusion.40), channel_id=1, source_target_pairs={{0,32},{8,40},{16,48},{24,56},{32,0},{40,8},{48,16},{56,24},{64,96... | collective-permute-start | bytes 786440 | tf_op jit(solution)/shard_map/ppermute | solution.py:183
  183.0 18.6 %collective-permute-start.18 = (bf16[1,256,256]{2,1,0:T(8,128)(2,1)S(1)}, bf16[1,256,256]{2,1,0:T(8,128)(2,1)S(1)}, u32[]{:S(2)}, u32[]{:S(2)}) collective-permute-start(bf16[1,256,256]{2,1,0:T(8,128)(2,1)S(1)} %fusion.43), channel_id=1, source_target_pairs={{0,64},{8,72},{16,80},{24,88},{32,96},{40,104},{48,112},{56,120},{... | collective-permute-start | bytes 393224 | tf_op jit(solution)/shard_map/ppermute | solution.py:183
  (5 other events, 30.0 us)
Sparse Core Ops, SparseCore 0:
  21.9 74.5 all-gather.1

commit v7 on v5

--- a/solution.py
+++ b/solution.py
@@ -51,8 +51,7 @@
         def _():
             dq_acc[...] = jnp.zeros_like(dq_acc)
 
-        @pl.when(j < scalar_ref[0])
-        def _():
+        def block(masked):
             k = k_ref[...]
             v = v_ref[...]
             row_pos = scalar_ref[1] + lax.broadcasted_iota(jnp.int32, (rows, block_rows), 0)
@@ -65,7 +64,8 @@
                 q = q_ref[:, cols]
                 do = do_ref[:, cols]
                 s = lax.dot_general(q, k, (((1,), (1,)), ((), ())), preferred_element_type=jnp.float32) * scaling
-                s = jnp.where(keep, s, NEGATIVE)
+                if masked:
+                    s = jnp.where(keep, s, NEGATIVE)
                 p = jnp.exp(s - lt_ref[:, h : h + 1])
                 dp = lax.dot_general(do, v, (((1,), (1,)), ((), ())), preferred_element_type=jnp.float32)
                 ds = (p * (dp - rd_ref[:, h : h + 1]) * scaling).astype(jnp.bfloat16)
@@ -74,6 +74,16 @@
                 dv += lax.dot_general(p.astype(jnp.bfloat16), do, (((0,), (0,)), ((), ())), preferred_element_type=jnp.float32)
             dkv_ref[:, :head_dim] = dk.astype(dkv_ref.dtype)
             dkv_ref[:, head_dim:] = dv.astype(dkv_ref.dtype)
+
+        below = j * block_rows + block_rows - 1 <= scalar_ref[1]
+
+        @pl.when(jnp.logical_and(j < scalar_ref[0], below))
+        def _():
+            block(False)
+
+        @pl.when(jnp.logical_and(j < scalar_ref[0], jnp.logical_not(below)))
+        def _():
+            block(True)
 
         @pl.when(j >= scalar_ref[0])
         def _():
@@ -206,6 +216,7 @@
         * loss_weight[:, None]
     ).astype(jnp.bfloat16)
     pair_all = causal_gather(jnp.concatenate([key_rows, value_rows], axis=1), "ctx")
+    hidden_gram, pair_all = lax.optimization_barrier((hidden_gram, pair_all))
     kv_width = key_rows.shape[1]
     keys_all, values_all = (pair_all[:, :kv_width], pair_all[:, kv_width:])
     tokens = keys_all.shape[0]

time: 204 us -> 223 us (1.093)
  waiting for transfers between devices: 72 us -> 88.9 us
    ppermute x15, waiting for transfers between devices: 42.6 us -> 59.3 us  [causal_reduce(): total = total + lax.ppermute(sent, axis_name, pairs).astype(jnp.float32)]
    ppermute x3, waiting for transfers between devices: 18.5 us -> 25.1 us  [butterfly_sum(): value = value + lax.ppermute(value, axis_name, pairs)]
    all_gather x1, waiting for transfers between devices: 10.6 us -> 4.27 us  [body(): lax.all_gather(grad_out, 'head', axis=1, tiled=True).astype(jnp.float32)]
    dot_general x1, matrix products: 1.68 us -> 5.08 us  [gram_squares(): lax.dot_general(left_side, left_side, (((1,), (1,)), ((), ())), preferred...]
    unnamed x45 -> x43, local copies, waits for them, and re-layouts: 4.39 us -> 4.89 us
  transfers between devices with their start and end apart: 34 -> 34, of which waited for: 17 -> 17; matrix products, arithmetic and copies ran while one was open for 9% -> 8% of each run, Pallas kernels for 0% -> 0%
where the time goes in v7:
time: 223 us; the launch traced here: 221 us
  waiting for transfers between devices  88.9 us (40%)
  starting transfers between devices  69.5 us (31%)
  matrix products  21.6 us (10%)
  between operations  14.8 us (7%)
  local copies, waits for them, and re-layouts  11.8 us (5%)
  Pallas kernels  9.31 us (4%)
  other arithmetic  4.65 us (2%)
    ppermute x15, waiting for transfers between devices, causal_reduce(): total = total + lax.ppermute(sent, axis_name, pairs).astype(jnp.float32)  59.3 us
    ppermute x15, starting transfers between devices, causal_gather(): received.append(lax.ppermute(value, axis_name, pairs))  42.7 us
    ppermute x3, waiting for transfers between devices, butterfly_sum(): value = value + lax.ppermute(value, axis_name, pairs)  25.1 us
    ppermute x15, starting transfers between devices, causal_reduce(): total = total + lax.ppermute(sent, axis_name, pairs).astype(jnp.float32)  20.5 us
    dot_general x1, matrix products, body(): lax.dot_general(piece_part, out_weight, (((1,), (1,)), ((), ())), preferr...  11.6 us
    pallas_call x1, Pallas kernels, flash_backward(): pl.pallas_call(kernel, grid_spec=grid_spec, out_shape=[jax.ShapeDtypeStru...  9.31 us
    ppermute x3, starting transfers between devices, butterfly_sum(): value = value + lax.ppermute(value, axis_name, pairs)  6.38 us
    dot_general x1, matrix products, gram_squares(): lax.dot_general(left_side, left_side, (((1,), (1,)), ((), ())), preferred...  5.08 us
  transfers between devices with their start and end apart: 34, of which 17 were waited for; matrix products, arithmetic and copies ran while one was open for 8% of the time, Pallas kernels for 0%

profile of v7, /device:TPU:1, one launch (start us, length us, event | category | flops | bytes accessed | tf_op | source)
XLA Modules:
  0.0 220.9 jit_solution(17649548811320611198)
XLA Ops:
  9.7 8.1 %collective-permute-start.4 = (bf16[256,256]{1,0:T(8,128)(2,1)S(1)}, bf16[256,256]{1,0:T(8,128)(2,1)S(1)}, u32[]{:S(2)}, u32[]{:S(2)}) collective-permute-start(bf16[256,256]{1,0:T(8,128)(2,1)S(1)} %constant_dynamic-update-slice_fusion), channel_id=1, source_target_pairs={{0,112},{8,120},{1,113},{9,121},{2,114},{10,122},{3,115},{11,123},... | collective-permute-start | bytes 393224 | tf_op jit(solution)/shard_map/ppermute | solution.py:154
  31.8 5.0 %collective-permute-start.12 = (bf16[256,256]{1,0:T(8,128)(2,1)S(1)}, bf16[256,256]{1,0:T(8,128)(2,1)S(1)}, u32[]{:S(2)}, u32[]{:S(2)}) collective-permute-start(bf16[256,256]{1,0:T(8,128)(2,1)S(1)} %constant_dynamic-update-slice_fusion), channel_id=1, source_target_pairs={{0,48},{8,56},{16,64},{24,72},{32,80},{40,88},{48,96},{56,104},{64... | collective-permute-start | bytes 393224 | tf_op jit(solution)/shard_map/ppermute | solution.py:154
  36.9 5.0 %collective-permute-start.13 = (bf16[256,256]{1,0:T(8,128)(2,1)S(1)}, bf16[256,256]{1,0:T(8,128)(2,1)S(1)}, u32[]{:S(2)}, u32[]{:S(2)}) collective-permute-start(bf16[256,256]{1,0:T(8,128)(2,1)S(1)} %constant_dynamic-update-slice_fusion), channel_id=1, source_target_pairs={{0,40},{8,48},{16,56},{24,64},{32,72},{40,80},{48,88},{56,96},{64,... | collective-permute-start | bytes 393224 | tf_op jit(solution)/shard_map/ppermute | solution.py:154
  42.1 6.3 %collective-permute-start.14 = (bf16[256,256]{1,0:T(8,128)(2,1)S(1)}, bf16[256,256]{1,0:T(8,128)(2,1)S(1)}, u32[]{:S(2)}, u32[]{:S(2)}) collective-permute-start(bf16[256,256]{1,0:T(8,128)(2,1)S(1)} %constant_dynamic-update-slice_fusion), channel_id=1, source_target_pairs={{0,32},{8,40},{16,48},{24,56},{32,64},{40,72},{48,80},{56,88},{64,... | collective-permute-start | bytes 393224 | tf_op jit(solution)/shard_map/ppermute | solution.py:154
  49.8 4.8 %collective-permute-start.16 = (bf16[256,256]{1,0:T(8,128)(2,1)S(1)}, bf16[256,256]{1,0:T(8,128)(2,1)S(1)}, u32[]{:S(2)}, u32[]{:S(2)}) collective-permute-start(bf16[256,256]{1,0:T(8,128)(2,1)S(1)} %constant_dynamic-update-slice_fusion), channel_id=1, source_target_pairs={{0,16},{8,24},{16,32},{24,40},{32,48},{40,56},{48,64},{56,72},{64,... | collective-permute-start | bytes 393224 | tf_op jit(solution)/shard_map/ppermute | solution.py:154
  57.0 2.7 %collective-permute-start = (f32[256,256]{1,0:T(8,128)S(1)}, f32[256,256]{1,0:T(8,128)S(1)}, u32[]{:S(2)}, u32[]{:S(2)}) collective-permute-start(f32[256,256]{1,0:T(8,128)S(1)} %fusion.53), channel_id=1, source_target_pairs={{0,1},{1,0},{2,3},{3,2},{4,5},{5,4},{6,7},{7,6},{8,9},{9,8},{10,11... | collective-permute-start | bytes 786440 | tf_op jit(solution)/shard_map/ppermute | solution.py:177
  60.1 11.1 %collective-permute-done = f32[256,256]{1,0:T(8,128)S(1)} collective-permute-done((f32[256,256]{1,0:T(8,128)S(1)}, f32[256,256]{1,0:T(8,128)S(1)}, u32[]{:S(2)}, u32[]{:S(2)}) %collective-permute-start) | collective-permute-done | bytes 262176 | tf_op jit(solution)/shard_map/ppermute | solution.py:177
  72.4 7.9 %collective-permute-done.1 = f32[256,256]{1,0:T(8,128)S(1)} collective-permute-done((f32[256,256]{1,0:T(8,128)S(1)}, f32[256,256]{1,0:T(8,128)S(1)}, u32[]{:S(2)}, u32[]{:S(2)}) %collective-permute-start.1) | collective-permute-done | bytes 262176 | tf_op jit(solution)/shard_map/ppermute | solution.py:177
  83.2 6.0 %collective-permute-done.2 = f32[256,256]{1,0:T(8,128)S(1)} collective-permute-done((f32[256,256]{1,0:T(8,128)S(1)}, f32[256,256]{1,0:T(8,128)S(1)}, u32[]{:S(2)}, u32[]{:S(2)}) %collective-permute-start.2) | collective-permute-done | bytes 262176 | tf_op jit(solution)/shard_map/ppermute | solution.py:177
  93.2 3.1 %while.25 = (s32[]{:T(128)}, f32[256,8,128]{2,0,1:T(8,128)S(1)}, s32[]{:T(128)}, bf16[4096,128]{1,0:T(8,128)(2,1)S(1)}, bf16[256,8,128]{2,1,0:T(8,128)(2,1)}, /*...) while((s32[]{:T(128)}, f32[256,8,128]{2,0,1:T(8,128)S(1)}, ...), condition=%wide.region_5.6_spmd.clone, body=%wide.region_4.5_spmd.clone.sunk | while | flops 541459200 | bytes 3161259 | solution.py:264
  93.3 2.8 %fusion.71 = f32[256,8,128]{2,0,1:T(8,128)S(1)} fusion(f32[256,8,128]{2,0,1:T(8,128)S(1)} %get-tuple-element.363, f32[256,8]{0,1:T(8,128)S(1)} %get-tuple-element.379, pred[256,512]{1,0:T(8,128)(4,1)S(1)} %broadcast_compare_fusion.5, bf16[256,8,128]{2,1,0:T(8,128)(2,1)} %get-tuple-element.378, bf16[4096,128]{1,0:T(8,128)(2,1)} %get-tuple-element.380, ...), kind=kOutput, calls=%fused_computation.18.clone.1 | convolution fusion | flops 541327360 | bytes 3023872 | tf_op jit(solution)/shard_map/while/body/tgk,kd->tgd/dot_general | solution.py:260
  96.3 4.3 %all-gather.2.cloned.1.call-done = bf16[256,8192]{1,0:T(8,128)(2,1)} async-done(((bf16[256,1024]{1,0:T(8,128)(2,1)}), bf16[256,8192]{1,0:T(8,128)(2,1)}) %all-gather.2.cloned.1.call-update) | async-done | bytes 4194320 | tf_op jit(solution)/shard_map/all_gather | solution.py:215
  100.6 11.6 %fusion.28.do_ref = bf16[256,1024]{1,0:T(8,128)(2,1)S(1)} fusion(bf16[1024,8192]{1,0:T(8,128)(2,1)} %param.15, bf16[256,8192]{1,0:T(8,128)(2,1)} %all-gather.2.cloned.1.call-done, f32[256]{0:T(256)S(1)} %convert_add_fusion.1), kind=kOutput, calls=%fused_computation.35 | convolution fusion | flops 4301520896 | bytes 21496832 | tf_op jit(solution)/shard_map/dot_general | solution.py:273
  113.3 9.3 %shard_map.110 = (bf16[256,1024]{1,0:T(8,128)(2,1)}, bf16[4096,256]{1,0:T(8,128)(2,1)}) custom-call(s32[2]{0:T(128)} %pad_add_fusion.scalar_ref, bf16[256,1024]{1,0:T(8,128)(2,1)} %q_ref.1, bf16[256,1024]{1,0:T(8,128)(2,1)} %copy-done.1, bf16[4096,128]{1,0:T(8,128)(2,1)S(1)} %get-tuple-element.388, bf16[4096,128]{1,0:T(8,128)(2,1)} %get-tuple-element.389, ...), custom_call_target="tpu_custom_call" | custom-call | tf_op jit(solution)/shard_map/pallas_call | solution.py:117
  122.7 3.0 %dynamic-slice_bitcast_fusion.14 = (bf16[256,256]{1,0:T(8,128)(2,1)S(1)}, bf16[256,256]{1,0:T(8,128)(2,1)S(1)}, bf16[256,256]{1,0:T(8,128)(2,1)S(1)}, bf16[256,2...) fusion(bf16[16,256,256]{2,1,0:T(8,128)(2,1)} %bitcast.162, ...), kind=kLoop, calls=%fused_computation.106 | loop fusion | bytes 3932220 | tf_op jit(solution)/shard_map/jit(dynamic_index_in_dim)/squeeze | solution.py:167
  125.6 2.7 %collective-permute-start.18 = (bf16[256,256]{1,0:T(8,128)(2,1)S(1)}, bf16[256,256]{1,0:T(8,128)(2,1)S(1)}, u32[]{:S(2)}, u32[]{:S(2)}) collective-permute-start(bf16[256,256]{1,0:T(8,128)(2,1)S(1)} %get-tuple-element.198), channel_id=1, source_target_pairs={{8,0},{16,8},{24,16},{32,24},{40,32},{48,40},{56,48},{64,56},{72,6... | collective-permute-start | bytes 393224 | tf_op jit(solution)/shard_map/ppermute | solution.py:168
  133.9 5.1 %fusion.26 = f32[256,256]{1,0:T(8,128)S(1)} fusion(bf16[256,8192]{1,0:T(8,128)(2,1)} %all-gather.2.cloned.1.call-done, f32[256]{0:T(256)S(1)} %convert_add_fusion.1), kind=kOutput, calls=%fused_computation.33 | convolution fusion | flops 1080033280 | bytes 4457472 | tf_op jit(solution)/shard_map/dot_general | solution.py:192
  142.7 8.2 %collective-permute-done.20 = bf16[256,256]{1,0:T(8,128)(2,1)S(1)} collective-permute-done((bf16[256,256]{1,0:T(8,128)(2,1)S(1)}, bf16[256,256]{1,0:T(8,128)(2,1)S(1)}, u32[]{:S(2)}, u32[]{:S(2)}) %collective-permute-start.20) | collective-permute-done | bytes 131104 | tf_op jit(solution)/shard_map/ppermute | solution.py:168
  155.4 7.8 %collective-permute-done.22 = bf16[256,256]{1,0:T(8,128)(2,1)S(1)} collective-permute-done((bf16[256,256]{1,0:T(8,128)(2,1)S(1)}, bf16[256,256]{1,0:T(8,128)(2,1)S(1)}, u32[]{:S(2)}, u32[]{:S(2)}) %collective-permute-start.22) | collective-permute-done | bytes 131104 | tf_op jit(solution)/shard_map/ppermute | solution.py:168
  165.1 7.4 %collective-permute-done.23 = bf16[256,256]{1,0:T(8,128)(2,1)S(1)} collective-permute-done((bf16[256,256]{1,0:T(8,128)(2,1)S(1)}, bf16[256,256]{1,0:T(8,128)(2,1)S(1)}, u32[]{:S(2)}, u32[]{:S(2)}) %collective-permute-start.23) | collective-permute-done | bytes 131104 | tf_op jit(solution)/shard_map/ppermute | solution.py:168
  173.8 2.8 %collective-permute-done.24 = bf16[256,256]{1,0:T(8,128)(2,1)S(1)} collective-permute-done((bf16[256,256]{1,0:T(8,128)(2,1)S(1)}, bf16[256,256]{1,0:T(8,128)(2,1)S(1)}, u32[]{:S(2)}, u32[]{:S(2)}) %collective-permute-start.24) | collective-permute-done | bytes 131104 | tf_op jit(solution)/shard_map/ppermute | solution.py:168
  180.7 13.2 %collective-permute-done.26 = bf16[256,256]{1,0:T(8,128)(2,1)S(1)} collective-permute-done((bf16[256,256]{1,0:T(8,128)(2,1)S(1)}, bf16[256,256]{1,0:T(8,128)(2,1)S(1)}, u32[]{:S(2)}, u32[]{:S(2)}) %collective-permute-start.26) | collective-permute-done | bytes 131104 | tf_op jit(solution)/shard_map/ppermute | solution.py:168
  196.4 3.7 %collective-permute-done.28 = bf16[256,256]{1,0:T(8,128)(2,1)S(1)} collective-permute-done((bf16[256,256]{1,0:T(8,128)(2,1)S(1)}, bf16[256,256]{1,0:T(8,128)(2,1)S(1)}, u32[]{:S(2)}, u32[]{:S(2)}) %collective-permute-start.28) | collective-permute-done | bytes 131104 | tf_op jit(solution)/shard_map/ppermute | solution.py:168
  201.5 8.2 %collective-permute-done.30 = bf16[256,256]{1,0:T(8,128)(2,1)S(1)} collective-permute-done((bf16[256,256]{1,0:T(8,128)(2,1)S(1)}, bf16[256,256]{1,0:T(8,128)(2,1)S(1)}, u32[]{:S(2)}, u32[]{:S(2)}) %collective-permute-start.30) | collective-permute-done | bytes 131104 | tf_op jit(solution)/shard_map/ppermute | solution.py:168
  (130 shorter events, 60.7 us)
Async XLA Ops:
  7.2 93.4 %all-gather.2.cloned.1.call-start = ((), (), s32[]{:S(2)}) async-start(), calls=%async_computation | async-start | bytes 4718592 | tf_op jit(solution)/shard_map/all_gather | solution.py:215
  9.0 17.5 %collective-permute-start.3 = (bf16[256,256]{1,0:T(8,128)(2,1)S(1)}, bf16[256,256]{1,0:T(8,128)(2,1)S(1)}, u32[]{:S(2)}, u32[]{:S(2)}) collective-permute-start(bf16[256,256]{1,0:T(8,128)(2,1)S(1)} %constant_dynamic-update-slice_fusion), channel_id=1, source_target_pairs={{0,120},{1,121},{2,122},{3,123},{4,124},{5,125},{6,126},{7,127}} | collective-permute-start | bytes 393224 | tf_op jit(solution)/shard_map/ppermute | solution.py:154
  9.7 18.1 %collective-permute-start.4 = (bf16[256,256]{1,0:T(8,128)(2,1)S(1)}, bf16[256,256]{1,0:T(8,128)(2,1)S(1)}, u32[]{:S(2)}, u32[]{:S(2)}) collective-permute-start(bf16[256,256]{1,0:T(8,128)(2,1)S(1)} %constant_dynamic-update-slice_fusion), channel_id=1, source_target_pairs={{0,112},{8,120},{1,113},{9,121},{2,114},{10,122},{3,115},{11,123},... | collective-permute-start | bytes 393224 | tf_op jit(solution)/shard_map/ppermute | solution.py:154
  27.8 14.3 %collective-permute-start.9 = (bf16[256,256]{1,0:T(8,128)(2,1)S(1)}, bf16[256,256]{1,0:T(8,128)(2,1)S(1)}, u32[]{:S(2)}, u32[]{:S(2)}) collective-permute-start(bf16[256,256]{1,0:T(8,128)(2,1)S(1)} %constant_dynamic-update-slice_fusion), channel_id=1, source_target_pairs={{0,72},{8,80},{16,88},{24,96},{32,104},{40,112},{48,120},{1,73},{9... | collective-permute-start | bytes 393224 | tf_op jit(solution)/shard_map/ppermute | solution.py:154
  29.1 19.3 %collective-permute-start.10 = (bf16[256,256]{1,0:T(8,128)(2,1)S(1)}, bf16[256,256]{1,0:T(8,128)(2,1)S(1)}, u32[]{:S(2)}, u32[]{:S(2)}) collective-permute-start(bf16[256,256]{1,0:T(8,128)(2,1)S(1)} %constant_dynamic-update-slice_fusion), channel_id=1, source_target_pairs={{0,64},{8,72},{16,80},{24,88},{32,96},{40,104},{48,112},{56,120},{... | collective-permute-start | bytes 393224 | tf_op jit(solution)/shard_map/ppermute | solution.py:154
  30.4 19.3 %collective-permute-start.11 = (bf16[256,256]{1,0:T(8,128)(2,1)S(1)}, bf16[256,256]{1,0:T(8,128)(2,1)S(1)}, u32[]{:S(2)}, u32[]{:S(2)}) collective-permute-start(bf16[256,256]{1,0:T(8,128)(2,1)S(1)} %constant_dynamic-update-slice_fusion), channel_id=1, source_target_pairs={{0,56},{8,64},{16,72},{24,80},{32,88},{40,96},{48,104},{56,112},{6... | collective-permute-start | bytes 393224 | tf_op jit(solution)/shard_map/ppermute | solution.py:154
  31.8 22.8 %collective-permute-start.12 = (bf16[256,256]{1,0:T(8,128)(2,1)S(1)}, bf16[256,256]{1,0:T(8,128)(2,1)S(1)}, u32[]{:S(2)}, u32[]{:S(2)}) collective-permute-start(bf16[256,256]{1,0:T(8,128)(2,1)S(1)} %constant_dynamic-update-slice_fusion), channel_id=1, source_target_pairs={{0,48},{8,56},{16,64},{24,72},{32,80},{40,88},{48,96},{56,104},{64... | collective-permute-start | bytes 393224 | tf_op jit(solution)/shard_map/ppermute | solution.py:154
  36.9 20.2 %collective-permute-start.13 = (bf16[256,256]{1,0:T(8,128)(2,1)S(1)}, bf16[256,256]{1,0:T(8,128)(2,1)S(1)}, u32[]{:S(2)}, u32[]{:S(2)}) collective-permute-start(bf16[256,256]{1,0:T(8,128)(2,1)S(1)} %constant_dynamic-update-slice_fusion), channel_id=1, source_target_pairs={{0,40},{8,48},{16,56},{24,64},{32,72},{40,80},{48,88},{56,96},{64,... | collective-permute-start | bytes 393224 | tf_op jit(solution)/shard_map/ppermute | solution.py:154
  42.1 17.6 %collective-permute-start.14 = (bf16[256,256]{1,0:T(8,128)(2,1)S(1)}, bf16[256,256]{1,0:T(8,128)(2,1)S(1)}, u32[]{:S(2)}, u32[]{:S(2)}) collective-permute-start(bf16[256,256]{1,0:T(8,128)(2,1)S(1)} %constant_dynamic-update-slice_fusion), channel_id=1, source_target_pairs={{0,32},{8,40},{16,48},{24,56},{32,64},{40,72},{48,80},{56,88},{64,... | collective-permute-start | bytes 393224 | tf_op jit(solution)/shard_map/ppermute | solution.py:154
  57.0 14.2 %collective-permute-start = (f32[256,256]{1,0:T(8,128)S(1)}, f32[256,256]{1,0:T(8,128)S(1)}, u32[]{:S(2)}, u32[]{:S(2)}) collective-permute-start(f32[256,256]{1,0:T(8,128)S(1)} %fusion.53), channel_id=1, source_target_pairs={{0,1},{1,0},{2,3},{3,2},{4,5},{5,4},{6,7},{7,6},{8,9},{9,8},{10,11... | collective-permute-start | bytes 786440 | tf_op jit(solution)/shard_map/ppermute | solution.py:177
  125.6 13.9 %collective-permute-start.18 = (bf16[256,256]{1,0:T(8,128)(2,1)S(1)}, bf16[256,256]{1,0:T(8,128)(2,1)S(1)}, u32[]{:S(2)}, u32[]{:S(2)}) collective-permute-start(bf16[256,256]{1,0:T(8,128)(2,1)S(1)} %get-tuple-element.198), channel_id=1, source_target_pairs={{8,0},{16,8},{24,16},{32,24},{40,32},{48,40},{56,48},{64,56},{72,6... | collective-permute-start | bytes 393224 | tf_op jit(solution)/shard_map/ppermute | solution.py:168
  129.7 21.2 %collective-permute-start.20 = (bf16[256,256]{1,0:T(8,128)(2,1)S(1)}, bf16[256,256]{1,0:T(8,128)(2,1)S(1)}, u32[]{:S(2)}, u32[]{:S(2)}) collective-permute-start(bf16[256,256]{1,0:T(8,128)(2,1)S(1)} %get-tuple-element.211), channel_id=1, source_target_pairs={{24,0},{32,8},{40,16},{48,24},{56,32},{64,40},{72,48},{80,56},{88,... | collective-permute-start | bytes 393224 | tf_op jit(solution)/shard_map/ppermute | solution.py:168
  131.0 23.2 %collective-permute-start.21 = (bf16[256,256]{1,0:T(8,128)(2,1)S(1)}, bf16[256,256]{1,0:T(8,128)(2,1)S(1)}, u32[]{:S(2)}, u32[]{:S(2)}) collective-permute-start(bf16[256,256]{1,0:T(8,128)(2,1)S(1)} %get-tuple-element.210), channel_id=1, source_target_pairs={{32,0},{40,8},{48,16},{56,24},{64,32},{72,40},{80,48},{88,56},{96,... | collective-permute-start | bytes 393224 | tf_op jit(solution)/shard_map/ppermute | solution.py:168
  132.3 31.0 %collective-permute-start.22 = (bf16[256,256]{1,0:T(8,128)(2,1)S(1)}, bf16[256,256]{1,0:T(8,128)(2,1)S(1)}, u32[]{:S(2)}, u32[]{:S(2)}) collective-permute-start(bf16[256,256]{1,0:T(8,128)(2,1)S(1)} %get-tuple-element.209), channel_id=1, source_target_pairs={{40,0},{48,8},{56,16},{64,24},{72,32},{80,40},{88,48},{96,56},{104... | collective-permute-start | bytes 393224 | tf_op jit(solution)/shard_map/ppermute | solution.py:168
  139.6 32.9 %collective-permute-start.23 = (bf16[256,256]{1,0:T(8,128)(2,1)S(1)}, bf16[256,256]{1,0:T(8,128)(2,1)S(1)}, u32[]{:S(2)}, u32[]{:S(2)}) collective-permute-start(bf16[256,256]{1,0:T(8,128)(2,1)S(1)} %get-tuple-element.208), channel_id=1, source_target_pairs={{48,0},{56,8},{64,16},{72,24},{80,32},{88,40},{96,48},{104,56},{11... | collective-permute-start | bytes 393224 | tf_op jit(solution)/shard_map/ppermute | solution.py:168
  141.4 35.2 %collective-permute-start.24 = (bf16[256,256]{1,0:T(8,128)(2,1)S(1)}, bf16[256,256]{1,0:T(8,128)(2,1)S(1)}, u32[]{:S(2)}, u32[]{:S(2)}) collective-permute-start(bf16[256,256]{1,0:T(8,128)(2,1)S(1)} %get-tuple-element.207), channel_id=1, source_target_pairs={{56,0},{64,8},{72,16},{80,24},{88,32},{96,40},{104,48},{112,56},{1... | collective-permute-start | bytes 393224 | tf_op jit(solution)/shard_map/ppermute | solution.py:168
  150.9 28.5 %collective-permute-start.25 = (bf16[256,256]{1,0:T(8,128)(2,1)S(1)}, bf16[256,256]{1,0:T(8,128)(2,1)S(1)}, u32[]{:S(2)}, u32[]{:S(2)}) collective-permute-start(bf16[256,256]{1,0:T(8,128)(2,1)S(1)} %get-tuple-element.206), channel_id=1, source_target_pairs={{64,0},{72,8},{80,16},{88,24},{96,32},{104,40},{112,48},{120,56},{... | collective-permute-start | bytes 393224 | tf_op jit(solution)/shard_map/ppermute | solution.py:168
  154.1 39.8 %collective-permute-start.26 = (bf16[256,256]{1,0:T(8,128)(2,1)S(1)}, bf16[256,256]{1,0:T(8,128)(2,1)S(1)}, u32[]{:S(2)}, u32[]{:S(2)}) collective-permute-start(bf16[256,256]{1,0:T(8,128)(2,1)S(1)} %get-tuple-element.205), channel_id=1, source_target_pairs={{72,0},{80,8},{88,16},{96,24},{104,32},{112,40},{120,48},{73,1},{8... | collective-permute-start | bytes 393224 | tf_op jit(solution)/shard_map/ppermute | solution.py:168
  163.2 32.0 %collective-permute-start.27 = (bf16[256,256]{1,0:T(8,128)(2,1)S(1)}, bf16[256,256]{1,0:T(8,128)(2,1)S(1)}, u32[]{:S(2)}, u32[]{:S(2)}) collective-permute-start(bf16[256,256]{1,0:T(8,128)(2,1)S(1)} %get-tuple-element.204), channel_id=1, source_target_pairs={{80,0},{88,8},{96,16},{104,24},{112,32},{120,40},{81,1},{89,9},{97... | collective-permute-start | bytes 393224 | tf_op jit(solution)/shard_map/ppermute | solution.py:168
  172.5 27.6 %collective-permute-start.28 = (bf16[256,256]{1,0:T(8,128)(2,1)S(1)}, bf16[256,256]{1,0:T(8,128)(2,1)S(1)}, u32[]{:S(2)}, u32[]{:S(2)}) collective-permute-start(bf16[256,256]{1,0:T(8,128)(2,1)S(1)} %get-tuple-element.203), channel_id=1, source_target_pairs={{88,0},{96,8},{104,16},{112,24},{120,32},{89,1},{97,9},{105,17},{1... | collective-permute-start | bytes 393224 | tf_op jit(solution)/shard_map/ppermute | solution.py:168
  176.6 24.9 %collective-permute-start.29 = (bf16[256,256]{1,0:T(8,128)(2,1)S(1)}, bf16[256,256]{1,0:T(8,128)(2,1)S(1)}, u32[]{:S(2)}, u32[]{:S(2)}) collective-permute-start(bf16[256,256]{1,0:T(8,128)(2,1)S(1)} %get-tuple-element.202), channel_id=1, source_target_pairs={{96,0},{104,8},{112,16},{120,24},{97,1},{105,9},{113,17},{121,25},... | collective-permute-start | bytes 393224 | tf_op jit(solution)/shard_map/ppermute | solution.py:168
  179.4 30.2 %collective-permute-start.30 = (bf16[256,256]{1,0:T(8,128)(2,1)S(1)}, bf16[256,256]{1,0:T(8,128)(2,1)S(1)}, u32[]{:S(2)}, u32[]{:S(2)}) collective-permute-start(bf16[256,256]{1,0:T(8,128)(2,1)S(1)} %get-tuple-element.201), channel_id=1, source_target_pairs={{104,0},{112,8},{120,16},{105,1},{113,9},{121,17},{106,2},{114,10}... | collective-permute-start | bytes 393224 | tf_op jit(solution)/shard_map/ppermute | solution.py:168
  193.9 18.3 %collective-permute-start.31 = (bf16[256,256]{1,0:T(8,128)(2,1)S(1)}, bf16[256,256]{1,0:T(8,128)(2,1)S(1)}, u32[]{:S(2)}, u32[]{:S(2)}) collective-permute-start(bf16[256,256]{1,0:T(8,128)(2,1)S(1)} %get-tuple-element.200), channel_id=1, source_target_pairs={{112,0},{120,8},{113,1},{121,9},{114,2},{122,10},{115,3},{123,11},... | collective-permute-start | bytes 393224 | tf_op jit(solution)/shard_map/ppermute | solution.py:168
  195.2 17.0 %collective-permute-start.32 = (bf16[256,256]{1,0:T(8,128)(2,1)S(1)}, bf16[256,256]{1,0:T(8,128)(2,1)S(1)}, u32[]{:S(2)}, u32[]{:S(2)}) collective-permute-start(bf16[256,256]{1,0:T(8,128)(2,1)S(1)} %get-tuple-element.199), channel_id=1, source_target_pairs={{120,0},{121,1},{122,2},{123,3},{124,4},{125,5},{126,6},{127,7}} | collective-permute-start | bytes 393224 | tf_op jit(solution)/shard_map/ppermute | solution.py:168
  (14 other events, 150.7 us)
Sparse Core Ops, SparseCore 0:
  21.9 78.6 all-gather.1

commit v8 on v7

--- a/solution.py
+++ b/solution.py
@@ -33,6 +33,101 @@
         product.shape[0], right_side.shape[1] // head_dim, head_dim
     )
     return jnp.sum(shaped, axis=(0, 2))
+
+
+def flash_forward(query_rows, keys_all, values_all, first_row, head_dim, block_rows):
+    rows, width = query_rows.shape
+    heads = width // head_dim
+    tokens = keys_all.shape[0]
+    blocks = tokens // block_rows
+    scaling = head_dim ** (-0.5)
+    needed = (first_row + rows - 1) // block_rows + 1
+    scalars = jnp.stack([needed, first_row]).astype(jnp.int32)
+
+    def kernel(scalar_ref, q_ref, k_ref, v_ref, att_ref, lt_ref, m_acc, l_acc, o_acc):
+        phase = pl.program_id(0)
+        j = pl.program_id(1)
+
+        @pl.when(jnp.logical_and(phase == 0, j == 0))
+        def _():
+            m_acc[...] = jnp.full(m_acc.shape, NEGATIVE, jnp.float32)
+            l_acc[...] = jnp.zeros_like(l_acc)
+            o_acc[...] = jnp.zeros_like(o_acc)
+
+        @pl.when(jnp.logical_and(phase == 1, j == 0))
+        def _():
+            lt_ref[...] = m_acc[...] + jnp.log(l_acc[...])
+
+        def block_scores(h, k, masked):
+            q = q_ref[:, h * head_dim : (h + 1) * head_dim]
+            s = lax.dot_general(q, k, (((1,), (1,)), ((), ())), preferred_element_type=jnp.float32) * scaling
+            if masked:
+                row_pos = scalar_ref[1] + lax.broadcasted_iota(jnp.int32, (rows, block_rows), 0)
+                col_pos = j * block_rows + lax.broadcasted_iota(jnp.int32, (rows, block_rows), 1)
+                s = jnp.where(row_pos >= col_pos, s, NEGATIVE)
+            return s
+
+        def stats_block(masked):
+            k = k_ref[...]
+            for h in range(heads):
+                s = block_scores(h, k, masked)
+                m_old = m_acc[:, h : h + 1]
+                m_new = jnp.maximum(m_old, jnp.max(s, axis=1, keepdims=True))
+                l_acc[:, h : h + 1] = l_acc[:, h : h + 1] * jnp.exp(m_old - m_new) + jnp.sum(
+                    jnp.exp(s - m_new), axis=1, keepdims=True
+                )
+                m_acc[:, h : h + 1] = m_new
+
+        def value_block(masked):
+            k = k_ref[...]
+            v = v_ref[...]
+            for h in range(heads):
+                s = block_scores(h, k, masked)
+                p = jnp.exp(s - lt_ref[:, h : h + 1]).astype(jnp.bfloat16)
+                o_acc[:, h * head_dim : (h + 1) * head_dim] += jnp.dot(p, v, preferred_element_type=jnp.float32)
+
+        active = j < scalar_ref[0]
+        for phase_id, step in ((0, stats_block), (1, value_block)):
+
+            @pl.when(jnp.logical_and(phase == phase_id, active))
+            def _(step=step):
+                step(True)
+
+        @pl.when(jnp.logical_and(phase == 1, j == blocks - 1))
+        def _():
+            att_ref[...] = o_acc[...].astype(att_ref.dtype)
+
+    def kv_map(p, j, s):
+        return (jnp.minimum(j, s[0] - 1), 0)
+
+    full = lambda p, j, s: (0, 0)
+    grid_spec = pltpu.PrefetchScalarGridSpec(
+        num_scalar_prefetch=1,
+        grid=(2, blocks),
+        in_specs=[
+            pl.BlockSpec((rows, width), full),
+            pl.BlockSpec((block_rows, head_dim), kv_map),
+            pl.BlockSpec((block_rows, head_dim), kv_map),
+        ],
+        out_specs=[
+            pl.BlockSpec((rows, width), full),
+            pl.BlockSpec((rows, heads), full),
+        ],
+        scratch_shapes=[
+            pltpu.VMEM((rows, heads), jnp.float32),
+            pltpu.VMEM((rows, heads), jnp.float32),
+            pltpu.VMEM((rows, width), jnp.float32),
+        ],
+    )
+    return pl.pallas_call(
+        kernel,
+        grid_spec=grid_spec,
+        out_shape=[
+            jax.ShapeDtypeStruct((rows, width), jnp.bfloat16),
+            jax.ShapeDtypeStruct((rows, heads), jnp.float32),
+        ],
+        compiler_params=pltpu.CompilerParams(dimension_semantics=("arbitrary", "arbitrary")),
+    )(scalars, query_rows, keys_all, values_all)
 
 
 def flash_backward(query_rows, grad_attended, keys_all, values_all, log_total, row_dot, first_row, head_dim, block_rows):
@@ -237,38 +332,11 @@
     shared_head = 0
     query_group = query_heads[:, shared_head]
 
-    def stats_step(block_number, carried):
-        running_max, running_sum = carried
-        key_block = fetch(keys_all, block_number)
-        scores = block_scores(query_group, key_block, scaling, row_pos, column_pos(block_number))
-        new_max = jnp.maximum(running_max, jnp.max(scores, axis=-1))
-        running_sum = running_sum * jnp.exp(running_max - new_max) + jnp.sum(
-            jnp.exp(scores - new_max[..., None]), axis=-1
-        )
-        return (new_max, running_sum)
-
-    start_max = jnp.full((rows, group_size), NEGATIVE, jnp.float32)
-    start_sum = jnp.zeros((rows, group_size), jnp.float32)
-    running_max, running_sum = lax.fori_loop(0, needed, stats_step, (start_max, start_sum))
-    log_total = running_max + jnp.log(running_sum)
-
-    def value_step(block_number, accumulated):
-        key_block = fetch(keys_all, block_number)
-        value_block = fetch(values_all, block_number)
-        scores = block_scores(query_group, key_block, scaling, row_pos, column_pos(block_number))
-        rounded = jnp.exp(scores - log_total[..., None]).astype(jnp.bfloat16)
-        return accumulated + jnp.einsum(
-            "tgk,kd->tgd", rounded, value_block, preferred_element_type=jnp.float32
-        )
-
-    accumulated = lax.fori_loop(
-        0, needed, value_step, jnp.zeros((rows, group_size, head_dim), jnp.float32)
+    attended_part, log_total = flash_forward(
+        query_group.reshape(rows, group_size * head_dim), keys_all, values_all, first_row,
+        head_dim, block_rows,
     )
     log_totals.append(log_total)
-    attended_list = [accumulated.astype(jnp.bfloat16)]
-    attended_part = jnp.stack(attended_list, axis=1).reshape(
-        rows, local_groups * group_size * head_dim
-    )
     log_totals, attended = (log_totals, attended_part)
     grad_sum = lax.dot_general(
         piece_part, out_weight, (((1,), (1,)), ((), ())), preferred_element_type=jnp.float32

time: 223 us -> 233 us (1.045)
  Pallas kernels: 9.31 us -> 19.1 us
  waiting for transfers between devices: 88.9 us -> 95.1 us
  matrix products: 21.6 us -> 18 us
  local copies, waits for them, and re-layouts: 11.8 us -> 8.32 us
  starting transfers between devices: 69.5 us -> 71.9 us
    pallas_call x0 -> x1, Pallas kernels: none -> 9.55 us  [flash_forward(): pl.pallas_call(kernel, grid_spec=grid_spec, out_shape=[jax.ShapeDtypeStru...]
    ppermute x15, waiting for transfers between devices: 59.3 us -> 67.3 us  [causal_reduce(): total = total + lax.ppermute(sent, axis_name, pairs).astype(jnp.float32)]
    all_gather x1, waiting for transfers between devices: 4.27 us -> 0.02 us  [body(): lax.all_gather(grad_out, 'head', axis=1, tiled=True).astype(jnp.float32)]
    dot_general x2 -> x0, matrix products: 3.57 us -> none  [the longest x1 2.79 us: value_step(): jnp.einsum('tgk,kd->tgd', rounded, value_block, preferred_element_type=jn...]
    ppermute x15, waiting for transfers between devices: 0.28 us -> 3.21 us  [causal_gather(): received.append(lax.ppermute(value, axis_name, pairs))]
    unnamed x43 -> x42, local copies, waits for them, and re-layouts: 4.89 us -> 2.59 us
  transfers between devices with their start and end apart: 34 -> 34, of which waited for: 17 -> 19; matrix products, arithmetic and copies ran while one was open for 8% -> 5% of each run, Pallas kernels for 0% -> 4%
where the time goes in v8:
time: 233 us; the launch traced here: 231 us
  waiting for transfers between devices  95.1 us (41%)
  starting transfers between devices  71.9 us (31%)
  Pallas kernels  19.1 us (8%)
  matrix products  18 us (8%)
  between operations  14.8 us (6%)
  local copies, waits for them, and re-layouts  8.32 us (4%)
  other arithmetic  4.23 us (2%)
    ppermute x15, waiting for transfers between devices, causal_reduce(): total = total + lax.ppermute(sent, axis_name, pairs).astype(jnp.float32)  67.3 us
    ppermute x15, starting transfers between devices, causal_gather(): received.append(lax.ppermute(value, axis_name, pairs))  42.8 us
    ppermute x3, waiting for transfers between devices, butterfly_sum(): value = value + lax.ppermute(value, axis_name, pairs)  24.5 us
    ppermute x15, starting transfers between devices, causal_reduce(): total = total + lax.ppermute(sent, axis_name, pairs).astype(jnp.float32)  22.4 us
    dot_general x1, matrix products, body(): lax.dot_general(piece_part, out_weight, (((1,), (1,)), ((), ())), preferr...  11.6 us
    pallas_call x1, Pallas kernels, flash_backward(): pl.pallas_call(kernel, grid_spec=grid_spec, out_shape=[jax.ShapeDtypeStru...  9.58 us
    pallas_call x1, Pallas kernels, flash_forward(): pl.pallas_call(kernel, grid_spec=grid_spec, out_shape=[jax.ShapeDtypeStru...  9.55 us
    ppermute x3, starting transfers between devices, butterfly_sum(): value = value + lax.ppermute(value, axis_name, pairs)  6.67 us
  transfers between devices with their start and end apart: 34, of which 19 were waited for; matrix products, arithmetic and copies ran while one was open for 5% of the time, Pallas kernels for 4%

profile of v8, /device:TPU:1, one launch (start us, length us, event | category | flops | bytes accessed | tf_op | source)
XLA Modules:
  0.0 231.5 jit_solution(12366959543889618443)
XLA Ops:
  9.7 8.1 %collective-permute-start.4 = (bf16[256,256]{1,0:T(8,128)(2,1)S(1)}, bf16[256,256]{1,0:T(8,128)(2,1)S(1)}, u32[]{:S(2)}, u32[]{:S(2)}) collective-permute-start(bf16[256,256]{1,0:T(8,128)(2,1)S(1)} %constant_dynamic-update-slice_fusion), channel_id=1, source_target_pairs={{0,112},{8,120},{1,113},{9,121},{2,114},{10,122},{3,115},{11,123},... | collective-permute-start | bytes 393224 | tf_op jit(solution)/shard_map/ppermute | solution.py:249
  31.6 5.2 %collective-permute-start.12 = (bf16[256,256]{1,0:T(8,128)(2,1)S(1)}, bf16[256,256]{1,0:T(8,128)(2,1)S(1)}, u32[]{:S(2)}, u32[]{:S(2)}) collective-permute-start(bf16[256,256]{1,0:T(8,128)(2,1)S(1)} %constant_dynamic-update-slice_fusion), channel_id=1, source_target_pairs={{0,48},{8,56},{16,64},{24,72},{32,80},{40,88},{48,96},{56,104},{64... | collective-permute-start | bytes 393224 | tf_op jit(solution)/shard_map/ppermute | solution.py:249
  36.9 5.0 %collective-permute-start.13 = (bf16[256,256]{1,0:T(8,128)(2,1)S(1)}, bf16[256,256]{1,0:T(8,128)(2,1)S(1)}, u32[]{:S(2)}, u32[]{:S(2)}) collective-permute-start(bf16[256,256]{1,0:T(8,128)(2,1)S(1)} %constant_dynamic-update-slice_fusion), channel_id=1, source_target_pairs={{0,40},{8,48},{16,56},{24,64},{32,72},{40,80},{48,88},{56,96},{64,... | collective-permute-start | bytes 393224 | tf_op jit(solution)/shard_map/ppermute | solution.py:249
  42.1 6.3 %collective-permute-start.14 = (bf16[256,256]{1,0:T(8,128)(2,1)S(1)}, bf16[256,256]{1,0:T(8,128)(2,1)S(1)}, u32[]{:S(2)}, u32[]{:S(2)}) collective-permute-start(bf16[256,256]{1,0:T(8,128)(2,1)S(1)} %constant_dynamic-update-slice_fusion), channel_id=1, source_target_pairs={{0,32},{8,40},{16,48},{24,56},{32,64},{40,72},{48,80},{56,88},{64,... | collective-permute-start | bytes 393224 | tf_op jit(solution)/shard_map/ppermute | solution.py:249
  49.8 4.8 %collective-permute-start.16 = (bf16[256,256]{1,0:T(8,128)(2,1)S(1)}, bf16[256,256]{1,0:T(8,128)(2,1)S(1)}, u32[]{:S(2)}, u32[]{:S(2)}) collective-permute-start(bf16[256,256]{1,0:T(8,128)(2,1)S(1)} %constant_dynamic-update-slice_fusion), channel_id=1, source_target_pairs={{0,16},{8,24},{16,32},{24,40},{32,48},{40,56},{48,64},{56,72},{64,... | collective-permute-start | bytes 393224 | tf_op jit(solution)/shard_map/ppermute | solution.py:249
  57.0 2.7 %collective-permute-start = (f32[256,256]{1,0:T(8,128)S(1)}, f32[256,256]{1,0:T(8,128)S(1)}, u32[]{:S(2)}, u32[]{:S(2)}) collective-permute-start(f32[256,256]{1,0:T(8,128)S(1)} %fusion.27), channel_id=1, source_target_pairs={{0,1},{1,0},{2,3},{3,2},{4,5},{5,4},{6,7},{7,6},{8,9},{9,8},{10,11... | collective-permute-start | bytes 786440 | tf_op jit(solution)/shard_map/ppermute | solution.py:272
  60.1 10.9 %collective-permute-done = f32[256,256]{1,0:T(8,128)S(1)} collective-permute-done((f32[256,256]{1,0:T(8,128)S(1)}, f32[256,256]{1,0:T(8,128)S(1)}, u32[]{:S(2)}, u32[]{:S(2)}) %collective-permute-start) | collective-permute-done | bytes 262176 | tf_op jit(solution)/shard_map/ppermute | solution.py:272
  72.3 7.7 %collective-permute-done.1 = f32[256,256]{1,0:T(8,128)S(1)} collective-permute-done((f32[256,256]{1,0:T(8,128)S(1)}, f32[256,256]{1,0:T(8,128)S(1)}, u32[]{:S(2)}, u32[]{:S(2)}) %collective-permute-start.1) | collective-permute-done | bytes 262176 | tf_op jit(solution)/shard_map/ppermute | solution.py:272
  80.0 2.8 %collective-permute-start.2 = (f32[256,256]{1,0:T(8,128)S(1)}, f32[256,256]{1,0:T(8,128)S(1)}, u32[]{:S(2)}, u32[]{:S(2)}) collective-permute-start(f32[256,256]{1,0:T(8,128)S(1)} %add.134), channel_id=1, source_target_pairs={{0,4},{1,5},{2,6},{3,7},{4,0},{5,1},{6,2},{7,3},{8,12},{9,13},{10,... | collective-permute-start | bytes 786440 | tf_op jit(solution)/shard_map/ppermute | solution.py:272
  83.1 5.9 %collective-permute-done.2 = f32[256,256]{1,0:T(8,128)S(1)} collective-permute-done((f32[256,256]{1,0:T(8,128)S(1)}, f32[256,256]{1,0:T(8,128)S(1)}, u32[]{:S(2)}, u32[]{:S(2)}) %collective-permute-start.2) | collective-permute-done | bytes 262176 | tf_op jit(solution)/shard_map/ppermute | solution.py:272
  90.5 9.5 %shard_map.110 = (bf16[256,1024]{1,0:T(8,128)(2,1)}, f32[256,8]{1,0:T(8,128)}) custom-call(s32[2]{0:T(128)} %pad_add_fusion.scalar_ref, bf16[256,1024]{1,0:T(8,128)(2,1)} %q_ref.3, bf16[4096,128]{1,0:T(8,128)(2,1)} %get-tuple-element.33.k_ref, bf16[4096,128]{1,0:T(8,128)(2,1)} %get-tuple-element.32.v_ref), custom_call_target="tpu_custom_call" | custom-call | tf_op jit(solution)/shard_map/pallas_call | solution.py:122
  101.2 11.6 %fusion.2.do_ref = bf16[256,1024]{1,0:T(8,128)(2,1)S(1)} fusion(bf16[1024,8192]{1,0:T(8,128)(2,1)} %param.11, bf16[256,8192]{1,0:T(8,128)(2,1)} %all-gather.2.cloned.1.call-done, f32[256]{0:T(256)S(1)} %convert_add_fusion.1), kind=kOutput, calls=%fused_computation.5 | convolution fusion | flops 4301520896 | bytes 21496832 | tf_op jit(solution)/shard_map/dot_general | solution.py:341
  114.1 9.6 %shard_map.111 = (bf16[256,1024]{1,0:T(8,128)(2,1)}, bf16[4096,256]{1,0:T(8,128)(2,1)}) custom-call(s32[2]{0:T(128)} %pad_add_fusion.scalar_ref, bf16[256,1024]{1,0:T(8,128)(2,1)} %q_ref.3, bf16[256,1024]{1,0:T(8,128)(2,1)} %copy-done.1, bf16[4096,128]{1,0:T(8,128)(2,1)} %get-tuple-element.33.k_ref, bf16[4096,128]{1,0:T(8,128)(2,1)} %get-tuple-element.32.v_ref, ...), custom_call_target="tpu_custom_call" | custom-call | tf_op jit(solution)/shard_map/pallas_call | solution.py:212
  126.2 4.9 %collective-permute-start.18 = (bf16[256,256]{1,0:T(8,128)(2,1)S(1)}, bf16[256,256]{1,0:T(8,128)(2,1)S(1)}, u32[]{:S(2)}, u32[]{:S(2)}) collective-permute-start(bf16[256,256]{1,0:T(8,128)(2,1)S(1)} %get-tuple-element.17), channel_id=1, source_target_pairs={{8,0},{16,8},{24,16},{32,24},{40,32},{48,40},{56,48},{64,56},{72,6... | collective-permute-start | bytes 393224 | tf_op jit(solution)/shard_map/ppermute | solution.py:263
  136.4 5.1 %fusion = f32[256,256]{1,0:T(8,128)S(1)} fusion(bf16[256,8192]{1,0:T(8,128)(2,1)} %all-gather.2.cloned.1.call-done, f32[256]{0:T(256)S(1)} %convert_add_fusion.1), kind=kOutput, calls=%fused_computation.3 | convolution fusion | flops 1080033280 | bytes 4457472 | tf_op jit(solution)/shard_map/dot_general | solution.py:287
  142.0 2.5 %collective-permute-done.18 = bf16[256,256]{1,0:T(8,128)(2,1)S(1)} collective-permute-done((bf16[256,256]{1,0:T(8,128)(2,1)S(1)}, bf16[256,256]{1,0:T(8,128)(2,1)S(1)}, u32[]{:S(2)}, u32[]{:S(2)}) %collective-permute-start.18) | collective-permute-done | bytes 131104 | tf_op jit(solution)/shard_map/ppermute | solution.py:263
  149.1 10.0 %collective-permute-done.20 = bf16[256,256]{1,0:T(8,128)(2,1)S(1)} collective-permute-done((bf16[256,256]{1,0:T(8,128)(2,1)S(1)}, bf16[256,256]{1,0:T(8,128)(2,1)S(1)}, u32[]{:S(2)}, u32[]{:S(2)}) %collective-permute-start.20) | collective-permute-done | bytes 131104 | tf_op jit(solution)/shard_map/ppermute | solution.py:263
  163.6 6.9 %collective-permute-done.22 = bf16[256,256]{1,0:T(8,128)(2,1)S(1)} collective-permute-done((bf16[256,256]{1,0:T(8,128)(2,1)S(1)}, bf16[256,256]{1,0:T(8,128)(2,1)S(1)}, u32[]{:S(2)}, u32[]{:S(2)}) %collective-permute-start.22) | collective-permute-done | bytes 131104 | tf_op jit(solution)/shard_map/ppermute | solution.py:263
  172.4 7.1 %collective-permute-done.23 = bf16[256,256]{1,0:T(8,128)(2,1)S(1)} collective-permute-done((bf16[256,256]{1,0:T(8,128)(2,1)S(1)}, bf16[256,256]{1,0:T(8,128)(2,1)S(1)}, u32[]{:S(2)}, u32[]{:S(2)}) %collective-permute-start.23) | collective-permute-done | bytes 131104 | tf_op jit(solution)/shard_map/ppermute | solution.py:263
  180.8 6.9 %collective-permute-done.24 = bf16[256,256]{1,0:T(8,128)(2,1)S(1)} collective-permute-done((bf16[256,256]{1,0:T(8,128)(2,1)S(1)}, bf16[256,256]{1,0:T(8,128)(2,1)S(1)}, u32[]{:S(2)}, u32[]{:S(2)}) %collective-permute-start.24) | collective-permute-done | bytes 131104 | tf_op jit(solution)/shard_map/ppermute | solution.py:263
  191.8 12.8 %collective-permute-done.26 = bf16[256,256]{1,0:T(8,128)(2,1)S(1)} collective-permute-done((bf16[256,256]{1,0:T(8,128)(2,1)S(1)}, bf16[256,256]{1,0:T(8,128)(2,1)S(1)}, u32[]{:S(2)}, u32[]{:S(2)}) %collective-permute-start.26) | collective-permute-done | bytes 131104 | tf_op jit(solution)/shard_map/ppermute | solution.py:263
  207.1 3.7 %collective-permute-done.28 = bf16[256,256]{1,0:T(8,128)(2,1)S(1)} collective-permute-done((bf16[256,256]{1,0:T(8,128)(2,1)S(1)}, bf16[256,256]{1,0:T(8,128)(2,1)S(1)}, u32[]{:S(2)}, u32[]{:S(2)}) %collective-permute-start.28) | collective-permute-done | bytes 131104 | tf_op jit(solution)/shard_map/ppermute | solution.py:263
  212.2 8.0 %collective-permute-done.30 = bf16[256,256]{1,0:T(8,128)(2,1)S(1)} collective-permute-done((bf16[256,256]{1,0:T(8,128)(2,1)S(1)}, bf16[256,256]{1,0:T(8,128)(2,1)S(1)}, u32[]{:S(2)}, u32[]{:S(2)}) %collective-permute-start.30) | collective-permute-done | bytes 131104 | tf_op jit(solution)/shard_map/ppermute | solution.py:263
  220.1 2.6 %collective-permute-done.31 = bf16[256,256]{1,0:T(8,128)(2,1)S(1)} collective-permute-done((bf16[256,256]{1,0:T(8,128)(2,1)S(1)}, bf16[256,256]{1,0:T(8,128)(2,1)S(1)}, u32[]{:S(2)}, u32[]{:S(2)}) %collective-permute-start.31) | collective-permute-done | bytes 131104 | tf_op jit(solution)/shard_map/ppermute | solution.py:263
  (109 shorter events, 56.1 us)
Async XLA Ops:
  7.2 94.0 %all-gather.2.cloned.1.call-start = ((), (), s32[]{:S(2)}) async-start(), calls=%async_computation | async-start | bytes 4718592 | tf_op jit(solution)/shard_map/all_gather | solution.py:310
  9.0 14.4 %collective-permute-start.3 = (bf16[256,256]{1,0:T(8,128)(2,1)S(1)}, bf16[256,256]{1,0:T(8,128)(2,1)S(1)}, u32[]{:S(2)}, u32[]{:S(2)}) collective-permute-start(bf16[256,256]{1,0:T(8,128)(2,1)S(1)} %constant_dynamic-update-slice_fusion), channel_id=1, source_target_pairs={{0,120},{1,121},{2,122},{3,123},{4,124},{5,125},{6,126},{7,127}} | collective-permute-start | bytes 393224 | tf_op jit(solution)/shard_map/ppermute | solution.py:249
  9.7 15.0 %collective-permute-start.4 = (bf16[256,256]{1,0:T(8,128)(2,1)S(1)}, bf16[256,256]{1,0:T(8,128)(2,1)S(1)}, u32[]{:S(2)}, u32[]{:S(2)}) collective-permute-start(bf16[256,256]{1,0:T(8,128)(2,1)S(1)} %constant_dynamic-update-slice_fusion), channel_id=1, source_target_pairs={{0,112},{8,120},{1,113},{9,121},{2,114},{10,122},{3,115},{11,123},... | collective-permute-start | bytes 393224 | tf_op jit(solution)/shard_map/ppermute | solution.py:249
  24.7 17.4 %collective-permute-start.9 = (bf16[256,256]{1,0:T(8,128)(2,1)S(1)}, bf16[256,256]{1,0:T(8,128)(2,1)S(1)}, u32[]{:S(2)}, u32[]{:S(2)}) collective-permute-start(bf16[256,256]{1,0:T(8,128)(2,1)S(1)} %constant_dynamic-update-slice_fusion), channel_id=1, source_target_pairs={{0,72},{8,80},{16,88},{24,96},{32,104},{40,112},{48,120},{1,73},{9... | collective-permute-start | bytes 393224 | tf_op jit(solution)/shard_map/ppermute | solution.py:249
  26.0 22.4 %collective-permute-start.10 = (bf16[256,256]{1,0:T(8,128)(2,1)S(1)}, bf16[256,256]{1,0:T(8,128)(2,1)S(1)}, u32[]{:S(2)}, u32[]{:S(2)}) collective-permute-start(bf16[256,256]{1,0:T(8,128)(2,1)S(1)} %constant_dynamic-update-slice_fusion), channel_id=1, source_target_pairs={{0,64},{8,72},{16,80},{24,88},{32,96},{40,104},{48,112},{56,120},{... | collective-permute-start | bytes 393224 | tf_op jit(solution)/shard_map/ppermute | solution.py:249
  28.0 21.8 %collective-permute-start.11 = (bf16[256,256]{1,0:T(8,128)(2,1)S(1)}, bf16[256,256]{1,0:T(8,128)(2,1)S(1)}, u32[]{:S(2)}, u32[]{:S(2)}) collective-permute-start(bf16[256,256]{1,0:T(8,128)(2,1)S(1)} %constant_dynamic-update-slice_fusion), channel_id=1, source_target_pairs={{0,56},{8,64},{16,72},{24,80},{32,88},{40,96},{48,104},{56,112},{6... | collective-permute-start | bytes 393224 | tf_op jit(solution)/shard_map/ppermute | solution.py:249
  31.6 23.0 %collective-permute-start.12 = (bf16[256,256]{1,0:T(8,128)(2,1)S(1)}, bf16[256,256]{1,0:T(8,128)(2,1)S(1)}, u32[]{:S(2)}, u32[]{:S(2)}) collective-permute-start(bf16[256,256]{1,0:T(8,128)(2,1)S(1)} %constant_dynamic-update-slice_fusion), channel_id=1, source_target_pairs={{0,48},{8,56},{16,64},{24,72},{32,80},{40,88},{48,96},{56,104},{64... | collective-permute-start | bytes 393224 | tf_op jit(solution)/shard_map/ppermute | solution.py:249
  36.9 20.2 %collective-permute-start.13 = (bf16[256,256]{1,0:T(8,128)(2,1)S(1)}, bf16[256,256]{1,0:T(8,128)(2,1)S(1)}, u32[]{:S(2)}, u32[]{:S(2)}) collective-permute-start(bf16[256,256]{1,0:T(8,128)(2,1)S(1)} %constant_dynamic-update-slice_fusion), channel_id=1, source_target_pairs={{0,40},{8,48},{16,56},{24,64},{32,72},{40,80},{48,88},{56,96},{64,... | collective-permute-start | bytes 393224 | tf_op jit(solution)/shard_map/ppermute | solution.py:249
  42.1 17.6 %collective-permute-start.14 = (bf16[256,256]{1,0:T(8,128)(2,1)S(1)}, bf16[256,256]{1,0:T(8,128)(2,1)S(1)}, u32[]{:S(2)}, u32[]{:S(2)}) collective-permute-start(bf16[256,256]{1,0:T(8,128)(2,1)S(1)} %constant_dynamic-update-slice_fusion), channel_id=1, source_target_pairs={{0,32},{8,40},{16,48},{24,56},{32,64},{40,72},{48,80},{56,88},{64,... | collective-permute-start | bytes 393224 | tf_op jit(solution)/shard_map/ppermute | solution.py:249
  126.2 18.4 %collective-permute-start.18 = (bf16[256,256]{1,0:T(8,128)(2,1)S(1)}, bf16[256,256]{1,0:T(8,128)(2,1)S(1)}, u32[]{:S(2)}, u32[]{:S(2)}) collective-permute-start(bf16[256,256]{1,0:T(8,128)(2,1)S(1)} %get-tuple-element.17), channel_id=1, source_target_pairs={{8,0},{16,8},{24,16},{32,24},{40,32},{48,40},{56,48},{64,56},{72,6... | collective-permute-start | bytes 393224 | tf_op jit(solution)/shard_map/ppermute | solution.py:263
  131.1 16.7 %collective-permute-start.19 = (bf16[256,256]{1,0:T(8,128)(2,1)S(1)}, bf16[256,256]{1,0:T(8,128)(2,1)S(1)}, u32[]{:S(2)}, u32[]{:S(2)}) collective-permute-start(bf16[256,256]{1,0:T(8,128)(2,1)S(1)} %get-tuple-element.31), channel_id=1, source_target_pairs={{16,0},{24,8},{32,16},{40,24},{48,32},{56,40},{64,48},{72,56},{80,... | collective-permute-start | bytes 393224 | tf_op jit(solution)/shard_map/ppermute | solution.py:263
  132.4 26.7 %collective-permute-start.20 = (bf16[256,256]{1,0:T(8,128)(2,1)S(1)}, bf16[256,256]{1,0:T(8,128)(2,1)S(1)}, u32[]{:S(2)}, u32[]{:S(2)}) collective-permute-start(bf16[256,256]{1,0:T(8,128)(2,1)S(1)} %get-tuple-element.30), channel_id=1, source_target_pairs={{24,0},{32,8},{40,16},{48,24},{56,32},{64,40},{72,48},{80,56},{88,... | collective-permute-start | bytes 393224 | tf_op jit(solution)/shard_map/ppermute | solution.py:263
  133.7 28.7 %collective-permute-start.21 = (bf16[256,256]{1,0:T(8,128)(2,1)S(1)}, bf16[256,256]{1,0:T(8,128)(2,1)S(1)}, u32[]{:S(2)}, u32[]{:S(2)}) collective-permute-start(bf16[256,256]{1,0:T(8,128)(2,1)S(1)} %get-tuple-element.29), channel_id=1, source_target_pairs={{32,0},{40,8},{48,16},{56,24},{64,32},{72,40},{80,48},{88,56},{96,... | collective-permute-start | bytes 393224 | tf_op jit(solution)/shard_map/ppermute | solution.py:263
  135.0 35.6 %collective-permute-start.22 = (bf16[256,256]{1,0:T(8,128)(2,1)S(1)}, bf16[256,256]{1,0:T(8,128)(2,1)S(1)}, u32[]{:S(2)}, u32[]{:S(2)}) collective-permute-start(bf16[256,256]{1,0:T(8,128)(2,1)S(1)} %get-tuple-element.28), channel_id=1, source_target_pairs={{40,0},{48,8},{56,16},{64,24},{72,32},{80,40},{88,48},{96,56},{104... | collective-permute-start | bytes 393224 | tf_op jit(solution)/shard_map/ppermute | solution.py:263
  144.5 35.0 %collective-permute-start.23 = (bf16[256,256]{1,0:T(8,128)(2,1)S(1)}, bf16[256,256]{1,0:T(8,128)(2,1)S(1)}, u32[]{:S(2)}, u32[]{:S(2)}) collective-permute-start(bf16[256,256]{1,0:T(8,128)(2,1)S(1)} %get-tuple-element.27), channel_id=1, source_target_pairs={{48,0},{56,8},{64,16},{72,24},{80,32},{88,40},{96,48},{104,56},{11... | collective-permute-start | bytes 393224 | tf_op jit(solution)/shard_map/ppermute | solution.py:263
  147.8 39.9 %collective-permute-start.24 = (bf16[256,256]{1,0:T(8,128)(2,1)S(1)}, bf16[256,256]{1,0:T(8,128)(2,1)S(1)}, u32[]{:S(2)}, u32[]{:S(2)}) collective-permute-start(bf16[256,256]{1,0:T(8,128)(2,1)S(1)} %get-tuple-element.26), channel_id=1, source_target_pairs={{56,0},{64,8},{72,16},{80,24},{88,32},{96,40},{104,48},{112,56},{1... | collective-permute-start | bytes 393224 | tf_op jit(solution)/shard_map/ppermute | solution.py:263
  159.1 31.4 %collective-permute-start.25 = (bf16[256,256]{1,0:T(8,128)(2,1)S(1)}, bf16[256,256]{1,0:T(8,128)(2,1)S(1)}, u32[]{:S(2)}, u32[]{:S(2)}) collective-permute-start(bf16[256,256]{1,0:T(8,128)(2,1)S(1)} %get-tuple-element.25), channel_id=1, source_target_pairs={{64,0},{72,8},{80,16},{88,24},{96,32},{104,40},{112,48},{120,56},{... | collective-permute-start | bytes 393224 | tf_op jit(solution)/shard_map/ppermute | solution.py:263
  162.3 42.3 %collective-permute-start.26 = (bf16[256,256]{1,0:T(8,128)(2,1)S(1)}, bf16[256,256]{1,0:T(8,128)(2,1)S(1)}, u32[]{:S(2)}, u32[]{:S(2)}) collective-permute-start(bf16[256,256]{1,0:T(8,128)(2,1)S(1)} %get-tuple-element.24), channel_id=1, source_target_pairs={{72,0},{80,8},{88,16},{96,24},{104,32},{112,40},{120,48},{73,1},{8... | collective-permute-start | bytes 393224 | tf_op jit(solution)/shard_map/ppermute | solution.py:263
  170.6 35.3 %collective-permute-start.27 = (bf16[256,256]{1,0:T(8,128)(2,1)S(1)}, bf16[256,256]{1,0:T(8,128)(2,1)S(1)}, u32[]{:S(2)}, u32[]{:S(2)}) collective-permute-start(bf16[256,256]{1,0:T(8,128)(2,1)S(1)} %get-tuple-element.23), channel_id=1, source_target_pairs={{80,0},{88,8},{96,16},{104,24},{112,32},{120,40},{81,1},{89,9},{97... | collective-permute-start | bytes 393224 | tf_op jit(solution)/shard_map/ppermute | solution.py:263
  179.5 31.3 %collective-permute-start.28 = (bf16[256,256]{1,0:T(8,128)(2,1)S(1)}, bf16[256,256]{1,0:T(8,128)(2,1)S(1)}, u32[]{:S(2)}, u32[]{:S(2)}) collective-permute-start(bf16[256,256]{1,0:T(8,128)(2,1)S(1)} %get-tuple-element.22), channel_id=1, source_target_pairs={{88,0},{96,8},{104,16},{112,24},{120,32},{89,1},{97,9},{105,17},{1... | collective-permute-start | bytes 393224 | tf_op jit(solution)/shard_map/ppermute | solution.py:263
  187.7 24.5 %collective-permute-start.29 = (bf16[256,256]{1,0:T(8,128)(2,1)S(1)}, bf16[256,256]{1,0:T(8,128)(2,1)S(1)}, u32[]{:S(2)}, u32[]{:S(2)}) collective-permute-start(bf16[256,256]{1,0:T(8,128)(2,1)S(1)} %get-tuple-element.21), channel_id=1, source_target_pairs={{96,0},{104,8},{112,16},{120,24},{97,1},{105,9},{113,17},{121,25},... | collective-permute-start | bytes 393224 | tf_op jit(solution)/shard_map/ppermute | solution.py:263
  190.5 29.6 %collective-permute-start.30 = (bf16[256,256]{1,0:T(8,128)(2,1)S(1)}, bf16[256,256]{1,0:T(8,128)(2,1)S(1)}, u32[]{:S(2)}, u32[]{:S(2)}) collective-permute-start(bf16[256,256]{1,0:T(8,128)(2,1)S(1)} %get-tuple-element.20), channel_id=1, source_target_pairs={{104,0},{112,8},{120,16},{105,1},{113,9},{121,17},{106,2},{114,10}... | collective-permute-start | bytes 393224 | tf_op jit(solution)/shard_map/ppermute | solution.py:263
  204.6 18.1 %collective-permute-start.31 = (bf16[256,256]{1,0:T(8,128)(2,1)S(1)}, bf16[256,256]{1,0:T(8,128)(2,1)S(1)}, u32[]{:S(2)}, u32[]{:S(2)}) collective-permute-start(bf16[256,256]{1,0:T(8,128)(2,1)S(1)} %get-tuple-element.19), channel_id=1, source_target_pairs={{112,0},{120,8},{113,1},{121,9},{114,2},{122,10},{115,3},{123,11},... | collective-permute-start | bytes 393224 | tf_op jit(solution)/shard_map/ppermute | solution.py:263
  205.9 16.8 %collective-permute-start.32 = (bf16[256,256]{1,0:T(8,128)(2,1)S(1)}, bf16[256,256]{1,0:T(8,128)(2,1)S(1)}, u32[]{:S(2)}, u32[]{:S(2)}) collective-permute-start(bf16[256,256]{1,0:T(8,128)(2,1)S(1)} %get-tuple-element.18), channel_id=1, source_target_pairs={{120,0},{121,1},{122,2},{123,3},{124,4},{125,5},{126,6},{127,7}} | collective-permute-start | bytes 393224 | tf_op jit(solution)/shard_map/ppermute | solution.py:263
  (14 other events, 159.5 us)
Sparse Core Ops, SparseCore 0:
  21.9 78.6 all-gather.1

commit v9 on v5

--- a/solution.py
+++ b/solution.py
@@ -159,6 +159,11 @@
     return total
 
 
+def exchange_reduce(parts, axis_name):
+    arrived = lax.all_to_all(parts, axis_name, 0, 0, tiled=True)
+    return jnp.sum(arrived.astype(jnp.float32), axis=0)
+
+
 def butterfly_sum(value, axis_name):
     size = lax.axis_size(axis_name)
     stride = 1
@@ -290,7 +295,7 @@
         block_rows,
     )
     ctx_size = lax.axis_size("ctx")
-    key_sums = causal_reduce(
+    key_sums = exchange_reduce(
         backward_buffer.reshape((ctx_size, tokens // ctx_size) + backward_buffer.shape[1:]), "ctx"
     )
     grad_key = key_sums[:, : local_groups * head_dim].astype(jnp.bfloat16)

time: 204 us -> 190 us (0.931)
  waiting for transfers between devices: 72 us -> 47.6 us
  starting transfers between devices: 69.2 us -> 79.8 us
  matrix products: 19.4 us -> 22.9 us
  local copies, waits for them, and re-layouts: 11.3 us -> 8.88 us
    ppermute x15 -> x0, waiting for transfers between devices: 42.6 us -> none  [causal_reduce(): total = total + lax.ppermute(sent, axis_name, pairs).astype(jnp.float32)]
    all_to_all x0 -> x1, starting transfers between devices: none -> 30.2 us  [exchange_reduce(): arrived = lax.all_to_all(parts, axis_name, 0, 0, tiled=True)]
    all_gather x1, waiting for transfers between devices: 10.6 us -> 33.1 us  [body(): lax.all_gather(grad_out, 'head', axis=1, tiled=True).astype(jnp.float32)]
    ppermute x15 -> x0, starting transfers between devices: 20.1 us -> none  [causal_reduce(): total = total + lax.ppermute(sent, axis_name, pairs).astype(jnp.float32)]
    ppermute x3, waiting for transfers between devices: 18.5 us -> 12.3 us  [butterfly_sum(): value = value + lax.ppermute(value, axis_name, pairs)]
    dot_general x1, matrix products: 1.68 us -> 5.15 us  [gram_squares(): lax.dot_general(left_side, left_side, (((1,), (1,)), ((), ())), preferred...]
    squeeze x1 -> x0, local copies, waits for them, and re-layouts: 2.98 us -> none  [causal_reduce(): lax.dynamic_index_in_dim(parts, jnp.maximum(own - shift, 0), 0, keepdims=...]
  transfers between devices with their start and end apart: 34 -> 20, of which waited for: 17 -> 5; matrix products, arithmetic and copies ran while one was open for 9% -> 18% of each run, Pallas kernels for 0% -> 5%
where the time goes in v9:
time: 190 us; the launch traced here: 189 us
  starting transfers between devices  79.8 us (42%)
  waiting for transfers between devices  47.6 us (25%)
  matrix products  22.9 us (12%)
  between operations  14.7 us (8%)
  Pallas kernels  9.32 us (5%)
  local copies, waits for them, and re-layouts  8.88 us (5%)
  other arithmetic  5.24 us (3%)
    ppermute x15, starting transfers between devices, causal_gather(): received.append(lax.ppermute(value, axis_name, pairs))  42.7 us
    all_gather x1, waiting for transfers between devices, body(): lax.all_gather(grad_out, 'head', axis=1, tiled=True).astype(jnp.float32)  33.1 us
    all_to_all x1, starting transfers between devices, exchange_reduce(): arrived = lax.all_to_all(parts, axis_name, 0, 0, tiled=True)  30.2 us
    ppermute x3, waiting for transfers between devices, butterfly_sum(): value = value + lax.ppermute(value, axis_name, pairs)  12.3 us
    dot_general x1, matrix products, body(): lax.dot_general(piece_part, out_weight, (((1,), (1,)), ((), ())), preferr...  11.6 us
    pallas_call x1, Pallas kernels, flash_backward(): pl.pallas_call(kernel, grid_spec=grid_spec, out_shape=[jax.ShapeDtypeStru...  9.32 us
    ppermute x3, starting transfers between devices, butterfly_sum(): value = value + lax.ppermute(value, axis_name, pairs)  6.85 us
    dot_general x1, matrix products, gram_squares(): lax.dot_general(left_side, left_side, (((1,), (1,)), ((), ())), preferred...  5.15 us
  transfers between devices with their start and end apart: 20, of which 5 were waited for; matrix products, arithmetic and copies ran while one was open for 18% of the time, Pallas kernels for 5%

profile of v9, /device:TPU:1, one launch (start us, length us, event | category | flops | bytes accessed | tf_op | source)
XLA Modules:
  0.0 188.7 jit_solution(17573116447328791443)
XLA Ops:
  9.7 8.1 %collective-permute-start.1 = (bf16[256,256]{1,0:T(8,128)(2,1)S(1)}, bf16[256,256]{1,0:T(8,128)(2,1)S(1)}, u32[]{:S(2)}, u32[]{:S(2)}) collective-permute-start(bf16[256,256]{1,0:T(8,128)(2,1)S(1)} %constant_dynamic-update-slice_fusion), channel_id=1, source_target_pairs={{0,112},{8,120},{1,113},{9,121},{2,114},{10,122},{3,115},{11,123},... | collective-permute-start | bytes 393224 | tf_op jit(solution)/shard_map/ppermute | solution.py:144
  17.8 1.3 collective-permute-start.2
  23.9 1.9 %copy.31 = bf16[32,8,8,128]{3,2,1,0:T(8,128)(2,1)} copy(bf16[32,8,8,128]{3,1,2,0:T(8,128)(2,1)} %bitcast.128) | data formatting | bytes 1048576
  30.5 1.3 collective-permute-start.8
  31.8 5.0 %collective-permute-start.9 = (bf16[256,256]{1,0:T(8,128)(2,1)S(1)}, bf16[256,256]{1,0:T(8,128)(2,1)S(1)}, u32[]{:S(2)}, u32[]{:S(2)}) collective-permute-start(bf16[256,256]{1,0:T(8,128)(2,1)S(1)} %constant_dynamic-update-slice_fusion), channel_id=1, source_target_pairs={{0,48},{8,56},{16,64},{24,72},{32,80},{40,88},{48,96},{56,104},{64... | collective-permute-start | bytes 393224 | tf_op jit(solution)/shard_map/ppermute | solution.py:144
  36.9 5.0 %collective-permute-start.10 = (bf16[256,256]{1,0:T(8,128)(2,1)S(1)}, bf16[256,256]{1,0:T(8,128)(2,1)S(1)}, u32[]{:S(2)}, u32[]{:S(2)}) collective-permute-start(bf16[256,256]{1,0:T(8,128)(2,1)S(1)} %constant_dynamic-update-slice_fusion), channel_id=1, source_target_pairs={{0,40},{8,48},{16,56},{24,64},{32,72},{40,80},{48,88},{56,96},{64,... | collective-permute-start | bytes 393224 | tf_op jit(solution)/shard_map/ppermute | solution.py:144
  42.1 6.3 %collective-permute-start.11 = (bf16[256,256]{1,0:T(8,128)(2,1)S(1)}, bf16[256,256]{1,0:T(8,128)(2,1)S(1)}, u32[]{:S(2)}, u32[]{:S(2)}) collective-permute-start(bf16[256,256]{1,0:T(8,128)(2,1)S(1)} %constant_dynamic-update-slice_fusion), channel_id=1, source_target_pairs={{0,32},{8,40},{16,48},{24,56},{32,64},{40,72},{48,80},{56,88},{64,... | collective-permute-start | bytes 393224 | tf_op jit(solution)/shard_map/ppermute | solution.py:144
  49.8 4.8 %collective-permute-start.13 = (bf16[256,256]{1,0:T(8,128)(2,1)S(1)}, bf16[256,256]{1,0:T(8,128)(2,1)S(1)}, u32[]{:S(2)}, u32[]{:S(2)}) collective-permute-start(bf16[256,256]{1,0:T(8,128)(2,1)S(1)} %constant_dynamic-update-slice_fusion), channel_id=1, source_target_pairs={{0,16},{8,24},{16,32},{24,40},{32,48},{40,56},{48,64},{56,72},{64,... | collective-permute-start | bytes 393224 | tf_op jit(solution)/shard_map/ppermute | solution.py:144
  54.6 2.4 %collective-permute-start.14 = (bf16[256,256]{1,0:T(8,128)(2,1)S(1)}, bf16[256,256]{1,0:T(8,128)(2,1)S(1)}, u32[]{:S(2)}, u32[]{:S(2)}) collective-permute-start(bf16[256,256]{1,0:T(8,128)(2,1)S(1)} %constant_dynamic-update-slice_fusion), channel_id=1, source_target_pairs={{0,8},{8,16},{16,24},{24,32},{32,40},{40,48},{48,56},{56,64},{64,7... | collective-permute-start | bytes 393224 | tf_op jit(solution)/shard_map/ppermute | solution.py:144
  57.0 2.7 %collective-permute-start.15 = (f32[256,256]{1,0:T(8,128)S(1)}, f32[256,256]{1,0:T(8,128)}, u32[]{:S(2)}, u32[]{:S(2)}) collective-permute-start(f32[256,256]{1,0:T(8,128)S(1)} %fusion.38), channel_id=1, source_target_pairs={{0,1},{1,0},{2,3},{3,2},{4,5},{5,4},{6,7},{7,6},{8,9},{9,8},{10,11... | collective-permute-start | bytes 786440 | tf_op jit(solution)/shard_map/ppermute | solution.py:172
  61.5 1.9 while.24
  64.4 3.1 %while.25 = (s32[]{:T(128)}, f32[256,8,128]{2,0,1:T(8,128)S(1)}, s32[]{:T(128)}, bf16[4096,128]{1,0:T(8,128)(2,1)S(1)}, bf16[256,8,128]{2,1,0:T(8,128)(2,1)}, /*...) while((s32[]{:T(128)}, f32[256,8,128]{2,0,1:T(8,128)S(1)}, ...), condition=%wide.region_5.6_spmd.clone, body=%wide.region_4.5_spmd.clone.sunk | while | flops 541459200 | bytes 3161259 | solution.py:258
  64.5 2.8 %fusion.56 = f32[256,8,128]{2,0,1:T(8,128)S(1)} fusion(f32[256,8,128]{2,0,1:T(8,128)S(1)} %get-tuple-element.342, f32[256,8]{0,1:T(8,128)S(1)} %get-tuple-element.358, pred[256,512]{1,0:T(8,128)(4,1)S(1)} %broadcast_compare_fusion.5, bf16[256,8,128]{2,1,0:T(8,128)(2,1)} %get-tuple-element.357, bf16[4096,128]{1,0:T(8,128)(2,1)} %get-tuple-element.359, ...), kind=kOutput, calls=%fused_computation.18.clone.1 | convolution fusion | flops 541327360 | bytes 3023872 | tf_op jit(solution)/shard_map/while/body/tgk,kd->tgd/dot_general | solution.py:254
  67.5 33.1 %all-gather.2.cloned.1.call-done = bf16[256,8192]{1,0:T(8,128)(2,1)} async-done(((bf16[256,1024]{1,0:T(8,128)(2,1)}), bf16[256,8192]{1,0:T(8,128)(2,1)}) %all-gather.2.cloned.1.call-update) | async-done | bytes 4194320 | tf_op jit(solution)/shard_map/all_gather | solution.py:210
  100.6 11.6 %fusion.28.do_ref = bf16[256,1024]{1,0:T(8,128)(2,1)S(1)} fusion(bf16[1024,8192]{1,0:T(8,128)(2,1)} %param.15, bf16[256,8192]{1,0:T(8,128)(2,1)} %all-gather.2.cloned.1.call-done, f32[256]{0:T(256)S(1)} %convert_add_fusion), kind=kOutput, calls=%fused_computation.35 | convolution fusion | flops 4301520896 | bytes 21496832 | tf_op jit(solution)/shard_map/dot_general | solution.py:267
  113.4 9.3 %shard_map.110 = (bf16[256,1024]{1,0:T(8,128)(2,1)}, bf16[4096,256]{1,0:T(8,128)(2,1)}) custom-call(s32[2]{0:T(128)} %pad_add_fusion.scalar_ref, bf16[256,1024]{1,0:T(8,128)(2,1)} %q_ref.1, bf16[256,1024]{1,0:T(8,128)(2,1)} %copy-done.3, bf16[4096,128]{1,0:T(8,128)(2,1)S(1)} %get-tuple-element.368, bf16[4096,128]{1,0:T(8,128)(2,1)} %get-tuple-element.369, ...), custom_call_target="tpu_custom_call" | custom-call | tf_op jit(solution)/shard_map/pallas_call | solution.py:107
  122.7 30.2 %all-to-all-start = ((bf16[16,256,256]{2,1,0:T(8,128)(2,1)}), bf16[16,256,256]{2,1,0:T(8,128)(2,1)S(1)}, u32[]{:S(2)}, u32[]{:S(2)}) async-start(bf16[16,256,256]{2,1,0:T(8,128)(2,1)} %bitcast.129), calls=%async_computation | async-start | bytes 4194304 | tf_op jit(solution)/shard_map/all_to_all | solution.py:163
  153.9 1.3 collective-permute-start.16
  155.2 6.6 %collective-permute-done.16 = f32[256,256]{1,0:T(8,128)S(1)} collective-permute-done((f32[256,256]{1,0:T(8,128)S(1)}, f32[256,256]{1,0:T(8,128)S(1)}, u32[]{:S(2)}, u32[]{:S(2)}) %collective-permute-start.16) | collective-permute-done | bytes 262176 | tf_op jit(solution)/shard_map/ppermute | solution.py:172
  161.9 2.8 %collective-permute-start.17 = (f32[256,256]{1,0:T(8,128)S(1)}, f32[256,256]{1,0:T(8,128)S(1)}, u32[]{:S(2)}, u32[]{:S(2)}) collective-permute-start(f32[256,256]{1,0:T(8,128)S(1)} %add.107), channel_id=1, source_target_pairs={{0,4},{1,5},{2,6},{3,7},{4,0},{5,1},{6,2},{7,3},{8,12},{9,13},{10,... | collective-permute-start | bytes 786440 | tf_op jit(solution)/shard_map/ppermute | solution.py:172
  164.8 5.7 %collective-permute-done.17 = f32[256,256]{1,0:T(8,128)S(1)} collective-permute-done((f32[256,256]{1,0:T(8,128)S(1)}, f32[256,256]{1,0:T(8,128)S(1)}, u32[]{:S(2)}, u32[]{:S(2)}) %collective-permute-start.17) | collective-permute-done | bytes 262176 | tf_op jit(solution)/shard_map/ppermute | solution.py:172
  170.5 1.7 multiply_reduce_fusion.1
  172.2 5.1 %fusion.26 = f32[256,256]{1,0:T(8,128)S(1)} fusion(bf16[256,8192]{1,0:T(8,128)(2,1)} %all-gather.2.cloned.1.call-done, f32[256]{0:T(256)S(1)} %convert_add_fusion), kind=kOutput, calls=%fused_computation.33 | convolution fusion | flops 1080033280 | bytes 4457472 | tf_op jit(solution)/shard_map/dot_general | solution.py:187
  179.0 1.9 %all-to-all-done = bf16[16,256,256]{2,1,0:T(8,128)(2,1)S(1)} async-done(((bf16[16,256,256]{2,1,0:T(8,128)(2,1)}), bf16[16,256,256]{2,1,0:T(8,128)(2,1)S(1)}, u32[]{:S(2)}, u32[]{:S(2)}) %all-to-all-start) | async-done | bytes 2097184 | tf_op jit(solution)/shard_map/all_to_all | solution.py:163
  (104 shorter events, 22.6 us)
Async XLA Ops:
  7.2 15.7 %copy-start = (bf16[256,1024]{1,0:T(8,128)(2,1)S(1)}, bf16[256,1024]{1,0:T(8,128)(2,1)}, u32[]{:S(2)}) copy-start(bf16[256,1024]{1,0:T(8,128)(2,1)} %param.11) | copy-start | bytes 1572868
  7.2 93.4 %all-gather.2.cloned.1.call-start = ((), (), s32[]{:S(2)}) async-start(), calls=%async_computation.1 | async-start | bytes 4718592 | tf_op jit(solution)/shard_map/all_gather | solution.py:210
  9.0 17.5 %collective-permute-start = (bf16[256,256]{1,0:T(8,128)(2,1)S(1)}, bf16[256,256]{1,0:T(8,128)(2,1)S(1)}, u32[]{:S(2)}, u32[]{:S(2)}) collective-permute-start(bf16[256,256]{1,0:T(8,128)(2,1)S(1)} %constant_dynamic-update-slice_fusion), channel_id=1, source_target_pairs={{0,120},{1,121},{2,122},{3,123},{4,124},{5,125},{6,126},{7,127}} | collective-permute-start | bytes 393224 | tf_op jit(solution)/shard_map/ppermute | solution.py:144
  9.7 18.1 %collective-permute-start.1 = (bf16[256,256]{1,0:T(8,128)(2,1)S(1)}, bf16[256,256]{1,0:T(8,128)(2,1)S(1)}, u32[]{:S(2)}, u32[]{:S(2)}) collective-permute-start(bf16[256,256]{1,0:T(8,128)(2,1)S(1)} %constant_dynamic-update-slice_fusion), channel_id=1, source_target_pairs={{0,112},{8,120},{1,113},{9,121},{2,114},{10,122},{3,115},{11,123},... | collective-permute-start | bytes 393224 | tf_op jit(solution)/shard_map/ppermute | solution.py:144
  17.8 11.3 %collective-permute-start.2 = (bf16[256,256]{1,0:T(8,128)(2,1)S(1)}, bf16[256,256]{1,0:T(8,128)(2,1)S(1)}, u32[]{:S(2)}, u32[]{:S(2)}) collective-permute-start(bf16[256,256]{1,0:T(8,128)(2,1)S(1)} %constant_dynamic-update-slice_fusion), channel_id=1, source_target_pairs={{0,104},{8,112},{16,120},{1,105},{9,113},{17,121},{2,106},{10,114}... | collective-permute-start | bytes 393224 | tf_op jit(solution)/shard_map/ppermute | solution.py:144
  19.1 11.3 %collective-permute-start.3 = (bf16[256,256]{1,0:T(8,128)(2,1)S(1)}, bf16[256,256]{1,0:T(8,128)(2,1)S(1)}, u32[]{:S(2)}, u32[]{:S(2)}) collective-permute-start(bf16[256,256]{1,0:T(8,128)(2,1)S(1)} %constant_dynamic-update-slice_fusion), channel_id=1, source_target_pairs={{0,96},{8,104},{16,112},{24,120},{1,97},{9,105},{17,113},{25,121},... | collective-permute-start | bytes 393224 | tf_op jit(solution)/shard_map/ppermute | solution.py:144
  20.4 11.4 %collective-permute-start.4 = (bf16[256,256]{1,0:T(8,128)(2,1)S(1)}, bf16[256,256]{1,0:T(8,128)(2,1)S(1)}, u32[]{:S(2)}, u32[]{:S(2)}) collective-permute-start(bf16[256,256]{1,0:T(8,128)(2,1)S(1)} %constant_dynamic-update-slice_fusion), channel_id=1, source_target_pairs={{0,88},{8,96},{16,104},{24,112},{32,120},{1,89},{9,97},{17,105},{2... | collective-permute-start | bytes 393224 | tf_op jit(solution)/shard_map/ppermute | solution.py:144
  26.5 10.4 %collective-permute-start.5 = (bf16[256,256]{1,0:T(8,128)(2,1)S(1)}, bf16[256,256]{1,0:T(8,128)(2,1)S(1)}, u32[]{:S(2)}, u32[]{:S(2)}) collective-permute-start(bf16[256,256]{1,0:T(8,128)(2,1)S(1)} %constant_dynamic-update-slice_fusion), channel_id=1, source_target_pairs={{0,80},{8,88},{16,96},{24,104},{32,112},{40,120},{1,81},{9,89},{17... | collective-permute-start | bytes 393224 | tf_op jit(solution)/shard_map/ppermute | solution.py:144
  27.8 14.3 %collective-permute-start.6 = (bf16[256,256]{1,0:T(8,128)(2,1)S(1)}, bf16[256,256]{1,0:T(8,128)(2,1)S(1)}, u32[]{:S(2)}, u32[]{:S(2)}) collective-permute-start(bf16[256,256]{1,0:T(8,128)(2,1)S(1)} %constant_dynamic-update-slice_fusion), channel_id=1, source_target_pairs={{0,72},{8,80},{16,88},{24,96},{32,104},{40,112},{48,120},{1,73},{9... | collective-permute-start | bytes 393224 | tf_op jit(solution)/shard_map/ppermute | solution.py:144
  29.1 19.3 %collective-permute-start.7 = (bf16[256,256]{1,0:T(8,128)(2,1)S(1)}, bf16[256,256]{1,0:T(8,128)(2,1)S(1)}, u32[]{:S(2)}, u32[]{:S(2)}) collective-permute-start(bf16[256,256]{1,0:T(8,128)(2,1)S(1)} %constant_dynamic-update-slice_fusion), channel_id=1, source_target_pairs={{0,64},{8,72},{16,80},{24,88},{32,96},{40,104},{48,112},{56,120},{... | collective-permute-start | bytes 393224 | tf_op jit(solution)/shard_map/ppermute | solution.py:144
  30.5 19.3 %collective-permute-start.8 = (bf16[256,256]{1,0:T(8,128)(2,1)S(1)}, bf16[256,256]{1,0:T(8,128)(2,1)S(1)}, u32[]{:S(2)}, u32[]{:S(2)}) collective-permute-start(bf16[256,256]{1,0:T(8,128)(2,1)S(1)} %constant_dynamic-update-slice_fusion), channel_id=1, source_target_pairs={{0,56},{8,64},{16,72},{24,80},{32,88},{40,96},{48,104},{56,112},{6... | collective-permute-start | bytes 393224 | tf_op jit(solution)/shard_map/ppermute | solution.py:144
  31.8 22.8 %collective-permute-start.9 = (bf16[256,256]{1,0:T(8,128)(2,1)S(1)}, bf16[256,256]{1,0:T(8,128)(2,1)S(1)}, u32[]{:S(2)}, u32[]{:S(2)}) collective-permute-start(bf16[256,256]{1,0:T(8,128)(2,1)S(1)} %constant_dynamic-update-slice_fusion), channel_id=1, source_target_pairs={{0,48},{8,56},{16,64},{24,72},{32,80},{40,88},{48,96},{56,104},{64... | collective-permute-start | bytes 393224 | tf_op jit(solution)/shard_map/ppermute | solution.py:144
  36.9 20.2 %collective-permute-start.10 = (bf16[256,256]{1,0:T(8,128)(2,1)S(1)}, bf16[256,256]{1,0:T(8,128)(2,1)S(1)}, u32[]{:S(2)}, u32[]{:S(2)}) collective-permute-start(bf16[256,256]{1,0:T(8,128)(2,1)S(1)} %constant_dynamic-update-slice_fusion), channel_id=1, source_target_pairs={{0,40},{8,48},{16,56},{24,64},{32,72},{40,80},{48,88},{56,96},{64,... | collective-permute-start | bytes 393224 | tf_op jit(solution)/shard_map/ppermute | solution.py:144
  42.1 17.6 %collective-permute-start.11 = (bf16[256,256]{1,0:T(8,128)(2,1)S(1)}, bf16[256,256]{1,0:T(8,128)(2,1)S(1)}, u32[]{:S(2)}, u32[]{:S(2)}) collective-permute-start(bf16[256,256]{1,0:T(8,128)(2,1)S(1)} %constant_dynamic-update-slice_fusion), channel_id=1, source_target_pairs={{0,32},{8,40},{16,48},{24,56},{32,64},{40,72},{48,80},{56,88},{64,... | collective-permute-start | bytes 393224 | tf_op jit(solution)/shard_map/ppermute | solution.py:144
  48.4 11.4 %collective-permute-start.12 = (bf16[256,256]{1,0:T(8,128)(2,1)S(1)}, bf16[256,256]{1,0:T(8,128)(2,1)S(1)}, u32[]{:S(2)}, u32[]{:S(2)}) collective-permute-start(bf16[256,256]{1,0:T(8,128)(2,1)S(1)} %constant_dynamic-update-slice_fusion), channel_id=1, source_target_pairs={{0,24},{8,32},{16,40},{24,48},{32,56},{40,64},{48,72},{56,80},{64,... | collective-permute-start | bytes 393224 | tf_op jit(solution)/shard_map/ppermute | solution.py:144
  49.8 10.1 %collective-permute-start.13 = (bf16[256,256]{1,0:T(8,128)(2,1)S(1)}, bf16[256,256]{1,0:T(8,128)(2,1)S(1)}, u32[]{:S(2)}, u32[]{:S(2)}) collective-permute-start(bf16[256,256]{1,0:T(8,128)(2,1)S(1)} %constant_dynamic-update-slice_fusion), channel_id=1, source_target_pairs={{0,16},{8,24},{16,32},{24,40},{32,48},{40,56},{48,64},{56,72},{64,... | collective-permute-start | bytes 393224 | tf_op jit(solution)/shard_map/ppermute | solution.py:144
  54.6 5.3 %collective-permute-start.14 = (bf16[256,256]{1,0:T(8,128)(2,1)S(1)}, bf16[256,256]{1,0:T(8,128)(2,1)S(1)}, u32[]{:S(2)}, u32[]{:S(2)}) collective-permute-start(bf16[256,256]{1,0:T(8,128)(2,1)S(1)} %constant_dynamic-update-slice_fusion), channel_id=1, source_target_pairs={{0,8},{8,16},{16,24},{24,32},{32,40},{40,48},{48,56},{56,64},{64,7... | collective-permute-start | bytes 393224 | tf_op jit(solution)/shard_map/ppermute | solution.py:144
  57.0 95.9 %collective-permute-start.15 = (f32[256,256]{1,0:T(8,128)S(1)}, f32[256,256]{1,0:T(8,128)}, u32[]{:S(2)}, u32[]{:S(2)}) collective-permute-start(f32[256,256]{1,0:T(8,128)S(1)} %fusion.38), channel_id=1, source_target_pairs={{0,1},{1,0},{2,3},{3,2},{4,5},{5,4},{6,7},{7,6},{8,9},{9,8},{10,11... | collective-permute-start | bytes 786440 | tf_op jit(solution)/shard_map/ppermute | solution.py:172
  67.5 44.7 %copy-start.1 = (f32[256,8,128]{2,0,1:T(8,128)}, f32[256,8,128]{2,0,1:T(8,128)S(1)}, u32[]{:S(2)}) copy-start(f32[256,8,128]{2,0,1:T(8,128)S(1)} %get-tuple-element.91) | copy-start | bytes 3145732
  112.2 1.2 copy-start.3
  122.7 58.2 %all-to-all-start = ((bf16[16,256,256]{2,1,0:T(8,128)(2,1)}), bf16[16,256,256]{2,1,0:T(8,128)(2,1)S(1)}, u32[]{:S(2)}, u32[]{:S(2)}) async-start(bf16[16,256,256]{2,1,0:T(8,128)(2,1)} %bitcast.129), calls=%async_computation | async-start | bytes 4194304 | tf_op jit(solution)/shard_map/all_to_all | solution.py:163
  153.9 7.9 %collective-permute-start.16 = (f32[256,256]{1,0:T(8,128)S(1)}, f32[256,256]{1,0:T(8,128)S(1)}, u32[]{:S(2)}, u32[]{:S(2)}) collective-permute-start(f32[256,256]{1,0:T(8,128)S(1)} %add.106), channel_id=1, source_target_pairs={{0,2},{1,3},{2,0},{3,1},{4,6},{5,7},{6,4},{7,5},{8,10},{9,11},{10,... | collective-permute-start | bytes 786440 | tf_op jit(solution)/shard_map/ppermute | solution.py:172
  161.9 8.5 %collective-permute-start.17 = (f32[256,256]{1,0:T(8,128)S(1)}, f32[256,256]{1,0:T(8,128)S(1)}, u32[]{:S(2)}, u32[]{:S(2)}) collective-permute-start(f32[256,256]{1,0:T(8,128)S(1)} %add.107), channel_id=1, source_target_pairs={{0,4},{1,5},{2,6},{3,7},{4,0},{5,1},{6,2},{7,3},{8,12},{9,13},{10,... | collective-permute-start | bytes 786440 | tf_op jit(solution)/shard_map/ppermute | solution.py:172
  172.2 5.2 %copy-start.2 = (f32[256,8,128]{2,0,1:T(8,128)S(1)}, f32[256,8,128]{2,0,1:T(8,128)}, u32[]{:S(2)}) copy-start(f32[256,8,128]{2,0,1:T(8,128)} %copy-done.1) | copy-start | bytes 3145732
  (1 other events, 0.7 us)
Sparse Core Ops, SparseCore 0:
  21.9 78.6 all-gather.1

commit v10 on v9

--- a/solution.py
+++ b/solution.py
@@ -200,16 +200,15 @@
     first_row = own_index * tok_dev
     loss_weight = 0.25 + answer_mask.astype(jnp.float32)
     weighted = (grad_out.astype(jnp.float32) * loss_weight[:, None]).astype(jnp.bfloat16)
-    hidden_gram = butterfly_sum(
-        lax.dot_general(
-            hidden_in, hidden_in, (((1,), (1,)), ((), ())), preferred_element_type=jnp.float32
-        ),
-        "head",
+    gram_part = lax.dot_general(
+        hidden_in, hidden_in, (((1,), (1,)), ((), ())), preferred_element_type=jnp.float32
     )
     piece_part = (
         lax.all_gather(grad_out, "head", axis=1, tiled=True).astype(jnp.float32)
         * loss_weight[:, None]
     ).astype(jnp.bfloat16)
+    gram_part, piece_part = lax.optimization_barrier((gram_part, piece_part))
+    hidden_gram = jnp.sum(lax.all_gather(gram_part, "head", axis=0, tiled=False), axis=0)
     pair_all = causal_gather(jnp.concatenate([key_rows, value_rows], axis=1), "ctx")
     kv_width = key_rows.shape[1]
     keys_all, values_all = (pair_all[:, :kv_width], pair_all[:, kv_width:])

time: 190 us -> 199 us (1.047)
  waiting for transfers between devices: 47.6 us -> 54.5 us
  other arithmetic: 5.24 us -> 10.7 us
  starting transfers between devices: 79.8 us -> 76.3 us
    all_to_all x1, waiting for transfers between devices: 1.93 us -> 22.6 us  [exchange_reduce(): arrived = lax.all_to_all(parts, axis_name, 0, 0, tiled=True)]
    ppermute x3 -> x0, waiting for transfers between devices: 12.3 us -> none  [butterfly_sum(): value = value + lax.ppermute(value, axis_name, pairs)]
    ppermute x3 -> x0, starting transfers between devices: 6.85 us -> none  [butterfly_sum(): value = value + lax.ppermute(value, axis_name, pairs)]
    convert_element_type x0 -> x1, other arithmetic: none -> 5.26 us  [body(): piece_part = (lax.all_gather(grad_out, 'head', axis=1, tiled=True).astype...]
    all_to_all x1, starting transfers between devices: 30.2 us -> 34.3 us  [exchange_reduce(): arrived = lax.all_to_all(parts, axis_name, 0, 0, tiled=True)]
    all_gather x1, waiting for transfers between devices: 33.1 us -> 29.5 us  [body(): lax.all_gather(grad_out, 'head', axis=1, tiled=True).astype(jnp.float32)]
    ppermute x15, waiting for transfers between devices: 0.28 us -> 2.31 us  [causal_gather(): received.append(lax.ppermute(value, axis_name, pairs))]
  transfers between devices with their start and end apart: 20 -> 18, of which waited for: 5 -> 4; matrix products, arithmetic and copies ran while one was open for 18% -> 16% of each run, Pallas kernels for 5% -> 5%
where the time goes in v10:
time: 199 us; the launch traced here: 198 us
  starting transfers between devices  76.3 us (38%)
  waiting for transfers between devices  54.5 us (27%)
  matrix products  23.3 us (12%)
  between operations  14.7 us (7%)
  other arithmetic  10.7 us (5%)
  Pallas kernels  9.3 us (5%)
  local copies, waits for them, and re-layouts  8.94 us (4%)
    ppermute x15, starting transfers between devices, causal_gather(): received.append(lax.ppermute(value, axis_name, pairs))  42 us
    all_to_all x1, starting transfers between devices, exchange_reduce(): arrived = lax.all_to_all(parts, axis_name, 0, 0, tiled=True)  34.3 us
    all_gather x1, waiting for transfers between devices, body(): lax.all_gather(grad_out, 'head', axis=1, tiled=True).astype(jnp.float32)  29.5 us
    all_to_all x1, waiting for transfers between devices, exchange_reduce(): arrived = lax.all_to_all(parts, axis_name, 0, 0, tiled=True)  22.6 us
    dot_general x1, matrix products, body(): lax.dot_general(piece_part, out_weight, (((1,), (1,)), ((), ())), preferr...  11.6 us
    pallas_call x1, Pallas kernels, flash_backward(): pl.pallas_call(kernel, grid_spec=grid_spec, out_shape=[jax.ShapeDtypeStru...  9.3 us
    convert_element_type x1, other arithmetic, body(): piece_part = (lax.all_gather(grad_out, 'head', axis=1, tiled=True).astype...  5.26 us
    unnamed x45, local copies, waits for them, and re-layouts  4.88 us
  transfers between devices with their start and end apart: 18, of which 4 were waited for; matrix products, arithmetic and copies ran while one was open for 16% of the time, Pallas kernels for 5%

profile of v10, /device:TPU:1, one launch (start us, length us, event | category | flops | bytes accessed | tf_op | source)
XLA Modules:
  0.0 198.0 jit_solution(10899568799644896852)
XLA Ops:
  9.7 8.1 %collective-permute-start.1 = (bf16[256,256]{1,0:T(8,128)(2,1)S(1)}, bf16[256,256]{1,0:T(8,128)(2,1)S(1)}, u32[]{:S(2)}, u32[]{:S(2)}) collective-permute-start(bf16[256,256]{1,0:T(8,128)(2,1)S(1)} %constant_dynamic-update-slice_fusion), channel_id=1, source_target_pairs={{0,112},{8,120},{1,113},{9,121},{2,114},{10,122},{3,115},{11,123},... | collective-permute-start | bytes 393224 | tf_op jit(solution)/shard_map/ppermute | solution.py:144
  17.8 1.3 collective-permute-start.2
  19.1 1.3 collective-permute-start.3
  20.4 1.3 collective-permute-start.4
  24.7 1.9 copy.31
  28.5 1.3 collective-permute-start.6
  32.5 4.3 %collective-permute-start.9 = (bf16[256,256]{1,0:T(8,128)(2,1)S(1)}, bf16[256,256]{1,0:T(8,128)(2,1)S(1)}, u32[]{:S(2)}, u32[]{:S(2)}) collective-permute-start(bf16[256,256]{1,0:T(8,128)(2,1)S(1)} %constant_dynamic-update-slice_fusion), channel_id=1, source_target_pairs={{0,48},{8,56},{16,64},{24,72},{32,80},{40,88},{48,96},{56,104},{64... | collective-permute-start | bytes 393224 | tf_op jit(solution)/shard_map/ppermute | solution.py:144
  36.9 5.0 %collective-permute-start.10 = (bf16[256,256]{1,0:T(8,128)(2,1)S(1)}, bf16[256,256]{1,0:T(8,128)(2,1)S(1)}, u32[]{:S(2)}, u32[]{:S(2)}) collective-permute-start(bf16[256,256]{1,0:T(8,128)(2,1)S(1)} %constant_dynamic-update-slice_fusion), channel_id=1, source_target_pairs={{0,40},{8,48},{16,56},{24,64},{32,72},{40,80},{48,88},{56,96},{64,... | collective-permute-start | bytes 393224 | tf_op jit(solution)/shard_map/ppermute | solution.py:144
  42.1 6.3 %collective-permute-start.11 = (bf16[256,256]{1,0:T(8,128)(2,1)S(1)}, bf16[256,256]{1,0:T(8,128)(2,1)S(1)}, u32[]{:S(2)}, u32[]{:S(2)}) collective-permute-start(bf16[256,256]{1,0:T(8,128)(2,1)S(1)} %constant_dynamic-update-slice_fusion), channel_id=1, source_target_pairs={{0,32},{8,40},{16,48},{24,56},{32,64},{40,72},{48,80},{56,88},{64,... | collective-permute-start | bytes 393224 | tf_op jit(solution)/shard_map/ppermute | solution.py:144
  49.7 4.8 %collective-permute-start.13 = (bf16[256,256]{1,0:T(8,128)(2,1)S(1)}, bf16[256,256]{1,0:T(8,128)(2,1)S(1)}, u32[]{:S(2)}, u32[]{:S(2)}) collective-permute-start(bf16[256,256]{1,0:T(8,128)(2,1)S(1)} %constant_dynamic-update-slice_fusion), channel_id=1, source_target_pairs={{0,16},{8,24},{16,32},{24,40},{32,48},{40,56},{48,64},{56,72},{64,... | collective-permute-start | bytes 393224 | tf_op jit(solution)/shard_map/ppermute | solution.py:144
  54.5 2.5 %collective-permute-start.14 = (bf16[256,256]{1,0:T(8,128)(2,1)S(1)}, bf16[256,256]{1,0:T(8,128)(2,1)S(1)}, u32[]{:S(2)}, u32[]{:S(2)}) collective-permute-start(bf16[256,256]{1,0:T(8,128)(2,1)S(1)} %constant_dynamic-update-slice_fusion), channel_id=1, source_target_pairs={{0,8},{8,16},{16,24},{24,32},{32,40},{40,48},{48,56},{56,64},{64,7... | collective-permute-start | bytes 393224 | tf_op jit(solution)/shard_map/ppermute | solution.py:144
  57.1 2.1 %collective-permute-done.14 = bf16[256,256]{1,0:T(8,128)(2,1)S(1)} collective-permute-done((bf16[256,256]{1,0:T(8,128)(2,1)S(1)}, bf16[256,256]{1,0:T(8,128)(2,1)S(1)}, u32[]{:S(2)}, u32[]{:S(2)}) %collective-permute-start.14) | collective-permute-done | bytes 131104 | tf_op jit(solution)/shard_map/ppermute | solution.py:144
  61.0 1.9 while.24
  63.8 3.1 %while.25 = (s32[]{:T(128)}, f32[256,8,128]{2,0,1:T(8,128)S(1)}, s32[]{:T(128)}, bf16[4096,128]{1,0:T(8,128)(2,1)S(1)}, bf16[256,8,128]{2,1,0:T(8,128)(2,1)}, /*...) while((s32[]{:T(128)}, f32[256,8,128]{2,0,1:T(8,128)S(1)}, ...), condition=%wide.region_5.6_spmd.clone, body=%wide.region_4.5_spmd.clone.sunk | while | flops 541459200 | bytes 3161259 | solution.py:257
  63.9 2.8 %fusion.54 = f32[256,8,128]{2,0,1:T(8,128)S(1)} fusion(f32[256,8,128]{2,0,1:T(8,128)S(1)} %get-tuple-element.348, f32[256,8]{0,1:T(8,128)S(1)} %get-tuple-element.364, pred[256,512]{1,0:T(8,128)(4,1)S(1)} %broadcast_compare_fusion.5, bf16[256,8,128]{2,1,0:T(8,128)(2,1)} %get-tuple-element.363, bf16[4096,128]{1,0:T(8,128)(2,1)} %get-tuple-element.365, ...), kind=kOutput, calls=%fused_computation.18.clone.1 | convolution fusion | flops 541327360 | bytes 3023872 | tf_op jit(solution)/shard_map/while/body/tgk,kd->tgd/dot_general | solution.py:253
  66.9 29.5 %all-gather.4.cloned.1.call-done = bf16[256,8192]{1,0:T(8,128)(2,1)} async-done(((bf16[256,1024]{1,0:T(8,128)(2,1)}), bf16[256,8192]{1,0:T(8,128)(2,1)}) %all-gather.4.cloned.1.call-update) | async-done | bytes 4194320 | tf_op jit(solution)/shard_map/all_gather | solution.py:207
  96.5 5.3 %multiply_convert_fusion = bf16[256,8192]{1,0:T(8,128)(2,1)} fusion(bf16[256,8192]{1,0:T(8,128)(2,1)} %all-gather.4.cloned.1.call-done, f32[256]{0:T(256)S(1)} %convert_add_fusion), kind=kLoop, calls=%fused_computation.30 | loop fusion | flops 6291456 | bytes 8389632 | tf_op jit(solution)/shard_map/convert_element_type | solution.py:209
  101.8 11.6 %convolution_convert_fusion.do_ref = bf16[256,1024]{1,0:T(8,128)(2,1)S(1)} fusion(bf16[256,8192]{1,0:T(8,128)(2,1)} %multiply_convert_fusion, bf16[1024,8192]{1,0:T(8,128)(2,1)} %param.15), kind=kOutput, calls=%fused_computation.33 | convolution fusion | flops 4295229440 | bytes 21495808 | tf_op jit(solution)/shard_map/dot_general | solution.py:266
  114.5 9.3 %shard_map.110 = (bf16[256,1024]{1,0:T(8,128)(2,1)}, bf16[4096,256]{1,0:T(8,128)(2,1)}) custom-call(s32[2]{0:T(128)} %pad_add_fusion.scalar_ref, bf16[256,1024]{1,0:T(8,128)(2,1)} %q_ref.1, bf16[256,1024]{1,0:T(8,128)(2,1)} %copy-done.3, bf16[4096,128]{1,0:T(8,128)(2,1)S(1)} %get-tuple-element.375, bf16[4096,128]{1,0:T(8,128)(2,1)} %get-tuple-element.377, ...), custom_call_target="tpu_custom_call" | custom-call | tf_op jit(solution)/shard_map/pallas_call | solution.py:107
  123.8 34.3 %all-to-all-start = ((bf16[16,256,256]{2,1,0:T(8,128)(2,1)}), bf16[16,256,256]{2,1,0:T(8,128)(2,1)S(1)}, u32[]{:S(2)}, u32[]{:S(2)}) async-start(bf16[16,256,256]{2,1,0:T(8,128)(2,1)} %bitcast.132), calls=%async_computation | async-start | bytes 4194304 | tf_op jit(solution)/shard_map/all_to_all | solution.py:163
  158.2 4.8 %fusion.33 = f32[256,256]{1,0:T(8,128)S(1)} fusion(bf16[256,8192]{1,0:T(8,128)(2,1)} %multiply_convert_fusion), kind=kOutput, calls=%fused_computation.83 | convolution fusion | flops 1073741824 | bytes 4456448 | tf_op jit(solution)/shard_map/dot_general | solution.py:187
  163.5 22.6 %all-to-all-done = bf16[16,256,256]{2,1,0:T(8,128)(2,1)S(1)} async-done(((bf16[16,256,256]{2,1,0:T(8,128)(2,1)}), bf16[16,256,256]{2,1,0:T(8,128)(2,1)S(1)}, u32[]{:S(2)}, u32[]{:S(2)}) %all-to-all-start) | async-done | bytes 2097184 | tf_op jit(solution)/shard_map/all_to_all | solution.py:163
  187.1 1.8 reduce_sum.56
  188.8 1.7 multiply_reduce_fusion.1
  (99 shorter events, 19.2 us)
Async XLA Ops:
  7.2 15.8 %copy-start = (bf16[256,1024]{1,0:T(8,128)(2,1)S(1)}, bf16[256,1024]{1,0:T(8,128)(2,1)}, u32[]{:S(2)}) copy-start(bf16[256,1024]{1,0:T(8,128)(2,1)} %param.11) | copy-start | bytes 1572868
  7.2 89.3 %all-gather.4.cloned.1.call-start = ((), (), s32[]{:S(2)}) async-start(), calls=%async_computation.1 | async-start | bytes 4718592 | tf_op jit(solution)/shard_map/all_gather | solution.py:207
  9.0 18.2 %collective-permute-start = (bf16[256,256]{1,0:T(8,128)(2,1)S(1)}, bf16[256,256]{1,0:T(8,128)(2,1)S(1)}, u32[]{:S(2)}, u32[]{:S(2)}) collective-permute-start(bf16[256,256]{1,0:T(8,128)(2,1)S(1)} %constant_dynamic-update-slice_fusion), channel_id=1, source_target_pairs={{0,120},{1,121},{2,122},{3,123},{4,124},{5,125},{6,126},{7,127}} | collective-permute-start | bytes 393224 | tf_op jit(solution)/shard_map/ppermute | solution.py:144
  9.7 18.9 %collective-permute-start.1 = (bf16[256,256]{1,0:T(8,128)(2,1)S(1)}, bf16[256,256]{1,0:T(8,128)(2,1)S(1)}, u32[]{:S(2)}, u32[]{:S(2)}) collective-permute-start(bf16[256,256]{1,0:T(8,128)(2,1)S(1)} %constant_dynamic-update-slice_fusion), channel_id=1, source_target_pairs={{0,112},{8,120},{1,113},{9,121},{2,114},{10,122},{3,115},{11,123},... | collective-permute-start | bytes 393224 | tf_op jit(solution)/shard_map/ppermute | solution.py:144
  17.8 12.0 %collective-permute-start.2 = (bf16[256,256]{1,0:T(8,128)(2,1)S(1)}, bf16[256,256]{1,0:T(8,128)(2,1)S(1)}, u32[]{:S(2)}, u32[]{:S(2)}) collective-permute-start(bf16[256,256]{1,0:T(8,128)(2,1)S(1)} %constant_dynamic-update-slice_fusion), channel_id=1, source_target_pairs={{0,104},{8,112},{16,120},{1,105},{9,113},{17,121},{2,106},{10,114}... | collective-permute-start | bytes 393224 | tf_op jit(solution)/shard_map/ppermute | solution.py:144
  19.1 12.1 %collective-permute-start.3 = (bf16[256,256]{1,0:T(8,128)(2,1)S(1)}, bf16[256,256]{1,0:T(8,128)(2,1)S(1)}, u32[]{:S(2)}, u32[]{:S(2)}) collective-permute-start(bf16[256,256]{1,0:T(8,128)(2,1)S(1)} %constant_dynamic-update-slice_fusion), channel_id=1, source_target_pairs={{0,96},{8,104},{16,112},{24,120},{1,97},{9,105},{17,113},{25,121},... | collective-permute-start | bytes 393224 | tf_op jit(solution)/shard_map/ppermute | solution.py:144
  20.4 12.1 %collective-permute-start.4 = (bf16[256,256]{1,0:T(8,128)(2,1)S(1)}, bf16[256,256]{1,0:T(8,128)(2,1)S(1)}, u32[]{:S(2)}, u32[]{:S(2)}) collective-permute-start(bf16[256,256]{1,0:T(8,128)(2,1)S(1)} %constant_dynamic-update-slice_fusion), channel_id=1, source_target_pairs={{0,88},{8,96},{16,104},{24,112},{32,120},{1,89},{9,97},{17,105},{2... | collective-permute-start | bytes 393224 | tf_op jit(solution)/shard_map/ppermute | solution.py:144
  21.8 165.3 %all-gather.6.cloned.1.call-start = ((), (), s32[]{:S(2)}) async-start(), calls=%async_computation.2 | async-start | bytes 2359296 | tf_op jit(solution)/shard_map/all_gather | solution.py:211
  27.2 9.7 %collective-permute-start.5 = (bf16[256,256]{1,0:T(8,128)(2,1)S(1)}, bf16[256,256]{1,0:T(8,128)(2,1)S(1)}, u32[]{:S(2)}, u32[]{:S(2)}) collective-permute-start(bf16[256,256]{1,0:T(8,128)(2,1)S(1)} %constant_dynamic-update-slice_fusion), channel_id=1, source_target_pairs={{0,80},{8,88},{16,96},{24,104},{32,112},{40,120},{1,81},{9,89},{17... | collective-permute-start | bytes 393224 | tf_op jit(solution)/shard_map/ppermute | solution.py:144
  28.5 13.6 %collective-permute-start.6 = (bf16[256,256]{1,0:T(8,128)(2,1)S(1)}, bf16[256,256]{1,0:T(8,128)(2,1)S(1)}, u32[]{:S(2)}, u32[]{:S(2)}) collective-permute-start(bf16[256,256]{1,0:T(8,128)(2,1)S(1)} %constant_dynamic-update-slice_fusion), channel_id=1, source_target_pairs={{0,72},{8,80},{16,88},{24,96},{32,104},{40,112},{48,120},{1,73},{9... | collective-permute-start | bytes 393224 | tf_op jit(solution)/shard_map/ppermute | solution.py:144
  29.9 18.5 %collective-permute-start.7 = (bf16[256,256]{1,0:T(8,128)(2,1)S(1)}, bf16[256,256]{1,0:T(8,128)(2,1)S(1)}, u32[]{:S(2)}, u32[]{:S(2)}) collective-permute-start(bf16[256,256]{1,0:T(8,128)(2,1)S(1)} %constant_dynamic-update-slice_fusion), channel_id=1, source_target_pairs={{0,64},{8,72},{16,80},{24,88},{32,96},{40,104},{48,112},{56,120},{... | collective-permute-start | bytes 393224 | tf_op jit(solution)/shard_map/ppermute | solution.py:144
  31.2 18.5 %collective-permute-start.8 = (bf16[256,256]{1,0:T(8,128)(2,1)S(1)}, bf16[256,256]{1,0:T(8,128)(2,1)S(1)}, u32[]{:S(2)}, u32[]{:S(2)}) collective-permute-start(bf16[256,256]{1,0:T(8,128)(2,1)S(1)} %constant_dynamic-update-slice_fusion), channel_id=1, source_target_pairs={{0,56},{8,64},{16,72},{24,80},{32,88},{40,96},{48,104},{56,112},{6... | collective-permute-start | bytes 393224 | tf_op jit(solution)/shard_map/ppermute | solution.py:144
  32.5 22.0 %collective-permute-start.9 = (bf16[256,256]{1,0:T(8,128)(2,1)S(1)}, bf16[256,256]{1,0:T(8,128)(2,1)S(1)}, u32[]{:S(2)}, u32[]{:S(2)}) collective-permute-start(bf16[256,256]{1,0:T(8,128)(2,1)S(1)} %constant_dynamic-update-slice_fusion), channel_id=1, source_target_pairs={{0,48},{8,56},{16,64},{24,72},{32,80},{40,88},{48,96},{56,104},{64... | collective-permute-start | bytes 393224 | tf_op jit(solution)/shard_map/ppermute | solution.py:144
  36.9 20.2 %collective-permute-start.10 = (bf16[256,256]{1,0:T(8,128)(2,1)S(1)}, bf16[256,256]{1,0:T(8,128)(2,1)S(1)}, u32[]{:S(2)}, u32[]{:S(2)}) collective-permute-start(bf16[256,256]{1,0:T(8,128)(2,1)S(1)} %constant_dynamic-update-slice_fusion), channel_id=1, source_target_pairs={{0,40},{8,48},{16,56},{24,64},{32,72},{40,80},{48,88},{56,96},{64,... | collective-permute-start | bytes 393224 | tf_op jit(solution)/shard_map/ppermute | solution.py:144
  42.1 15.0 %collective-permute-start.11 = (bf16[256,256]{1,0:T(8,128)(2,1)S(1)}, bf16[256,256]{1,0:T(8,128)(2,1)S(1)}, u32[]{:S(2)}, u32[]{:S(2)}) collective-permute-start(bf16[256,256]{1,0:T(8,128)(2,1)S(1)} %constant_dynamic-update-slice_fusion), channel_id=1, source_target_pairs={{0,32},{8,40},{16,48},{24,56},{32,64},{40,72},{48,80},{56,88},{64,... | collective-permute-start | bytes 393224 | tf_op jit(solution)/shard_map/ppermute | solution.py:144
  48.4 8.7 %collective-permute-start.12 = (bf16[256,256]{1,0:T(8,128)(2,1)S(1)}, bf16[256,256]{1,0:T(8,128)(2,1)S(1)}, u32[]{:S(2)}, u32[]{:S(2)}) collective-permute-start(bf16[256,256]{1,0:T(8,128)(2,1)S(1)} %constant_dynamic-update-slice_fusion), channel_id=1, source_target_pairs={{0,24},{8,32},{16,40},{24,48},{32,56},{40,64},{48,72},{56,80},{64,... | collective-permute-start | bytes 393224 | tf_op jit(solution)/shard_map/ppermute | solution.py:144
  49.7 7.4 %collective-permute-start.13 = (bf16[256,256]{1,0:T(8,128)(2,1)S(1)}, bf16[256,256]{1,0:T(8,128)(2,1)S(1)}, u32[]{:S(2)}, u32[]{:S(2)}) collective-permute-start(bf16[256,256]{1,0:T(8,128)(2,1)S(1)} %constant_dynamic-update-slice_fusion), channel_id=1, source_target_pairs={{0,16},{8,24},{16,32},{24,40},{32,48},{40,56},{48,64},{56,72},{64,... | collective-permute-start | bytes 393224 | tf_op jit(solution)/shard_map/ppermute | solution.py:144
  54.5 4.7 %collective-permute-start.14 = (bf16[256,256]{1,0:T(8,128)(2,1)S(1)}, bf16[256,256]{1,0:T(8,128)(2,1)S(1)}, u32[]{:S(2)}, u32[]{:S(2)}) collective-permute-start(bf16[256,256]{1,0:T(8,128)(2,1)S(1)} %constant_dynamic-update-slice_fusion), channel_id=1, source_target_pairs={{0,8},{8,16},{16,24},{24,32},{32,40},{40,48},{48,56},{56,64},{64,7... | collective-permute-start | bytes 393224 | tf_op jit(solution)/shard_map/ppermute | solution.py:144
  63.1 0.6 copy-start.4
  66.9 46.4 %copy-start.1 = (f32[256,8,128]{2,0,1:T(8,128)}, f32[256,8,128]{2,0,1:T(8,128)S(1)}, u32[]{:S(2)}) copy-start(f32[256,8,128]{2,0,1:T(8,128)S(1)} %get-tuple-element.94) | copy-start | bytes 3145732
  113.3 1.2 copy-start.3
  123.8 62.3 %all-to-all-start = ((bf16[16,256,256]{2,1,0:T(8,128)(2,1)}), bf16[16,256,256]{2,1,0:T(8,128)(2,1)S(1)}, u32[]{:S(2)}, u32[]{:S(2)}) async-start(bf16[16,256,256]{2,1,0:T(8,128)(2,1)} %bitcast.132), calls=%async_computation | async-start | bytes 4194304 | tf_op jit(solution)/shard_map/all_to_all | solution.py:163
  158.1 4.8 %copy-start.2 = (f32[256,8,128]{2,0,1:T(8,128)S(1)}, f32[256,8,128]{2,0,1:T(8,128)}, u32[]{:S(2)}) copy-start(f32[256,8,128]{2,0,1:T(8,128)} %copy-done.1) | copy-start | bytes 3145732
Sparse Core Ops, SparseCore 0:
  21.9 74.5 all-gather.3
  101.9 57.2 all-gather.5

commit v11 on v9

--- a/solution.py
+++ b/solution.py
@@ -269,6 +269,7 @@
     )
     grad_sum, squares_out = (grad_sum, gram_squares(piece_part, attended, head_dim))
     grad_attended, squares_out = (grad_sum.astype(jnp.bfloat16), squares_out)
+    hidden_gram, grad_attended = lax.optimization_barrier((hidden_gram, grad_attended))
     backward_buffer = buffer
     rows = query_rows.shape[0]
     backward_row_pos = first_row + jnp.arange(rows, dtype=jnp.int32)

time: 190 us -> 194 us (1.021)
  starting transfers between devices: 79.8 us -> 83.8 us
  waiting for transfers between devices: 47.6 us -> 50.5 us
    all_gather x1, waiting for transfers between devices: 33.1 us -> 10.6 us  [body(): lax.all_gather(grad_out, 'head', axis=1, tiled=True).astype(jnp.float32)]
    all_to_all x1, waiting for transfers between devices: 1.93 us -> 21.2 us  [exchange_reduce(): arrived = lax.all_to_all(parts, axis_name, 0, 0, tiled=True)]
    ppermute x3, waiting for transfers between devices: 12.3 us -> 18.4 us  [butterfly_sum(): value = value + lax.ppermute(value, axis_name, pairs)]
    all_to_all x1, starting transfers between devices: 30.2 us -> 34.7 us  [exchange_reduce(): arrived = lax.all_to_all(parts, axis_name, 0, 0, tiled=True)]
    unnamed x45 -> x49, local copies, waits for them, and re-layouts: 4.89 us -> 4.4 us
  transfers between devices with their start and end apart: 20 -> 20, of which waited for: 5 -> 6; matrix products, arithmetic and copies ran while one was open for 18% -> 10% of each run, Pallas kernels for 5% -> 0%
where the time goes in v11:
time: 194 us; the launch traced here: 193 us
  starting transfers between devices  83.8 us (43%)
  waiting for transfers between devices  50.5 us (26%)
  matrix products  21.7 us (11%)
  between operations  14.7 us (8%)
  Pallas kernels  9.29 us (5%)
  local copies, waits for them, and re-layouts  8.35 us (4%)
  other arithmetic  4.49 us (2%)
    ppermute x15, starting transfers between devices, causal_gather(): received.append(lax.ppermute(value, axis_name, pairs))  42.7 us
    all_to_all x1, starting transfers between devices, exchange_reduce(): arrived = lax.all_to_all(parts, axis_name, 0, 0, tiled=True)  34.7 us
    all_to_all x1, waiting for transfers between devices, exchange_reduce(): arrived = lax.all_to_all(parts, axis_name, 0, 0, tiled=True)  21.2 us
    ppermute x3, waiting for transfers between devices, butterfly_sum(): value = value + lax.ppermute(value, axis_name, pairs)  18.4 us
    dot_general x1, matrix products, body(): lax.dot_general(piece_part, out_weight, (((1,), (1,)), ((), ())), preferr...  11.6 us
    all_gather x1, waiting for transfers between devices, body(): lax.all_gather(grad_out, 'head', axis=1, tiled=True).astype(jnp.float32)  10.6 us
    pallas_call x1, Pallas kernels, flash_backward(): pl.pallas_call(kernel, grid_spec=grid_spec, out_shape=[jax.ShapeDtypeStru...  9.29 us
    ppermute x3, starting transfers between devices, butterfly_sum(): value = value + lax.ppermute(value, axis_name, pairs)  6.38 us
  transfers between devices with their start and end apart: 20, of which 6 were waited for; matrix products, arithmetic and copies ran while one was open for 10% of the time, Pallas kernels for 0%

profile of v11, /device:TPU:1, one launch (start us, length us, event | category | flops | bytes accessed | tf_op | source)
XLA Modules:
  0.0 193.2 jit_solution(12327341942911849651)
XLA Ops:
  9.7 8.1 %collective-permute-start.4 = (bf16[256,256]{1,0:T(8,128)(2,1)S(1)}, bf16[256,256]{1,0:T(8,128)(2,1)S(1)}, u32[]{:S(2)}, u32[]{:S(2)}) collective-permute-start(bf16[256,256]{1,0:T(8,128)(2,1)S(1)} %constant_dynamic-update-slice_fusion), channel_id=1, source_target_pairs={{0,112},{8,120},{1,113},{9,121},{2,114},{10,122},{3,115},{11,123},... | collective-permute-start | bytes 393224 | tf_op jit(solution)/shard_map/ppermute | solution.py:144
  17.8 1.3 collective-permute-start.5
  19.1 1.3 collective-permute-start.6
  20.4 1.3 collective-permute-start.7
  23.9 1.9 %copy.31 = bf16[32,8,8,128]{3,2,1,0:T(8,128)(2,1)} copy(bf16[32,8,8,128]{3,1,2,0:T(8,128)(2,1)} %bitcast.128) | data formatting | bytes 1048576
  31.8 5.0 %collective-permute-start.12 = (bf16[256,256]{1,0:T(8,128)(2,1)S(1)}, bf16[256,256]{1,0:T(8,128)(2,1)S(1)}, u32[]{:S(2)}, u32[]{:S(2)}) collective-permute-start(bf16[256,256]{1,0:T(8,128)(2,1)S(1)} %constant_dynamic-update-slice_fusion), channel_id=1, source_target_pairs={{0,48},{8,56},{16,64},{24,72},{32,80},{40,88},{48,96},{56,104},{64... | collective-permute-start | bytes 393224 | tf_op jit(solution)/shard_map/ppermute | solution.py:144
  36.9 5.0 %collective-permute-start.13 = (bf16[256,256]{1,0:T(8,128)(2,1)S(1)}, bf16[256,256]{1,0:T(8,128)(2,1)S(1)}, u32[]{:S(2)}, u32[]{:S(2)}) collective-permute-start(bf16[256,256]{1,0:T(8,128)(2,1)S(1)} %constant_dynamic-update-slice_fusion), channel_id=1, source_target_pairs={{0,40},{8,48},{16,56},{24,64},{32,72},{40,80},{48,88},{56,96},{64,... | collective-permute-start | bytes 393224 | tf_op jit(solution)/shard_map/ppermute | solution.py:144
  42.1 6.3 %collective-permute-start.14 = (bf16[256,256]{1,0:T(8,128)(2,1)S(1)}, bf16[256,256]{1,0:T(8,128)(2,1)S(1)}, u32[]{:S(2)}, u32[]{:S(2)}) collective-permute-start(bf16[256,256]{1,0:T(8,128)(2,1)S(1)} %constant_dynamic-update-slice_fusion), channel_id=1, source_target_pairs={{0,32},{8,40},{16,48},{24,56},{32,64},{40,72},{48,80},{56,88},{64,... | collective-permute-start | bytes 393224 | tf_op jit(solution)/shard_map/ppermute | solution.py:144
  49.8 4.8 %collective-permute-start.16 = (bf16[256,256]{1,0:T(8,128)(2,1)S(1)}, bf16[256,256]{1,0:T(8,128)(2,1)S(1)}, u32[]{:S(2)}, u32[]{:S(2)}) collective-permute-start(bf16[256,256]{1,0:T(8,128)(2,1)S(1)} %constant_dynamic-update-slice_fusion), channel_id=1, source_target_pairs={{0,16},{8,24},{16,32},{24,40},{32,48},{40,56},{48,64},{56,72},{64,... | collective-permute-start | bytes 393224 | tf_op jit(solution)/shard_map/ppermute | solution.py:144
  54.6 2.4 %collective-permute-start.17 = (bf16[256,256]{1,0:T(8,128)(2,1)S(1)}, bf16[256,256]{1,0:T(8,128)(2,1)S(1)}, u32[]{:S(2)}, u32[]{:S(2)}) collective-permute-start(bf16[256,256]{1,0:T(8,128)(2,1)S(1)} %constant_dynamic-update-slice_fusion), channel_id=1, source_target_pairs={{0,8},{8,16},{16,24},{24,32},{32,40},{40,48},{48,56},{56,64},{64,7... | collective-permute-start | bytes 393224 | tf_op jit(solution)/shard_map/ppermute | solution.py:144
  57.0 2.7 %collective-permute-start = (f32[256,256]{1,0:T(8,128)S(1)}, f32[256,256]{1,0:T(8,128)S(1)}, u32[]{:S(2)}, u32[]{:S(2)}) collective-permute-start(f32[256,256]{1,0:T(8,128)S(1)} %fusion.38), channel_id=1, source_target_pairs={{0,1},{1,0},{2,3},{3,2},{4,5},{5,4},{6,7},{7,6},{8,9},{9,8},{10,11... | collective-permute-start | bytes 786440 | tf_op jit(solution)/shard_map/ppermute | solution.py:172
  61.5 9.7 %collective-permute-done = f32[256,256]{1,0:T(8,128)S(1)} collective-permute-done((f32[256,256]{1,0:T(8,128)S(1)}, f32[256,256]{1,0:T(8,128)S(1)}, u32[]{:S(2)}, u32[]{:S(2)}) %collective-permute-start) | collective-permute-done | bytes 262176 | tf_op jit(solution)/shard_map/ppermute | solution.py:172
  72.4 1.9 while.24
  74.6 5.7 %collective-permute-done.1 = f32[256,256]{1,0:T(8,128)S(1)} collective-permute-done((f32[256,256]{1,0:T(8,128)S(1)}, f32[256,256]{1,0:T(8,128)S(1)}, u32[]{:S(2)}, u32[]{:S(2)}) %collective-permute-start.1) | collective-permute-done | bytes 262176 | tf_op jit(solution)/shard_map/ppermute | solution.py:172
  80.4 2.6 %collective-permute-start.2 = (f32[256,256]{1,0:T(8,128)S(1)}, f32[256,256]{1,0:T(8,128)S(1)}, u32[]{:S(2)}, u32[]{:S(2)}) collective-permute-start(f32[256,256]{1,0:T(8,128)S(1)} %add.101), channel_id=1, source_target_pairs={{0,4},{1,5},{2,6},{3,7},{4,0},{5,1},{6,2},{7,3},{8,12},{9,13},{10,... | collective-permute-start | bytes 786440 | tf_op jit(solution)/shard_map/ppermute | solution.py:172
  83.1 3.2 %while.25 = (s32[]{:T(128)}, f32[256,8,128]{2,0,1:T(8,128)S(1)}, s32[]{:T(128)}, bf16[4096,128]{1,0:T(8,128)(2,1)S(1)}, bf16[256,8,128]{2,1,0:T(8,128)(2,1)}, /*...) while((s32[]{:T(128)}, f32[256,8,128]{2,0,1:T(8,128)S(1)}, ...), condition=%wide.region_5.6_spmd.clone, body=%wide.region_4.5_spmd.clone.sunk | while | flops 541459200 | bytes 3161259 | solution.py:258
  83.3 2.8 %fusion.56 = f32[256,8,128]{2,0,1:T(8,128)S(1)} fusion(f32[256,8,128]{2,0,1:T(8,128)S(1)} %get-tuple-element.348, f32[256,8]{0,1:T(8,128)S(1)} %get-tuple-element.364, pred[256,512]{1,0:T(8,128)(4,1)S(1)} %broadcast_compare_fusion.5, bf16[256,8,128]{2,1,0:T(8,128)(2,1)} %get-tuple-element.363, bf16[4096,128]{1,0:T(8,128)(2,1)} %get-tuple-element.365, ...), kind=kOutput, calls=%fused_computation.18.clone.1 | convolution fusion | flops 541327360 | bytes 3023872 | tf_op jit(solution)/shard_map/while/body/tgk,kd->tgd/dot_general | solution.py:254
  86.3 3.0 %collective-permute-done.2 = f32[256,256]{1,0:T(8,128)S(1)} collective-permute-done((f32[256,256]{1,0:T(8,128)S(1)}, f32[256,256]{1,0:T(8,128)S(1)}, u32[]{:S(2)}, u32[]{:S(2)}) %collective-permute-start.2) | collective-permute-done | bytes 262176 | tf_op jit(solution)/shard_map/ppermute | solution.py:172
  90.0 10.6 %all-gather.2.cloned.1.call-done = bf16[256,8192]{1,0:T(8,128)(2,1)} async-done(((bf16[256,1024]{1,0:T(8,128)(2,1)}), bf16[256,8192]{1,0:T(8,128)(2,1)}) %all-gather.2.cloned.1.call-update) | async-done | bytes 4194320 | tf_op jit(solution)/shard_map/all_gather | solution.py:210
  100.6 11.6 %fusion.28.do_ref = bf16[256,1024]{1,0:T(8,128)(2,1)S(1)} fusion(bf16[1024,8192]{1,0:T(8,128)(2,1)} %param.15, bf16[256,8192]{1,0:T(8,128)(2,1)} %all-gather.2.cloned.1.call-done, f32[256]{0:T(256)S(1)} %convert_add_fusion), kind=kOutput, calls=%fused_computation.35 | convolution fusion | flops 4301520896 | bytes 21496832 | tf_op jit(solution)/shard_map/dot_general | solution.py:267
  113.3 9.3 %shard_map.110 = (bf16[256,1024]{1,0:T(8,128)(2,1)}, bf16[4096,256]{1,0:T(8,128)(2,1)}) custom-call(s32[2]{0:T(128)} %pad_add_fusion.scalar_ref, bf16[256,1024]{1,0:T(8,128)(2,1)} %q_ref.1, bf16[256,1024]{1,0:T(8,128)(2,1)} %copy-done.3, bf16[4096,128]{1,0:T(8,128)(2,1)S(1)} %get-tuple-element.374, bf16[4096,128]{1,0:T(8,128)(2,1)} %get-tuple-element.375, ...), custom_call_target="tpu_custom_call" | custom-call | tf_op jit(solution)/shard_map/pallas_call | solution.py:107
  122.6 34.7 %all-to-all-start = ((bf16[16,256,256]{2,1,0:T(8,128)(2,1)}), bf16[16,256,256]{2,1,0:T(8,128)(2,1)S(1)}, u32[]{:S(2)}, u32[]{:S(2)}) async-start(bf16[16,256,256]{2,1,0:T(8,128)(2,1)} %bitcast.129), calls=%async_computation | async-start | bytes 4194304 | tf_op jit(solution)/shard_map/all_to_all | solution.py:163
  157.9 5.1 %fusion.26 = f32[256,256]{1,0:T(8,128)S(1)} fusion(bf16[256,8192]{1,0:T(8,128)(2,1)} %all-gather.2.cloned.1.call-done, f32[256]{0:T(256)S(1)} %convert_add_fusion), kind=kOutput, calls=%fused_computation.33 | convolution fusion | flops 1080033280 | bytes 4457472 | tf_op jit(solution)/shard_map/dot_general | solution.py:187
  164.2 21.2 %all-to-all-done = bf16[16,256,256]{2,1,0:T(8,128)(2,1)S(1)} async-done(((bf16[16,256,256]{2,1,0:T(8,128)(2,1)}), bf16[16,256,256]{2,1,0:T(8,128)(2,1)S(1)}, u32[]{:S(2)}, u32[]{:S(2)}) %all-to-all-start) | async-done | bytes 2097184 | tf_op jit(solution)/shard_map/all_to_all | solution.py:163
  (107 shorter events, 21.7 us)
Async XLA Ops:
  7.2 15.7 %copy-start = (bf16[256,1024]{1,0:T(8,128)(2,1)S(1)}, bf16[256,1024]{1,0:T(8,128)(2,1)}, u32[]{:S(2)}) copy-start(bf16[256,1024]{1,0:T(8,128)(2,1)} %param.11) | copy-start | bytes 1572868
  7.2 93.4 %all-gather.2.cloned.1.call-start = ((), (), s32[]{:S(2)}) async-start(), calls=%async_computation.1 | async-start | bytes 4718592 | tf_op jit(solution)/shard_map/all_gather | solution.py:210
  9.0 17.5 %collective-permute-start.3 = (bf16[256,256]{1,0:T(8,128)(2,1)S(1)}, bf16[256,256]{1,0:T(8,128)(2,1)S(1)}, u32[]{:S(2)}, u32[]{:S(2)}) collective-permute-start(bf16[256,256]{1,0:T(8,128)(2,1)S(1)} %constant_dynamic-update-slice_fusion), channel_id=1, source_target_pairs={{0,120},{1,121},{2,122},{3,123},{4,124},{5,125},{6,126},{7,127}} | collective-permute-start | bytes 393224 | tf_op jit(solution)/shard_map/ppermute | solution.py:144
  9.7 18.1 %collective-permute-start.4 = (bf16[256,256]{1,0:T(8,128)(2,1)S(1)}, bf16[256,256]{1,0:T(8,128)(2,1)S(1)}, u32[]{:S(2)}, u32[]{:S(2)}) collective-permute-start(bf16[256,256]{1,0:T(8,128)(2,1)S(1)} %constant_dynamic-update-slice_fusion), channel_id=1, source_target_pairs={{0,112},{8,120},{1,113},{9,121},{2,114},{10,122},{3,115},{11,123},... | collective-permute-start | bytes 393224 | tf_op jit(solution)/shard_map/ppermute | solution.py:144
  17.8 11.3 %collective-permute-start.5 = (bf16[256,256]{1,0:T(8,128)(2,1)S(1)}, bf16[256,256]{1,0:T(8,128)(2,1)S(1)}, u32[]{:S(2)}, u32[]{:S(2)}) collective-permute-start(bf16[256,256]{1,0:T(8,128)(2,1)S(1)} %constant_dynamic-update-slice_fusion), channel_id=1, source_target_pairs={{0,104},{8,112},{16,120},{1,105},{9,113},{17,121},{2,106},{10,114}... | collective-permute-start | bytes 393224 | tf_op jit(solution)/shard_map/ppermute | solution.py:144
  19.1 11.3 %collective-permute-start.6 = (bf16[256,256]{1,0:T(8,128)(2,1)S(1)}, bf16[256,256]{1,0:T(8,128)(2,1)S(1)}, u32[]{:S(2)}, u32[]{:S(2)}) collective-permute-start(bf16[256,256]{1,0:T(8,128)(2,1)S(1)} %constant_dynamic-update-slice_fusion), channel_id=1, source_target_pairs={{0,96},{8,104},{16,112},{24,120},{1,97},{9,105},{17,113},{25,121},... | collective-permute-start | bytes 393224 | tf_op jit(solution)/shard_map/ppermute | solution.py:144
  20.4 11.4 %collective-permute-start.7 = (bf16[256,256]{1,0:T(8,128)(2,1)S(1)}, bf16[256,256]{1,0:T(8,128)(2,1)S(1)}, u32[]{:S(2)}, u32[]{:S(2)}) collective-permute-start(bf16[256,256]{1,0:T(8,128)(2,1)S(1)} %constant_dynamic-update-slice_fusion), channel_id=1, source_target_pairs={{0,88},{8,96},{16,104},{24,112},{32,120},{1,89},{9,97},{17,105},{2... | collective-permute-start | bytes 393224 | tf_op jit(solution)/shard_map/ppermute | solution.py:144
  26.5 10.4 %collective-permute-start.8 = (bf16[256,256]{1,0:T(8,128)(2,1)S(1)}, bf16[256,256]{1,0:T(8,128)(2,1)S(1)}, u32[]{:S(2)}, u32[]{:S(2)}) collective-permute-start(bf16[256,256]{1,0:T(8,128)(2,1)S(1)} %constant_dynamic-update-slice_fusion), channel_id=1, source_target_pairs={{0,80},{8,88},{16,96},{24,104},{32,112},{40,120},{1,81},{9,89},{17... | collective-permute-start | bytes 393224 | tf_op jit(solution)/shard_map/ppermute | solution.py:144
  27.8 14.3 %collective-permute-start.9 = (bf16[256,256]{1,0:T(8,128)(2,1)S(1)}, bf16[256,256]{1,0:T(8,128)(2,1)S(1)}, u32[]{:S(2)}, u32[]{:S(2)}) collective-permute-start(bf16[256,256]{1,0:T(8,128)(2,1)S(1)} %constant_dynamic-update-slice_fusion), channel_id=1, source_target_pairs={{0,72},{8,80},{16,88},{24,96},{32,104},{40,112},{48,120},{1,73},{9... | collective-permute-start | bytes 393224 | tf_op jit(solution)/shard_map/ppermute | solution.py:144
  29.1 19.3 %collective-permute-start.10 = (bf16[256,256]{1,0:T(8,128)(2,1)S(1)}, bf16[256,256]{1,0:T(8,128)(2,1)S(1)}, u32[]{:S(2)}, u32[]{:S(2)}) collective-permute-start(bf16[256,256]{1,0:T(8,128)(2,1)S(1)} %constant_dynamic-update-slice_fusion), channel_id=1, source_target_pairs={{0,64},{8,72},{16,80},{24,88},{32,96},{40,104},{48,112},{56,120},{... | collective-permute-start | bytes 393224 | tf_op jit(solution)/shard_map/ppermute | solution.py:144
  30.5 19.3 %collective-permute-start.11 = (bf16[256,256]{1,0:T(8,128)(2,1)S(1)}, bf16[256,256]{1,0:T(8,128)(2,1)S(1)}, u32[]{:S(2)}, u32[]{:S(2)}) collective-permute-start(bf16[256,256]{1,0:T(8,128)(2,1)S(1)} %constant_dynamic-update-slice_fusion), channel_id=1, source_target_pairs={{0,56},{8,64},{16,72},{24,80},{32,88},{40,96},{48,104},{56,112},{6... | collective-permute-start | bytes 393224 | tf_op jit(solution)/shard_map/ppermute | solution.py:144
  31.8 22.8 %collective-permute-start.12 = (bf16[256,256]{1,0:T(8,128)(2,1)S(1)}, bf16[256,256]{1,0:T(8,128)(2,1)S(1)}, u32[]{:S(2)}, u32[]{:S(2)}) collective-permute-start(bf16[256,256]{1,0:T(8,128)(2,1)S(1)} %constant_dynamic-update-slice_fusion), channel_id=1, source_target_pairs={{0,48},{8,56},{16,64},{24,72},{32,80},{40,88},{48,96},{56,104},{64... | collective-permute-start | bytes 393224 | tf_op jit(solution)/shard_map/ppermute | solution.py:144
  36.9 20.2 %collective-permute-start.13 = (bf16[256,256]{1,0:T(8,128)(2,1)S(1)}, bf16[256,256]{1,0:T(8,128)(2,1)S(1)}, u32[]{:S(2)}, u32[]{:S(2)}) collective-permute-start(bf16[256,256]{1,0:T(8,128)(2,1)S(1)} %constant_dynamic-update-slice_fusion), channel_id=1, source_target_pairs={{0,40},{8,48},{16,56},{24,64},{32,72},{40,80},{48,88},{56,96},{64,... | collective-permute-start | bytes 393224 | tf_op jit(solution)/shard_map/ppermute | solution.py:144
  42.1 17.6 %collective-permute-start.14 = (bf16[256,256]{1,0:T(8,128)(2,1)S(1)}, bf16[256,256]{1,0:T(8,128)(2,1)S(1)}, u32[]{:S(2)}, u32[]{:S(2)}) collective-permute-start(bf16[256,256]{1,0:T(8,128)(2,1)S(1)} %constant_dynamic-update-slice_fusion), channel_id=1, source_target_pairs={{0,32},{8,40},{16,48},{24,56},{32,64},{40,72},{48,80},{56,88},{64,... | collective-permute-start | bytes 393224 | tf_op jit(solution)/shard_map/ppermute | solution.py:144
  48.4 11.4 %collective-permute-start.15 = (bf16[256,256]{1,0:T(8,128)(2,1)S(1)}, bf16[256,256]{1,0:T(8,128)(2,1)S(1)}, u32[]{:S(2)}, u32[]{:S(2)}) collective-permute-start(bf16[256,256]{1,0:T(8,128)(2,1)S(1)} %constant_dynamic-update-slice_fusion), channel_id=1, source_target_pairs={{0,24},{8,32},{16,40},{24,48},{32,56},{40,64},{48,72},{56,80},{64,... | collective-permute-start | bytes 393224 | tf_op jit(solution)/shard_map/ppermute | solution.py:144
  49.8 10.1 %collective-permute-start.16 = (bf16[256,256]{1,0:T(8,128)(2,1)S(1)}, bf16[256,256]{1,0:T(8,128)(2,1)S(1)}, u32[]{:S(2)}, u32[]{:S(2)}) collective-permute-start(bf16[256,256]{1,0:T(8,128)(2,1)S(1)} %constant_dynamic-update-slice_fusion), channel_id=1, source_target_pairs={{0,16},{8,24},{16,32},{24,40},{32,48},{40,56},{48,64},{56,72},{64,... | collective-permute-start | bytes 393224 | tf_op jit(solution)/shard_map/ppermute | solution.py:144
  54.6 5.3 %collective-permute-start.17 = (bf16[256,256]{1,0:T(8,128)(2,1)S(1)}, bf16[256,256]{1,0:T(8,128)(2,1)S(1)}, u32[]{:S(2)}, u32[]{:S(2)}) collective-permute-start(bf16[256,256]{1,0:T(8,128)(2,1)S(1)} %constant_dynamic-update-slice_fusion), channel_id=1, source_target_pairs={{0,8},{8,16},{16,24},{24,32},{32,40},{40,48},{48,56},{56,64},{64,7... | collective-permute-start | bytes 393224 | tf_op jit(solution)/shard_map/ppermute | solution.py:144
  57.0 14.2 %collective-permute-start = (f32[256,256]{1,0:T(8,128)S(1)}, f32[256,256]{1,0:T(8,128)S(1)}, u32[]{:S(2)}, u32[]{:S(2)}) collective-permute-start(f32[256,256]{1,0:T(8,128)S(1)} %fusion.38), channel_id=1, source_target_pairs={{0,1},{1,0},{2,3},{3,2},{4,5},{5,4},{6,7},{7,6},{8,9},{9,8},{10,11... | collective-permute-start | bytes 786440 | tf_op jit(solution)/shard_map/ppermute | solution.py:172
  71.3 9.1 %collective-permute-start.1 = (f32[256,256]{1,0:T(8,128)S(1)}, f32[256,256]{1,0:T(8,128)S(1)}, u32[]{:S(2)}, u32[]{:S(2)}) collective-permute-start(f32[256,256]{1,0:T(8,128)S(1)} %add.100), channel_id=1, source_target_pairs={{0,2},{1,3},{2,0},{3,1},{4,6},{5,7},{6,4},{7,5},{8,10},{9,11},{10,... | collective-permute-start | bytes 786440 | tf_op jit(solution)/shard_map/ppermute | solution.py:172
  80.4 8.8 %collective-permute-start.2 = (f32[256,256]{1,0:T(8,128)S(1)}, f32[256,256]{1,0:T(8,128)S(1)}, u32[]{:S(2)}, u32[]{:S(2)}) collective-permute-start(f32[256,256]{1,0:T(8,128)S(1)} %add.101), channel_id=1, source_target_pairs={{0,4},{1,5},{2,6},{3,7},{4,0},{5,1},{6,2},{7,3},{8,12},{9,13},{10,... | collective-permute-start | bytes 786440 | tf_op jit(solution)/shard_map/ppermute | solution.py:172
  86.2 25.9 %copy-start.1 = (f32[256,8,128]{2,0,1:T(8,128)}, f32[256,8,128]{2,0,1:T(8,128)S(1)}, u32[]{:S(2)}) copy-start(f32[256,8,128]{2,0,1:T(8,128)S(1)} %get-tuple-element.94) | copy-start | bytes 3145732
  112.6 44.8 %copy-start.5 = (f32[256,256]{1,0:T(8,128)S(1)}, f32[256,256]{1,0:T(8,128)}, u32[]{:S(2)}) copy-start(f32[256,256]{1,0:T(8,128)} %add.102) | copy-start | bytes 786436
  122.6 34.7 %copy-start.6 = (bf16[256,1024]{1,0:T(8,128)(2,1)S(1)}, bf16[256,1024]{1,0:T(8,128)(2,1)}, u32[]{:S(2)}) copy-start(bf16[256,1024]{1,0:T(8,128)(2,1)} %get-tuple-element.86) | copy-start | bytes 1572868
  122.6 62.7 %all-to-all-start = ((bf16[16,256,256]{2,1,0:T(8,128)(2,1)}), bf16[16,256,256]{2,1,0:T(8,128)(2,1)S(1)}, u32[]{:S(2)}, u32[]{:S(2)}) async-start(bf16[16,256,256]{2,1,0:T(8,128)(2,1)} %bitcast.129), calls=%async_computation | async-start | bytes 4194304 | tf_op jit(solution)/shard_map/all_to_all | solution.py:163
  (3 other events, 14.8 us)
Sparse Core Ops, SparseCore 0:
  21.9 78.6 all-gather.1

commit v12 on v9

--- a/solution.py
+++ b/solution.py
@@ -164,6 +164,14 @@
     return jnp.sum(arrived.astype(jnp.float32), axis=0)
 
 
+def staged_gather(value, axis_name):
+    size = lax.axis_size(axis_name)
+    pairs = [[2 * i, 2 * i + 1] for i in range(size // 2)]
+    across = [list(range(0, size, 2)), list(range(1, size, 2))]
+    value = lax.all_gather(value, axis_name, axis=1, tiled=True, axis_index_groups=pairs)
+    return lax.all_gather(value, axis_name, axis=1, tiled=True, axis_index_groups=across)
+
+
 def butterfly_sum(value, axis_name):
     size = lax.axis_size(axis_name)
     stride = 1
@@ -207,7 +215,7 @@
         "head",
     )
     piece_part = (
-        lax.all_gather(grad_out, "head", axis=1, tiled=True).astype(jnp.float32)
+        staged_gather(grad_out, "head").astype(jnp.float32)
         * loss_weight[:, None]
     ).astype(jnp.bfloat16)
     pair_all = causal_gather(jnp.concatenate([key_rows, value_rows], axis=1), "ctx")

time: 190 us -> 208 us (1.095)
  waiting for transfers between devices: 47.6 us -> 66.9 us
    all_gather x1 -> x2, waiting for transfers between devices: 33.1 us -> 47 us  [the longest x1 47 us: staged_gather(): lax.all_gather(value, axis_name, axis=1, tiled=True, axis_index_groups=ac...]
    ppermute x15, waiting for transfers between devices: 0.28 us -> 4.07 us  [causal_gather(): received.append(lax.ppermute(value, axis_name, pairs))]
  transfers between devices with their start and end apart: 20 -> 21, of which waited for: 5 -> 7; matrix products, arithmetic and copies ran while one was open for 18% -> 16% of each run, Pallas kernels for 5% -> 4%
where the time goes in v12:
time: 208 us; the launch traced here: 207 us
  starting transfers between devices  79.2 us (38%)
  waiting for transfers between devices  66.9 us (32%)
  matrix products  22.9 us (11%)
  between operations  14.7 us (7%)
  Pallas kernels  9.32 us (4%)
  local copies, waits for them, and re-layouts  8.85 us (4%)
  other arithmetic  5.24 us (3%)
    all_gather x1, waiting for transfers between devices, staged_gather(): lax.all_gather(value, axis_name, axis=1, tiled=True, axis_index_groups=ac...  47 us
    ppermute x15, starting transfers between devices, causal_gather(): received.append(lax.ppermute(value, axis_name, pairs))  42 us
    all_to_all x1, starting transfers between devices, exchange_reduce(): arrived = lax.all_to_all(parts, axis_name, 0, 0, tiled=True)  31.8 us
    ppermute x3, waiting for transfers between devices, butterfly_sum(): value = value + lax.ppermute(value, axis_name, pairs)  13.9 us
    dot_general x1, matrix products, body(): lax.dot_general(piece_part, out_weight, (((1,), (1,)), ((), ())), preferr...  11.6 us
    pallas_call x1, Pallas kernels, flash_backward(): pl.pallas_call(kernel, grid_spec=grid_spec, out_shape=[jax.ShapeDtypeStru...  9.32 us
    ppermute x3, starting transfers between devices, butterfly_sum(): value = value + lax.ppermute(value, axis_name, pairs)  5.29 us
    dot_general x1, matrix products, gram_squares(): lax.dot_general(left_side, left_side, (((1,), (1,)), ((), ())), preferred...  5.15 us
  transfers between devices with their start and end apart: 21, of which 7 were waited for; matrix products, arithmetic and copies ran while one was open for 16% of the time, Pallas kernels for 4%

profile of v12, /device:TPU:1, one launch (start us, length us, event | category | flops | bytes accessed | tf_op | source)
XLA Modules:
  0.0 207.4 jit_solution(5144904205731331275)
XLA Ops:
  9.7 8.1 %collective-permute-start.1 = (bf16[256,256]{1,0:T(8,128)(2,1)S(1)}, bf16[256,256]{1,0:T(8,128)(2,1)S(1)}, u32[]{:S(2)}, u32[]{:S(2)}) collective-permute-start(bf16[256,256]{1,0:T(8,128)(2,1)S(1)} %constant_dynamic-update-slice_fusion), channel_id=1, source_target_pairs={{0,112},{8,120},{1,113},{9,121},{2,114},{10,122},{3,115},{11,123},... | collective-permute-start | bytes 393224 | tf_op jit(solution)/shard_map/ppermute | solution.py:144
  17.8 1.3 collective-permute-start.2
  19.1 1.3 collective-permute-start.3
  24.0 1.9 copy.31
  31.8 5.0 %collective-permute-start.9 = (bf16[256,256]{1,0:T(8,128)(2,1)S(1)}, bf16[256,256]{1,0:T(8,128)(2,1)S(1)}, u32[]{:S(2)}, u32[]{:S(2)}) collective-permute-start(bf16[256,256]{1,0:T(8,128)(2,1)S(1)} %constant_dynamic-update-slice_fusion), channel_id=1, source_target_pairs={{0,48},{8,56},{16,64},{24,72},{32,80},{40,88},{48,96},{56,104},{64... | collective-permute-start | bytes 393224 | tf_op jit(solution)/shard_map/ppermute | solution.py:144
  37.1 4.7 %collective-permute-start.10 = (bf16[256,256]{1,0:T(8,128)(2,1)S(1)}, bf16[256,256]{1,0:T(8,128)(2,1)S(1)}, u32[]{:S(2)}, u32[]{:S(2)}) collective-permute-start(bf16[256,256]{1,0:T(8,128)(2,1)S(1)} %constant_dynamic-update-slice_fusion), channel_id=1, source_target_pairs={{0,40},{8,48},{16,56},{24,64},{32,72},{40,80},{48,88},{56,96},{64,... | collective-permute-start | bytes 393224 | tf_op jit(solution)/shard_map/ppermute | solution.py:144
  42.7 6.3 %collective-permute-start.11 = (bf16[256,256]{1,0:T(8,128)(2,1)S(1)}, bf16[256,256]{1,0:T(8,128)(2,1)S(1)}, u32[]{:S(2)}, u32[]{:S(2)}) collective-permute-start(bf16[256,256]{1,0:T(8,128)(2,1)S(1)} %constant_dynamic-update-slice_fusion), channel_id=1, source_target_pairs={{0,32},{8,40},{16,48},{24,56},{32,64},{40,72},{48,80},{56,88},{64,... | collective-permute-start | bytes 393224 | tf_op jit(solution)/shard_map/ppermute | solution.py:144
  50.4 2.9 %collective-permute-done.8 = bf16[256,256]{1,0:T(8,128)(2,1)S(1)} collective-permute-done((bf16[256,256]{1,0:T(8,128)(2,1)S(1)}, bf16[256,256]{1,0:T(8,128)(2,1)S(1)}, u32[]{:S(2)}, u32[]{:S(2)}) %collective-permute-start.8) | collective-permute-done | bytes 131104 | tf_op jit(solution)/shard_map/ppermute | solution.py:144
  53.3 1.9 collective-permute-start.13
  55.2 5.0 %collective-permute-start.14 = (bf16[256,256]{1,0:T(8,128)(2,1)S(1)}, bf16[256,256]{1,0:T(8,128)(2,1)S(1)}, u32[]{:S(2)}, u32[]{:S(2)}) collective-permute-start(bf16[256,256]{1,0:T(8,128)(2,1)S(1)} %constant_dynamic-update-slice_fusion), channel_id=1, source_target_pairs={{0,8},{8,16},{16,24},{24,32},{32,40},{40,48},{48,56},{56,64},{64,7... | collective-permute-start | bytes 393224 | tf_op jit(solution)/shard_map/ppermute | solution.py:144
  60.2 2.7 %collective-permute-start.15 = (f32[256,256]{1,0:T(8,128)S(1)}, f32[256,256]{1,0:T(8,128)}, u32[]{:S(2)}, u32[]{:S(2)}) collective-permute-start(f32[256,256]{1,0:T(8,128)S(1)} %fusion.38), channel_id=1, source_target_pairs={{0,1},{1,0},{2,3},{3,2},{4,5},{5,4},{6,7},{7,6},{8,9},{9,8},{10,11... | collective-permute-start | bytes 786440 | tf_op jit(solution)/shard_map/ppermute | solution.py:180
  64.8 1.9 while.24
  67.7 3.1 %while.25 = (s32[]{:T(128)}, f32[256,8,128]{2,0,1:T(8,128)S(1)}, s32[]{:T(128)}, bf16[4096,128]{1,0:T(8,128)(2,1)S(1)}, bf16[256,8,128]{2,1,0:T(8,128)(2,1)}, /*...) while((s32[]{:T(128)}, f32[256,8,128]{2,0,1:T(8,128)S(1)}, ...), condition=%wide.region_5.6_spmd.clone, body=%wide.region_4.5_spmd.clone.sunk | while | flops 541459200 | bytes 3161259 | solution.py:266
  67.8 2.8 %fusion.56 = f32[256,8,128]{2,0,1:T(8,128)S(1)} fusion(f32[256,8,128]{2,0,1:T(8,128)S(1)} %get-tuple-element.342, f32[256,8]{0,1:T(8,128)S(1)} %get-tuple-element.358, pred[256,512]{1,0:T(8,128)(4,1)S(1)} %broadcast_compare_fusion.5, bf16[256,8,128]{2,1,0:T(8,128)(2,1)} %get-tuple-element.357, bf16[4096,128]{1,0:T(8,128)(2,1)} %get-tuple-element.359, ...), kind=kOutput, calls=%fused_computation.18.clone.1 | convolution fusion | flops 541327360 | bytes 3023872 | tf_op jit(solution)/shard_map/while/body/tgk,kd->tgd/dot_general | solution.py:262
  70.8 47.0 %all-gather.5.cloned.1.call-done = bf16[256,8192]{1,0:T(8,128)(2,1)} async-done(((bf16[256,2048]{1,0:T(8,128)(2,1)}), bf16[256,8192]{1,0:T(8,128)(2,1)}) %all-gather.5.cloned.1.call-update) | async-done | bytes 4194320 | tf_op jit(solution)/shard_map/all_gather | solution.py:172
  117.8 11.6 %fusion.28.do_ref = bf16[256,1024]{1,0:T(8,128)(2,1)S(1)} fusion(bf16[1024,8192]{1,0:T(8,128)(2,1)} %param.15, bf16[256,8192]{1,0:T(8,128)(2,1)} %all-gather.5.cloned.1.call-done, f32[256]{0:T(256)S(1)} %convert_add_fusion), kind=kOutput, calls=%fused_computation.35 | convolution fusion | flops 4301520896 | bytes 21496832 | tf_op jit(solution)/shard_map/dot_general | solution.py:275
  130.5 9.3 %shard_map.110 = (bf16[256,1024]{1,0:T(8,128)(2,1)}, bf16[4096,256]{1,0:T(8,128)(2,1)}) custom-call(s32[2]{0:T(128)} %pad_add_fusion.scalar_ref, bf16[256,1024]{1,0:T(8,128)(2,1)} %q_ref.1, bf16[256,1024]{1,0:T(8,128)(2,1)} %copy-done.3, bf16[4096,128]{1,0:T(8,128)(2,1)S(1)} %get-tuple-element.369, bf16[4096,128]{1,0:T(8,128)(2,1)} %get-tuple-element.370, ...), custom_call_target="tpu_custom_call" | custom-call | tf_op jit(solution)/shard_map/pallas_call | solution.py:107
  139.8 31.8 %all-to-all-start = ((bf16[16,256,256]{2,1,0:T(8,128)(2,1)}), bf16[16,256,256]{2,1,0:T(8,128)(2,1)S(1)}, u32[]{:S(2)}, u32[]{:S(2)}) async-start(bf16[16,256,256]{2,1,0:T(8,128)(2,1)} %bitcast.129), calls=%async_computation | async-start | bytes 4194304 | tf_op jit(solution)/shard_map/all_to_all | solution.py:163
  173.3 7.3 %collective-permute-done.16 = f32[256,256]{1,0:T(8,128)S(1)} collective-permute-done((f32[256,256]{1,0:T(8,128)S(1)}, f32[256,256]{1,0:T(8,128)S(1)}, u32[]{:S(2)}, u32[]{:S(2)}) %collective-permute-start.16) | collective-permute-done | bytes 262176 | tf_op jit(solution)/shard_map/ppermute | solution.py:180
  180.6 1.9 collective-permute-start.17
  182.5 6.7 %collective-permute-done.17 = f32[256,256]{1,0:T(8,128)S(1)} collective-permute-done((f32[256,256]{1,0:T(8,128)S(1)}, f32[256,256]{1,0:T(8,128)S(1)}, u32[]{:S(2)}, u32[]{:S(2)}) %collective-permute-start.17) | collective-permute-done | bytes 262176 | tf_op jit(solution)/shard_map/ppermute | solution.py:180
  189.2 1.7 multiply_reduce_fusion.1
  190.9 5.1 %fusion.26 = f32[256,256]{1,0:T(8,128)S(1)} fusion(bf16[256,8192]{1,0:T(8,128)(2,1)} %all-gather.5.cloned.1.call-done, f32[256]{0:T(256)S(1)} %convert_add_fusion), kind=kOutput, calls=%fused_computation.33 | convolution fusion | flops 1080033280 | bytes 4457472 | tf_op jit(solution)/shard_map/dot_general | solution.py:195
  197.7 1.9 all-to-all-done
  (107 shorter events, 24.2 us)
Async XLA Ops:
  7.2 15.8 %copy-start = (bf16[256,1024]{1,0:T(8,128)(2,1)S(1)}, bf16[256,1024]{1,0:T(8,128)(2,1)}, u32[]{:S(2)}) copy-start(bf16[256,1024]{1,0:T(8,128)(2,1)} %param.11) | copy-start | bytes 1572868
  7.2 57.6 %all-gather.3.cloned.1.call-start = ((), (), s32[]{:S(2)}) async-start(), calls=%async_computation.1 | async-start | bytes 1572864 | tf_op jit(solution)/shard_map/all_gather | solution.py:171
  9.0 17.5 %collective-permute-start = (bf16[256,256]{1,0:T(8,128)(2,1)S(1)}, bf16[256,256]{1,0:T(8,128)(2,1)S(1)}, u32[]{:S(2)}, u32[]{:S(2)}) collective-permute-start(bf16[256,256]{1,0:T(8,128)(2,1)S(1)} %constant_dynamic-update-slice_fusion), channel_id=1, source_target_pairs={{0,120},{1,121},{2,122},{3,123},{4,124},{5,125},{6,126},{7,127}} | collective-permute-start | bytes 393224 | tf_op jit(solution)/shard_map/ppermute | solution.py:144
  9.7 18.1 %collective-permute-start.1 = (bf16[256,256]{1,0:T(8,128)(2,1)S(1)}, bf16[256,256]{1,0:T(8,128)(2,1)S(1)}, u32[]{:S(2)}, u32[]{:S(2)}) collective-permute-start(bf16[256,256]{1,0:T(8,128)(2,1)S(1)} %constant_dynamic-update-slice_fusion), channel_id=1, source_target_pairs={{0,112},{8,120},{1,113},{9,121},{2,114},{10,122},{3,115},{11,123},... | collective-permute-start | bytes 393224 | tf_op jit(solution)/shard_map/ppermute | solution.py:144
  17.8 11.3 %collective-permute-start.2 = (bf16[256,256]{1,0:T(8,128)(2,1)S(1)}, bf16[256,256]{1,0:T(8,128)(2,1)S(1)}, u32[]{:S(2)}, u32[]{:S(2)}) collective-permute-start(bf16[256,256]{1,0:T(8,128)(2,1)S(1)} %constant_dynamic-update-slice_fusion), channel_id=1, source_target_pairs={{0,104},{8,112},{16,120},{1,105},{9,113},{17,121},{2,106},{10,114}... | collective-permute-start | bytes 393224 | tf_op jit(solution)/shard_map/ppermute | solution.py:144
  19.1 11.4 %collective-permute-start.3 = (bf16[256,256]{1,0:T(8,128)(2,1)S(1)}, bf16[256,256]{1,0:T(8,128)(2,1)S(1)}, u32[]{:S(2)}, u32[]{:S(2)}) collective-permute-start(bf16[256,256]{1,0:T(8,128)(2,1)S(1)} %constant_dynamic-update-slice_fusion), channel_id=1, source_target_pairs={{0,96},{8,104},{16,112},{24,120},{1,97},{9,105},{17,113},{25,121},... | collective-permute-start | bytes 393224 | tf_op jit(solution)/shard_map/ppermute | solution.py:144
  20.4 11.4 %collective-permute-start.4 = (bf16[256,256]{1,0:T(8,128)(2,1)S(1)}, bf16[256,256]{1,0:T(8,128)(2,1)S(1)}, u32[]{:S(2)}, u32[]{:S(2)}) collective-permute-start(bf16[256,256]{1,0:T(8,128)(2,1)S(1)} %constant_dynamic-update-slice_fusion), channel_id=1, source_target_pairs={{0,88},{8,96},{16,104},{24,112},{32,120},{1,89},{9,97},{17,105},{2... | collective-permute-start | bytes 393224 | tf_op jit(solution)/shard_map/ppermute | solution.py:144
  21.8 96.0 %all-gather.5.cloned.1.call-start = ((), (), s32[]{:S(2)}) async-start(), calls=%async_computation.2 | async-start | bytes 5242880 | tf_op jit(solution)/shard_map/all_gather | solution.py:172
  26.5 10.6 %collective-permute-start.5 = (bf16[256,256]{1,0:T(8,128)(2,1)S(1)}, bf16[256,256]{1,0:T(8,128)(2,1)S(1)}, u32[]{:S(2)}, u32[]{:S(2)}) collective-permute-start(bf16[256,256]{1,0:T(8,128)(2,1)S(1)} %constant_dynamic-update-slice_fusion), channel_id=1, source_target_pairs={{0,80},{8,88},{16,96},{24,104},{32,112},{40,120},{1,81},{9,89},{17... | collective-permute-start | bytes 393224 | tf_op jit(solution)/shard_map/ppermute | solution.py:144
  27.8 14.9 %collective-permute-start.6 = (bf16[256,256]{1,0:T(8,128)(2,1)S(1)}, bf16[256,256]{1,0:T(8,128)(2,1)S(1)}, u32[]{:S(2)}, u32[]{:S(2)}) collective-permute-start(bf16[256,256]{1,0:T(8,128)(2,1)S(1)} %constant_dynamic-update-slice_fusion), channel_id=1, source_target_pairs={{0,72},{8,80},{16,88},{24,96},{32,104},{40,112},{48,120},{1,73},{9... | collective-permute-start | bytes 393224 | tf_op jit(solution)/shard_map/ppermute | solution.py:144
  29.2 19.9 %collective-permute-start.7 = (bf16[256,256]{1,0:T(8,128)(2,1)S(1)}, bf16[256,256]{1,0:T(8,128)(2,1)S(1)}, u32[]{:S(2)}, u32[]{:S(2)}) collective-permute-start(bf16[256,256]{1,0:T(8,128)(2,1)S(1)} %constant_dynamic-update-slice_fusion), channel_id=1, source_target_pairs={{0,64},{8,72},{16,80},{24,88},{32,96},{40,104},{48,112},{56,120},{... | collective-permute-start | bytes 393224 | tf_op jit(solution)/shard_map/ppermute | solution.py:144
  30.5 22.8 %collective-permute-start.8 = (bf16[256,256]{1,0:T(8,128)(2,1)S(1)}, bf16[256,256]{1,0:T(8,128)(2,1)S(1)}, u32[]{:S(2)}, u32[]{:S(2)}) collective-permute-start(bf16[256,256]{1,0:T(8,128)(2,1)S(1)} %constant_dynamic-update-slice_fusion), channel_id=1, source_target_pairs={{0,56},{8,64},{16,72},{24,80},{32,88},{40,96},{48,104},{56,112},{6... | collective-permute-start | bytes 393224 | tf_op jit(solution)/shard_map/ppermute | solution.py:144
  31.8 23.4 %collective-permute-start.9 = (bf16[256,256]{1,0:T(8,128)(2,1)S(1)}, bf16[256,256]{1,0:T(8,128)(2,1)S(1)}, u32[]{:S(2)}, u32[]{:S(2)}) collective-permute-start(bf16[256,256]{1,0:T(8,128)(2,1)S(1)} %constant_dynamic-update-slice_fusion), channel_id=1, source_target_pairs={{0,48},{8,56},{16,64},{24,72},{32,80},{40,88},{48,96},{56,104},{64... | collective-permute-start | bytes 393224 | tf_op jit(solution)/shard_map/ppermute | solution.py:144
  37.1 23.1 %collective-permute-start.10 = (bf16[256,256]{1,0:T(8,128)(2,1)S(1)}, bf16[256,256]{1,0:T(8,128)(2,1)S(1)}, u32[]{:S(2)}, u32[]{:S(2)}) collective-permute-start(bf16[256,256]{1,0:T(8,128)(2,1)S(1)} %constant_dynamic-update-slice_fusion), channel_id=1, source_target_pairs={{0,40},{8,48},{16,56},{24,64},{32,72},{40,80},{48,88},{56,96},{64,... | collective-permute-start | bytes 393224 | tf_op jit(solution)/shard_map/ppermute | solution.py:144
  42.7 20.2 %collective-permute-start.11 = (bf16[256,256]{1,0:T(8,128)(2,1)S(1)}, bf16[256,256]{1,0:T(8,128)(2,1)S(1)}, u32[]{:S(2)}, u32[]{:S(2)}) collective-permute-start(bf16[256,256]{1,0:T(8,128)(2,1)S(1)} %constant_dynamic-update-slice_fusion), channel_id=1, source_target_pairs={{0,32},{8,40},{16,48},{24,56},{32,64},{40,72},{48,80},{56,88},{64,... | collective-permute-start | bytes 393224 | tf_op jit(solution)/shard_map/ppermute | solution.py:144
  49.0 14.0 %collective-permute-start.12 = (bf16[256,256]{1,0:T(8,128)(2,1)S(1)}, bf16[256,256]{1,0:T(8,128)(2,1)S(1)}, u32[]{:S(2)}, u32[]{:S(2)}) collective-permute-start(bf16[256,256]{1,0:T(8,128)(2,1)S(1)} %constant_dynamic-update-slice_fusion), channel_id=1, source_target_pairs={{0,24},{8,32},{16,40},{24,48},{32,56},{40,64},{48,72},{56,80},{64,... | collective-permute-start | bytes 393224 | tf_op jit(solution)/shard_map/ppermute | solution.py:144
  53.3 9.8 %collective-permute-start.13 = (bf16[256,256]{1,0:T(8,128)(2,1)S(1)}, bf16[256,256]{1,0:T(8,128)(2,1)S(1)}, u32[]{:S(2)}, u32[]{:S(2)}) collective-permute-start(bf16[256,256]{1,0:T(8,128)(2,1)S(1)} %constant_dynamic-update-slice_fusion), channel_id=1, source_target_pairs={{0,16},{8,24},{16,32},{24,40},{32,48},{40,56},{48,64},{56,72},{64,... | collective-permute-start | bytes 393224 | tf_op jit(solution)/shard_map/ppermute | solution.py:144
  55.2 7.9 %collective-permute-start.14 = (bf16[256,256]{1,0:T(8,128)(2,1)S(1)}, bf16[256,256]{1,0:T(8,128)(2,1)S(1)}, u32[]{:S(2)}, u32[]{:S(2)}) collective-permute-start(bf16[256,256]{1,0:T(8,128)(2,1)S(1)} %constant_dynamic-update-slice_fusion), channel_id=1, source_target_pairs={{0,8},{8,16},{16,24},{24,32},{32,40},{40,48},{48,56},{56,64},{64,7... | collective-permute-start | bytes 393224 | tf_op jit(solution)/shard_map/ppermute | solution.py:144
  60.2 111.4 %collective-permute-start.15 = (f32[256,256]{1,0:T(8,128)S(1)}, f32[256,256]{1,0:T(8,128)}, u32[]{:S(2)}, u32[]{:S(2)}) collective-permute-start(f32[256,256]{1,0:T(8,128)S(1)} %fusion.38), channel_id=1, source_target_pairs={{0,1},{1,0},{2,3},{3,2},{4,5},{5,4},{6,7},{7,6},{8,9},{9,8},{10,11... | collective-permute-start | bytes 786440 | tf_op jit(solution)/shard_map/ppermute | solution.py:180
  70.8 58.6 %copy-start.1 = (f32[256,8,128]{2,0,1:T(8,128)}, f32[256,8,128]{2,0,1:T(8,128)S(1)}, u32[]{:S(2)}) copy-start(f32[256,8,128]{2,0,1:T(8,128)S(1)} %get-tuple-element.91) | copy-start | bytes 3145732
  139.8 59.8 %all-to-all-start = ((bf16[16,256,256]{2,1,0:T(8,128)(2,1)}), bf16[16,256,256]{2,1,0:T(8,128)(2,1)S(1)}, u32[]{:S(2)}, u32[]{:S(2)}) async-start(bf16[16,256,256]{2,1,0:T(8,128)(2,1)} %bitcast.129), calls=%async_computation | async-start | bytes 4194304 | tf_op jit(solution)/shard_map/all_to_all | solution.py:163
  172.6 7.9 %collective-permute-start.16 = (f32[256,256]{1,0:T(8,128)S(1)}, f32[256,256]{1,0:T(8,128)S(1)}, u32[]{:S(2)}, u32[]{:S(2)}) collective-permute-start(f32[256,256]{1,0:T(8,128)S(1)} %add.106), channel_id=1, source_target_pairs={{0,2},{1,3},{2,0},{3,1},{4,6},{5,7},{6,4},{7,5},{8,10},{9,11},{10,... | collective-permute-start | bytes 786440 | tf_op jit(solution)/shard_map/ppermute | solution.py:180
  180.6 8.5 %collective-permute-start.17 = (f32[256,256]{1,0:T(8,128)S(1)}, f32[256,256]{1,0:T(8,128)S(1)}, u32[]{:S(2)}, u32[]{:S(2)}) collective-permute-start(f32[256,256]{1,0:T(8,128)S(1)} %add.107), channel_id=1, source_target_pairs={{0,4},{1,5},{2,6},{3,7},{4,0},{5,1},{6,2},{7,3},{8,12},{9,13},{10,... | collective-permute-start | bytes 786440 | tf_op jit(solution)/shard_map/ppermute | solution.py:180
  190.9 5.2 %copy-start.2 = (f32[256,8,128]{2,0,1:T(8,128)S(1)}, f32[256,8,128]{2,0,1:T(8,128)}, u32[]{:S(2)}) copy-start(f32[256,8,128]{2,0,1:T(8,128)} %copy-done.1) | copy-start | bytes 3145732
  (2 other events, 1.8 us)
Sparse Core Ops, SparseCore 0:
  21.9 35.0 all-gather.2
  64.9 52.8 all-gather.4

commit v13 on v9

--- a/solution.py
+++ b/solution.py
@@ -68,11 +68,11 @@
                 s = jnp.where(keep, s, NEGATIVE)
                 p = jnp.exp(s - lt_ref[:, h : h + 1])
                 dp = lax.dot_general(do, v, (((1,), (1,)), ((), ())), preferred_element_type=jnp.float32)
-                ds = (p * (dp - rd_ref[:, h : h + 1]) * scaling).astype(jnp.bfloat16)
+                ds = (p * (dp - rd_ref[:, h : h + 1])).astype(jnp.bfloat16)
                 dq_acc[:, cols] += jnp.dot(ds, k, preferred_element_type=jnp.float32)
                 dk += lax.dot_general(ds, q, (((0,), (0,)), ((), ())), preferred_element_type=jnp.float32)
                 dv += lax.dot_general(p.astype(jnp.bfloat16), do, (((0,), (0,)), ((), ())), preferred_element_type=jnp.float32)
-            dkv_ref[:, :head_dim] = dk.astype(dkv_ref.dtype)
+            dkv_ref[:, :head_dim] = (dk * scaling).astype(dkv_ref.dtype)
             dkv_ref[:, head_dim:] = dv.astype(dkv_ref.dtype)
 
         @pl.when(j >= scalar_ref[0])
@@ -81,7 +81,7 @@
 
         @pl.when(j == blocks - 1)
         def _():
-            dq_ref[...] = dq_acc[...].astype(dq_ref.dtype)
+            dq_ref[...] = (dq_acc[...] * scaling).astype(dq_ref.dtype)
 
     def kv_map(j, s):
         return (jnp.minimum(j, s[0] - 1), 0)

time: 190 us -> 189 us (level)
  no operation moved by 1% of the time
where the time goes in v13:
time: 189 us; the launch traced here: 188 us
  starting transfers between devices  79.1 us (42%)
  waiting for transfers between devices  47.6 us (25%)
  matrix products  22.9 us (12%)
  between operations  14.7 us (8%)
  Pallas kernels  9.25 us (5%)
  local copies, waits for them, and re-layouts  8.88 us (5%)
  other arithmetic  5.24 us (3%)
    ppermute x15, starting transfers between devices, causal_gather(): received.append(lax.ppermute(value, axis_name, pairs))  42.7 us
    all_gather x1, waiting for transfers between devices, body(): lax.all_gather(grad_out, 'head', axis=1, tiled=True).astype(jnp.float32)  33.1 us
    all_to_all x1, starting transfers between devices, exchange_reduce(): arrived = lax.all_to_all(parts, axis_name, 0, 0, tiled=True)  29.5 us
    ppermute x3, waiting for transfers between devices, butterfly_sum(): value = value + lax.ppermute(value, axis_name, pairs)  12.3 us
    dot_general x1, matrix products, body(): lax.dot_general(piece_part, out_weight, (((1,), (1,)), ((), ())), preferr...  11.6 us
    pallas_call x1, Pallas kernels, flash_backward(): pl.pallas_call(kernel, grid_spec=grid_spec, out_shape=[jax.ShapeDtypeStru...  9.25 us
    ppermute x3, starting transfers between devices, butterfly_sum(): value = value + lax.ppermute(value, axis_name, pairs)  6.85 us
    dot_general x1, matrix products, gram_squares(): lax.dot_general(left_side, left_side, (((1,), (1,)), ((), ())), preferred...  5.15 us
  transfers between devices with their start and end apart: 20, of which 5 were waited for; matrix products, arithmetic and copies ran while one was open for 18% of the time, Pallas kernels for 5%

profile of v13, /device:TPU:1, one launch (start us, length us, event | category | flops | bytes accessed | tf_op | source)
XLA Modules:
  0.0 187.9 jit_solution(10204889850847652019)
XLA Ops:
  9.7 8.1 %collective-permute-start.1 = (bf16[256,256]{1,0:T(8,128)(2,1)S(1)}, bf16[256,256]{1,0:T(8,128)(2,1)S(1)}, u32[]{:S(2)}, u32[]{:S(2)}) collective-permute-start(bf16[256,256]{1,0:T(8,128)(2,1)S(1)} %constant_dynamic-update-slice_fusion), channel_id=1, source_target_pairs={{0,112},{8,120},{1,113},{9,121},{2,114},{10,122},{3,115},{11,123},... | collective-permute-start | bytes 393224 | tf_op jit(solution)/shard_map/ppermute | solution.py:144
  17.8 1.3 collective-permute-start.2
  23.9 1.9 %copy.31 = bf16[32,8,8,128]{3,2,1,0:T(8,128)(2,1)} copy(bf16[32,8,8,128]{3,1,2,0:T(8,128)(2,1)} %bitcast.128) | data formatting | bytes 1048576
  30.5 1.3 collective-permute-start.8
  31.8 5.0 %collective-permute-start.9 = (bf16[256,256]{1,0:T(8,128)(2,1)S(1)}, bf16[256,256]{1,0:T(8,128)(2,1)S(1)}, u32[]{:S(2)}, u32[]{:S(2)}) collective-permute-start(bf16[256,256]{1,0:T(8,128)(2,1)S(1)} %constant_dynamic-update-slice_fusion), channel_id=1, source_target_pairs={{0,48},{8,56},{16,64},{24,72},{32,80},{40,88},{48,96},{56,104},{64... | collective-permute-start | bytes 393224 | tf_op jit(solution)/shard_map/ppermute | solution.py:144
  36.9 5.0 %collective-permute-start.10 = (bf16[256,256]{1,0:T(8,128)(2,1)S(1)}, bf16[256,256]{1,0:T(8,128)(2,1)S(1)}, u32[]{:S(2)}, u32[]{:S(2)}) collective-permute-start(bf16[256,256]{1,0:T(8,128)(2,1)S(1)} %constant_dynamic-update-slice_fusion), channel_id=1, source_target_pairs={{0,40},{8,48},{16,56},{24,64},{32,72},{40,80},{48,88},{56,96},{64,... | collective-permute-start | bytes 393224 | tf_op jit(solution)/shard_map/ppermute | solution.py:144
  42.1 6.3 %collective-permute-start.11 = (bf16[256,256]{1,0:T(8,128)(2,1)S(1)}, bf16[256,256]{1,0:T(8,128)(2,1)S(1)}, u32[]{:S(2)}, u32[]{:S(2)}) collective-permute-start(bf16[256,256]{1,0:T(8,128)(2,1)S(1)} %constant_dynamic-update-slice_fusion), channel_id=1, source_target_pairs={{0,32},{8,40},{16,48},{24,56},{32,64},{40,72},{48,80},{56,88},{64,... | collective-permute-start | bytes 393224 | tf_op jit(solution)/shard_map/ppermute | solution.py:144
  49.8 4.8 %collective-permute-start.13 = (bf16[256,256]{1,0:T(8,128)(2,1)S(1)}, bf16[256,256]{1,0:T(8,128)(2,1)S(1)}, u32[]{:S(2)}, u32[]{:S(2)}) collective-permute-start(bf16[256,256]{1,0:T(8,128)(2,1)S(1)} %constant_dynamic-update-slice_fusion), channel_id=1, source_target_pairs={{0,16},{8,24},{16,32},{24,40},{32,48},{40,56},{48,64},{56,72},{64,... | collective-permute-start | bytes 393224 | tf_op jit(solution)/shard_map/ppermute | solution.py:144
  54.6 2.4 %collective-permute-start.14 = (bf16[256,256]{1,0:T(8,128)(2,1)S(1)}, bf16[256,256]{1,0:T(8,128)(2,1)S(1)}, u32[]{:S(2)}, u32[]{:S(2)}) collective-permute-start(bf16[256,256]{1,0:T(8,128)(2,1)S(1)} %constant_dynamic-update-slice_fusion), channel_id=1, source_target_pairs={{0,8},{8,16},{16,24},{24,32},{32,40},{40,48},{48,56},{56,64},{64,7... | collective-permute-start | bytes 393224 | tf_op jit(solution)/shard_map/ppermute | solution.py:144
  57.0 2.7 %collective-permute-start.15 = (f32[256,256]{1,0:T(8,128)S(1)}, f32[256,256]{1,0:T(8,128)}, u32[]{:S(2)}, u32[]{:S(2)}) collective-permute-start(f32[256,256]{1,0:T(8,128)S(1)} %fusion.38), channel_id=1, source_target_pairs={{0,1},{1,0},{2,3},{3,2},{4,5},{5,4},{6,7},{7,6},{8,9},{9,8},{10,11... | collective-permute-start | bytes 786440 | tf_op jit(solution)/shard_map/ppermute | solution.py:172
  61.5 1.9 while.24
  64.4 3.1 %while.25 = (s32[]{:T(128)}, f32[256,8,128]{2,0,1:T(8,128)S(1)}, s32[]{:T(128)}, bf16[4096,128]{1,0:T(8,128)(2,1)S(1)}, bf16[256,8,128]{2,1,0:T(8,128)(2,1)}, /*...) while((s32[]{:T(128)}, f32[256,8,128]{2,0,1:T(8,128)S(1)}, ...), condition=%wide.region_5.6_spmd.clone, body=%wide.region_4.5_spmd.clone.sunk | while | flops 541459200 | bytes 3161259 | solution.py:258
  64.5 2.8 %fusion.56 = f32[256,8,128]{2,0,1:T(8,128)S(1)} fusion(f32[256,8,128]{2,0,1:T(8,128)S(1)} %get-tuple-element.342, f32[256,8]{0,1:T(8,128)S(1)} %get-tuple-element.358, pred[256,512]{1,0:T(8,128)(4,1)S(1)} %broadcast_compare_fusion.5, bf16[256,8,128]{2,1,0:T(8,128)(2,1)} %get-tuple-element.357, bf16[4096,128]{1,0:T(8,128)(2,1)} %get-tuple-element.359, ...), kind=kOutput, calls=%fused_computation.18.clone.1 | convolution fusion | flops 541327360 | bytes 3023872 | tf_op jit(solution)/shard_map/while/body/tgk,kd->tgd/dot_general | solution.py:254
  67.5 33.1 %all-gather.2.cloned.1.call-done = bf16[256,8192]{1,0:T(8,128)(2,1)} async-done(((bf16[256,1024]{1,0:T(8,128)(2,1)}), bf16[256,8192]{1,0:T(8,128)(2,1)}) %all-gather.2.cloned.1.call-update) | async-done | bytes 4194320 | tf_op jit(solution)/shard_map/all_gather | solution.py:210
  100.6 11.6 %fusion.28.do_ref = bf16[256,1024]{1,0:T(8,128)(2,1)S(1)} fusion(bf16[1024,8192]{1,0:T(8,128)(2,1)} %param.15, bf16[256,8192]{1,0:T(8,128)(2,1)} %all-gather.2.cloned.1.call-done, f32[256]{0:T(256)S(1)} %convert_add_fusion), kind=kOutput, calls=%fused_computation.35 | convolution fusion | flops 4301520896 | bytes 21496832 | tf_op jit(solution)/shard_map/dot_general | solution.py:267
  113.4 9.2 %shard_map.110 = (bf16[256,1024]{1,0:T(8,128)(2,1)}, bf16[4096,256]{1,0:T(8,128)(2,1)}) custom-call(s32[2]{0:T(128)} %pad_add_fusion.scalar_ref, bf16[256,1024]{1,0:T(8,128)(2,1)} %q_ref.1, bf16[256,1024]{1,0:T(8,128)(2,1)} %copy-done.3, bf16[4096,128]{1,0:T(8,128)(2,1)S(1)} %get-tuple-element.368, bf16[4096,128]{1,0:T(8,128)(2,1)} %get-tuple-element.369, ...), custom_call_target="tpu_custom_call" | custom-call | tf_op jit(solution)/shard_map/pallas_call | solution.py:107
  122.6 29.5 %all-to-all-start = ((bf16[16,256,256]{2,1,0:T(8,128)(2,1)}), bf16[16,256,256]{2,1,0:T(8,128)(2,1)S(1)}, u32[]{:S(2)}, u32[]{:S(2)}) async-start(bf16[16,256,256]{2,1,0:T(8,128)(2,1)} %bitcast.129), calls=%async_computation | async-start | bytes 4194304 | tf_op jit(solution)/shard_map/all_to_all | solution.py:163
  153.1 1.3 collective-permute-start.16
  154.5 6.6 %collective-permute-done.16 = f32[256,256]{1,0:T(8,128)S(1)} collective-permute-done((f32[256,256]{1,0:T(8,128)S(1)}, f32[256,256]{1,0:T(8,128)S(1)}, u32[]{:S(2)}, u32[]{:S(2)}) %collective-permute-start.16) | collective-permute-done | bytes 262176 | tf_op jit(solution)/shard_map/ppermute | solution.py:172
  161.1 2.8 %collective-permute-start.17 = (f32[256,256]{1,0:T(8,128)S(1)}, f32[256,256]{1,0:T(8,128)S(1)}, u32[]{:S(2)}, u32[]{:S(2)}) collective-permute-start(f32[256,256]{1,0:T(8,128)S(1)} %add.107), channel_id=1, source_target_pairs={{0,4},{1,5},{2,6},{3,7},{4,0},{5,1},{6,2},{7,3},{8,12},{9,13},{10,... | collective-permute-start | bytes 786440 | tf_op jit(solution)/shard_map/ppermute | solution.py:172
  164.0 5.7 %collective-permute-done.17 = f32[256,256]{1,0:T(8,128)S(1)} collective-permute-done((f32[256,256]{1,0:T(8,128)S(1)}, f32[256,256]{1,0:T(8,128)S(1)}, u32[]{:S(2)}, u32[]{:S(2)}) %collective-permute-start.17) | collective-permute-done | bytes 262176 | tf_op jit(solution)/shard_map/ppermute | solution.py:172
  169.7 1.7 multiply_reduce_fusion.1
  171.4 5.2 %fusion.26 = f32[256,256]{1,0:T(8,128)S(1)} fusion(bf16[256,8192]{1,0:T(8,128)(2,1)} %all-gather.2.cloned.1.call-done, f32[256]{0:T(256)S(1)} %convert_add_fusion), kind=kOutput, calls=%fused_computation.33 | convolution fusion | flops 1080033280 | bytes 4457472 | tf_op jit(solution)/shard_map/dot_general | solution.py:187
  178.2 1.9 %all-to-all-done = bf16[16,256,256]{2,1,0:T(8,128)(2,1)S(1)} async-done(((bf16[16,256,256]{2,1,0:T(8,128)(2,1)}), bf16[16,256,256]{2,1,0:T(8,128)(2,1)S(1)}, u32[]{:S(2)}, u32[]{:S(2)}) %all-to-all-start) | async-done | bytes 2097184 | tf_op jit(solution)/shard_map/all_to_all | solution.py:163
  (104 shorter events, 22.6 us)
Async XLA Ops:
  7.2 15.7 %copy-start = (bf16[256,1024]{1,0:T(8,128)(2,1)S(1)}, bf16[256,1024]{1,0:T(8,128)(2,1)}, u32[]{:S(2)}) copy-start(bf16[256,1024]{1,0:T(8,128)(2,1)} %param.11) | copy-start | bytes 1572868
  7.2 93.4 %all-gather.2.cloned.1.call-start = ((), (), s32[]{:S(2)}) async-start(), calls=%async_computation.1 | async-start | bytes 4718592 | tf_op jit(solution)/shard_map/all_gather | solution.py:210
  9.0 17.5 %collective-permute-start = (bf16[256,256]{1,0:T(8,128)(2,1)S(1)}, bf16[256,256]{1,0:T(8,128)(2,1)S(1)}, u32[]{:S(2)}, u32[]{:S(2)}) collective-permute-start(bf16[256,256]{1,0:T(8,128)(2,1)S(1)} %constant_dynamic-update-slice_fusion), channel_id=1, source_target_pairs={{0,120},{1,121},{2,122},{3,123},{4,124},{5,125},{6,126},{7,127}} | collective-permute-start | bytes 393224 | tf_op jit(solution)/shard_map/ppermute | solution.py:144
  9.7 18.1 %collective-permute-start.1 = (bf16[256,256]{1,0:T(8,128)(2,1)S(1)}, bf16[256,256]{1,0:T(8,128)(2,1)S(1)}, u32[]{:S(2)}, u32[]{:S(2)}) collective-permute-start(bf16[256,256]{1,0:T(8,128)(2,1)S(1)} %constant_dynamic-update-slice_fusion), channel_id=1, source_target_pairs={{0,112},{8,120},{1,113},{9,121},{2,114},{10,122},{3,115},{11,123},... | collective-permute-start | bytes 393224 | tf_op jit(solution)/shard_map/ppermute | solution.py:144
  17.8 11.3 %collective-permute-start.2 = (bf16[256,256]{1,0:T(8,128)(2,1)S(1)}, bf16[256,256]{1,0:T(8,128)(2,1)S(1)}, u32[]{:S(2)}, u32[]{:S(2)}) collective-permute-start(bf16[256,256]{1,0:T(8,128)(2,1)S(1)} %constant_dynamic-update-slice_fusion), channel_id=1, source_target_pairs={{0,104},{8,112},{16,120},{1,105},{9,113},{17,121},{2,106},{10,114}... | collective-permute-start | bytes 393224 | tf_op jit(solution)/shard_map/ppermute | solution.py:144
  19.1 11.3 %collective-permute-start.3 = (bf16[256,256]{1,0:T(8,128)(2,1)S(1)}, bf16[256,256]{1,0:T(8,128)(2,1)S(1)}, u32[]{:S(2)}, u32[]{:S(2)}) collective-permute-start(bf16[256,256]{1,0:T(8,128)(2,1)S(1)} %constant_dynamic-update-slice_fusion), channel_id=1, source_target_pairs={{0,96},{8,104},{16,112},{24,120},{1,97},{9,105},{17,113},{25,121},... | collective-permute-start | bytes 393224 | tf_op jit(solution)/shard_map/ppermute | solution.py:144
  20.4 11.4 %collective-permute-start.4 = (bf16[256,256]{1,0:T(8,128)(2,1)S(1)}, bf16[256,256]{1,0:T(8,128)(2,1)S(1)}, u32[]{:S(2)}, u32[]{:S(2)}) collective-permute-start(bf16[256,256]{1,0:T(8,128)(2,1)S(1)} %constant_dynamic-update-slice_fusion), channel_id=1, source_target_pairs={{0,88},{8,96},{16,104},{24,112},{32,120},{1,89},{9,97},{17,105},{2... | collective-permute-start | bytes 393224 | tf_op jit(solution)/shard_map/ppermute | solution.py:144
  26.5 10.4 %collective-permute-start.5 = (bf16[256,256]{1,0:T(8,128)(2,1)S(1)}, bf16[256,256]{1,0:T(8,128)(2,1)S(1)}, u32[]{:S(2)}, u32[]{:S(2)}) collective-permute-start(bf16[256,256]{1,0:T(8,128)(2,1)S(1)} %constant_dynamic-update-slice_fusion), channel_id=1, source_target_pairs={{0,80},{8,88},{16,96},{24,104},{32,112},{40,120},{1,81},{9,89},{17... | collective-permute-start | bytes 393224 | tf_op jit(solution)/shard_map/ppermute | solution.py:144
  27.8 14.3 %collective-permute-start.6 = (bf16[256,256]{1,0:T(8,128)(2,1)S(1)}, bf16[256,256]{1,0:T(8,128)(2,1)S(1)}, u32[]{:S(2)}, u32[]{:S(2)}) collective-permute-start(bf16[256,256]{1,0:T(8,128)(2,1)S(1)} %constant_dynamic-update-slice_fusion), channel_id=1, source_target_pairs={{0,72},{8,80},{16,88},{24,96},{32,104},{40,112},{48,120},{1,73},{9... | collective-permute-start | bytes 393224 | tf_op jit(solution)/shard_map/ppermute | solution.py:144
  29.1 19.3 %collective-permute-start.7 = (bf16[256,256]{1,0:T(8,128)(2,1)S(1)}, bf16[256,256]{1,0:T(8,128)(2,1)S(1)}, u32[]{:S(2)}, u32[]{:S(2)}) collective-permute-start(bf16[256,256]{1,0:T(8,128)(2,1)S(1)} %constant_dynamic-update-slice_fusion), channel_id=1, source_target_pairs={{0,64},{8,72},{16,80},{24,88},{32,96},{40,104},{48,112},{56,120},{... | collective-permute-start | bytes 393224 | tf_op jit(solution)/shard_map/ppermute | solution.py:144
  30.5 19.3 %collective-permute-start.8 = (bf16[256,256]{1,0:T(8,128)(2,1)S(1)}, bf16[256,256]{1,0:T(8,128)(2,1)S(1)}, u32[]{:S(2)}, u32[]{:S(2)}) collective-permute-start(bf16[256,256]{1,0:T(8,128)(2,1)S(1)} %constant_dynamic-update-slice_fusion), channel_id=1, source_target_pairs={{0,56},{8,64},{16,72},{24,80},{32,88},{40,96},{48,104},{56,112},{6... | collective-permute-start | bytes 393224 | tf_op jit(solution)/shard_map/ppermute | solution.py:144
  31.8 22.8 %collective-permute-start.9 = (bf16[256,256]{1,0:T(8,128)(2,1)S(1)}, bf16[256,256]{1,0:T(8,128)(2,1)S(1)}, u32[]{:S(2)}, u32[]{:S(2)}) collective-permute-start(bf16[256,256]{1,0:T(8,128)(2,1)S(1)} %constant_dynamic-update-slice_fusion), channel_id=1, source_target_pairs={{0,48},{8,56},{16,64},{24,72},{32,80},{40,88},{48,96},{56,104},{64... | collective-permute-start | bytes 393224 | tf_op jit(solution)/shard_map/ppermute | solution.py:144
  36.9 20.2 %collective-permute-start.10 = (bf16[256,256]{1,0:T(8,128)(2,1)S(1)}, bf16[256,256]{1,0:T(8,128)(2,1)S(1)}, u32[]{:S(2)}, u32[]{:S(2)}) collective-permute-start(bf16[256,256]{1,0:T(8,128)(2,1)S(1)} %constant_dynamic-update-slice_fusion), channel_id=1, source_target_pairs={{0,40},{8,48},{16,56},{24,64},{32,72},{40,80},{48,88},{56,96},{64,... | collective-permute-start | bytes 393224 | tf_op jit(solution)/shard_map/ppermute | solution.py:144
  42.1 17.6 %collective-permute-start.11 = (bf16[256,256]{1,0:T(8,128)(2,1)S(1)}, bf16[256,256]{1,0:T(8,128)(2,1)S(1)}, u32[]{:S(2)}, u32[]{:S(2)}) collective-permute-start(bf16[256,256]{1,0:T(8,128)(2,1)S(1)} %constant_dynamic-update-slice_fusion), channel_id=1, source_target_pairs={{0,32},{8,40},{16,48},{24,56},{32,64},{40,72},{48,80},{56,88},{64,... | collective-permute-start | bytes 393224 | tf_op jit(solution)/shard_map/ppermute | solution.py:144
  48.4 11.4 %collective-permute-start.12 = (bf16[256,256]{1,0:T(8,128)(2,1)S(1)}, bf16[256,256]{1,0:T(8,128)(2,1)S(1)}, u32[]{:S(2)}, u32[]{:S(2)}) collective-permute-start(bf16[256,256]{1,0:T(8,128)(2,1)S(1)} %constant_dynamic-update-slice_fusion), channel_id=1, source_target_pairs={{0,24},{8,32},{16,40},{24,48},{32,56},{40,64},{48,72},{56,80},{64,... | collective-permute-start | bytes 393224 | tf_op jit(solution)/shard_map/ppermute | solution.py:144
  49.8 10.1 %collective-permute-start.13 = (bf16[256,256]{1,0:T(8,128)(2,1)S(1)}, bf16[256,256]{1,0:T(8,128)(2,1)S(1)}, u32[]{:S(2)}, u32[]{:S(2)}) collective-permute-start(bf16[256,256]{1,0:T(8,128)(2,1)S(1)} %constant_dynamic-update-slice_fusion), channel_id=1, source_target_pairs={{0,16},{8,24},{16,32},{24,40},{32,48},{40,56},{48,64},{56,72},{64,... | collective-permute-start | bytes 393224 | tf_op jit(solution)/shard_map/ppermute | solution.py:144
  54.6 5.3 %collective-permute-start.14 = (bf16[256,256]{1,0:T(8,128)(2,1)S(1)}, bf16[256,256]{1,0:T(8,128)(2,1)S(1)}, u32[]{:S(2)}, u32[]{:S(2)}) collective-permute-start(bf16[256,256]{1,0:T(8,128)(2,1)S(1)} %constant_dynamic-update-slice_fusion), channel_id=1, source_target_pairs={{0,8},{8,16},{16,24},{24,32},{32,40},{40,48},{48,56},{56,64},{64,7... | collective-permute-start | bytes 393224 | tf_op jit(solution)/shard_map/ppermute | solution.py:144
  57.0 95.1 %collective-permute-start.15 = (f32[256,256]{1,0:T(8,128)S(1)}, f32[256,256]{1,0:T(8,128)}, u32[]{:S(2)}, u32[]{:S(2)}) collective-permute-start(f32[256,256]{1,0:T(8,128)S(1)} %fusion.38), channel_id=1, source_target_pairs={{0,1},{1,0},{2,3},{3,2},{4,5},{5,4},{6,7},{7,6},{8,9},{9,8},{10,11... | collective-permute-start | bytes 786440 | tf_op jit(solution)/shard_map/ppermute | solution.py:172
  67.5 44.7 %copy-start.1 = (f32[256,8,128]{2,0,1:T(8,128)}, f32[256,8,128]{2,0,1:T(8,128)S(1)}, u32[]{:S(2)}) copy-start(f32[256,8,128]{2,0,1:T(8,128)S(1)} %get-tuple-element.91) | copy-start | bytes 3145732
  112.2 1.2 copy-start.3
  122.6 57.5 %all-to-all-start = ((bf16[16,256,256]{2,1,0:T(8,128)(2,1)}), bf16[16,256,256]{2,1,0:T(8,128)(2,1)S(1)}, u32[]{:S(2)}, u32[]{:S(2)}) async-start(bf16[16,256,256]{2,1,0:T(8,128)(2,1)} %bitcast.129), calls=%async_computation | async-start | bytes 4194304 | tf_op jit(solution)/shard_map/all_to_all | solution.py:163
  153.1 7.9 %collective-permute-start.16 = (f32[256,256]{1,0:T(8,128)S(1)}, f32[256,256]{1,0:T(8,128)S(1)}, u32[]{:S(2)}, u32[]{:S(2)}) collective-permute-start(f32[256,256]{1,0:T(8,128)S(1)} %add.106), channel_id=1, source_target_pairs={{0,2},{1,3},{2,0},{3,1},{4,6},{5,7},{6,4},{7,5},{8,10},{9,11},{10,... | collective-permute-start | bytes 786440 | tf_op jit(solution)/shard_map/ppermute | solution.py:172
  161.1 8.5 %collective-permute-start.17 = (f32[256,256]{1,0:T(8,128)S(1)}, f32[256,256]{1,0:T(8,128)S(1)}, u32[]{:S(2)}, u32[]{:S(2)}) collective-permute-start(f32[256,256]{1,0:T(8,128)S(1)} %add.107), channel_id=1, source_target_pairs={{0,4},{1,5},{2,6},{3,7},{4,0},{5,1},{6,2},{7,3},{8,12},{9,13},{10,... | collective-permute-start | bytes 786440 | tf_op jit(solution)/shard_map/ppermute | solution.py:172
  171.4 5.2 %copy-start.2 = (f32[256,8,128]{2,0,1:T(8,128)S(1)}, f32[256,8,128]{2,0,1:T(8,128)}, u32[]{:S(2)}) copy-start(f32[256,8,128]{2,0,1:T(8,128)} %copy-done.1) | copy-start | bytes 3145732
  (1 other events, 0.7 us)
Sparse Core Ops, SparseCore 0:
  21.9 78.6 all-gather.1

commit v14 on v13

--- a/solution.py
+++ b/solution.py
@@ -159,6 +159,13 @@
     return total
 
 
+def exchange_gather(value, axis_name):
+    size = lax.axis_size(axis_name)
+    copies = jnp.broadcast_to(value[None], (size,) + value.shape)
+    arrived = lax.all_to_all(copies, axis_name, 0, 0, tiled=True)
+    return arrived.reshape((size * value.shape[0],) + value.shape[1:])
+
+
 def exchange_reduce(parts, axis_name):
     arrived = lax.all_to_all(parts, axis_name, 0, 0, tiled=True)
     return jnp.sum(arrived.astype(jnp.float32), axis=0)
@@ -210,7 +217,7 @@
         lax.all_gather(grad_out, "head", axis=1, tiled=True).astype(jnp.float32)
         * loss_weight[:, None]
     ).astype(jnp.bfloat16)
-    pair_all = causal_gather(jnp.concatenate([key_rows, value_rows], axis=1), "ctx")
+    pair_all = exchange_gather(jnp.concatenate([key_rows, value_rows], axis=1), "ctx")
     kv_width = key_rows.shape[1]
     keys_all, values_all = (pair_all[:, :kv_width], pair_all[:, kv_width:])
     tokens = keys_all.shape[0]

time: 189 us -> 189 us (level)
  waiting for transfers between devices: 47.6 us -> 80.4 us
  starting transfers between devices: 79.1 us -> 47.6 us
    ppermute x15 -> x0, starting transfers between devices: 42.7 us -> none  [causal_gather(): received.append(lax.ppermute(value, axis_name, pairs))]
    all_to_all x0 -> x1, waiting for transfers between devices: none -> 27.3 us  [exchange_gather(): arrived = lax.all_to_all(copies, axis_name, 0, 0, tiled=True)]
    all_to_all x0 -> x1, starting transfers between devices: none -> 7.84 us  [exchange_gather(): arrived = lax.all_to_all(copies, axis_name, 0, 0, tiled=True)]
    all_gather x1, waiting for transfers between devices: 33.1 us -> 38 us  [body(): lax.all_gather(grad_out, 'head', axis=1, tiled=True).astype(jnp.float32)]
    all_to_all x1, starting transfers between devices: 29.5 us -> 33 us  [exchange_reduce(): arrived = lax.all_to_all(parts, axis_name, 0, 0, tiled=True)]
    unnamed x45 -> x21, local copies, waits for them, and re-layouts: 4.89 us -> 2.62 us
  transfers between devices with their start and end apart: 20 -> 6, of which waited for: 5 -> 5; matrix products, arithmetic and copies ran while one was open for 18% -> 17% of each run, Pallas kernels for 5% -> 5%
where the time goes in v14:
time: 189 us; the launch traced here: 188 us
  waiting for transfers between devices  80.4 us (43%)
  starting transfers between devices  47.6 us (25%)
  matrix products  23.7 us (13%)
  between operations  14.2 us (8%)
  Pallas kernels  9.18 us (5%)
  local copies, waits for them, and re-layouts  7.4 us (4%)
  other arithmetic  5.49 us (3%)
    all_gather x1, waiting for transfers between devices, body(): lax.all_gather(grad_out, 'head', axis=1, tiled=True).astype(jnp.float32)  38 us
    all_to_all x1, starting transfers between devices, exchange_reduce(): arrived = lax.all_to_all(parts, axis_name, 0, 0, tiled=True)  33 us
    all_to_all x1, waiting for transfers between devices, exchange_gather(): arrived = lax.all_to_all(copies, axis_name, 0, 0, tiled=True)  27.3 us
    ppermute x3, waiting for transfers between devices, butterfly_sum(): value = value + lax.ppermute(value, axis_name, pairs)  12.5 us
    dot_general x1, matrix products, body(): lax.dot_general(piece_part, out_weight, (((1,), (1,)), ((), ())), preferr...  11.6 us
    pallas_call x1, Pallas kernels, flash_backward(): pl.pallas_call(kernel, grid_spec=grid_spec, out_shape=[jax.ShapeDtypeStru...  9.18 us
    all_to_all x1, starting transfers between devices, exchange_gather(): arrived = lax.all_to_all(copies, axis_name, 0, 0, tiled=True)  7.84 us
    ppermute x3, starting transfers between devices, butterfly_sum(): value = value + lax.ppermute(value, axis_name, pairs)  6.75 us
  transfers between devices with their start and end apart: 6, of which 5 were waited for; matrix products, arithmetic and copies ran while one was open for 17% of the time, Pallas kernels for 5%

profile of v14, /device:TPU:1, one launch (start us, length us, event | category | flops | bytes accessed | tf_op | source)
XLA Modules:
  0.0 188.2 jit_solution(14010589770040820031)
XLA Ops:
  7.2 0.9 pad_maximum_fusion
  8.2 1.5 broadcast_in_dim.44
  9.7 7.8 %all-to-all-start = ((bf16[16,256,256]{2,1,0:T(8,128)(2,1)}), bf16[16,256,256]{2,1,0:T(8,128)(2,1)S(1)}, u32[]{:S(2)}, u32[]{:S(2)}) async-start(bf16[16,256,256]{2,1,0:T(8,128)(2,1)} %broadcast_in_dim.44), calls=%async_computation | async-start | bytes 4194304 | tf_op jit(solution)/shard_map/all_to_all | solution.py:165
  18.6 2.7 %collective-permute-start = (f32[256,256]{1,0:T(8,128)S(1)}, f32[256,256]{1,0:T(8,128)}, u32[]{:S(2)}, u32[]{:S(2)}) collective-permute-start(f32[256,256]{1,0:T(8,128)S(1)} %fusion.38), channel_id=1, source_target_pairs={{0,1},{1,0},{2,3},{3,2},{4,5},{5,4},{6,7},{7,6},{8,9},{9,8},{10,11... | collective-permute-start | bytes 786440 | tf_op jit(solution)/shard_map/ppermute | solution.py:179
  21.3 0.9 copy.31
  22.8 1.1 copy_bitcast_fusion
  24.0 27.3 %all-to-all-done = bf16[16,256,256]{2,1,0:T(8,128)(2,1)S(1)} async-done(((bf16[16,256,256]{2,1,0:T(8,128)(2,1)}), bf16[16,256,256]{2,1,0:T(8,128)(2,1)S(1)}, u32[]{:S(2)}, u32[]{:S(2)}) %all-to-all-start) | async-done | bytes 2097184 | tf_op jit(solution)/shard_map/all_to_all | solution.py:165
  51.2 1.5 fusion.36
  52.7 2.8 %while.24 = (s32[]{:T(128)}, f32[256,8]{0,1:T(8,128)S(1)}, f32[256,8]{0,1:T(8,128)S(1)}, s32[]{:T(128)}, bf16[4096,128]{1,0:T(8,128)(2,1)}, /*index=5*/bf16[256,...) while((s32[]{:T(128)}, f32[256,8]{0,1:T(8,128)S(1)}, ...), condition=%wide.region_3.4_spmd.clone, body=%wide.region_0.3_spmd.clone.sunk | while | flops 275911424 | bytes 9549991 | solution.py:253
  52.9 1.7 fusion.52
  56.5 3.0 %while.25 = (s32[]{:T(128)}, f32[256,8,128]{2,0,1:T(8,128)S(1)}, s32[]{:T(128)}, bf16[4096,128]{1,0:T(8,128)(2,1)}, bf16[256,8,128]{2,1,0:T(8,128)(2,1)S(1)}, /*...) while((s32[]{:T(128)}, f32[256,8,128]{2,0,1:T(8,128)S(1)}, ...), condition=%wide.region_5.6_spmd.clone, body=%wide.region_4.5_spmd.clone.sunk | while | flops 541459200 | bytes 3161259 | solution.py:265
  56.6 2.7 %fusion.56 = f32[256,8,128]{2,0,1:T(8,128)S(1)} fusion(f32[256,8,128]{2,0,1:T(8,128)S(1)} %get-tuple-element.342, f32[256,8]{0,1:T(8,128)S(1)} %get-tuple-element.358, pred[256,512]{1,0:T(8,128)(4,1)S(1)} %broadcast_compare_fusion.5, bf16[256,8,128]{2,1,0:T(8,128)(2,1)S(1)} %get-tuple-element.357, bf16[4096,128]{1,0:T(8,128)(2,1)} %get-tuple-element.359, ...), kind=kOutput, calls=%fused_computation.18.clone.1 | convolution fusion | flops 541327360 | bytes 3023872 | tf_op jit(solution)/shard_map/while/body/tgk,kd->tgd/dot_general | solution.py:261
  59.5 38.0 %all-gather.2.cloned.1.call-done = bf16[256,8192]{1,0:T(8,128)(2,1)} async-done(((bf16[256,1024]{1,0:T(8,128)(2,1)}), bf16[256,8192]{1,0:T(8,128)(2,1)}) %all-gather.2.cloned.1.call-update) | async-done | bytes 4194320 | tf_op jit(solution)/shard_map/all_gather | solution.py:217
  97.5 11.6 %fusion.28.do_ref = bf16[256,1024]{1,0:T(8,128)(2,1)S(1)} fusion(bf16[1024,8192]{1,0:T(8,128)(2,1)} %param.15, bf16[256,8192]{1,0:T(8,128)(2,1)} %all-gather.2.cloned.1.call-done, f32[256]{0:T(256)S(1)} %convert_add_fusion), kind=kOutput, calls=%fused_computation.35 | convolution fusion | flops 4301520896 | bytes 21496832 | tf_op jit(solution)/shard_map/dot_general | solution.py:274
  110.3 9.2 %shard_map.110 = (bf16[256,1024]{1,0:T(8,128)(2,1)}, bf16[4096,256]{1,0:T(8,128)(2,1)}) custom-call(s32[2]{0:T(128)} %pad_add_fusion.scalar_ref, bf16[256,1024]{1,0:T(8,128)(2,1)} %q_ref.1, bf16[256,1024]{1,0:T(8,128)(2,1)} %copy-done.5, bf16[4096,128]{1,0:T(8,128)(2,1)S(1)} %copy-done.1, bf16[4096,128]{1,0:T(8,128)(2,1)} %get-tuple-element.372, ...), custom_call_target="tpu_custom_call" | custom-call | tf_op jit(solution)/shard_map/pallas_call | solution.py:107
  119.5 33.0 %all-to-all-start.1 = ((bf16[16,256,256]{2,1,0:T(8,128)(2,1)}), bf16[16,256,256]{2,1,0:T(8,128)(2,1)S(1)}, u32[]{:S(2)}, u32[]{:S(2)}) async-start(bf16[16,256,256]{2,1,0:T(8,128)(2,1)} %bitcast.81), calls=%async_computation.1 | async-start | bytes 4194304 | tf_op jit(solution)/shard_map/all_to_all | solution.py:170
  152.5 1.0 add.101
  153.5 1.2 collective-permute-start.1
  154.7 6.7 %collective-permute-done.1 = f32[256,256]{1,0:T(8,128)S(1)} collective-permute-done((f32[256,256]{1,0:T(8,128)S(1)}, f32[256,256]{1,0:T(8,128)S(1)}, u32[]{:S(2)}, u32[]{:S(2)}) %collective-permute-start.1) | collective-permute-done | bytes 262176 | tf_op jit(solution)/shard_map/ppermute | solution.py:179
  161.4 2.8 %collective-permute-start.2 = (f32[256,256]{1,0:T(8,128)S(1)}, f32[256,256]{1,0:T(8,128)S(1)}, u32[]{:S(2)}, u32[]{:S(2)}) collective-permute-start(f32[256,256]{1,0:T(8,128)S(1)} %add.102), channel_id=1, source_target_pairs={{0,4},{1,5},{2,6},{3,7},{4,0},{5,1},{6,2},{7,3},{8,12},{9,13},{10,... | collective-permute-start | bytes 786440 | tf_op jit(solution)/shard_map/ppermute | solution.py:179
  164.2 5.8 %collective-permute-done.2 = f32[256,256]{1,0:T(8,128)S(1)} collective-permute-done((f32[256,256]{1,0:T(8,128)S(1)}, f32[256,256]{1,0:T(8,128)S(1)}, u32[]{:S(2)}, u32[]{:S(2)}) %collective-permute-start.2) | collective-permute-done | bytes 262176 | tf_op jit(solution)/shard_map/ppermute | solution.py:179
  170.0 1.7 multiply_reduce_fusion.1
  171.8 5.1 %fusion.26 = f32[256,256]{1,0:T(8,128)S(1)} fusion(bf16[256,8192]{1,0:T(8,128)(2,1)} %all-gather.2.cloned.1.call-done, f32[256]{0:T(256)S(1)} %convert_add_fusion), kind=kOutput, calls=%fused_computation.33 | convolution fusion | flops 1080033280 | bytes 4457472 | tf_op jit(solution)/shard_map/dot_general | solution.py:194
  178.5 1.9 %all-to-all-done.1 = bf16[16,256,256]{2,1,0:T(8,128)(2,1)S(1)} async-done(((bf16[16,256,256]{2,1,0:T(8,128)(2,1)}), bf16[16,256,256]{2,1,0:T(8,128)(2,1)S(1)}, u32[]{:S(2)}, u32[]{:S(2)}) %all-to-all-start.1) | async-done | bytes 2097184 | tf_op jit(solution)/shard_map/all_to_all | solution.py:170
  (51 shorter events, 7.5 us)
Async XLA Ops:
  7.2 11.1 %copy-start = (bf16[256,1024]{1,0:T(8,128)(2,1)S(1)}, bf16[256,1024]{1,0:T(8,128)(2,1)}, u32[]{:S(2)}) copy-start(bf16[256,1024]{1,0:T(8,128)(2,1)} %param.11) | copy-start | bytes 1572868
  8.1 13.2 %copy-start.2 = (bf16[256,1024]{1,0:T(8,128)(2,1)S(1)}, bf16[256,1024]{1,0:T(8,128)(2,1)}, u32[]{:S(2)}) copy-start(bf16[256,1024]{1,0:T(8,128)(2,1)} %q_ref.1) | copy-start | bytes 1572868
  8.1 14.7 %copy-start.8 = (s32[256]{0:T(256)S(1)}, s32[256]{0:T(256)}, u32[]{:S(2)}) copy-start(s32[256]{0:T(256)} %param.17) | copy-start | bytes 3076
  9.7 41.6 %all-to-all-start = ((bf16[16,256,256]{2,1,0:T(8,128)(2,1)}), bf16[16,256,256]{2,1,0:T(8,128)(2,1)S(1)}, u32[]{:S(2)}, u32[]{:S(2)}) async-start(bf16[16,256,256]{2,1,0:T(8,128)(2,1)} %broadcast_in_dim.44), calls=%async_computation | async-start | bytes 4194304 | tf_op jit(solution)/shard_map/all_to_all | solution.py:165
  17.5 80.0 %all-gather.2.cloned.1.call-start = ((), (), s32[]{:S(2)}) async-start(), calls=%async_computation.2 | async-start | bytes 4718592 | tf_op jit(solution)/shard_map/all_gather | solution.py:217
  18.6 133.8 %collective-permute-start = (f32[256,256]{1,0:T(8,128)S(1)}, f32[256,256]{1,0:T(8,128)}, u32[]{:S(2)}, u32[]{:S(2)}) collective-permute-start(f32[256,256]{1,0:T(8,128)S(1)} %fusion.38), channel_id=1, source_target_pairs={{0,1},{1,0},{2,3},{3,2},{4,5},{5,4},{6,7},{7,6},{8,9},{9,8},{10,11... | collective-permute-start | bytes 786440 | tf_op jit(solution)/shard_map/ppermute | solution.py:179
  52.7 3.2 %copy-start.7 = (bf16[32,8,8,128]{3,2,1,0:T(8,128)(2,1)S(1)}, bf16[32,8,8,128]{3,2,1,0:T(8,128)(2,1)}, u32[]{:S(2)}) copy-start(bf16[32,8,8,128]{3,2,1,0:T(8,128)(2,1)} %copy.31) | copy-start | bytes 1572868
  55.8 0.7 copy-start.6
  59.5 49.6 %copy-start.3 = (f32[256,8,128]{2,0,1:T(8,128)}, f32[256,8,128]{2,0,1:T(8,128)S(1)}, u32[]{:S(2)}) copy-start(f32[256,8,128]{2,0,1:T(8,128)S(1)} %get-tuple-element.91) | copy-start | bytes 3145732
  59.5 50.8 %copy-start.1 = (bf16[4096,128]{1,0:T(8,128)(2,1)S(1)}, bf16[4096,128]{1,0:T(8,128)(2,1)}, u32[]{:S(2)}) copy-start(bf16[4096,128]{1,0:T(8,128)(2,1)} %get-tuple-element.371) | copy-start | bytes 3145732
  109.1 1.2 copy-start.5
  119.5 61.0 %all-to-all-start.1 = ((bf16[16,256,256]{2,1,0:T(8,128)(2,1)}), bf16[16,256,256]{2,1,0:T(8,128)(2,1)S(1)}, u32[]{:S(2)}, u32[]{:S(2)}) async-start(bf16[16,256,256]{2,1,0:T(8,128)(2,1)} %bitcast.81), calls=%async_computation.1 | async-start | bytes 4194304 | tf_op jit(solution)/shard_map/all_to_all | solution.py:170
  153.5 8.0 %collective-permute-start.1 = (f32[256,256]{1,0:T(8,128)S(1)}, f32[256,256]{1,0:T(8,128)S(1)}, u32[]{:S(2)}, u32[]{:S(2)}) collective-permute-start(f32[256,256]{1,0:T(8,128)S(1)} %add.101), channel_id=1, source_target_pairs={{0,2},{1,3},{2,0},{3,1},{4,6},{5,7},{6,4},{7,5},{8,10},{9,11},{10,... | collective-permute-start | bytes 786440 | tf_op jit(solution)/shard_map/ppermute | solution.py:179
  161.4 8.5 %collective-permute-start.2 = (f32[256,256]{1,0:T(8,128)S(1)}, f32[256,256]{1,0:T(8,128)S(1)}, u32[]{:S(2)}, u32[]{:S(2)}) collective-permute-start(f32[256,256]{1,0:T(8,128)S(1)} %add.102), channel_id=1, source_target_pairs={{0,4},{1,5},{2,6},{3,7},{4,0},{5,1},{6,2},{7,3},{8,12},{9,13},{10,... | collective-permute-start | bytes 786440 | tf_op jit(solution)/shard_map/ppermute | solution.py:179
  171.7 5.2 %copy-start.4 = (f32[256,8,128]{2,0,1:T(8,128)S(1)}, f32[256,8,128]{2,0,1:T(8,128)}, u32[]{:S(2)}) copy-start(f32[256,8,128]{2,0,1:T(8,128)} %copy-done.3) | copy-start | bytes 3145732
Sparse Core Ops, SparseCore 0:
  20.7 76.7 all-gather.1

commit v15 on v14

--- a/solution.py
+++ b/solution.py
@@ -207,17 +207,16 @@
     first_row = own_index * tok_dev
     loss_weight = 0.25 + answer_mask.astype(jnp.float32)
     weighted = (grad_out.astype(jnp.float32) * loss_weight[:, None]).astype(jnp.bfloat16)
-    hidden_gram = butterfly_sum(
-        lax.dot_general(
-            hidden_in, hidden_in, (((1,), (1,)), ((), ())), preferred_element_type=jnp.float32
-        ),
-        "head",
+    gram_part = lax.dot_general(
+        hidden_in, hidden_in, (((1,), (1,)), ((), ())), preferred_element_type=jnp.float32
     )
     piece_part = (
         lax.all_gather(grad_out, "head", axis=1, tiled=True).astype(jnp.float32)
         * loss_weight[:, None]
     ).astype(jnp.bfloat16)
     pair_all = exchange_gather(jnp.concatenate([key_rows, value_rows], axis=1), "ctx")
+    gram_part, pair_all = lax.optimization_barrier((gram_part, pair_all))
+    hidden_gram = butterfly_sum(gram_part, "head")
     kv_width = key_rows.shape[1]
     keys_all, values_all = (pair_all[:, :kv_width], pair_all[:, kv_width:])
     tokens = keys_all.shape[0]
@@ -276,6 +275,9 @@
     )
     grad_sum, squares_out = (grad_sum, gram_squares(piece_part, attended, head_dim))
     grad_attended, squares_out = (grad_sum.astype(jnp.bfloat16), squares_out)
+    hidden_gram, squares_out, grad_attended = lax.optimization_barrier(
+        (hidden_gram, squares_out, grad_attended)
+    )
     backward_buffer = buffer
     rows = query_rows.shape[0]
     backward_row_pos = first_row + jnp.arange(rows, dtype=jnp.int32)

time: 189 us -> 206 us (1.090)
  starting transfers between devices: 47.6 us -> 60.2 us
  waiting for transfers between devices: 80.4 us -> 88.4 us
    all_to_all x1, waiting for transfers between devices: 1.95 us -> 26.9 us  [exchange_reduce(): arrived = lax.all_to_all(parts, axis_name, 0, 0, tiled=True)]
    all_gather x1, waiting for transfers between devices: 38 us -> 16.5 us  [body(): lax.all_gather(grad_out, 'head', axis=1, tiled=True).astype(jnp.float32)]
    all_to_all x1, starting transfers between devices: 33 us -> 44.9 us  [exchange_reduce(): arrived = lax.all_to_all(parts, axis_name, 0, 0, tiled=True)]
    all_to_all x1, waiting for transfers between devices: 27.3 us -> 29.9 us  [exchange_gather(): arrived = lax.all_to_all(copies, axis_name, 0, 0, tiled=True)]
  transfers between devices with their start and end apart: 6 -> 6, of which waited for: 5 -> 6; matrix products, arithmetic and copies ran while one was open for 17% -> 6% of each run, Pallas kernels for 5% -> 0%
where the time goes in v15:
time: 206 us
  waiting for transfers between devices  88.4 us (43%)
  starting transfers between devices  60.2 us (29%)
  matrix products  22.6 us (11%)
  between operations  14.2 us (7%)
  Pallas kernels  9.15 us (4%)
  local copies, waits for them, and re-layouts  6.9 us (3%)
  other arithmetic  4.05 us (2%)
    all_to_all x1, starting transfers between devices, exchange_reduce(): arrived = lax.all_to_all(parts, axis_name, 0, 0, tiled=True)  44.9 us
    all_to_all x1, waiting for transfers between devices, exchange_gather(): arrived = lax.all_to_all(copies, axis_name, 0, 0, tiled=True)  29.9 us
    all_to_all x1, waiting for transfers between devices, exchange_reduce(): arrived = lax.all_to_all(parts, axis_name, 0, 0, tiled=True)  26.9 us
    all_gather x1, waiting for transfers between devices, body(): lax.all_gather(grad_out, 'head', axis=1, tiled=True).astype(jnp.float32)  16.5 us
    ppermute x3, waiting for transfers between devices, butterfly_sum(): value = value + lax.ppermute(value, axis_name, pairs)  14.4 us
    dot_general x1, matrix products, body(): lax.dot_general(piece_part, out_weight, (((1,), (1,)), ((), ())), preferr...  11.6 us
    pallas_call x1, Pallas kernels, flash_backward(): pl.pallas_call(kernel, grid_spec=grid_spec, out_shape=[jax.ShapeDtypeStru...  9.15 us
    all_to_all x1, starting transfers between devices, exchange_gather(): arrived = lax.all_to_all(copies, axis_name, 0, 0, tiled=True)  7.84 us
  transfers between devices with their start and end apart: 6, of which 6 were waited for; matrix products, arithmetic and copies ran while one was open for 6% of the time, Pallas kernels for 0%

profile of v15, /device:TPU:1, one launch (start us, length us, event | category | flops | bytes accessed | tf_op | source)
XLA Modules:
  0.0 205.9 jit_solution(3794650172688721446)
XLA Ops:
  7.2 1.0 pad_maximum_fusion
  8.2 1.5 broadcast_in_dim.44
  9.7 7.8 %all-to-all-start = ((bf16[16,256,256]{2,1,0:T(8,128)(2,1)}), bf16[16,256,256]{2,1,0:T(8,128)(2,1)S(1)}, u32[]{:S(2)}, u32[]{:S(2)}) async-start(bf16[16,256,256]{2,1,0:T(8,128)(2,1)} %broadcast_in_dim.44), calls=%async_computation | async-start | bytes 4194304 | tf_op jit(solution)/shard_map/all_to_all | solution.py:165
  18.3 0.9 copy.31
  19.8 1.1 copy_bitcast_fusion
  21.3 29.9 %all-to-all-done = bf16[16,256,256]{2,1,0:T(8,128)(2,1)S(1)} async-done(((bf16[16,256,256]{2,1,0:T(8,128)(2,1)}), bf16[16,256,256]{2,1,0:T(8,128)(2,1)S(1)}, u32[]{:S(2)}, u32[]{:S(2)}) %all-to-all-start) | async-done | bytes 2097184 | tf_op jit(solution)/shard_map/all_to_all | solution.py:165
  51.2 2.6 %collective-permute-start = (f32[256,256]{1,0:T(8,128)S(1)}, f32[256,256]{1,0:T(8,128)S(1)}, u32[]{:S(2)}, u32[]{:S(2)}) collective-permute-start(f32[256,256]{1,0:T(8,128)S(1)} %fusion.38), channel_id=1, source_target_pairs={{0,1},{1,0},{2,3},{3,2},{4,5},{5,4},{6,7},{7,6},{8,9},{9,8},{10,11... | collective-permute-start | bytes 786440 | tf_op jit(solution)/shard_map/ppermute | solution.py:179
  53.8 1.5 fusion.36
  55.2 4.4 %collective-permute-done = f32[256,256]{1,0:T(8,128)S(1)} collective-permute-done((f32[256,256]{1,0:T(8,128)S(1)}, f32[256,256]{1,0:T(8,128)S(1)}, u32[]{:S(2)}, u32[]{:S(2)}) %collective-permute-start) | collective-permute-done | bytes 262176 | tf_op jit(solution)/shard_map/ppermute | solution.py:179
  59.7 1.3 collective-permute-start.1
  61.0 2.9 %while.24 = (s32[]{:T(128)}, f32[256,8]{0,1:T(8,128)S(1)}, f32[256,8]{0,1:T(8,128)S(1)}, s32[]{:T(128)}, bf16[4096,128]{1,0:T(8,128)(2,1)}, /*index=5*/bf16[256,...) while((s32[]{:T(128)}, f32[256,8]{0,1:T(8,128)S(1)}, ...), condition=%wide.region_3.4_spmd.clone, body=%wide.region_0.3_spmd.clone.sunk | while | flops 275911424 | bytes 9549991 | solution.py:252
  61.1 1.8 fusion.52
  62.9 0.9 exponential_reduce_fusion.2
  64.2 7.6 %collective-permute-done.1 = f32[256,256]{1,0:T(8,128)S(1)} collective-permute-done((f32[256,256]{1,0:T(8,128)S(1)}, f32[256,256]{1,0:T(8,128)S(1)}, u32[]{:S(2)}, u32[]{:S(2)}) %collective-permute-start.1) | collective-permute-done | bytes 262176 | tf_op jit(solution)/shard_map/ppermute | solution.py:179
  71.8 3.5 %collective-permute-start.2 = (f32[256,256]{1,0:T(8,128)S(1)}, f32[256,256]{1,0:T(8,128)S(1)}, u32[]{:S(2)}, u32[]{:S(2)}) collective-permute-start(f32[256,256]{1,0:T(8,128)S(1)} %add.89), channel_id=1, source_target_pairs={{0,4},{1,5},{2,6},{3,7},{4,0},{5,1},{6,2},{7,3},{8,12},{9,13},{10,... | collective-permute-start | bytes 786440 | tf_op jit(solution)/shard_map/ppermute | solution.py:179
  75.5 3.1 %while.25 = (s32[]{:T(128)}, f32[256,8,128]{2,0,1:T(8,128)S(1)}, s32[]{:T(128)}, bf16[4096,128]{1,0:T(8,128)(2,1)}, bf16[256,8,128]{2,1,0:T(8,128)(2,1)S(1)}, /*...) while((s32[]{:T(128)}, f32[256,8,128]{2,0,1:T(8,128)S(1)}, ...), condition=%wide.region_5.6_spmd.clone, body=%wide.region_4.5_spmd.clone.sunk | while | flops 541459200 | bytes 3161259 | solution.py:264
  75.7 2.7 %fusion.56 = f32[256,8,128]{2,0,1:T(8,128)S(1)} fusion(f32[256,8,128]{2,0,1:T(8,128)S(1)} %get-tuple-element.354, f32[256,8]{0,1:T(8,128)S(1)} %get-tuple-element.370, pred[256,512]{1,0:T(8,128)(4,1)S(1)} %broadcast_compare_fusion.5, bf16[256,8,128]{2,1,0:T(8,128)(2,1)S(1)} %get-tuple-element.369, bf16[4096,128]{1,0:T(8,128)(2,1)} %get-tuple-element.371, ...), kind=kOutput, calls=%fused_computation.18.clone.1 | convolution fusion | flops 541327360 | bytes 3023872 | tf_op jit(solution)/shard_map/while/body/tgk,kd->tgd/dot_general | solution.py:260
  78.6 2.5 %collective-permute-done.2 = f32[256,256]{1,0:T(8,128)S(1)} collective-permute-done((f32[256,256]{1,0:T(8,128)S(1)}, f32[256,256]{1,0:T(8,128)S(1)}, u32[]{:S(2)}, u32[]{:S(2)}) %collective-permute-start.2) | collective-permute-done | bytes 262176 | tf_op jit(solution)/shard_map/ppermute | solution.py:179
  81.1 16.5 %all-gather.2.cloned.1.call-done = bf16[256,8192]{1,0:T(8,128)(2,1)} async-done(((bf16[256,1024]{1,0:T(8,128)(2,1)}), bf16[256,8192]{1,0:T(8,128)(2,1)}) %all-gather.2.cloned.1.call-update) | async-done | bytes 4194320 | tf_op jit(solution)/shard_map/all_gather | solution.py:214
  97.6 5.1 %fusion.27 = f32[256,256]{1,0:T(8,128)S(1)} fusion(bf16[256,8192]{1,0:T(8,128)(2,1)} %all-gather.2.cloned.1.call-done, f32[256]{0:T(256)S(1)} %convert_add_fusion), kind=kOutput, calls=%fused_computation.34 | convolution fusion | flops 1080033280 | bytes 4457472 | tf_op jit(solution)/shard_map/dot_general | solution.py:194
  103.2 11.6 %fusion.28.do_ref = bf16[256,1024]{1,0:T(8,128)(2,1)S(1)} fusion(bf16[1024,8192]{1,0:T(8,128)(2,1)} %param.15, bf16[256,8192]{1,0:T(8,128)(2,1)} %all-gather.2.cloned.1.call-done, f32[256]{0:T(256)S(1)} %convert_add_fusion), kind=kOutput, calls=%fused_computation.35 | convolution fusion | flops 4301520896 | bytes 21496832 | tf_op jit(solution)/shard_map/dot_general | solution.py:273
  116.1 9.2 %shard_map.110 = (bf16[256,1024]{1,0:T(8,128)(2,1)}, bf16[4096,256]{1,0:T(8,128)(2,1)}) custom-call(s32[2]{0:T(128)} %pad_add_fusion.scalar_ref, bf16[256,1024]{1,0:T(8,128)(2,1)} %q_ref.1, bf16[256,1024]{1,0:T(8,128)(2,1)} %copy-done.3, bf16[4096,128]{1,0:T(8,128)(2,1)S(1)} %copy-done.1, bf16[4096,128]{1,0:T(8,128)(2,1)} %get-tuple-element.384, ...), custom_call_target="tpu_custom_call" | custom-call | tf_op jit(solution)/shard_map/pallas_call | solution.py:107
  125.2 44.9 %all-to-all-start.1 = ((bf16[16,256,256]{2,1,0:T(8,128)(2,1)}), bf16[16,256,256]{2,1,0:T(8,128)(2,1)S(1)}, u32[]{:S(2)}, u32[]{:S(2)}) async-start(bf16[16,256,256]{2,1,0:T(8,128)(2,1)} %bitcast.81), calls=%async_computation.1 | async-start | bytes 4194304 | tf_op jit(solution)/shard_map/all_to_all | solution.py:170
  171.2 26.9 %all-to-all-done.1 = bf16[16,256,256]{2,1,0:T(8,128)(2,1)S(1)} async-done(((bf16[16,256,256]{2,1,0:T(8,128)(2,1)}), bf16[16,256,256]{2,1,0:T(8,128)(2,1)S(1)}, u32[]{:S(2)}, u32[]{:S(2)}) %all-to-all-start.1) | async-done | bytes 2097184 | tf_op jit(solution)/shard_map/all_to_all | solution.py:170
  (48 shorter events, 6.2 us)
Async XLA Ops:
  7.2 13.8 %copy-start = (bf16[256,1024]{1,0:T(8,128)(2,1)S(1)}, bf16[256,1024]{1,0:T(8,128)(2,1)}, u32[]{:S(2)}) copy-start(bf16[256,1024]{1,0:T(8,128)(2,1)} %param.11) | copy-start | bytes 1572868
  7.2 11.1 %copy-start.2 = (bf16[256,1024]{1,0:T(8,128)(2,1)S(1)}, bf16[256,1024]{1,0:T(8,128)(2,1)}, u32[]{:S(2)}) copy-start(bf16[256,1024]{1,0:T(8,128)(2,1)} %q_ref.1) | copy-start | bytes 1572868
  7.2 12.6 %copy-start.6 = (s32[256]{0:T(256)S(1)}, s32[256]{0:T(256)}, u32[]{:S(2)}) copy-start(s32[256]{0:T(256)} %param.17) | copy-start | bytes 3076
  9.7 41.5 %all-to-all-start = ((bf16[16,256,256]{2,1,0:T(8,128)(2,1)}), bf16[16,256,256]{2,1,0:T(8,128)(2,1)S(1)}, u32[]{:S(2)}, u32[]{:S(2)}) async-start(bf16[16,256,256]{2,1,0:T(8,128)(2,1)} %broadcast_in_dim.44), calls=%async_computation | async-start | bytes 4194304 | tf_op jit(solution)/shard_map/all_to_all | solution.py:165
  17.6 80.0 %all-gather.2.cloned.1.call-start = ((), (), s32[]{:S(2)}) async-start(), calls=%async_computation.2 | async-start | bytes 4718592 | tf_op jit(solution)/shard_map/all_gather | solution.py:214
  51.2 8.5 %collective-permute-start = (f32[256,256]{1,0:T(8,128)S(1)}, f32[256,256]{1,0:T(8,128)S(1)}, u32[]{:S(2)}, u32[]{:S(2)}) collective-permute-start(f32[256,256]{1,0:T(8,128)S(1)} %fusion.38), channel_id=1, source_target_pairs={{0,1},{1,0},{2,3},{3,2},{4,5},{5,4},{6,7},{7,6},{8,9},{9,8},{10,11... | collective-permute-start | bytes 786440 | tf_op jit(solution)/shard_map/ppermute | solution.py:179
  59.7 12.1 %collective-permute-start.1 = (f32[256,256]{1,0:T(8,128)S(1)}, f32[256,256]{1,0:T(8,128)S(1)}, u32[]{:S(2)}, u32[]{:S(2)}) collective-permute-start(f32[256,256]{1,0:T(8,128)S(1)} %add.88), channel_id=1, source_target_pairs={{0,2},{1,3},{2,0},{3,1},{4,6},{5,7},{6,4},{7,5},{8,10},{9,11},{10,... | collective-permute-start | bytes 786440 | tf_op jit(solution)/shard_map/ppermute | solution.py:179
  60.9 14.5 %copy-start.5 = (bf16[32,8,8,128]{3,2,1,0:T(8,128)(2,1)S(1)}, bf16[32,8,8,128]{3,2,1,0:T(8,128)(2,1)}, u32[]{:S(2)}) copy-start(bf16[32,8,8,128]{3,2,1,0:T(8,128)(2,1)} %copy.31) | copy-start | bytes 1572868
  64.1 11.3 %copy-start.4 = (f32[256,8]{1,0:T(8,128)}, f32[256,8]{1,0:T(8,128)S(1)}, u32[]{:S(2)}) copy-start(f32[256,8]{1,0:T(8,128)S(1)} %add.93.lt_ref) | copy-start | bytes 24580
  71.8 9.2 %collective-permute-start.2 = (f32[256,256]{1,0:T(8,128)S(1)}, f32[256,256]{1,0:T(8,128)S(1)}, u32[]{:S(2)}, u32[]{:S(2)}) collective-permute-start(f32[256,256]{1,0:T(8,128)S(1)} %add.89), channel_id=1, source_target_pairs={{0,4},{1,5},{2,6},{3,7},{4,0},{5,1},{6,2},{7,3},{8,12},{9,13},{10,... | collective-permute-start | bytes 786440 | tf_op jit(solution)/shard_map/ppermute | solution.py:179
  103.2 12.8 %copy-start.1 = (bf16[4096,128]{1,0:T(8,128)(2,1)S(1)}, bf16[4096,128]{1,0:T(8,128)(2,1)}, u32[]{:S(2)}) copy-start(bf16[4096,128]{1,0:T(8,128)(2,1)} %get-tuple-element.383) | copy-start | bytes 3145732
  114.9 1.2 copy-start.3
  125.2 44.9 %copy-start.7 = (bf16[256,1024]{1,0:T(8,128)(2,1)S(1)}, bf16[256,1024]{1,0:T(8,128)(2,1)}, u32[]{:S(2)}) copy-start(bf16[256,1024]{1,0:T(8,128)(2,1)} %get-tuple-element.89) | copy-start | bytes 1572868
  125.2 72.9 %all-to-all-start.1 = ((bf16[16,256,256]{2,1,0:T(8,128)(2,1)}), bf16[16,256,256]{2,1,0:T(8,128)(2,1)S(1)}, u32[]{:S(2)}, u32[]{:S(2)}) async-start(bf16[16,256,256]{2,1,0:T(8,128)(2,1)} %bitcast.81), calls=%async_computation.1 | async-start | bytes 4194304 | tf_op jit(solution)/shard_map/all_to_all | solution.py:170
Sparse Core Ops, SparseCore 0:
  20.7 76.8 all-gather.1

commit v16 on v7

--- a/solution.py
+++ b/solution.py
@@ -54,8 +54,9 @@
         def block(masked):
             k = k_ref[...]
             v = v_ref[...]
-            row_pos = scalar_ref[1] + lax.broadcasted_iota(jnp.int32, (rows, block_rows), 0)
-            col_pos = j * block_rows + lax.broadcasted_iota(jnp.int32, (rows, block_rows), 1)
+            k_turned = k.T
+            col_pos = j * block_rows + lax.broadcasted_iota(jnp.int32, (block_rows, rows), 0)
+            row_pos = scalar_ref[1] + lax.broadcasted_iota(jnp.int32, (block_rows, rows), 1)
             keep = row_pos >= col_pos
             dk = jnp.zeros((block_rows, head_dim), jnp.float32)
             dv = jnp.zeros((block_rows, head_dim), jnp.float32)
@@ -63,16 +64,16 @@
                 cols = slice(h * head_dim, (h + 1) * head_dim)
                 q = q_ref[:, cols]
                 do = do_ref[:, cols]
-                s = lax.dot_general(q, k, (((1,), (1,)), ((), ())), preferred_element_type=jnp.float32) * scaling
+                s = lax.dot_general(k, q, (((1,), (1,)), ((), ())), preferred_element_type=jnp.float32) * scaling
                 if masked:
                     s = jnp.where(keep, s, NEGATIVE)
-                p = jnp.exp(s - lt_ref[:, h : h + 1])
-                dp = lax.dot_general(do, v, (((1,), (1,)), ((), ())), preferred_element_type=jnp.float32)
-                ds = (p * (dp - rd_ref[:, h : h + 1]) * scaling).astype(jnp.bfloat16)
-                dq_acc[:, cols] += jnp.dot(ds, k, preferred_element_type=jnp.float32)
-                dk += lax.dot_general(ds, q, (((0,), (0,)), ((), ())), preferred_element_type=jnp.float32)
-                dv += lax.dot_general(p.astype(jnp.bfloat16), do, (((0,), (0,)), ((), ())), preferred_element_type=jnp.float32)
-            dkv_ref[:, :head_dim] = dk.astype(dkv_ref.dtype)
+                p = jnp.exp(s - lt_ref[h : h + 1, :])
+                dp = lax.dot_general(v, do, (((1,), (1,)), ((), ())), preferred_element_type=jnp.float32)
+                ds = (p * (dp - rd_ref[h : h + 1, :])).astype(jnp.bfloat16)
+                dq_acc[cols, :] += jnp.dot(k_turned, ds, preferred_element_type=jnp.float32)
+                dk += jnp.dot(ds, q, preferred_element_type=jnp.float32)
+                dv += jnp.dot(p.astype(jnp.bfloat16), do, preferred_element_type=jnp.float32)
+            dkv_ref[:, :head_dim] = (dk * scaling).astype(dkv_ref.dtype)
             dkv_ref[:, head_dim:] = dv.astype(dkv_ref.dtype)
 
         below = j * block_rows + block_rows - 1 <= scalar_ref[1]
@@ -91,7 +92,7 @@
 
         @pl.when(j == blocks - 1)
         def _():
-            dq_ref[...] = dq_acc[...].astype(dq_ref.dtype)
+            dq_ref[...] = (dq_acc[...].T * scaling).astype(dq_ref.dtype)
 
     def kv_map(j, s):
         return (jnp.minimum(j, s[0] - 1), 0)
@@ -105,14 +106,14 @@
             pl.BlockSpec((rows, width), full),
             pl.BlockSpec((block_rows, head_dim), kv_map),
             pl.BlockSpec((block_rows, head_dim), kv_map),
-            pl.BlockSpec((rows, heads), full),
-            pl.BlockSpec((rows, heads), full),
+            pl.BlockSpec((heads, rows), full),
+            pl.BlockSpec((heads, rows), full),
         ],
         out_specs=[
             pl.BlockSpec((rows, width), full),
             pl.BlockSpec((block_rows, 2 * head_dim), lambda j, s: (j, 0)),
         ],
-        scratch_shapes=[pltpu.VMEM((rows, width), jnp.float32)],
+        scratch_shapes=[pltpu.VMEM((width, rows), jnp.float32)],
     )
     return pl.pallas_call(
         kernel,
@@ -122,7 +123,7 @@
             jax.ShapeDtypeStruct((tokens, 2 * head_dim), jnp.bfloat16),
         ],
         compiler_params=pltpu.CompilerParams(dimension_semantics=("arbitrary",)),
-    )(scalars, query_rows, grad_attended, keys_all, values_all, log_total, row_dot)
+    )(scalars, query_rows, grad_attended, keys_all, values_all, log_total.T, row_dot.T)
 
 
 def butterfly_gather(value, axis_name):
@@ -169,6 +170,11 @@
     return total
 
 
+def exchange_reduce(parts, axis_name):
+    arrived = lax.all_to_all(parts, axis_name, 0, 0, tiled=True)
+    return jnp.sum(arrived.astype(jnp.float32), axis=0)
+
+
 def butterfly_sum(value, axis_name):
     size = lax.axis_size(axis_name)
     stride = 1
@@ -216,7 +222,6 @@
         * loss_weight[:, None]
     ).astype(jnp.bfloat16)
     pair_all = causal_gather(jnp.concatenate([key_rows, value_rows], axis=1), "ctx")
-    hidden_gram, pair_all = lax.optimization_barrier((hidden_gram, pair_all))
     kv_width = key_rows.shape[1]
     keys_all, values_all = (pair_all[:, :kv_width], pair_all[:, kv_width:])
     tokens = keys_all.shape[0]
@@ -301,7 +306,7 @@
         block_rows,
     )
     ctx_size = lax.axis_size("ctx")
-    key_sums = causal_reduce(
+    key_sums = exchange_reduce(
         backward_buffer.reshape((ctx_size, tokens // ctx_size) + backward_buffer.shape[1:]), "ctx"
     )
     grad_key = key_sums[:, : local_groups * head_dim].astype(jnp.bfloat16)

time: 223 us -> 186 us (0.83)
  waiting for transfers between devices: 88.9 us -> 48.3 us
  starting transfers between devices: 69.5 us -> 76.6 us
  local copies, waits for them, and re-layouts: 11.8 us -> 7.28 us
    ppermute x15 -> x0, waiting for transfers between devices: 59.3 us -> none  [causal_reduce(): total = total + lax.ppermute(sent, axis_name, pairs).astype(jnp.float32)]
    all_gather x1, waiting for transfers between devices: 4.27 us -> 33.9 us  [body(): lax.all_gather(grad_out, 'head', axis=1, tiled=True).astype(jnp.float32)]
    all_to_all x0 -> x1, starting transfers between devices: none -> 26.8 us  [exchange_reduce(): arrived = lax.all_to_all(parts, axis_name, 0, 0, tiled=True)]
    ppermute x15 -> x0, starting transfers between devices: 20.5 us -> none  [causal_reduce(): total = total + lax.ppermute(sent, axis_name, pairs).astype(jnp.float32)]
    ppermute x3, waiting for transfers between devices: 25.1 us -> 12.3 us  [butterfly_sum(): value = value + lax.ppermute(value, axis_name, pairs)]
    squeeze x1 -> x0, local copies, waits for them, and re-layouts: 2.97 us -> none  [causal_reduce(): lax.dynamic_index_in_dim(parts, jnp.maximum(own - shift, 0), 0, keepdims=...]
    unnamed x43 -> x42, local copies, waits for them, and re-layouts: 4.89 us -> 4.33 us
  transfers between devices with their start and end apart: 34 -> 20, of which waited for: 17 -> 5; matrix products, arithmetic and copies ran while one was open for 8% -> 18% of each run, Pallas kernels for 0% -> 5%
where the time goes in v16:
time: 186 us; the launch traced here: 185 us
  starting transfers between devices  76.6 us (41%)
  waiting for transfers between devices  48.3 us (26%)
  matrix products  22.9 us (12%)
  between operations  14.6 us (8%)
  Pallas kernels  9.24 us (5%)
  local copies, waits for them, and re-layouts  7.28 us (4%)
  other arithmetic  5.81 us (3%)
    ppermute x15, starting transfers between devices, causal_gather(): received.append(lax.ppermute(value, axis_name, pairs))  42.7 us
    all_gather x1, waiting for transfers between devices, body(): lax.all_gather(grad_out, 'head', axis=1, tiled=True).astype(jnp.float32)  33.9 us
    all_to_all x1, starting transfers between devices, exchange_reduce(): arrived = lax.all_to_all(parts, axis_name, 0, 0, tiled=True)  26.8 us
    ppermute x3, waiting for transfers between devices, butterfly_sum(): value = value + lax.ppermute(value, axis_name, pairs)  12.3 us
    dot_general x1, matrix products, body(): lax.dot_general(piece_part, out_weight, (((1,), (1,)), ((), ())), preferr...  11.6 us
    pallas_call x1, Pallas kernels, flash_backward(): pl.pallas_call(kernel, grid_spec=grid_spec, out_shape=[jax.ShapeDtypeStru...  9.24 us
    ppermute x3, starting transfers between devices, butterfly_sum(): value = value + lax.ppermute(value, axis_name, pairs)  7.06 us
    dot_general x1, matrix products, gram_squares(): lax.dot_general(left_side, left_side, (((1,), (1,)), ((), ())), preferred...  5.15 us
  transfers between devices with their start and end apart: 20, of which 5 were waited for; matrix products, arithmetic and copies ran while one was open for 18% of the time, Pallas kernels for 5%

profile of v16, /device:TPU:1, one launch (start us, length us, event | category | flops | bytes accessed | tf_op | source)
XLA Modules:
  0.0 185.0 jit_solution(1737120522129649459)
XLA Ops:
  9.7 8.1 %collective-permute-start.1 = (bf16[256,256]{1,0:T(8,128)(2,1)S(1)}, bf16[256,256]{1,0:T(8,128)(2,1)S(1)}, u32[]{:S(2)}, u32[]{:S(2)}) collective-permute-start(bf16[256,256]{1,0:T(8,128)(2,1)S(1)} %constant_dynamic-update-slice_fusion), channel_id=1, source_target_pairs={{0,112},{8,120},{1,113},{9,121},{2,114},{10,122},{3,115},{11,123},... | collective-permute-start | bytes 393224 | tf_op jit(solution)/shard_map/ppermute | solution.py:155
  17.8 1.3 collective-permute-start.2
  19.1 1.3 collective-permute-start.3
  23.9 1.9 %copy.20 = bf16[32,8,8,128]{3,2,1,0:T(8,128)(2,1)} copy(bf16[32,8,8,128]{3,1,2,0:T(8,128)(2,1)} %bitcast.130) | data formatting | bytes 1048576
  31.8 5.0 %collective-permute-start.9 = (bf16[256,256]{1,0:T(8,128)(2,1)S(1)}, bf16[256,256]{1,0:T(8,128)(2,1)S(1)}, u32[]{:S(2)}, u32[]{:S(2)}) collective-permute-start(bf16[256,256]{1,0:T(8,128)(2,1)S(1)} %constant_dynamic-update-slice_fusion), channel_id=1, source_target_pairs={{0,48},{8,56},{16,64},{24,72},{32,80},{40,88},{48,96},{56,104},{64... | collective-permute-start | bytes 393224 | tf_op jit(solution)/shard_map/ppermute | solution.py:155
  36.9 5.0 %collective-permute-start.10 = (bf16[256,256]{1,0:T(8,128)(2,1)S(1)}, bf16[256,256]{1,0:T(8,128)(2,1)S(1)}, u32[]{:S(2)}, u32[]{:S(2)}) collective-permute-start(bf16[256,256]{1,0:T(8,128)(2,1)S(1)} %constant_dynamic-update-slice_fusion), channel_id=1, source_target_pairs={{0,40},{8,48},{16,56},{24,64},{32,72},{40,80},{48,88},{56,96},{64,... | collective-permute-start | bytes 393224 | tf_op jit(solution)/shard_map/ppermute | solution.py:155
  42.1 6.3 %collective-permute-start.11 = (bf16[256,256]{1,0:T(8,128)(2,1)S(1)}, bf16[256,256]{1,0:T(8,128)(2,1)S(1)}, u32[]{:S(2)}, u32[]{:S(2)}) collective-permute-start(bf16[256,256]{1,0:T(8,128)(2,1)S(1)} %constant_dynamic-update-slice_fusion), channel_id=1, source_target_pairs={{0,32},{8,40},{16,48},{24,56},{32,64},{40,72},{48,80},{56,88},{64,... | collective-permute-start | bytes 393224 | tf_op jit(solution)/shard_map/ppermute | solution.py:155
  49.8 4.8 %collective-permute-start.13 = (bf16[256,256]{1,0:T(8,128)(2,1)S(1)}, bf16[256,256]{1,0:T(8,128)(2,1)S(1)}, u32[]{:S(2)}, u32[]{:S(2)}) collective-permute-start(bf16[256,256]{1,0:T(8,128)(2,1)S(1)} %constant_dynamic-update-slice_fusion), channel_id=1, source_target_pairs={{0,16},{8,24},{16,32},{24,40},{32,48},{40,56},{48,64},{56,72},{64,... | collective-permute-start | bytes 393224 | tf_op jit(solution)/shard_map/ppermute | solution.py:155
  54.6 2.4 %collective-permute-start.14 = (bf16[256,256]{1,0:T(8,128)(2,1)S(1)}, bf16[256,256]{1,0:T(8,128)(2,1)S(1)}, u32[]{:S(2)}, u32[]{:S(2)}) collective-permute-start(bf16[256,256]{1,0:T(8,128)(2,1)S(1)} %constant_dynamic-update-slice_fusion), channel_id=1, source_target_pairs={{0,8},{8,16},{16,24},{24,32},{32,40},{40,48},{48,56},{56,64},{64,7... | collective-permute-start | bytes 393224 | tf_op jit(solution)/shard_map/ppermute | solution.py:155
  57.0 2.7 %collective-permute-start.15 = (f32[256,256]{1,0:T(8,128)S(1)}, f32[256,256]{1,0:T(8,128)}, u32[]{:S(2)}, u32[]{:S(2)}) collective-permute-start(f32[256,256]{1,0:T(8,128)S(1)} %fusion.38), channel_id=1, source_target_pairs={{0,1},{1,0},{2,3},{3,2},{4,5},{5,4},{6,7},{7,6},{8,9},{9,8},{10,11... | collective-permute-start | bytes 786440 | tf_op jit(solution)/shard_map/ppermute | solution.py:183
  61.5 1.9 %while.24 = (s32[]{:T(128)}, f32[256,8]{0,1:T(8,128)S(1)}, f32[256,8]{0,1:T(8,128)S(1)}, s32[]{:T(128)}, bf16[4096,128]{1,0:T(8,128)(2,1)S(1)}, /*index=5*/bf16[...) while((s32[]{:T(128)}, f32[256,8]{0,1:T(8,128)S(1)}, ...), condition=%wide.region_3.4_spmd.clone, body=%wide.region_0.3_spmd.clone.sunk | while | flops 275911424 | bytes 9549991 | solution.py:257
  63.5 3.2 %while.25 = (s32[]{:T(128)}, f32[256,8,128]{2,0,1:T(8,128)S(1)}, s32[]{:T(128)}, bf16[4096,128]{1,0:T(8,128)(2,1)S(1)}, bf16[256,8,128]{2,1,0:T(8,128)(2,1)}, /*...) while((s32[]{:T(128)}, f32[256,8,128]{2,0,1:T(8,128)S(1)}, ...), condition=%wide.region_5.6_spmd.clone, body=%wide.region_4.5_spmd.clone.sunk | while | flops 541459200 | bytes 3161259 | solution.py:269
  63.7 2.8 %fusion.56 = f32[256,8,128]{2,0,1:T(8,128)S(1)} fusion(f32[256,8,128]{2,0,1:T(8,128)S(1)} %get-tuple-element.319, f32[256,8]{0,1:T(8,128)S(1)} %get-tuple-element.335, pred[256,512]{1,0:T(8,128)(4,1)S(1)} %broadcast_compare_fusion.5, bf16[256,8,128]{2,1,0:T(8,128)(2,1)} %get-tuple-element.334, bf16[4096,128]{1,0:T(8,128)(2,1)} %get-tuple-element.336, ...), kind=kOutput, calls=%fused_computation.18.clone.1 | convolution fusion | flops 541327360 | bytes 3023872 | tf_op jit(solution)/shard_map/while/body/tgk,kd->tgd/dot_general | solution.py:265
  66.7 33.9 %all-gather.2.cloned.1.call-done = bf16[256,8192]{1,0:T(8,128)(2,1)} async-done(((bf16[256,1024]{1,0:T(8,128)(2,1)}), bf16[256,8192]{1,0:T(8,128)(2,1)}) %all-gather.2.cloned.1.call-update) | async-done | bytes 4194320 | tf_op jit(solution)/shard_map/all_gather | solution.py:221
  100.6 11.6 %fusion.28.do_ref = bf16[256,1024]{1,0:T(8,128)(2,1)S(1)} fusion(bf16[1024,8192]{1,0:T(8,128)(2,1)} %param.15, bf16[256,8192]{1,0:T(8,128)(2,1)} %all-gather.2.cloned.1.call-done, f32[256]{0:T(256)S(1)} %convert_add_fusion), kind=kOutput, calls=%fused_computation.35 | convolution fusion | flops 4301520896 | bytes 21496832 | tf_op jit(solution)/shard_map/dot_general | solution.py:278
  113.2 9.2 %shard_map.110 = (bf16[256,1024]{1,0:T(8,128)(2,1)}, bf16[4096,256]{1,0:T(8,128)(2,1)}) custom-call(s32[2]{0:T(128)} %pad_add_fusion.scalar_ref, bf16[256,1024]{1,0:T(8,128)(2,1)} %q_ref.1, bf16[256,1024]{1,0:T(8,128)(2,1)} %copy-done.3, bf16[4096,128]{1,0:T(8,128)(2,1)S(1)} %get-tuple-element.345, bf16[4096,128]{1,0:T(8,128)(2,1)} %get-tuple-element.346, ...), custom_call_target="tpu_custom_call" | custom-call | tf_op jit(solution)/shard_map/pallas_call | solution.py:118
  122.4 26.8 %all-to-all-start = ((bf16[16,256,256]{2,1,0:T(8,128)(2,1)}), bf16[16,256,256]{2,1,0:T(8,128)(2,1)S(1)}, u32[]{:S(2)}, u32[]{:S(2)}) async-start(bf16[16,256,256]{2,1,0:T(8,128)(2,1)} %bitcast.131), calls=%async_computation | async-start | bytes 4194304 | tf_op jit(solution)/shard_map/all_to_all | solution.py:174
  150.2 1.3 collective-permute-start.16
  151.5 6.6 %collective-permute-done.16 = f32[256,256]{1,0:T(8,128)S(1)} collective-permute-done((f32[256,256]{1,0:T(8,128)S(1)}, f32[256,256]{1,0:T(8,128)S(1)}, u32[]{:S(2)}, u32[]{:S(2)}) %collective-permute-start.16) | collective-permute-done | bytes 262176 | tf_op jit(solution)/shard_map/ppermute | solution.py:183
  158.2 3.0 %collective-permute-start.17 = (f32[256,256]{1,0:T(8,128)S(1)}, f32[256,256]{1,0:T(8,128)S(1)}, u32[]{:S(2)}, u32[]{:S(2)}) collective-permute-start(f32[256,256]{1,0:T(8,128)S(1)} %add.107), channel_id=1, source_target_pairs={{0,4},{1,5},{2,6},{3,7},{4,0},{5,1},{6,2},{7,3},{8,12},{9,13},{10,... | collective-permute-start | bytes 786440 | tf_op jit(solution)/shard_map/ppermute | solution.py:183
  161.3 5.7 %collective-permute-done.17 = f32[256,256]{1,0:T(8,128)S(1)} collective-permute-done((f32[256,256]{1,0:T(8,128)S(1)}, f32[256,256]{1,0:T(8,128)S(1)}, u32[]{:S(2)}, u32[]{:S(2)}) %collective-permute-start.17) | collective-permute-done | bytes 262176 | tf_op jit(solution)/shard_map/ppermute | solution.py:183
  167.0 1.7 multiply_reduce_fusion.1
  168.7 5.1 %fusion.26 = f32[256,256]{1,0:T(8,128)S(1)} fusion(bf16[256,8192]{1,0:T(8,128)(2,1)} %all-gather.2.cloned.1.call-done, f32[256]{0:T(256)S(1)} %convert_add_fusion), kind=kOutput, calls=%fused_computation.33 | convolution fusion | flops 1080033280 | bytes 4457472 | tf_op jit(solution)/shard_map/dot_general | solution.py:198
  175.5 1.7 all-to-all-done
  (97 shorter events, 21.6 us)
Async XLA Ops:
  7.2 15.7 %copy-start = (bf16[256,1024]{1,0:T(8,128)(2,1)S(1)}, bf16[256,1024]{1,0:T(8,128)(2,1)}, u32[]{:S(2)}) copy-start(bf16[256,1024]{1,0:T(8,128)(2,1)} %param.11) | copy-start | bytes 1572868
  7.2 93.4 %all-gather.2.cloned.1.call-start = ((), (), s32[]{:S(2)}) async-start(), calls=%async_computation.1 | async-start | bytes 4718592 | tf_op jit(solution)/shard_map/all_gather | solution.py:221
  9.0 17.5 %collective-permute-start = (bf16[256,256]{1,0:T(8,128)(2,1)S(1)}, bf16[256,256]{1,0:T(8,128)(2,1)S(1)}, u32[]{:S(2)}, u32[]{:S(2)}) collective-permute-start(bf16[256,256]{1,0:T(8,128)(2,1)S(1)} %constant_dynamic-update-slice_fusion), channel_id=1, source_target_pairs={{0,120},{1,121},{2,122},{3,123},{4,124},{5,125},{6,126},{7,127}} | collective-permute-start | bytes 393224 | tf_op jit(solution)/shard_map/ppermute | solution.py:155
  9.7 18.1 %collective-permute-start.1 = (bf16[256,256]{1,0:T(8,128)(2,1)S(1)}, bf16[256,256]{1,0:T(8,128)(2,1)S(1)}, u32[]{:S(2)}, u32[]{:S(2)}) collective-permute-start(bf16[256,256]{1,0:T(8,128)(2,1)S(1)} %constant_dynamic-update-slice_fusion), channel_id=1, source_target_pairs={{0,112},{8,120},{1,113},{9,121},{2,114},{10,122},{3,115},{11,123},... | collective-permute-start | bytes 393224 | tf_op jit(solution)/shard_map/ppermute | solution.py:155
  17.8 11.3 %collective-permute-start.2 = (bf16[256,256]{1,0:T(8,128)(2,1)S(1)}, bf16[256,256]{1,0:T(8,128)(2,1)S(1)}, u32[]{:S(2)}, u32[]{:S(2)}) collective-permute-start(bf16[256,256]{1,0:T(8,128)(2,1)S(1)} %constant_dynamic-update-slice_fusion), channel_id=1, source_target_pairs={{0,104},{8,112},{16,120},{1,105},{9,113},{17,121},{2,106},{10,114}... | collective-permute-start | bytes 393224 | tf_op jit(solution)/shard_map/ppermute | solution.py:155
  19.1 11.3 %collective-permute-start.3 = (bf16[256,256]{1,0:T(8,128)(2,1)S(1)}, bf16[256,256]{1,0:T(8,128)(2,1)S(1)}, u32[]{:S(2)}, u32[]{:S(2)}) collective-permute-start(bf16[256,256]{1,0:T(8,128)(2,1)S(1)} %constant_dynamic-update-slice_fusion), channel_id=1, source_target_pairs={{0,96},{8,104},{16,112},{24,120},{1,97},{9,105},{17,113},{25,121},... | collective-permute-start | bytes 393224 | tf_op jit(solution)/shard_map/ppermute | solution.py:155
  20.4 11.4 %collective-permute-start.4 = (bf16[256,256]{1,0:T(8,128)(2,1)S(1)}, bf16[256,256]{1,0:T(8,128)(2,1)S(1)}, u32[]{:S(2)}, u32[]{:S(2)}) collective-permute-start(bf16[256,256]{1,0:T(8,128)(2,1)S(1)} %constant_dynamic-update-slice_fusion), channel_id=1, source_target_pairs={{0,88},{8,96},{16,104},{24,112},{32,120},{1,89},{9,97},{17,105},{2... | collective-permute-start | bytes 393224 | tf_op jit(solution)/shard_map/ppermute | solution.py:155
  26.5 10.4 %collective-permute-start.5 = (bf16[256,256]{1,0:T(8,128)(2,1)S(1)}, bf16[256,256]{1,0:T(8,128)(2,1)S(1)}, u32[]{:S(2)}, u32[]{:S(2)}) collective-permute-start(bf16[256,256]{1,0:T(8,128)(2,1)S(1)} %constant_dynamic-update-slice_fusion), channel_id=1, source_target_pairs={{0,80},{8,88},{16,96},{24,104},{32,112},{40,120},{1,81},{9,89},{17... | collective-permute-start | bytes 393224 | tf_op jit(solution)/shard_map/ppermute | solution.py:155
  27.8 14.3 %collective-permute-start.6 = (bf16[256,256]{1,0:T(8,128)(2,1)S(1)}, bf16[256,256]{1,0:T(8,128)(2,1)S(1)}, u32[]{:S(2)}, u32[]{:S(2)}) collective-permute-start(bf16[256,256]{1,0:T(8,128)(2,1)S(1)} %constant_dynamic-update-slice_fusion), channel_id=1, source_target_pairs={{0,72},{8,80},{16,88},{24,96},{32,104},{40,112},{48,120},{1,73},{9... | collective-permute-start | bytes 393224 | tf_op jit(solution)/shard_map/ppermute | solution.py:155
  29.1 19.3 %collective-permute-start.7 = (bf16[256,256]{1,0:T(8,128)(2,1)S(1)}, bf16[256,256]{1,0:T(8,128)(2,1)S(1)}, u32[]{:S(2)}, u32[]{:S(2)}) collective-permute-start(bf16[256,256]{1,0:T(8,128)(2,1)S(1)} %constant_dynamic-update-slice_fusion), channel_id=1, source_target_pairs={{0,64},{8,72},{16,80},{24,88},{32,96},{40,104},{48,112},{56,120},{... | collective-permute-start | bytes 393224 | tf_op jit(solution)/shard_map/ppermute | solution.py:155
  30.5 19.3 %collective-permute-start.8 = (bf16[256,256]{1,0:T(8,128)(2,1)S(1)}, bf16[256,256]{1,0:T(8,128)(2,1)S(1)}, u32[]{:S(2)}, u32[]{:S(2)}) collective-permute-start(bf16[256,256]{1,0:T(8,128)(2,1)S(1)} %constant_dynamic-update-slice_fusion), channel_id=1, source_target_pairs={{0,56},{8,64},{16,72},{24,80},{32,88},{40,96},{48,104},{56,112},{6... | collective-permute-start | bytes 393224 | tf_op jit(solution)/shard_map/ppermute | solution.py:155
  31.8 22.8 %collective-permute-start.9 = (bf16[256,256]{1,0:T(8,128)(2,1)S(1)}, bf16[256,256]{1,0:T(8,128)(2,1)S(1)}, u32[]{:S(2)}, u32[]{:S(2)}) collective-permute-start(bf16[256,256]{1,0:T(8,128)(2,1)S(1)} %constant_dynamic-update-slice_fusion), channel_id=1, source_target_pairs={{0,48},{8,56},{16,64},{24,72},{32,80},{40,88},{48,96},{56,104},{64... | collective-permute-start | bytes 393224 | tf_op jit(solution)/shard_map/ppermute | solution.py:155
  36.9 20.2 %collective-permute-start.10 = (bf16[256,256]{1,0:T(8,128)(2,1)S(1)}, bf16[256,256]{1,0:T(8,128)(2,1)S(1)}, u32[]{:S(2)}, u32[]{:S(2)}) collective-permute-start(bf16[256,256]{1,0:T(8,128)(2,1)S(1)} %constant_dynamic-update-slice_fusion), channel_id=1, source_target_pairs={{0,40},{8,48},{16,56},{24,64},{32,72},{40,80},{48,88},{56,96},{64,... | collective-permute-start | bytes 393224 | tf_op jit(solution)/shard_map/ppermute | solution.py:155
  42.1 17.6 %collective-permute-start.11 = (bf16[256,256]{1,0:T(8,128)(2,1)S(1)}, bf16[256,256]{1,0:T(8,128)(2,1)S(1)}, u32[]{:S(2)}, u32[]{:S(2)}) collective-permute-start(bf16[256,256]{1,0:T(8,128)(2,1)S(1)} %constant_dynamic-update-slice_fusion), channel_id=1, source_target_pairs={{0,32},{8,40},{16,48},{24,56},{32,64},{40,72},{48,80},{56,88},{64,... | collective-permute-start | bytes 393224 | tf_op jit(solution)/shard_map/ppermute | solution.py:155
  48.4 11.4 %collective-permute-start.12 = (bf16[256,256]{1,0:T(8,128)(2,1)S(1)}, bf16[256,256]{1,0:T(8,128)(2,1)S(1)}, u32[]{:S(2)}, u32[]{:S(2)}) collective-permute-start(bf16[256,256]{1,0:T(8,128)(2,1)S(1)} %constant_dynamic-update-slice_fusion), channel_id=1, source_target_pairs={{0,24},{8,32},{16,40},{24,48},{32,56},{40,64},{48,72},{56,80},{64,... | collective-permute-start | bytes 393224 | tf_op jit(solution)/shard_map/ppermute | solution.py:155
  49.8 10.1 %collective-permute-start.13 = (bf16[256,256]{1,0:T(8,128)(2,1)S(1)}, bf16[256,256]{1,0:T(8,128)(2,1)S(1)}, u32[]{:S(2)}, u32[]{:S(2)}) collective-permute-start(bf16[256,256]{1,0:T(8,128)(2,1)S(1)} %constant_dynamic-update-slice_fusion), channel_id=1, source_target_pairs={{0,16},{8,24},{16,32},{24,40},{32,48},{40,56},{48,64},{56,72},{64,... | collective-permute-start | bytes 393224 | tf_op jit(solution)/shard_map/ppermute | solution.py:155
  54.6 5.3 %collective-permute-start.14 = (bf16[256,256]{1,0:T(8,128)(2,1)S(1)}, bf16[256,256]{1,0:T(8,128)(2,1)S(1)}, u32[]{:S(2)}, u32[]{:S(2)}) collective-permute-start(bf16[256,256]{1,0:T(8,128)(2,1)S(1)} %constant_dynamic-update-slice_fusion), channel_id=1, source_target_pairs={{0,8},{8,16},{16,24},{24,32},{32,40},{40,48},{48,56},{56,64},{64,7... | collective-permute-start | bytes 393224 | tf_op jit(solution)/shard_map/ppermute | solution.py:155
  57.0 92.2 %collective-permute-start.15 = (f32[256,256]{1,0:T(8,128)S(1)}, f32[256,256]{1,0:T(8,128)}, u32[]{:S(2)}, u32[]{:S(2)}) collective-permute-start(f32[256,256]{1,0:T(8,128)S(1)} %fusion.38), channel_id=1, source_target_pairs={{0,1},{1,0},{2,3},{3,2},{4,5},{5,4},{6,7},{7,6},{8,9},{9,8},{10,11... | collective-permute-start | bytes 786440 | tf_op jit(solution)/shard_map/ppermute | solution.py:183
  66.7 45.5 %copy-start.1 = (f32[256,8,128]{2,0,1:T(8,128)}, f32[256,8,128]{2,0,1:T(8,128)S(1)}, u32[]{:S(2)}) copy-start(f32[256,8,128]{2,0,1:T(8,128)S(1)} %get-tuple-element.91) | copy-start | bytes 3145732
  112.2 1.0 copy-start.3
  122.4 54.8 %all-to-all-start = ((bf16[16,256,256]{2,1,0:T(8,128)(2,1)}), bf16[16,256,256]{2,1,0:T(8,128)(2,1)S(1)}, u32[]{:S(2)}, u32[]{:S(2)}) async-start(bf16[16,256,256]{2,1,0:T(8,128)(2,1)} %bitcast.131), calls=%async_computation | async-start | bytes 4194304 | tf_op jit(solution)/shard_map/all_to_all | solution.py:174
  150.2 8.0 %collective-permute-start.16 = (f32[256,256]{1,0:T(8,128)S(1)}, f32[256,256]{1,0:T(8,128)S(1)}, u32[]{:S(2)}, u32[]{:S(2)}) collective-permute-start(f32[256,256]{1,0:T(8,128)S(1)} %add.106), channel_id=1, source_target_pairs={{0,2},{1,3},{2,0},{3,1},{4,6},{5,7},{6,4},{7,5},{8,10},{9,11},{10,... | collective-permute-start | bytes 786440 | tf_op jit(solution)/shard_map/ppermute | solution.py:183
  158.2 8.8 %collective-permute-start.17 = (f32[256,256]{1,0:T(8,128)S(1)}, f32[256,256]{1,0:T(8,128)S(1)}, u32[]{:S(2)}, u32[]{:S(2)}) collective-permute-start(f32[256,256]{1,0:T(8,128)S(1)} %add.107), channel_id=1, source_target_pairs={{0,4},{1,5},{2,6},{3,7},{4,0},{5,1},{6,2},{7,3},{8,12},{9,13},{10,... | collective-permute-start | bytes 786440 | tf_op jit(solution)/shard_map/ppermute | solution.py:183
  168.7 5.2 %copy-start.2 = (f32[256,8,128]{2,0,1:T(8,128)S(1)}, f32[256,8,128]{2,0,1:T(8,128)}, u32[]{:S(2)}) copy-start(f32[256,8,128]{2,0,1:T(8,128)} %copy-done.1) | copy-start | bytes 3145732
Sparse Core Ops, SparseCore 0:
  21.9 78.6 all-gather.1

commit v17 on v16

--- a/solution.py
+++ b/solution.py
@@ -126,6 +126,36 @@
     )(scalars, query_rows, grad_attended, keys_all, values_all, log_total.T, row_dot.T)
 
 
+def weighted_matmul(gathered, loss_weight, out_weight, tile=256, chunk=1024):
+    rows, depth = gathered.shape
+    width = out_weight.shape[0]
+
+    def kernel(x_ref, lw_ref, w_ref, o_ref, xw):
+        @pl.when(pl.program_id(0) == 0)
+        def _():
+            for c in range(depth // chunk):
+                part = slice(c * chunk, (c + 1) * chunk)
+                xw[:, part] = (x_ref[:, part].astype(jnp.float32) * lw_ref[...]).astype(xw.dtype)
+
+        o_ref[...] = lax.dot_general(
+            xw[...], w_ref[...], (((1,), (1,)), ((), ())), preferred_element_type=jnp.float32
+        ).astype(o_ref.dtype)
+
+    return pl.pallas_call(
+        kernel,
+        grid=(width // tile,),
+        in_specs=[
+            pl.BlockSpec((rows, depth), lambda n: (0, 0)),
+            pl.BlockSpec((rows, 1), lambda n: (0, 0)),
+            pl.BlockSpec((tile, depth), lambda n: (n, 0)),
+        ],
+        out_specs=pl.BlockSpec((rows, tile), lambda n: (0, n)),
+        out_shape=jax.ShapeDtypeStruct((rows, width), jnp.bfloat16),
+        scratch_shapes=[pltpu.VMEM((rows, depth), jnp.bfloat16)],
+        compiler_params=pltpu.CompilerParams(dimension_semantics=("arbitrary",)),
+    )(gathered, loss_weight[:, None], out_weight)
+
+
 def butterfly_gather(value, axis_name):
     size = lax.axis_size(axis_name)
     own = lax.axis_index(axis_name)
@@ -217,10 +247,8 @@
         ),
         "head",
     )
-    piece_part = (
-        lax.all_gather(grad_out, "head", axis=1, tiled=True).astype(jnp.float32)
-        * loss_weight[:, None]
-    ).astype(jnp.bfloat16)
+    gathered_out = lax.all_gather(grad_out, "head", axis=1, tiled=True)
+    piece_part = (gathered_out.astype(jnp.float32) * loss_weight[:, None]).astype(jnp.bfloat16)
     pair_all = causal_gather(jnp.concatenate([key_rows, value_rows], axis=1), "ctx")
     kv_width = key_rows.shape[1]
     keys_all, values_all = (pair_all[:, :kv_width], pair_all[:, kv_width:])
@@ -275,11 +303,8 @@
         rows, local_groups * group_size * head_dim
     )
     log_totals, attended = (log_totals, attended_part)
-    grad_sum = lax.dot_general(
-        piece_part, out_weight, (((1,), (1,)), ((), ())), preferred_element_type=jnp.float32
-    )
-    grad_sum, squares_out = (grad_sum, gram_squares(piece_part, attended, head_dim))
-    grad_attended, squares_out = (grad_sum.astype(jnp.bfloat16), squares_out)
+    grad_attended = weighted_matmul(gathered_out, loss_weight, out_weight)
+    squares_out = gram_squares(piece_part, attended, head_dim)
     backward_buffer = buffer
     rows = query_rows.shape[0]
     backward_row_pos = first_row + jnp.arange(rows, dtype=jnp.int32)

time: 186 us -> 187 us (level)
  matrix products: 22.9 us -> 11.3 us
  Pallas kernels: 9.24 us -> 20.5 us
    dot_general x1 -> x0, matrix products: 11.6 us -> none  [body(): lax.dot_general(piece_part, out_weight, (((1,), (1,)), ((), ())), preferr...]
    pallas_call x0 -> x1, Pallas kernels: none -> 11.2 us  [weighted_matmul(): pl.pallas_call(kernel, grid=(width // tile,), in_specs=[pl.BlockSpec((row...]
    unnamed x42 -> x40, local copies, waits for them, and re-layouts: 4.33 us -> 4.33 us
  transfers between devices with their start and end apart: 20 -> 20, of which waited for: 5 -> 5; matrix products, arithmetic and copies ran while one was open for 18% -> 13% of each run, Pallas kernels for 5% -> 11%
where the time goes in v17:
time: 187 us; the launch traced here: 186 us
  starting transfers between devices  75.5 us (40%)
  waiting for transfers between devices  48.7 us (26%)
  Pallas kernels  20.5 us (11%)
  between operations  14.6 us (8%)
  matrix products  11.3 us (6%)
  local copies, waits for them, and re-layouts  8.08 us (4%)
  other arithmetic  6.82 us (4%)
    ppermute x15, starting transfers between devices, causal_gather(): received.append(lax.ppermute(value, axis_name, pairs))  41.9 us
    all_gather x1, waiting for transfers between devices, body(): gathered_out = lax.all_gather(grad_out, 'head', axis=1, tiled=True)  33.9 us
    all_to_all x1, starting transfers between devices, exchange_reduce(): arrived = lax.all_to_all(parts, axis_name, 0, 0, tiled=True)  26.9 us
    ppermute x3, waiting for transfers between devices, butterfly_sum(): value = value + lax.ppermute(value, axis_name, pairs)  12.5 us
    pallas_call x1, Pallas kernels, weighted_matmul(): pl.pallas_call(kernel, grid=(width // tile,), in_specs=[pl.BlockSpec((row...  11.2 us
    pallas_call x1, Pallas kernels, flash_backward(): pl.pallas_call(kernel, grid_spec=grid_spec, out_shape=[jax.ShapeDtypeStru...  9.27 us
    ppermute x3, starting transfers between devices, butterfly_sum(): value = value + lax.ppermute(value, axis_name, pairs)  6.67 us
    dot_general x1, matrix products, gram_squares(): lax.dot_general(left_side, left_side, (((1,), (1,)), ((), ())), preferred...  5.15 us
  transfers between devices with their start and end apart: 20, of which 5 were waited for; matrix products, arithmetic and copies ran while one was open for 13% of the time, Pallas kernels for 11%

profile of v17, /device:TPU:1, one launch (start us, length us, event | category | flops | bytes accessed | tf_op | source)
XLA Modules:
  0.0 185.8 jit_solution(8360919307819934095)
XLA Ops:
  9.7 8.1 %collective-permute-start.1 = (bf16[256,256]{1,0:T(8,128)(2,1)S(1)}, bf16[256,256]{1,0:T(8,128)(2,1)S(1)}, u32[]{:S(2)}, u32[]{:S(2)}) collective-permute-start(bf16[256,256]{1,0:T(8,128)(2,1)S(1)} %constant_dynamic-update-slice_fusion), channel_id=1, source_target_pairs={{0,112},{8,120},{1,113},{9,121},{2,114},{10,122},{3,115},{11,123},... | collective-permute-start | bytes 393224 | tf_op jit(solution)/shard_map/ppermute | solution.py:185
  17.8 1.3 collective-permute-start.2
  19.1 1.3 collective-permute-start.3
  23.9 1.9 %copy.25 = bf16[32,8,8,128]{3,2,1,0:T(8,128)(2,1)} copy(bf16[32,8,8,128]{3,1,2,0:T(8,128)(2,1)} %bitcast.130) | data formatting | bytes 1048576
  32.6 4.2 %collective-permute-start.9 = (bf16[256,256]{1,0:T(8,128)(2,1)S(1)}, bf16[256,256]{1,0:T(8,128)(2,1)S(1)}, u32[]{:S(2)}, u32[]{:S(2)}) collective-permute-start(bf16[256,256]{1,0:T(8,128)(2,1)S(1)} %constant_dynamic-update-slice_fusion), channel_id=1, source_target_pairs={{0,48},{8,56},{16,64},{24,72},{32,80},{40,88},{48,96},{56,104},{64... | collective-permute-start | bytes 393224 | tf_op jit(solution)/shard_map/ppermute | solution.py:185
  36.9 5.0 %collective-permute-start.10 = (bf16[256,256]{1,0:T(8,128)(2,1)S(1)}, bf16[256,256]{1,0:T(8,128)(2,1)S(1)}, u32[]{:S(2)}, u32[]{:S(2)}) collective-permute-start(bf16[256,256]{1,0:T(8,128)(2,1)S(1)} %constant_dynamic-update-slice_fusion), channel_id=1, source_target_pairs={{0,40},{8,48},{16,56},{24,64},{32,72},{40,80},{48,88},{56,96},{64,... | collective-permute-start | bytes 393224 | tf_op jit(solution)/shard_map/ppermute | solution.py:185
  42.1 6.3 %collective-permute-start.11 = (bf16[256,256]{1,0:T(8,128)(2,1)S(1)}, bf16[256,256]{1,0:T(8,128)(2,1)S(1)}, u32[]{:S(2)}, u32[]{:S(2)}) collective-permute-start(bf16[256,256]{1,0:T(8,128)(2,1)S(1)} %constant_dynamic-update-slice_fusion), channel_id=1, source_target_pairs={{0,32},{8,40},{16,48},{24,56},{32,64},{40,72},{48,80},{56,88},{64,... | collective-permute-start | bytes 393224 | tf_op jit(solution)/shard_map/ppermute | solution.py:185
  49.8 4.8 %collective-permute-start.13 = (bf16[256,256]{1,0:T(8,128)(2,1)S(1)}, bf16[256,256]{1,0:T(8,128)(2,1)S(1)}, u32[]{:S(2)}, u32[]{:S(2)}) collective-permute-start(bf16[256,256]{1,0:T(8,128)(2,1)S(1)} %constant_dynamic-update-slice_fusion), channel_id=1, source_target_pairs={{0,16},{8,24},{16,32},{24,40},{32,48},{40,56},{48,64},{56,72},{64,... | collective-permute-start | bytes 393224 | tf_op jit(solution)/shard_map/ppermute | solution.py:185
  54.6 2.4 %collective-permute-start.14 = (bf16[256,256]{1,0:T(8,128)(2,1)S(1)}, bf16[256,256]{1,0:T(8,128)(2,1)S(1)}, u32[]{:S(2)}, u32[]{:S(2)}) collective-permute-start(bf16[256,256]{1,0:T(8,128)(2,1)S(1)} %constant_dynamic-update-slice_fusion), channel_id=1, source_target_pairs={{0,8},{8,16},{16,24},{24,32},{32,40},{40,48},{48,56},{56,64},{64,7... | collective-permute-start | bytes 393224 | tf_op jit(solution)/shard_map/ppermute | solution.py:185
  57.0 2.7 %collective-permute-start.15 = (f32[256,256]{1,0:T(8,128)S(1)}, f32[256,256]{1,0:T(8,128)}, u32[]{:S(2)}, u32[]{:S(2)}) collective-permute-start(f32[256,256]{1,0:T(8,128)S(1)} %fusion.37), channel_id=1, source_target_pairs={{0,1},{1,0},{2,3},{3,2},{4,5},{5,4},{6,7},{7,6},{8,9},{9,8},{10,11... | collective-permute-start | bytes 786440 | tf_op jit(solution)/shard_map/ppermute | solution.py:213
  61.5 1.9 %while.24 = (s32[]{:T(128)}, f32[256,8]{0,1:T(8,128)S(1)}, f32[256,8]{0,1:T(8,128)S(1)}, s32[]{:T(128)}, bf16[4096,128]{1,0:T(8,128)(2,1)S(1)}, /*index=5*/bf16[...) while((s32[]{:T(128)}, f32[256,8]{0,1:T(8,128)S(1)}, ...), condition=%wide.region_3.4_spmd.clone, body=%wide.region_0.3_spmd.clone.sunk | while | flops 275911424 | bytes 9549991 | solution.py:285
  63.5 3.2 %while.25 = (s32[]{:T(128)}, f32[256,8,128]{2,0,1:T(8,128)S(1)}, s32[]{:T(128)}, bf16[4096,128]{1,0:T(8,128)(2,1)S(1)}, bf16[256,8,128]{2,1,0:T(8,128)(2,1)}, /*...) while((s32[]{:T(128)}, f32[256,8,128]{2,0,1:T(8,128)S(1)}, ...), condition=%wide.region_5.6_spmd.clone, body=%wide.region_4.5_spmd.clone.sunk | while | flops 541459200 | bytes 3161259 | solution.py:297
  63.7 2.8 %fusion.54 = f32[256,8,128]{2,0,1:T(8,128)S(1)} fusion(f32[256,8,128]{2,0,1:T(8,128)S(1)} %get-tuple-element.326, f32[256,8]{0,1:T(8,128)S(1)} %get-tuple-element.342, pred[256,512]{1,0:T(8,128)(4,1)S(1)} %broadcast_compare_fusion.5, bf16[256,8,128]{2,1,0:T(8,128)(2,1)} %get-tuple-element.341, bf16[4096,128]{1,0:T(8,128)(2,1)} %get-tuple-element.343, ...), kind=kOutput, calls=%fused_computation.18.clone.1 | convolution fusion | flops 541327360 | bytes 3023872 | tf_op jit(solution)/shard_map/while/body/tgk,kd->tgd/dot_general | solution.py:293
  66.7 33.9 %all-gather.2.cloned.1.call-done.x_ref = bf16[256,8192]{1,0:T(8,128)(2,1)} async-done(((bf16[256,1024]{1,0:T(8,128)(2,1)}), bf16[256,8192]{1,0:T(8,128)(2,1)}) %all-gather.2.cloned.1.call-update) | async-done | bytes 4194320 | tf_op jit(solution)/shard_map/all_gather | solution.py:250
  100.6 11.2 %shard_map.110.do_ref = bf16[256,1024]{1,0:T(8,128)(2,1)} custom-call(bf16[256,8192]{1,0:T(8,128)(2,1)} %all-gather.2.cloned.1.call-done.x_ref, f32[256,1]{1,0:T(8,128)} %copy.16.lw_ref, bf16[1024,8192]{1,0:T(8,128)(2,1)} %w_ref.1), custom_call_target="tpu_custom_call" | custom-call | tf_op jit(solution)/shard_map/pallas_call | solution.py:144
  111.8 2.0 %fusion.28 = f32[256,8]{0,1:T(8,128)} fusion(f32[256,8,128]{2,0,1:T(8,128)S(1)} %get-tuple-element.91, bf16[256,1024]{1,0:T(8,128)(2,1)} %shard_map.110.do_ref), kind=kLoop, calls=%fused_computation.36 | loop fusion | flops 1308672 | bytes 1581056 | tf_op jit(solution)/shard_map/reduce_sum | solution.py:319
  113.8 9.3 %shard_map.111 = (bf16[256,1024]{1,0:T(8,128)(2,1)}, bf16[4096,256]{1,0:T(8,128)(2,1)}) custom-call(s32[2]{0:T(128)} %pad_add_fusion.scalar_ref, bf16[256,1024]{1,0:T(8,128)(2,1)} %q_ref.1, bf16[256,1024]{1,0:T(8,128)(2,1)} %shard_map.110.do_ref, bf16[4096,128]{1,0:T(8,128)(2,1)S(1)} %get-tuple-element.352, bf16[4096,128]{1,0:T(8,128)(2,1)} %get-tuple-element.353, ...), custom_call_target="tpu_custom_call" | custom-call | tf_op jit(solution)/shard_map/pallas_call | solution.py:118
  123.1 26.9 %all-to-all-start = ((bf16[16,256,256]{2,1,0:T(8,128)(2,1)}), bf16[16,256,256]{2,1,0:T(8,128)(2,1)S(1)}, u32[]{:S(2)}, u32[]{:S(2)}) async-start(bf16[16,256,256]{2,1,0:T(8,128)(2,1)} %bitcast.131), calls=%async_computation | async-start | bytes 4194304 | tf_op jit(solution)/shard_map/all_to_all | solution.py:204
  152.2 6.7 %collective-permute-done.16 = f32[256,256]{1,0:T(8,128)S(1)} collective-permute-done((f32[256,256]{1,0:T(8,128)S(1)}, f32[256,256]{1,0:T(8,128)S(1)}, u32[]{:S(2)}, u32[]{:S(2)}) %collective-permute-start.16) | collective-permute-done | bytes 262176 | tf_op jit(solution)/shard_map/ppermute | solution.py:213
  159.0 2.7 %collective-permute-start.17 = (f32[256,256]{1,0:T(8,128)S(1)}, f32[256,256]{1,0:T(8,128)S(1)}, u32[]{:S(2)}, u32[]{:S(2)}) collective-permute-start(f32[256,256]{1,0:T(8,128)S(1)} %add.107), channel_id=1, source_target_pairs={{0,4},{1,5},{2,6},{3,7},{4,0},{5,1},{6,2},{7,3},{8,12},{9,13},{10,... | collective-permute-start | bytes 786440 | tf_op jit(solution)/shard_map/ppermute | solution.py:213
  161.7 5.8 %collective-permute-done.17 = f32[256,256]{1,0:T(8,128)S(1)} collective-permute-done((f32[256,256]{1,0:T(8,128)S(1)}, f32[256,256]{1,0:T(8,128)S(1)}, u32[]{:S(2)}, u32[]{:S(2)}) %collective-permute-start.17) | collective-permute-done | bytes 262176 | tf_op jit(solution)/shard_map/ppermute | solution.py:213
  167.6 1.7 multiply_reduce_fusion.1
  169.3 5.1 %fusion.26 = f32[256,256]{1,0:T(8,128)S(1)} fusion(bf16[256,8192]{1,0:T(8,128)(2,1)} %all-gather.2.cloned.1.call-done.x_ref, f32[256]{0:T(256)S(1)} %convert_add_fusion), kind=kOutput, calls=%fused_computation.31 | convolution fusion | flops 1080033280 | bytes 4457472 | tf_op jit(solution)/shard_map/dot_general | solution.py:228
  176.0 2.0 %all-to-all-done = bf16[16,256,256]{2,1,0:T(8,128)(2,1)S(1)} async-done(((bf16[16,256,256]{2,1,0:T(8,128)(2,1)}), bf16[16,256,256]{2,1,0:T(8,128)(2,1)S(1)}, u32[]{:S(2)}, u32[]{:S(2)}) %all-to-all-start) | async-done | bytes 2097184 | tf_op jit(solution)/shard_map/all_to_all | solution.py:204
  (96 shorter events, 22.7 us)
Async XLA Ops:
  7.2 15.7 %copy-start = (bf16[256,1024]{1,0:T(8,128)(2,1)S(1)}, bf16[256,1024]{1,0:T(8,128)(2,1)}, u32[]{:S(2)}) copy-start(bf16[256,1024]{1,0:T(8,128)(2,1)} %param.11) | copy-start | bytes 1572868
  7.2 93.4 %all-gather.2.cloned.1.call-start = ((), (), s32[]{:S(2)}) async-start(), calls=%async_computation.1 | async-start | bytes 4718592 | tf_op jit(solution)/shard_map/all_gather | solution.py:250
  9.0 18.3 %collective-permute-start = (bf16[256,256]{1,0:T(8,128)(2,1)S(1)}, bf16[256,256]{1,0:T(8,128)(2,1)S(1)}, u32[]{:S(2)}, u32[]{:S(2)}) collective-permute-start(bf16[256,256]{1,0:T(8,128)(2,1)S(1)} %constant_dynamic-update-slice_fusion), channel_id=1, source_target_pairs={{0,120},{1,121},{2,122},{3,123},{4,124},{5,125},{6,126},{7,127}} | collective-permute-start | bytes 393224 | tf_op jit(solution)/shard_map/ppermute | solution.py:185
  9.7 18.9 %collective-permute-start.1 = (bf16[256,256]{1,0:T(8,128)(2,1)S(1)}, bf16[256,256]{1,0:T(8,128)(2,1)S(1)}, u32[]{:S(2)}, u32[]{:S(2)}) collective-permute-start(bf16[256,256]{1,0:T(8,128)(2,1)S(1)} %constant_dynamic-update-slice_fusion), channel_id=1, source_target_pairs={{0,112},{8,120},{1,113},{9,121},{2,114},{10,122},{3,115},{11,123},... | collective-permute-start | bytes 393224 | tf_op jit(solution)/shard_map/ppermute | solution.py:185
  17.8 12.1 %collective-permute-start.2 = (bf16[256,256]{1,0:T(8,128)(2,1)S(1)}, bf16[256,256]{1,0:T(8,128)(2,1)S(1)}, u32[]{:S(2)}, u32[]{:S(2)}) collective-permute-start(bf16[256,256]{1,0:T(8,128)(2,1)S(1)} %constant_dynamic-update-slice_fusion), channel_id=1, source_target_pairs={{0,104},{8,112},{16,120},{1,105},{9,113},{17,121},{2,106},{10,114}... | collective-permute-start | bytes 393224 | tf_op jit(solution)/shard_map/ppermute | solution.py:185
  19.1 12.1 %collective-permute-start.3 = (bf16[256,256]{1,0:T(8,128)(2,1)S(1)}, bf16[256,256]{1,0:T(8,128)(2,1)S(1)}, u32[]{:S(2)}, u32[]{:S(2)}) collective-permute-start(bf16[256,256]{1,0:T(8,128)(2,1)S(1)} %constant_dynamic-update-slice_fusion), channel_id=1, source_target_pairs={{0,96},{8,104},{16,112},{24,120},{1,97},{9,105},{17,113},{25,121},... | collective-permute-start | bytes 393224 | tf_op jit(solution)/shard_map/ppermute | solution.py:185
  20.4 12.2 %collective-permute-start.4 = (bf16[256,256]{1,0:T(8,128)(2,1)S(1)}, bf16[256,256]{1,0:T(8,128)(2,1)S(1)}, u32[]{:S(2)}, u32[]{:S(2)}) collective-permute-start(bf16[256,256]{1,0:T(8,128)(2,1)S(1)} %constant_dynamic-update-slice_fusion), channel_id=1, source_target_pairs={{0,88},{8,96},{16,104},{24,112},{32,120},{1,89},{9,97},{17,105},{2... | collective-permute-start | bytes 393224 | tf_op jit(solution)/shard_map/ppermute | solution.py:185
  27.3 9.6 %collective-permute-start.5 = (bf16[256,256]{1,0:T(8,128)(2,1)S(1)}, bf16[256,256]{1,0:T(8,128)(2,1)S(1)}, u32[]{:S(2)}, u32[]{:S(2)}) collective-permute-start(bf16[256,256]{1,0:T(8,128)(2,1)S(1)} %constant_dynamic-update-slice_fusion), channel_id=1, source_target_pairs={{0,80},{8,88},{16,96},{24,104},{32,112},{40,120},{1,81},{9,89},{17... | collective-permute-start | bytes 393224 | tf_op jit(solution)/shard_map/ppermute | solution.py:185
  28.6 13.5 %collective-permute-start.6 = (bf16[256,256]{1,0:T(8,128)(2,1)S(1)}, bf16[256,256]{1,0:T(8,128)(2,1)S(1)}, u32[]{:S(2)}, u32[]{:S(2)}) collective-permute-start(bf16[256,256]{1,0:T(8,128)(2,1)S(1)} %constant_dynamic-update-slice_fusion), channel_id=1, source_target_pairs={{0,72},{8,80},{16,88},{24,96},{32,104},{40,112},{48,120},{1,73},{9... | collective-permute-start | bytes 393224 | tf_op jit(solution)/shard_map/ppermute | solution.py:185
  29.9 18.5 %collective-permute-start.7 = (bf16[256,256]{1,0:T(8,128)(2,1)S(1)}, bf16[256,256]{1,0:T(8,128)(2,1)S(1)}, u32[]{:S(2)}, u32[]{:S(2)}) collective-permute-start(bf16[256,256]{1,0:T(8,128)(2,1)S(1)} %constant_dynamic-update-slice_fusion), channel_id=1, source_target_pairs={{0,64},{8,72},{16,80},{24,88},{32,96},{40,104},{48,112},{56,120},{... | collective-permute-start | bytes 393224 | tf_op jit(solution)/shard_map/ppermute | solution.py:185
  31.3 18.5 %collective-permute-start.8 = (bf16[256,256]{1,0:T(8,128)(2,1)S(1)}, bf16[256,256]{1,0:T(8,128)(2,1)S(1)}, u32[]{:S(2)}, u32[]{:S(2)}) collective-permute-start(bf16[256,256]{1,0:T(8,128)(2,1)S(1)} %constant_dynamic-update-slice_fusion), channel_id=1, source_target_pairs={{0,56},{8,64},{16,72},{24,80},{32,88},{40,96},{48,104},{56,112},{6... | collective-permute-start | bytes 393224 | tf_op jit(solution)/shard_map/ppermute | solution.py:185
  32.6 22.0 %collective-permute-start.9 = (bf16[256,256]{1,0:T(8,128)(2,1)S(1)}, bf16[256,256]{1,0:T(8,128)(2,1)S(1)}, u32[]{:S(2)}, u32[]{:S(2)}) collective-permute-start(bf16[256,256]{1,0:T(8,128)(2,1)S(1)} %constant_dynamic-update-slice_fusion), channel_id=1, source_target_pairs={{0,48},{8,56},{16,64},{24,72},{32,80},{40,88},{48,96},{56,104},{64... | collective-permute-start | bytes 393224 | tf_op jit(solution)/shard_map/ppermute | solution.py:185
  36.9 20.2 %collective-permute-start.10 = (bf16[256,256]{1,0:T(8,128)(2,1)S(1)}, bf16[256,256]{1,0:T(8,128)(2,1)S(1)}, u32[]{:S(2)}, u32[]{:S(2)}) collective-permute-start(bf16[256,256]{1,0:T(8,128)(2,1)S(1)} %constant_dynamic-update-slice_fusion), channel_id=1, source_target_pairs={{0,40},{8,48},{16,56},{24,64},{32,72},{40,80},{48,88},{56,96},{64,... | collective-permute-start | bytes 393224 | tf_op jit(solution)/shard_map/ppermute | solution.py:185
  42.1 17.6 %collective-permute-start.11 = (bf16[256,256]{1,0:T(8,128)(2,1)S(1)}, bf16[256,256]{1,0:T(8,128)(2,1)S(1)}, u32[]{:S(2)}, u32[]{:S(2)}) collective-permute-start(bf16[256,256]{1,0:T(8,128)(2,1)S(1)} %constant_dynamic-update-slice_fusion), channel_id=1, source_target_pairs={{0,32},{8,40},{16,48},{24,56},{32,64},{40,72},{48,80},{56,88},{64,... | collective-permute-start | bytes 393224 | tf_op jit(solution)/shard_map/ppermute | solution.py:185
  48.4 11.4 %collective-permute-start.12 = (bf16[256,256]{1,0:T(8,128)(2,1)S(1)}, bf16[256,256]{1,0:T(8,128)(2,1)S(1)}, u32[]{:S(2)}, u32[]{:S(2)}) collective-permute-start(bf16[256,256]{1,0:T(8,128)(2,1)S(1)} %constant_dynamic-update-slice_fusion), channel_id=1, source_target_pairs={{0,24},{8,32},{16,40},{24,48},{32,56},{40,64},{48,72},{56,80},{64,... | collective-permute-start | bytes 393224 | tf_op jit(solution)/shard_map/ppermute | solution.py:185
  49.8 10.1 %collective-permute-start.13 = (bf16[256,256]{1,0:T(8,128)(2,1)S(1)}, bf16[256,256]{1,0:T(8,128)(2,1)S(1)}, u32[]{:S(2)}, u32[]{:S(2)}) collective-permute-start(bf16[256,256]{1,0:T(8,128)(2,1)S(1)} %constant_dynamic-update-slice_fusion), channel_id=1, source_target_pairs={{0,16},{8,24},{16,32},{24,40},{32,48},{40,56},{48,64},{56,72},{64,... | collective-permute-start | bytes 393224 | tf_op jit(solution)/shard_map/ppermute | solution.py:185
  54.6 5.3 %collective-permute-start.14 = (bf16[256,256]{1,0:T(8,128)(2,1)S(1)}, bf16[256,256]{1,0:T(8,128)(2,1)S(1)}, u32[]{:S(2)}, u32[]{:S(2)}) collective-permute-start(bf16[256,256]{1,0:T(8,128)(2,1)S(1)} %constant_dynamic-update-slice_fusion), channel_id=1, source_target_pairs={{0,8},{8,16},{16,24},{24,32},{32,40},{40,48},{48,56},{56,64},{64,7... | collective-permute-start | bytes 393224 | tf_op jit(solution)/shard_map/ppermute | solution.py:185
  57.0 93.0 %collective-permute-start.15 = (f32[256,256]{1,0:T(8,128)S(1)}, f32[256,256]{1,0:T(8,128)}, u32[]{:S(2)}, u32[]{:S(2)}) collective-permute-start(f32[256,256]{1,0:T(8,128)S(1)} %fusion.37), channel_id=1, source_target_pairs={{0,1},{1,0},{2,3},{3,2},{4,5},{5,4},{6,7},{7,6},{8,9},{9,8},{10,11... | collective-permute-start | bytes 786440 | tf_op jit(solution)/shard_map/ppermute | solution.py:213
  66.7 45.1 %copy-start.1 = (f32[256,8,128]{2,0,1:T(8,128)}, f32[256,8,128]{2,0,1:T(8,128)S(1)}, u32[]{:S(2)}) copy-start(f32[256,8,128]{2,0,1:T(8,128)S(1)} %get-tuple-element.91) | copy-start | bytes 3145732
  123.1 54.9 %all-to-all-start = ((bf16[16,256,256]{2,1,0:T(8,128)(2,1)}), bf16[16,256,256]{2,1,0:T(8,128)(2,1)S(1)}, u32[]{:S(2)}, u32[]{:S(2)}) async-start(bf16[16,256,256]{2,1,0:T(8,128)(2,1)} %bitcast.131), calls=%async_computation | async-start | bytes 4194304 | tf_op jit(solution)/shard_map/all_to_all | solution.py:204
  151.0 8.0 %collective-permute-start.16 = (f32[256,256]{1,0:T(8,128)S(1)}, f32[256,256]{1,0:T(8,128)S(1)}, u32[]{:S(2)}, u32[]{:S(2)}) collective-permute-start(f32[256,256]{1,0:T(8,128)S(1)} %add.106), channel_id=1, source_target_pairs={{0,2},{1,3},{2,0},{3,1},{4,6},{5,7},{6,4},{7,5},{8,10},{9,11},{10,... | collective-permute-start | bytes 786440 | tf_op jit(solution)/shard_map/ppermute | solution.py:213
  159.0 8.5 %collective-permute-start.17 = (f32[256,256]{1,0:T(8,128)S(1)}, f32[256,256]{1,0:T(8,128)S(1)}, u32[]{:S(2)}, u32[]{:S(2)}) collective-permute-start(f32[256,256]{1,0:T(8,128)S(1)} %add.107), channel_id=1, source_target_pairs={{0,4},{1,5},{2,6},{3,7},{4,0},{5,1},{6,2},{7,3},{8,12},{9,13},{10,... | collective-permute-start | bytes 786440 | tf_op jit(solution)/shard_map/ppermute | solution.py:213
  169.3 5.2 %copy-start.2 = (f32[256,8,128]{2,0,1:T(8,128)S(1)}, f32[256,8,128]{2,0,1:T(8,128)}, u32[]{:S(2)}) copy-start(f32[256,8,128]{2,0,1:T(8,128)} %copy-done.1) | copy-start | bytes 3145732
Sparse Core Ops, SparseCore 0:
  21.9 78.6 all-gather.1

commit v18 on v16

--- a/solution.py
+++ b/solution.py
@@ -303,7 +303,7 @@
         row_dot,
         first_row,
         head_dim,
-        block_rows,
+        2 * block_rows,
     )
     ctx_size = lax.axis_size("ctx")
     key_sums = exchange_reduce(

time: 186 us -> 180 us (0.968)
  starting transfers between devices: 76.6 us -> 69.8 us
    all_to_all x1, starting transfers between devices: 26.8 us -> 20 us  [exchange_reduce(): arrived = lax.all_to_all(parts, axis_name, 0, 0, tiled=True)]
  transfers between devices with their start and end apart: 20 -> 20, of which waited for: 5 -> 5; matrix products, arithmetic and copies ran while one was open for 18% -> 19% of each run, Pallas kernels for 5% -> 6%
where the time goes in v18:
time: 180 us
  starting transfers between devices  69.8 us (39%)
  waiting for transfers between devices  48.4 us (27%)
  matrix products  22.9 us (13%)
  between operations  14.6 us (8%)
  Pallas kernels  10.6 us (6%)
  local copies, waits for them, and re-layouts  7.28 us (4%)
  other arithmetic  5.81 us (3%)
    ppermute x15, starting transfers between devices, causal_gather(): received.append(lax.ppermute(value, axis_name, pairs))  42.7 us
    all_gather x1, waiting for transfers between devices, body(): lax.all_gather(grad_out, 'head', axis=1, tiled=True).astype(jnp.float32)  34.1 us
    all_to_all x1, starting transfers between devices, exchange_reduce(): arrived = lax.all_to_all(parts, axis_name, 0, 0, tiled=True)  20 us
    ppermute x3, waiting for transfers between devices, butterfly_sum(): value = value + lax.ppermute(value, axis_name, pairs)  12.3 us
    dot_general x1, matrix products, body(): lax.dot_general(piece_part, out_weight, (((1,), (1,)), ((), ())), preferr...  11.6 us
    pallas_call x1, Pallas kernels, flash_backward(): pl.pallas_call(kernel, grid_spec=grid_spec, out_shape=[jax.ShapeDtypeStru...  10.6 us
    ppermute x3, starting transfers between devices, butterfly_sum(): value = value + lax.ppermute(value, axis_name, pairs)  7.06 us
    dot_general x1, matrix products, gram_squares(): lax.dot_general(left_side, left_side, (((1,), (1,)), ((), ())), preferred...  5.15 us
  transfers between devices with their start and end apart: 20, of which 5 were waited for; matrix products, arithmetic and copies ran while one was open for 19% of the time, Pallas kernels for 6%

profile of v18, /device:TPU:1, one launch (start us, length us, event | category | flops | bytes accessed | tf_op | source)
XLA Modules:
  0.0 179.6 jit_solution(17061950757155798381)
XLA Ops:
  9.7 8.1 %collective-permute-start.1 = (bf16[256,256]{1,0:T(8,128)(2,1)S(1)}, bf16[256,256]{1,0:T(8,128)(2,1)S(1)}, u32[]{:S(2)}, u32[]{:S(2)}) collective-permute-start(bf16[256,256]{1,0:T(8,128)(2,1)S(1)} %constant_dynamic-update-slice_fusion), channel_id=1, source_target_pairs={{0,112},{8,120},{1,113},{9,121},{2,114},{10,122},{3,115},{11,123},... | collective-permute-start | bytes 393224 | tf_op jit(solution)/shard_map/ppermute | solution.py:155
  17.8 1.3 collective-permute-start.2
  19.1 1.3 collective-permute-start.3
  23.9 1.9 %copy.20 = bf16[32,8,8,128]{3,2,1,0:T(8,128)(2,1)} copy(bf16[32,8,8,128]{3,1,2,0:T(8,128)(2,1)} %bitcast.130) | data formatting | bytes 1048576
  31.8 5.0 %collective-permute-start.9 = (bf16[256,256]{1,0:T(8,128)(2,1)S(1)}, bf16[256,256]{1,0:T(8,128)(2,1)S(1)}, u32[]{:S(2)}, u32[]{:S(2)}) collective-permute-start(bf16[256,256]{1,0:T(8,128)(2,1)S(1)} %constant_dynamic-update-slice_fusion), channel_id=1, source_target_pairs={{0,48},{8,56},{16,64},{24,72},{32,80},{40,88},{48,96},{56,104},{64... | collective-permute-start | bytes 393224 | tf_op jit(solution)/shard_map/ppermute | solution.py:155
  36.9 5.0 %collective-permute-start.10 = (bf16[256,256]{1,0:T(8,128)(2,1)S(1)}, bf16[256,256]{1,0:T(8,128)(2,1)S(1)}, u32[]{:S(2)}, u32[]{:S(2)}) collective-permute-start(bf16[256,256]{1,0:T(8,128)(2,1)S(1)} %constant_dynamic-update-slice_fusion), channel_id=1, source_target_pairs={{0,40},{8,48},{16,56},{24,64},{32,72},{40,80},{48,88},{56,96},{64,... | collective-permute-start | bytes 393224 | tf_op jit(solution)/shard_map/ppermute | solution.py:155
  42.1 6.3 %collective-permute-start.11 = (bf16[256,256]{1,0:T(8,128)(2,1)S(1)}, bf16[256,256]{1,0:T(8,128)(2,1)S(1)}, u32[]{:S(2)}, u32[]{:S(2)}) collective-permute-start(bf16[256,256]{1,0:T(8,128)(2,1)S(1)} %constant_dynamic-update-slice_fusion), channel_id=1, source_target_pairs={{0,32},{8,40},{16,48},{24,56},{32,64},{40,72},{48,80},{56,88},{64,... | collective-permute-start | bytes 393224 | tf_op jit(solution)/shard_map/ppermute | solution.py:155
  49.8 4.8 %collective-permute-start.13 = (bf16[256,256]{1,0:T(8,128)(2,1)S(1)}, bf16[256,256]{1,0:T(8,128)(2,1)S(1)}, u32[]{:S(2)}, u32[]{:S(2)}) collective-permute-start(bf16[256,256]{1,0:T(8,128)(2,1)S(1)} %constant_dynamic-update-slice_fusion), channel_id=1, source_target_pairs={{0,16},{8,24},{16,32},{24,40},{32,48},{40,56},{48,64},{56,72},{64,... | collective-permute-start | bytes 393224 | tf_op jit(solution)/shard_map/ppermute | solution.py:155
  54.6 2.4 %collective-permute-start.14 = (bf16[256,256]{1,0:T(8,128)(2,1)S(1)}, bf16[256,256]{1,0:T(8,128)(2,1)S(1)}, u32[]{:S(2)}, u32[]{:S(2)}) collective-permute-start(bf16[256,256]{1,0:T(8,128)(2,1)S(1)} %constant_dynamic-update-slice_fusion), channel_id=1, source_target_pairs={{0,8},{8,16},{16,24},{24,32},{32,40},{40,48},{48,56},{56,64},{64,7... | collective-permute-start | bytes 393224 | tf_op jit(solution)/shard_map/ppermute | solution.py:155
  57.0 2.7 %collective-permute-start.15 = (f32[256,256]{1,0:T(8,128)S(1)}, f32[256,256]{1,0:T(8,128)}, u32[]{:S(2)}, u32[]{:S(2)}) collective-permute-start(f32[256,256]{1,0:T(8,128)S(1)} %fusion.38), channel_id=1, source_target_pairs={{0,1},{1,0},{2,3},{3,2},{4,5},{5,4},{6,7},{7,6},{8,9},{9,8},{10,11... | collective-permute-start | bytes 786440 | tf_op jit(solution)/shard_map/ppermute | solution.py:183
  61.5 1.9 %while.24 = (s32[]{:T(128)}, f32[256,8]{0,1:T(8,128)S(1)}, f32[256,8]{0,1:T(8,128)S(1)}, s32[]{:T(128)}, bf16[4096,128]{1,0:T(8,128)(2,1)S(1)}, /*index=5*/bf16[...) while((s32[]{:T(128)}, f32[256,8]{0,1:T(8,128)S(1)}, ...), condition=%wide.region_3.4_spmd.clone, body=%wide.region_0.3_spmd.clone.sunk | while | flops 275911424 | bytes 9549991 | solution.py:257
  63.5 3.0 %while.25 = (s32[]{:T(128)}, f32[256,8,128]{2,0,1:T(8,128)S(1)}, s32[]{:T(128)}, bf16[4096,128]{1,0:T(8,128)(2,1)S(1)}, bf16[256,8,128]{2,1,0:T(8,128)(2,1)}, /*...) while((s32[]{:T(128)}, f32[256,8,128]{2,0,1:T(8,128)S(1)}, ...), condition=%wide.region_5.6_spmd.clone, body=%wide.region_4.5_spmd.clone.sunk | while | flops 541459200 | bytes 3161259 | solution.py:269
  63.7 2.8 %fusion.56 = f32[256,8,128]{2,0,1:T(8,128)S(1)} fusion(f32[256,8,128]{2,0,1:T(8,128)S(1)} %get-tuple-element.319, f32[256,8]{0,1:T(8,128)S(1)} %get-tuple-element.335, pred[256,512]{1,0:T(8,128)(4,1)S(1)} %broadcast_compare_fusion.5, bf16[256,8,128]{2,1,0:T(8,128)(2,1)} %get-tuple-element.334, bf16[4096,128]{1,0:T(8,128)(2,1)} %get-tuple-element.336, ...), kind=kOutput, calls=%fused_computation.18.clone.1 | convolution fusion | flops 541327360 | bytes 3023872 | tf_op jit(solution)/shard_map/while/body/tgk,kd->tgd/dot_general | solution.py:265
  66.5 34.1 %all-gather.2.cloned.1.call-done = bf16[256,8192]{1,0:T(8,128)(2,1)} async-done(((bf16[256,1024]{1,0:T(8,128)(2,1)}), bf16[256,8192]{1,0:T(8,128)(2,1)}) %all-gather.2.cloned.1.call-update) | async-done | bytes 4194320 | tf_op jit(solution)/shard_map/all_gather | solution.py:221
  100.6 11.6 %fusion.28.do_ref = bf16[256,1024]{1,0:T(8,128)(2,1)S(1)} fusion(bf16[1024,8192]{1,0:T(8,128)(2,1)} %param.15, bf16[256,8192]{1,0:T(8,128)(2,1)} %all-gather.2.cloned.1.call-done, f32[256]{0:T(256)S(1)} %convert_add_fusion), kind=kOutput, calls=%fused_computation.35 | convolution fusion | flops 4301520896 | bytes 21496832 | tf_op jit(solution)/shard_map/dot_general | solution.py:278
  113.2 10.6 %shard_map.110 = (bf16[256,1024]{1,0:T(8,128)(2,1)}, bf16[4096,256]{1,0:T(8,128)(2,1)}) custom-call(s32[2]{0:T(128)} %pad_add_fusion.scalar_ref, bf16[256,1024]{1,0:T(8,128)(2,1)} %q_ref.1, bf16[256,1024]{1,0:T(8,128)(2,1)} %copy-done.3, bf16[4096,128]{1,0:T(8,128)(2,1)S(1)} %get-tuple-element.345, bf16[4096,128]{1,0:T(8,128)(2,1)} %get-tuple-element.346, ...), custom_call_target="tpu_custom_call" | custom-call | tf_op jit(solution)/shard_map/pallas_call | solution.py:118
  123.8 20.0 %all-to-all-start = ((bf16[16,256,256]{2,1,0:T(8,128)(2,1)}), bf16[16,256,256]{2,1,0:T(8,128)(2,1)S(1)}, u32[]{:S(2)}, u32[]{:S(2)}) async-start(bf16[16,256,256]{2,1,0:T(8,128)(2,1)} %bitcast.131), calls=%async_computation | async-start | bytes 4194304 | tf_op jit(solution)/shard_map/all_to_all | solution.py:174
  144.8 1.3 collective-permute-start.16
  146.1 6.6 %collective-permute-done.16 = f32[256,256]{1,0:T(8,128)S(1)} collective-permute-done((f32[256,256]{1,0:T(8,128)S(1)}, f32[256,256]{1,0:T(8,128)S(1)}, u32[]{:S(2)}, u32[]{:S(2)}) %collective-permute-start.16) | collective-permute-done | bytes 262176 | tf_op jit(solution)/shard_map/ppermute | solution.py:183
  152.8 3.0 %collective-permute-start.17 = (f32[256,256]{1,0:T(8,128)S(1)}, f32[256,256]{1,0:T(8,128)S(1)}, u32[]{:S(2)}, u32[]{:S(2)}) collective-permute-start(f32[256,256]{1,0:T(8,128)S(1)} %add.111), channel_id=1, source_target_pairs={{0,4},{1,5},{2,6},{3,7},{4,0},{5,1},{6,2},{7,3},{8,12},{9,13},{10,... | collective-permute-start | bytes 786440 | tf_op jit(solution)/shard_map/ppermute | solution.py:183
  155.8 5.7 %collective-permute-done.17 = f32[256,256]{1,0:T(8,128)S(1)} collective-permute-done((f32[256,256]{1,0:T(8,128)S(1)}, f32[256,256]{1,0:T(8,128)S(1)}, u32[]{:S(2)}, u32[]{:S(2)}) %collective-permute-start.17) | collective-permute-done | bytes 262176 | tf_op jit(solution)/shard_map/ppermute | solution.py:183
  161.6 1.7 multiply_reduce_fusion.1
  163.3 5.1 %fusion.26 = f32[256,256]{1,0:T(8,128)S(1)} fusion(bf16[256,8192]{1,0:T(8,128)(2,1)} %all-gather.2.cloned.1.call-done, f32[256]{0:T(256)S(1)} %convert_add_fusion), kind=kOutput, calls=%fused_computation.33 | convolution fusion | flops 1080033280 | bytes 4457472 | tf_op jit(solution)/shard_map/dot_general | solution.py:198
  170.1 1.7 all-to-all-done
  (97 shorter events, 21.6 us)
Async XLA Ops:
  7.2 15.7 %copy-start = (bf16[256,1024]{1,0:T(8,128)(2,1)S(1)}, bf16[256,1024]{1,0:T(8,128)(2,1)}, u32[]{:S(2)}) copy-start(bf16[256,1024]{1,0:T(8,128)(2,1)} %param.11) | copy-start | bytes 1572868
  7.2 93.4 %all-gather.2.cloned.1.call-start = ((), (), s32[]{:S(2)}) async-start(), calls=%async_computation.1 | async-start | bytes 4718592 | tf_op jit(solution)/shard_map/all_gather | solution.py:221
  9.0 17.5 %collective-permute-start = (bf16[256,256]{1,0:T(8,128)(2,1)S(1)}, bf16[256,256]{1,0:T(8,128)(2,1)S(1)}, u32[]{:S(2)}, u32[]{:S(2)}) collective-permute-start(bf16[256,256]{1,0:T(8,128)(2,1)S(1)} %constant_dynamic-update-slice_fusion), channel_id=1, source_target_pairs={{0,120},{1,121},{2,122},{3,123},{4,124},{5,125},{6,126},{7,127}} | collective-permute-start | bytes 393224 | tf_op jit(solution)/shard_map/ppermute | solution.py:155
  9.7 18.1 %collective-permute-start.1 = (bf16[256,256]{1,0:T(8,128)(2,1)S(1)}, bf16[256,256]{1,0:T(8,128)(2,1)S(1)}, u32[]{:S(2)}, u32[]{:S(2)}) collective-permute-start(bf16[256,256]{1,0:T(8,128)(2,1)S(1)} %constant_dynamic-update-slice_fusion), channel_id=1, source_target_pairs={{0,112},{8,120},{1,113},{9,121},{2,114},{10,122},{3,115},{11,123},... | collective-permute-start | bytes 393224 | tf_op jit(solution)/shard_map/ppermute | solution.py:155
  17.8 11.3 %collective-permute-start.2 = (bf16[256,256]{1,0:T(8,128)(2,1)S(1)}, bf16[256,256]{1,0:T(8,128)(2,1)S(1)}, u32[]{:S(2)}, u32[]{:S(2)}) collective-permute-start(bf16[256,256]{1,0:T(8,128)(2,1)S(1)} %constant_dynamic-update-slice_fusion), channel_id=1, source_target_pairs={{0,104},{8,112},{16,120},{1,105},{9,113},{17,121},{2,106},{10,114}... | collective-permute-start | bytes 393224 | tf_op jit(solution)/shard_map/ppermute | solution.py:155
  19.1 11.3 %collective-permute-start.3 = (bf16[256,256]{1,0:T(8,128)(2,1)S(1)}, bf16[256,256]{1,0:T(8,128)(2,1)S(1)}, u32[]{:S(2)}, u32[]{:S(2)}) collective-permute-start(bf16[256,256]{1,0:T(8,128)(2,1)S(1)} %constant_dynamic-update-slice_fusion), channel_id=1, source_target_pairs={{0,96},{8,104},{16,112},{24,120},{1,97},{9,105},{17,113},{25,121},... | collective-permute-start | bytes 393224 | tf_op jit(solution)/shard_map/ppermute | solution.py:155
  20.4 11.4 %collective-permute-start.4 = (bf16[256,256]{1,0:T(8,128)(2,1)S(1)}, bf16[256,256]{1,0:T(8,128)(2,1)S(1)}, u32[]{:S(2)}, u32[]{:S(2)}) collective-permute-start(bf16[256,256]{1,0:T(8,128)(2,1)S(1)} %constant_dynamic-update-slice_fusion), channel_id=1, source_target_pairs={{0,88},{8,96},{16,104},{24,112},{32,120},{1,89},{9,97},{17,105},{2... | collective-permute-start | bytes 393224 | tf_op jit(solution)/shard_map/ppermute | solution.py:155
  26.5 10.4 %collective-permute-start.5 = (bf16[256,256]{1,0:T(8,128)(2,1)S(1)}, bf16[256,256]{1,0:T(8,128)(2,1)S(1)}, u32[]{:S(2)}, u32[]{:S(2)}) collective-permute-start(bf16[256,256]{1,0:T(8,128)(2,1)S(1)} %constant_dynamic-update-slice_fusion), channel_id=1, source_target_pairs={{0,80},{8,88},{16,96},{24,104},{32,112},{40,120},{1,81},{9,89},{17... | collective-permute-start | bytes 393224 | tf_op jit(solution)/shard_map/ppermute | solution.py:155
  27.8 14.3 %collective-permute-start.6 = (bf16[256,256]{1,0:T(8,128)(2,1)S(1)}, bf16[256,256]{1,0:T(8,128)(2,1)S(1)}, u32[]{:S(2)}, u32[]{:S(2)}) collective-permute-start(bf16[256,256]{1,0:T(8,128)(2,1)S(1)} %constant_dynamic-update-slice_fusion), channel_id=1, source_target_pairs={{0,72},{8,80},{16,88},{24,96},{32,104},{40,112},{48,120},{1,73},{9... | collective-permute-start | bytes 393224 | tf_op jit(solution)/shard_map/ppermute | solution.py:155
  29.1 19.3 %collective-permute-start.7 = (bf16[256,256]{1,0:T(8,128)(2,1)S(1)}, bf16[256,256]{1,0:T(8,128)(2,1)S(1)}, u32[]{:S(2)}, u32[]{:S(2)}) collective-permute-start(bf16[256,256]{1,0:T(8,128)(2,1)S(1)} %constant_dynamic-update-slice_fusion), channel_id=1, source_target_pairs={{0,64},{8,72},{16,80},{24,88},{32,96},{40,104},{48,112},{56,120},{... | collective-permute-start | bytes 393224 | tf_op jit(solution)/shard_map/ppermute | solution.py:155
  30.5 19.3 %collective-permute-start.8 = (bf16[256,256]{1,0:T(8,128)(2,1)S(1)}, bf16[256,256]{1,0:T(8,128)(2,1)S(1)}, u32[]{:S(2)}, u32[]{:S(2)}) collective-permute-start(bf16[256,256]{1,0:T(8,128)(2,1)S(1)} %constant_dynamic-update-slice_fusion), channel_id=1, source_target_pairs={{0,56},{8,64},{16,72},{24,80},{32,88},{40,96},{48,104},{56,112},{6... | collective-permute-start | bytes 393224 | tf_op jit(solution)/shard_map/ppermute | solution.py:155
  31.8 22.8 %collective-permute-start.9 = (bf16[256,256]{1,0:T(8,128)(2,1)S(1)}, bf16[256,256]{1,0:T(8,128)(2,1)S(1)}, u32[]{:S(2)}, u32[]{:S(2)}) collective-permute-start(bf16[256,256]{1,0:T(8,128)(2,1)S(1)} %constant_dynamic-update-slice_fusion), channel_id=1, source_target_pairs={{0,48},{8,56},{16,64},{24,72},{32,80},{40,88},{48,96},{56,104},{64... | collective-permute-start | bytes 393224 | tf_op jit(solution)/shard_map/ppermute | solution.py:155
  36.9 20.2 %collective-permute-start.10 = (bf16[256,256]{1,0:T(8,128)(2,1)S(1)}, bf16[256,256]{1,0:T(8,128)(2,1)S(1)}, u32[]{:S(2)}, u32[]{:S(2)}) collective-permute-start(bf16[256,256]{1,0:T(8,128)(2,1)S(1)} %constant_dynamic-update-slice_fusion), channel_id=1, source_target_pairs={{0,40},{8,48},{16,56},{24,64},{32,72},{40,80},{48,88},{56,96},{64,... | collective-permute-start | bytes 393224 | tf_op jit(solution)/shard_map/ppermute | solution.py:155
  42.1 17.6 %collective-permute-start.11 = (bf16[256,256]{1,0:T(8,128)(2,1)S(1)}, bf16[256,256]{1,0:T(8,128)(2,1)S(1)}, u32[]{:S(2)}, u32[]{:S(2)}) collective-permute-start(bf16[256,256]{1,0:T(8,128)(2,1)S(1)} %constant_dynamic-update-slice_fusion), channel_id=1, source_target_pairs={{0,32},{8,40},{16,48},{24,56},{32,64},{40,72},{48,80},{56,88},{64,... | collective-permute-start | bytes 393224 | tf_op jit(solution)/shard_map/ppermute | solution.py:155
  48.4 11.4 %collective-permute-start.12 = (bf16[256,256]{1,0:T(8,128)(2,1)S(1)}, bf16[256,256]{1,0:T(8,128)(2,1)S(1)}, u32[]{:S(2)}, u32[]{:S(2)}) collective-permute-start(bf16[256,256]{1,0:T(8,128)(2,1)S(1)} %constant_dynamic-update-slice_fusion), channel_id=1, source_target_pairs={{0,24},{8,32},{16,40},{24,48},{32,56},{40,64},{48,72},{56,80},{64,... | collective-permute-start | bytes 393224 | tf_op jit(solution)/shard_map/ppermute | solution.py:155
  49.8 10.1 %collective-permute-start.13 = (bf16[256,256]{1,0:T(8,128)(2,1)S(1)}, bf16[256,256]{1,0:T(8,128)(2,1)S(1)}, u32[]{:S(2)}, u32[]{:S(2)}) collective-permute-start(bf16[256,256]{1,0:T(8,128)(2,1)S(1)} %constant_dynamic-update-slice_fusion), channel_id=1, source_target_pairs={{0,16},{8,24},{16,32},{24,40},{32,48},{40,56},{48,64},{56,72},{64,... | collective-permute-start | bytes 393224 | tf_op jit(solution)/shard_map/ppermute | solution.py:155
  54.6 5.3 %collective-permute-start.14 = (bf16[256,256]{1,0:T(8,128)(2,1)S(1)}, bf16[256,256]{1,0:T(8,128)(2,1)S(1)}, u32[]{:S(2)}, u32[]{:S(2)}) collective-permute-start(bf16[256,256]{1,0:T(8,128)(2,1)S(1)} %constant_dynamic-update-slice_fusion), channel_id=1, source_target_pairs={{0,8},{8,16},{16,24},{24,32},{32,40},{40,48},{48,56},{56,64},{64,7... | collective-permute-start | bytes 393224 | tf_op jit(solution)/shard_map/ppermute | solution.py:155
  57.0 86.8 %collective-permute-start.15 = (f32[256,256]{1,0:T(8,128)S(1)}, f32[256,256]{1,0:T(8,128)}, u32[]{:S(2)}, u32[]{:S(2)}) collective-permute-start(f32[256,256]{1,0:T(8,128)S(1)} %fusion.38), channel_id=1, source_target_pairs={{0,1},{1,0},{2,3},{3,2},{4,5},{5,4},{6,7},{7,6},{8,9},{9,8},{10,11... | collective-permute-start | bytes 786440 | tf_op jit(solution)/shard_map/ppermute | solution.py:183
  66.5 45.7 %copy-start.1 = (f32[256,8,128]{2,0,1:T(8,128)}, f32[256,8,128]{2,0,1:T(8,128)S(1)}, u32[]{:S(2)}) copy-start(f32[256,8,128]{2,0,1:T(8,128)S(1)} %get-tuple-element.91) | copy-start | bytes 3145732
  112.2 1.0 copy-start.3
  123.8 48.0 %all-to-all-start = ((bf16[16,256,256]{2,1,0:T(8,128)(2,1)}), bf16[16,256,256]{2,1,0:T(8,128)(2,1)S(1)}, u32[]{:S(2)}, u32[]{:S(2)}) async-start(bf16[16,256,256]{2,1,0:T(8,128)(2,1)} %bitcast.131), calls=%async_computation | async-start | bytes 4194304 | tf_op jit(solution)/shard_map/all_to_all | solution.py:174
  144.8 8.0 %collective-permute-start.16 = (f32[256,256]{1,0:T(8,128)S(1)}, f32[256,256]{1,0:T(8,128)S(1)}, u32[]{:S(2)}, u32[]{:S(2)}) collective-permute-start(f32[256,256]{1,0:T(8,128)S(1)} %add.110), channel_id=1, source_target_pairs={{0,2},{1,3},{2,0},{3,1},{4,6},{5,7},{6,4},{7,5},{8,10},{9,11},{10,... | collective-permute-start | bytes 786440 | tf_op jit(solution)/shard_map/ppermute | solution.py:183
  152.8 8.8 %collective-permute-start.17 = (f32[256,256]{1,0:T(8,128)S(1)}, f32[256,256]{1,0:T(8,128)S(1)}, u32[]{:S(2)}, u32[]{:S(2)}) collective-permute-start(f32[256,256]{1,0:T(8,128)S(1)} %add.111), channel_id=1, source_target_pairs={{0,4},{1,5},{2,6},{3,7},{4,0},{5,1},{6,2},{7,3},{8,12},{9,13},{10,... | collective-permute-start | bytes 786440 | tf_op jit(solution)/shard_map/ppermute | solution.py:183
  163.3 5.2 %copy-start.2 = (f32[256,8,128]{2,0,1:T(8,128)S(1)}, f32[256,8,128]{2,0,1:T(8,128)}, u32[]{:S(2)}) copy-start(f32[256,8,128]{2,0,1:T(8,128)} %copy-done.1) | copy-start | bytes 3145732
Sparse Core Ops, SparseCore 0:
  21.9 78.6 all-gather.1

commit v19 on v16

--- a/solution.py
+++ b/solution.py
@@ -170,6 +170,13 @@
     return total
 
 
+def exchange_gather(value, axis_name):
+    size = lax.axis_size(axis_name)
+    copies = jnp.broadcast_to(value[None], (size,) + value.shape)
+    arrived = lax.all_to_all(copies, axis_name, 0, 0, tiled=True)
+    return arrived.reshape((size * value.shape[0],) + value.shape[1:])
+
+
 def exchange_reduce(parts, axis_name):
     arrived = lax.all_to_all(parts, axis_name, 0, 0, tiled=True)
     return jnp.sum(arrived.astype(jnp.float32), axis=0)
@@ -221,11 +228,11 @@
         lax.all_gather(grad_out, "head", axis=1, tiled=True).astype(jnp.float32)
         * loss_weight[:, None]
     ).astype(jnp.bfloat16)
-    pair_all = causal_gather(jnp.concatenate([key_rows, value_rows], axis=1), "ctx")
+    pair_all = exchange_gather(jnp.concatenate([key_rows, value_rows], axis=1), "ctx")
     kv_width = key_rows.shape[1]
     keys_all, values_all = (pair_all[:, :kv_width], pair_all[:, kv_width:])
     tokens = keys_all.shape[0]
-    block_rows = math.gcd(512, tokens)
+    block_rows = math.gcd(1024, tokens)
 
     def fetch(table, block_number):
         return lax.dynamic_slice_in_dim(table, block_number * block_rows, block_rows, 0)

time: 186 us -> 179 us (0.962)
  starting transfers between devices: 76.6 us -> 34.5 us
  waiting for transfers between devices: 48.3 us -> 81.1 us
  matrix products: 22.9 us -> 25 us
    ppermute x15 -> x0, starting transfers between devices: 42.7 us -> none  [causal_gather(): received.append(lax.ppermute(value, axis_name, pairs))]
    all_to_all x0 -> x1, waiting for transfers between devices: none -> 28.3 us  [exchange_gather(): arrived = lax.all_to_all(copies, axis_name, 0, 0, tiled=True)]
    all_to_all x0 -> x1, starting transfers between devices: none -> 7.84 us  [exchange_gather(): arrived = lax.all_to_all(copies, axis_name, 0, 0, tiled=True)]
    all_to_all x1, starting transfers between devices: 26.8 us -> 22.3 us  [exchange_reduce(): arrived = lax.all_to_all(parts, axis_name, 0, 0, tiled=True)]
    unnamed x42 -> x14, local copies, waits for them, and re-layouts: 4.33 us -> 1.02 us
    ppermute x3, starting transfers between devices: 7.06 us -> 4.33 us  [butterfly_sum(): value = value + lax.ppermute(value, axis_name, pairs)]
    ppermute x3, waiting for transfers between devices: 12.3 us -> 15.1 us  [butterfly_sum(): value = value + lax.ppermute(value, axis_name, pairs)]
  transfers between devices with their start and end apart: 20 -> 6, of which waited for: 5 -> 5; matrix products, arithmetic and copies ran while one was open for 18% -> 19% of each run, Pallas kernels for 5% -> 6%
where the time goes in v19:
time: 179 us
  waiting for transfers between devices  81.1 us (45%)
  starting transfers between devices  34.5 us (19%)
  matrix products  25 us (14%)
  between operations  14.2 us (8%)
  Pallas kernels  10.5 us (6%)
  other arithmetic  7.18 us (4%)
  local copies, waits for them, and re-layouts  5.97 us (3%)
    all_gather x1, waiting for transfers between devices, body(): lax.all_gather(grad_out, 'head', axis=1, tiled=True).astype(jnp.float32)  35.3 us
    all_to_all x1, waiting for transfers between devices, exchange_gather(): arrived = lax.all_to_all(copies, axis_name, 0, 0, tiled=True)  28.3 us
    all_to_all x1, starting transfers between devices, exchange_reduce(): arrived = lax.all_to_all(parts, axis_name, 0, 0, tiled=True)  22.3 us
    ppermute x3, waiting for transfers between devices, butterfly_sum(): value = value + lax.ppermute(value, axis_name, pairs)  15.1 us
    dot_general x1, matrix products, body(): lax.dot_general(piece_part, out_weight, (((1,), (1,)), ((), ())), preferr...  11.6 us
    pallas_call x1, Pallas kernels, flash_backward(): pl.pallas_call(kernel, grid_spec=grid_spec, out_shape=[jax.ShapeDtypeStru...  10.5 us
    all_to_all x1, starting transfers between devices, exchange_gather(): arrived = lax.all_to_all(copies, axis_name, 0, 0, tiled=True)  7.84 us
    dot_general x1, matrix products, gram_squares(): lax.dot_general(left_side, left_side, (((1,), (1,)), ((), ())), preferred...  5.08 us
  transfers between devices with their start and end apart: 6, of which 5 were waited for; matrix products, arithmetic and copies ran while one was open for 19% of the time, Pallas kernels for 6%

profile of v19, /device:TPU:1, one launch (start us, length us, event | category | flops | bytes accessed | tf_op | source)
XLA Modules:
  0.0 178.7 jit_solution(14724138104206749491)
XLA Ops:
  7.2 1.0 pad_maximum_fusion
  8.2 1.5 broadcast_in_dim.44
  9.7 7.8 %all-to-all-start = ((bf16[16,256,256]{2,1,0:T(8,128)(2,1)}), bf16[16,256,256]{2,1,0:T(8,128)(2,1)}, u32[]{:S(2)}, u32[]{:S(2)}) async-start(bf16[16,256,256]{2,1,0:T(8,128)(2,1)} %broadcast_in_dim.44), calls=%async_computation | async-start | bytes 4194304 | tf_op jit(solution)/shard_map/all_to_all | solution.py:176
  18.6 2.7 %collective-permute-start = (f32[256,256]{1,0:T(8,128)S(1)}, f32[256,256]{1,0:T(8,128)}, u32[]{:S(2)}, u32[]{:S(2)}) collective-permute-start(f32[256,256]{1,0:T(8,128)S(1)} %fusion.44), channel_id=1, source_target_pairs={{0,1},{1,0},{2,3},{3,2},{4,5},{5,4},{6,7},{7,6},{8,9},{9,8},{10,11... | collective-permute-start | bytes 786440 | tf_op jit(solution)/shard_map/ppermute | solution.py:190
  21.3 0.9 copy.20
  22.9 28.3 %all-to-all-done = bf16[16,256,256]{2,1,0:T(8,128)(2,1)} async-done(((bf16[16,256,256]{2,1,0:T(8,128)(2,1)}), bf16[16,256,256]{2,1,0:T(8,128)(2,1)}, u32[]{:S(2)}, u32[]{:S(2)}) %all-to-all-start) | async-done | bytes 2097184 | tf_op jit(solution)/shard_map/all_to_all | solution.py:176
  51.3 2.7 %fusion.42 = (bf16[4096,128]{1,0:T(8,128)(2,1)}, bf16[4096,128]{1,0:T(8,128)(2,1)S(1)}) fusion(bf16[4096,256]{1,0:T(8,128)(2,1)} %bitcast.2), kind=kLoop, calls=%fused_computation.52 | loop fusion | bytes 4194304 | tf_op jit(solution)/shard_map/slice | solution.py:233
  54.0 3.4 %while.24 = (s32[]{:T(128)}, f32[256,8]{0,1:T(8,128)S(1)}, f32[256,8]{0,1:T(8,128)S(1)}, s32[]{:T(128)}, bf16[4096,128]{1,0:T(8,128)(2,1)S(1)}, /*index=5*/bf16[...) while((s32[]{:T(128)}, f32[256,8]{0,1:T(8,128)S(1)}, ...), condition=%wide.region_3.4_spmd.clone, body=%wide.region_0.3_spmd.clone.sunk | while | flops 551818496 | bytes 18466984 | solution.py:264
  54.2 1.4 fusion.59
  55.6 1.7 exponential_reduce_fusion.2
  57.5 4.8 %while.25 = (s32[]{:T(128)}, f32[256,8,128]{2,0,1:T(8,128)S(1)}, s32[]{:T(128)}, bf16[4096,128]{1,0:T(8,128)(2,1)S(1)}, bf16[256,8,128]{2,1,0:T(8,128)(2,1)}, /*...) while((s32[]{:T(128)}, f32[256,8,128]{2,0,1:T(8,128)S(1)}, ...), condition=%wide.region_5.6_spmd.clone, body=%wide.region_4.5_spmd.clone.sunk | while | flops 1082656000 | bytes 3689643 | solution.py:276
  57.7 4.4 %fusion.64 = f32[256,8,128]{2,0,1:T(8,128)S(1)} fusion(f32[256,8,128]{2,0,1:T(8,128)S(1)} %get-tuple-element.319, f32[256,8]{0,1:T(8,128)S(1)} %get-tuple-element.335, pred[256,1024]{1,0:T(8,128)(4,1)S(1)} %broadcast_compare_fusion.5, bf16[256,8,128]{2,1,0:T(8,128)(2,1)} %get-tuple-element.334, bf16[4096,128]{1,0:T(8,128)(2,1)} %get-tuple-element.336, ...), kind=kOutput, calls=%fused_computation.20.clone.1 | convolution fusion | flops 1082392576 | bytes 3417088 | tf_op jit(solution)/shard_map/while/body/tgk,kd->tgd/dot_general | solution.py:272
  62.3 35.3 %all-gather.2.cloned.1.call-done = bf16[256,8192]{1,0:T(8,128)(2,1)} async-done(((bf16[256,1024]{1,0:T(8,128)(2,1)}), bf16[256,8192]{1,0:T(8,128)(2,1)}) %all-gather.2.cloned.1.call-update) | async-done | bytes 4194320 | tf_op jit(solution)/shard_map/all_gather | solution.py:228
  97.6 11.6 %fusion.34.do_ref = bf16[256,1024]{1,0:T(8,128)(2,1)S(1)} fusion(bf16[1024,8192]{1,0:T(8,128)(2,1)} %param.15, bf16[256,8192]{1,0:T(8,128)(2,1)} %all-gather.2.cloned.1.call-done, f32[256]{0:T(256)S(1)} %convert_add_fusion), kind=kOutput, calls=%fused_computation.37 | convolution fusion | flops 4301520896 | bytes 21496832 | tf_op jit(solution)/shard_map/dot_general | solution.py:285
  109.2 1.0 fusion.35
  110.2 10.5 %shard_map.110 = (bf16[256,1024]{1,0:T(8,128)(2,1)}, bf16[4096,256]{1,0:T(8,128)(2,1)}) custom-call(s32[2]{0:T(128)} %pad_add_fusion.scalar_ref, bf16[256,1024]{1,0:T(8,128)(2,1)} %q_ref.1, bf16[256,1024]{1,0:T(8,128)(2,1)} %copy-done.4, bf16[4096,128]{1,0:T(8,128)(2,1)S(1)} %get-tuple-element.344, bf16[4096,128]{1,0:T(8,128)(2,1)} %get-tuple-element.346, ...), custom_call_target="tpu_custom_call" | custom-call | tf_op jit(solution)/shard_map/pallas_call | solution.py:118
  120.6 22.3 %all-to-all-start.1 = ((bf16[16,256,256]{2,1,0:T(8,128)(2,1)}), bf16[16,256,256]{2,1,0:T(8,128)(2,1)S(1)}, u32[]{:S(2)}, u32[]{:S(2)}) async-start(bf16[16,256,256]{2,1,0:T(8,128)(2,1)} %bitcast.81), calls=%async_computation.1 | async-start | bytes 4194304 | tf_op jit(solution)/shard_map/all_to_all | solution.py:181
  142.9 1.1 add.101
  144.1 7.8 %collective-permute-done.1 = f32[256,256]{1,0:T(8,128)S(1)} collective-permute-done((f32[256,256]{1,0:T(8,128)S(1)}, f32[256,256]{1,0:T(8,128)S(1)}, u32[]{:S(2)}, u32[]{:S(2)}) %collective-permute-start.1) | collective-permute-done | bytes 262176 | tf_op jit(solution)/shard_map/ppermute | solution.py:190
  152.0 1.5 collective-permute-start.2
  153.5 7.2 %collective-permute-done.2 = f32[256,256]{1,0:T(8,128)S(1)} collective-permute-done((f32[256,256]{1,0:T(8,128)S(1)}, f32[256,256]{1,0:T(8,128)S(1)}, u32[]{:S(2)}, u32[]{:S(2)}) %collective-permute-start.2) | collective-permute-done | bytes 262176 | tf_op jit(solution)/shard_map/ppermute | solution.py:190
  160.8 1.7 multiply_reduce_fusion.1
  162.5 5.1 %fusion.32 = f32[256,256]{1,0:T(8,128)S(1)} fusion(bf16[256,8192]{1,0:T(8,128)(2,1)} %all-gather.2.cloned.1.call-done, f32[256]{0:T(256)S(1)} %convert_add_fusion), kind=kOutput, calls=%fused_computation.35 | convolution fusion | flops 1080033280 | bytes 4457472 | tf_op jit(solution)/shard_map/dot_general | solution.py:205
  169.2 1.7 all-to-all-done.1
  (40 shorter events, 5.0 us)
Async XLA Ops:
  7.2 11.1 %copy-start = (bf16[256,1024]{1,0:T(8,128)(2,1)S(1)}, bf16[256,1024]{1,0:T(8,128)(2,1)}, u32[]{:S(2)}) copy-start(bf16[256,1024]{1,0:T(8,128)(2,1)} %param.11) | copy-start | bytes 1572868
  7.2 14.2 %copy-start.1 = (bf16[256,1024]{1,0:T(8,128)(2,1)S(1)}, bf16[256,1024]{1,0:T(8,128)(2,1)}, u32[]{:S(2)}) copy-start(bf16[256,1024]{1,0:T(8,128)(2,1)} %q_ref.1) | copy-start | bytes 1572868
  7.2 15.6 %copy-start.5 = (s32[256]{0:T(256)S(1)}, s32[256]{0:T(256)}, u32[]{:S(2)}) copy-start(s32[256]{0:T(256)} %param.17) | copy-start | bytes 3076
  9.7 41.6 %all-to-all-start = ((bf16[16,256,256]{2,1,0:T(8,128)(2,1)}), bf16[16,256,256]{2,1,0:T(8,128)(2,1)}, u32[]{:S(2)}, u32[]{:S(2)}) async-start(bf16[16,256,256]{2,1,0:T(8,128)(2,1)} %broadcast_in_dim.44), calls=%async_computation | async-start | bytes 4194304 | tf_op jit(solution)/shard_map/all_to_all | solution.py:176
  17.6 80.0 %all-gather.2.cloned.1.call-start = ((), (), s32[]{:S(2)}) async-start(), calls=%async_computation.2 | async-start | bytes 4718592 | tf_op jit(solution)/shard_map/all_gather | solution.py:228
  18.6 124.3 %collective-permute-start = (f32[256,256]{1,0:T(8,128)S(1)}, f32[256,256]{1,0:T(8,128)}, u32[]{:S(2)}, u32[]{:S(2)}) collective-permute-start(f32[256,256]{1,0:T(8,128)S(1)} %fusion.44), channel_id=1, source_target_pairs={{0,1},{1,0},{2,3},{3,2},{4,5},{5,4},{6,7},{7,6},{8,9},{9,8},{10,11... | collective-permute-start | bytes 786440 | tf_op jit(solution)/shard_map/ppermute | solution.py:190
  62.3 46.9 %copy-start.2 = (f32[256,8,128]{2,0,1:T(8,128)}, f32[256,8,128]{2,0,1:T(8,128)S(1)}, u32[]{:S(2)}) copy-start(f32[256,8,128]{2,0,1:T(8,128)S(1)} %get-tuple-element.91) | copy-start | bytes 3145732
  109.2 1.0 copy-start.4
  120.6 50.3 %all-to-all-start.1 = ((bf16[16,256,256]{2,1,0:T(8,128)(2,1)}), bf16[16,256,256]{2,1,0:T(8,128)(2,1)S(1)}, u32[]{:S(2)}, u32[]{:S(2)}) async-start(bf16[16,256,256]{2,1,0:T(8,128)(2,1)} %bitcast.81), calls=%async_computation.1 | async-start | bytes 4194304 | tf_op jit(solution)/shard_map/all_to_all | solution.py:181
  142.9 24.7 %copy-start.3 = (f32[256,8,128]{2,0,1:T(8,128)S(1)}, f32[256,8,128]{2,0,1:T(8,128)}, u32[]{:S(2)}) copy-start(f32[256,8,128]{2,0,1:T(8,128)} %copy-done.2) | copy-start | bytes 3145732
  144.0 8.0 %collective-permute-start.1 = (f32[256,256]{1,0:T(8,128)S(1)}, f32[256,256]{1,0:T(8,128)S(1)}, u32[]{:S(2)}, u32[]{:S(2)}) collective-permute-start(f32[256,256]{1,0:T(8,128)S(1)} %add.101), channel_id=1, source_target_pairs={{0,2},{1,3},{2,0},{3,1},{4,6},{5,7},{6,4},{7,5},{8,10},{9,11},{10,... | collective-permute-start | bytes 786440 | tf_op jit(solution)/shard_map/ppermute | solution.py:190
  152.0 8.8 %collective-permute-start.2 = (f32[256,256]{1,0:T(8,128)S(1)}, f32[256,256]{1,0:T(8,128)S(1)}, u32[]{:S(2)}, u32[]{:S(2)}) collective-permute-start(f32[256,256]{1,0:T(8,128)S(1)} %add.102), channel_id=1, source_target_pairs={{0,4},{1,5},{2,6},{3,7},{4,0},{5,1},{6,2},{7,3},{8,12},{9,13},{10,... | collective-permute-start | bytes 786440 | tf_op jit(solution)/shard_map/ppermute | solution.py:190
Sparse Core Ops, SparseCore 0:
  20.7 76.8 all-gather.1

commit v20 on v19

--- a/solution.py
+++ b/solution.py
@@ -218,17 +218,16 @@
     first_row = own_index * tok_dev
     loss_weight = 0.25 + answer_mask.astype(jnp.float32)
     weighted = (grad_out.astype(jnp.float32) * loss_weight[:, None]).astype(jnp.bfloat16)
-    hidden_gram = butterfly_sum(
-        lax.dot_general(
-            hidden_in, hidden_in, (((1,), (1,)), ((), ())), preferred_element_type=jnp.float32
-        ),
-        "head",
+    gram_part = lax.dot_general(
+        hidden_in, hidden_in, (((1,), (1,)), ((), ())), preferred_element_type=jnp.float32
     )
     piece_part = (
         lax.all_gather(grad_out, "head", axis=1, tiled=True).astype(jnp.float32)
         * loss_weight[:, None]
     ).astype(jnp.bfloat16)
     pair_all = exchange_gather(jnp.concatenate([key_rows, value_rows], axis=1), "ctx")
+    gram_part, pair_all = lax.optimization_barrier((gram_part, pair_all))
+    hidden_gram = butterfly_sum(gram_part, "head")
     kv_width = key_rows.shape[1]
     keys_all, values_all = (pair_all[:, :kv_width], pair_all[:, kv_width:])
     tokens = keys_all.shape[0]
@@ -287,6 +286,7 @@
     )
     grad_sum, squares_out = (grad_sum, gram_squares(piece_part, attended, head_dim))
     grad_attended, squares_out = (grad_sum.astype(jnp.bfloat16), squares_out)
+    hidden_gram, grad_attended = lax.optimization_barrier((hidden_gram, grad_attended))
     backward_buffer = buffer
     rows = query_rows.shape[0]
     backward_row_pos = first_row + jnp.arange(rows, dtype=jnp.int32)

time: 179 us -> 182 us (1.017)
  starting transfers between devices: 34.5 us -> 39 us
  waiting for transfers between devices: 81.1 us -> 77.2 us
    all_gather x1, waiting for transfers between devices: 35.3 us -> 15.2 us  [body(): lax.all_gather(grad_out, 'head', axis=1, tiled=True).astype(jnp.float32)]
    all_to_all x1, waiting for transfers between devices: 1.7 us -> 20.2 us  [exchange_reduce(): arrived = lax.all_to_all(parts, axis_name, 0, 0, tiled=True)]
    ppermute x3, waiting for transfers between devices: 15.1 us -> 11.8 us  [butterfly_sum(): value = value + lax.ppermute(value, axis_name, pairs)]
    ppermute x3, starting transfers between devices: 4.33 us -> 7.43 us  [butterfly_sum(): value = value + lax.ppermute(value, axis_name, pairs)]
  transfers between devices with their start and end apart: 6 -> 6, of which waited for: 5 -> 6; matrix products, arithmetic and copies ran while one was open for 19% -> 13% of each run, Pallas kernels for 6% -> 0%
where the time goes in v20:
time: 182 us
  waiting for transfers between devices  77.2 us (42%)
  starting transfers between devices  39 us (21%)
  matrix products  25 us (14%)
  between operations  14.2 us (8%)
  Pallas kernels  10.4 us (6%)
  other arithmetic  8.62 us (5%)
  local copies, waits for them, and re-layouts  7.01 us (4%)
    all_to_all x1, waiting for transfers between devices, exchange_gather(): arrived = lax.all_to_all(copies, axis_name, 0, 0, tiled=True)  29.3 us
    all_to_all x1, starting transfers between devices, exchange_reduce(): arrived = lax.all_to_all(parts, axis_name, 0, 0, tiled=True)  23.7 us
    all_to_all x1, waiting for transfers between devices, exchange_reduce(): arrived = lax.all_to_all(parts, axis_name, 0, 0, tiled=True)  20.2 us
    all_gather x1, waiting for transfers between devices, body(): lax.all_gather(grad_out, 'head', axis=1, tiled=True).astype(jnp.float32)  15.2 us
    ppermute x3, waiting for transfers between devices, butterfly_sum(): value = value + lax.ppermute(value, axis_name, pairs)  11.8 us
    dot_general x1, matrix products, body(): lax.dot_general(piece_part, out_weight, (((1,), (1,)), ((), ())), preferr...  11.6 us
    pallas_call x1, Pallas kernels, flash_backward(): pl.pallas_call(kernel, grid_spec=grid_spec, out_shape=[jax.ShapeDtypeStru...  10.4 us
    all_to_all x1, starting transfers between devices, exchange_gather(): arrived = lax.all_to_all(copies, axis_name, 0, 0, tiled=True)  7.84 us
  transfers between devices with their start and end apart: 6, of which 6 were waited for; matrix products, arithmetic and copies ran while one was open for 13% of the time, Pallas kernels for 0%

profile of v20, /device:TPU:1, one launch (start us, length us, event | category | flops | bytes accessed | tf_op | source)
XLA Modules:
  0.0 181.8 jit_solution(4079873977538674958)
XLA Ops:
  7.2 1.0 pad_maximum_fusion
  8.2 1.5 broadcast_in_dim.44
  9.7 7.8 %all-to-all-start = ((bf16[16,256,256]{2,1,0:T(8,128)(2,1)}), bf16[16,256,256]{2,1,0:T(8,128)(2,1)}, u32[]{:S(2)}, u32[]{:S(2)}) async-start(bf16[16,256,256]{2,1,0:T(8,128)(2,1)} %broadcast_in_dim.44), calls=%async_computation | async-start | bytes 4194304 | tf_op jit(solution)/shard_map/all_to_all | solution.py:176
  18.3 1.9 %copy.20 = bf16[32,8,8,128]{3,2,1,0:T(8,128)(2,1)} copy(bf16[32,8,8,128]{3,1,2,0:T(8,128)(2,1)} %bitcast.80) | data formatting | bytes 1048576
  22.0 29.3 %all-to-all-done = bf16[16,256,256]{2,1,0:T(8,128)(2,1)} async-done(((bf16[16,256,256]{2,1,0:T(8,128)(2,1)}), bf16[16,256,256]{2,1,0:T(8,128)(2,1)}, u32[]{:S(2)}, u32[]{:S(2)}) %all-to-all-start) | async-done | bytes 2097184 | tf_op jit(solution)/shard_map/all_to_all | solution.py:176
  51.3 2.6 %collective-permute-start = (f32[256,256]{1,0:T(8,128)S(1)}, f32[256,256]{1,0:T(8,128)S(1)}, u32[]{:S(2)}, u32[]{:S(2)}) collective-permute-start(f32[256,256]{1,0:T(8,128)S(1)} %fusion.44), channel_id=1, source_target_pairs={{0,1},{1,0},{2,3},{3,2},{4,5},{5,4},{6,7},{7,6},{8,9},{9,8},{10,11... | collective-permute-start | bytes 786440 | tf_op jit(solution)/shard_map/ppermute | solution.py:190
  53.9 2.7 %fusion.42 = (bf16[4096,128]{1,0:T(8,128)(2,1)}, bf16[4096,128]{1,0:T(8,128)(2,1)S(1)}) fusion(bf16[4096,256]{1,0:T(8,128)(2,1)} %bitcast.2), kind=kLoop, calls=%fused_computation.52 | loop fusion | bytes 4194304 | tf_op jit(solution)/shard_map/slice | solution.py:232
  56.6 3.2 %collective-permute-done = f32[256,256]{1,0:T(8,128)S(1)} collective-permute-done((f32[256,256]{1,0:T(8,128)S(1)}, f32[256,256]{1,0:T(8,128)S(1)}, u32[]{:S(2)}, u32[]{:S(2)}) %collective-permute-start) | collective-permute-done | bytes 262176 | tf_op jit(solution)/shard_map/ppermute | solution.py:190
  59.8 1.3 collective-permute-start.1
  61.1 3.4 %while.24 = (s32[]{:T(128)}, f32[256,8]{0,1:T(8,128)S(1)}, f32[256,8]{0,1:T(8,128)S(1)}, s32[]{:T(128)}, bf16[4096,128]{1,0:T(8,128)(2,1)S(1)}, /*index=5*/bf16[...) while((s32[]{:T(128)}, f32[256,8]{0,1:T(8,128)S(1)}, ...), condition=%wide.region_3.4_spmd.clone, body=%wide.region_0.3_spmd.clone.sunk | while | flops 551818496 | bytes 18466984 | solution.py:263
  61.3 1.4 fusion.59
  62.7 1.7 exponential_reduce_fusion.2
  64.5 7.7 %collective-permute-done.1 = f32[256,256]{1,0:T(8,128)S(1)} collective-permute-done((f32[256,256]{1,0:T(8,128)S(1)}, f32[256,256]{1,0:T(8,128)S(1)}, u32[]{:S(2)}, u32[]{:S(2)}) %collective-permute-start.1) | collective-permute-done | bytes 262176 | tf_op jit(solution)/shard_map/ppermute | solution.py:190
  72.2 3.5 %collective-permute-start.2 = (f32[256,256]{1,0:T(8,128)S(1)}, f32[256,256]{1,0:T(8,128)S(1)}, u32[]{:S(2)}, u32[]{:S(2)}) collective-permute-start(f32[256,256]{1,0:T(8,128)S(1)} %add.97), channel_id=1, source_target_pairs={{0,4},{1,5},{2,6},{3,7},{4,0},{5,1},{6,2},{7,3},{8,12},{9,13},{10,... | collective-permute-start | bytes 786440 | tf_op jit(solution)/shard_map/ppermute | solution.py:190
  75.8 4.9 %while.25 = (s32[]{:T(128)}, f32[256,8,128]{2,0,1:T(8,128)S(1)}, s32[]{:T(128)}, bf16[4096,128]{1,0:T(8,128)(2,1)S(1)}, bf16[256,8,128]{2,1,0:T(8,128)(2,1)}, /*...) while((s32[]{:T(128)}, f32[256,8,128]{2,0,1:T(8,128)S(1)}, ...), condition=%wide.region_5.6_spmd.clone, body=%wide.region_4.5_spmd.clone.sunk | while | flops 1082656000 | bytes 3689643 | solution.py:275
  76.1 4.4 %fusion.64 = f32[256,8,128]{2,0,1:T(8,128)S(1)} fusion(f32[256,8,128]{2,0,1:T(8,128)S(1)} %get-tuple-element.329, f32[256,8]{0,1:T(8,128)S(1)} %get-tuple-element.345, pred[256,1024]{1,0:T(8,128)(4,1)S(1)} %broadcast_compare_fusion.5, bf16[256,8,128]{2,1,0:T(8,128)(2,1)} %get-tuple-element.344, bf16[4096,128]{1,0:T(8,128)(2,1)} %get-tuple-element.346, ...), kind=kOutput, calls=%fused_computation.20.clone.1 | convolution fusion | flops 1082392576 | bytes 3417088 | tf_op jit(solution)/shard_map/while/body/tgk,kd->tgd/dot_general | solution.py:271
  82.3 15.2 %all-gather.2.cloned.1.call-done = bf16[256,8192]{1,0:T(8,128)(2,1)} async-done(((bf16[256,1024]{1,0:T(8,128)(2,1)}), bf16[256,8192]{1,0:T(8,128)(2,1)}) %all-gather.2.cloned.1.call-update) | async-done | bytes 4194320 | tf_op jit(solution)/shard_map/all_gather | solution.py:225
  97.6 11.6 %fusion.34.do_ref = bf16[256,1024]{1,0:T(8,128)(2,1)S(1)} fusion(bf16[1024,8192]{1,0:T(8,128)(2,1)} %param.15, bf16[256,8192]{1,0:T(8,128)(2,1)} %all-gather.2.cloned.1.call-done, f32[256]{0:T(256)S(1)} %convert_add_fusion), kind=kOutput, calls=%fused_computation.37 | convolution fusion | flops 4301520896 | bytes 21496832 | tf_op jit(solution)/shard_map/dot_general | solution.py:284
  110.2 10.4 %shard_map.110 = (bf16[256,1024]{1,0:T(8,128)(2,1)}, bf16[4096,256]{1,0:T(8,128)(2,1)}) custom-call(s32[2]{0:T(128)} %pad_add_fusion.scalar_ref, bf16[256,1024]{1,0:T(8,128)(2,1)} %q_ref.1, bf16[256,1024]{1,0:T(8,128)(2,1)} %copy-done.2, bf16[4096,128]{1,0:T(8,128)(2,1)S(1)} %get-tuple-element.354, bf16[4096,128]{1,0:T(8,128)(2,1)} %get-tuple-element.357, ...), custom_call_target="tpu_custom_call" | custom-call | tf_op jit(solution)/shard_map/pallas_call | solution.py:118
  120.6 23.7 %all-to-all-start.1 = ((bf16[16,256,256]{2,1,0:T(8,128)(2,1)}), bf16[16,256,256]{2,1,0:T(8,128)(2,1)}, u32[]{:S(2)}, u32[]{:S(2)}) async-start(bf16[16,256,256]{2,1,0:T(8,128)(2,1)} %bitcast.81), calls=%async_computation.1 | async-start | bytes 4194304 | tf_op jit(solution)/shard_map/all_to_all | solution.py:181
  144.3 1.7 multiply_reduce_fusion.1
  146.0 5.1 %fusion.32 = f32[256,256]{1,0:T(8,128)S(1)} fusion(bf16[256,8192]{1,0:T(8,128)(2,1)} %all-gather.2.cloned.1.call-done, f32[256]{0:T(256)S(1)} %convert_add_fusion), kind=kOutput, calls=%fused_computation.35 | convolution fusion | flops 1080033280 | bytes 4457472 | tf_op jit(solution)/shard_map/dot_general | solution.py:205
  152.2 20.2 %all-to-all-done.1 = bf16[16,256,256]{2,1,0:T(8,128)(2,1)} async-done(((bf16[16,256,256]{2,1,0:T(8,128)(2,1)}), bf16[16,256,256]{2,1,0:T(8,128)(2,1)}, u32[]{:S(2)}, u32[]{:S(2)}) %all-to-all-start.1) | async-done | bytes 2097184 | tf_op jit(solution)/shard_map/all_to_all | solution.py:181
  172.4 1.9 %reduce = bf16[256,256]{1,0:T(8,128)(2,1)S(1)} reduce(bf16[16,256,256]{2,1,0:T(8,128)(2,1)} %all-to-all-done.1, bf16[]{:T(256)} %constant.73), dimensions={0}, to_apply=%region_7.8.clone | reduce | flops 983040 | bytes 2228226 | tf_op jit(solution)/shard_map/reduce_sum | solution.py:182
  (35 shorter events, 7.4 us)
Async XLA Ops:
  7.2 14.4 %copy-start = (bf16[256,1024]{1,0:T(8,128)(2,1)S(1)}, bf16[256,1024]{1,0:T(8,128)(2,1)}, u32[]{:S(2)}) copy-start(bf16[256,1024]{1,0:T(8,128)(2,1)} %param.11) | copy-start | bytes 1572868
  7.2 14.3 %copy-start.1 = (bf16[256,1024]{1,0:T(8,128)(2,1)S(1)}, bf16[256,1024]{1,0:T(8,128)(2,1)}, u32[]{:S(2)}) copy-start(bf16[256,1024]{1,0:T(8,128)(2,1)} %q_ref.1) | copy-start | bytes 1572868
  9.7 41.6 %all-to-all-start = ((bf16[16,256,256]{2,1,0:T(8,128)(2,1)}), bf16[16,256,256]{2,1,0:T(8,128)(2,1)}, u32[]{:S(2)}, u32[]{:S(2)}) async-start(bf16[16,256,256]{2,1,0:T(8,128)(2,1)} %broadcast_in_dim.44), calls=%async_computation | async-start | bytes 4194304 | tf_op jit(solution)/shard_map/all_to_all | solution.py:176
  17.6 80.0 %all-gather.2.cloned.1.call-start = ((), (), s32[]{:S(2)}) async-start(), calls=%async_computation.2 | async-start | bytes 4718592 | tf_op jit(solution)/shard_map/all_gather | solution.py:225
  51.3 8.5 %collective-permute-start = (f32[256,256]{1,0:T(8,128)S(1)}, f32[256,256]{1,0:T(8,128)S(1)}, u32[]{:S(2)}, u32[]{:S(2)}) collective-permute-start(f32[256,256]{1,0:T(8,128)S(1)} %fusion.44), channel_id=1, source_target_pairs={{0,1},{1,0},{2,3},{3,2},{4,5},{5,4},{6,7},{7,6},{8,9},{9,8},{10,11... | collective-permute-start | bytes 786440 | tf_op jit(solution)/shard_map/ppermute | solution.py:190
  59.8 12.4 %collective-permute-start.1 = (f32[256,256]{1,0:T(8,128)S(1)}, f32[256,256]{1,0:T(8,128)S(1)}, u32[]{:S(2)}, u32[]{:S(2)}) collective-permute-start(f32[256,256]{1,0:T(8,128)S(1)} %add.96), channel_id=1, source_target_pairs={{0,2},{1,3},{2,0},{3,1},{4,6},{5,7},{6,4},{7,5},{8,10},{9,11},{10,... | collective-permute-start | bytes 786440 | tf_op jit(solution)/shard_map/ppermute | solution.py:190
  72.2 9.3 %collective-permute-start.2 = (f32[256,256]{1,0:T(8,128)S(1)}, f32[256,256]{1,0:T(8,128)S(1)}, u32[]{:S(2)}, u32[]{:S(2)}) collective-permute-start(f32[256,256]{1,0:T(8,128)S(1)} %add.97), channel_id=1, source_target_pairs={{0,4},{1,5},{2,6},{3,7},{4,0},{5,1},{6,2},{7,3},{8,12},{9,13},{10,... | collective-permute-start | bytes 786440 | tf_op jit(solution)/shard_map/ppermute | solution.py:190
  109.2 1.0 copy-start.2
  109.2 35.1 %copy-start.3 = (f32[256,256]{1,0:T(8,128)S(1)}, f32[256,256]{1,0:T(8,128)}, u32[]{:S(2)}) copy-start(f32[256,256]{1,0:T(8,128)} %add.98) | copy-start | bytes 786436
  120.6 51.8 %all-to-all-start.1 = ((bf16[16,256,256]{2,1,0:T(8,128)(2,1)}), bf16[16,256,256]{2,1,0:T(8,128)(2,1)}, u32[]{:S(2)}, u32[]{:S(2)}) async-start(bf16[16,256,256]{2,1,0:T(8,128)(2,1)} %bitcast.81), calls=%async_computation.1 | async-start | bytes 4194304 | tf_op jit(solution)/shard_map/all_to_all | solution.py:181
Sparse Core Ops, SparseCore 0:
  20.7 76.8 all-gather.1
